TPU v7x, 32 devices: a whole 2x2x4 slice. The times are simulated.
32 devices in a mesh: groups: 2 (over x), row: 8 (over z, y), col: 2 (over core).
Axes of the slice: x: 2, y: 2, z: 4, core: 2. Of those that a mesh axis runs over, the one named last changes fastest.
Arguments:
- tokens: bfloat16 [512, 16384], P(('groups', 'col'), 'row'), parts along dimension 0, may hold values from -6 to 6
- q_weight: bfloat16 [16384, 8192], P('row', 'col'), may hold values from -0.046875 to 0.046875
- key_matrix: bfloat16 [16384, 512], P('row', 'col'), may hold values from -0.046875 to 0.046875
- value_matrix: bfloat16 [16384, 512], P('row', 'col'), may hold values from -0.046875 to 0.046875
- o_weight: bfloat16 [8192, 16384], P('col', 'row'), may hold values from -0.0625 to 0.0625
- k_cache: bfloat16 [32, 1536, 4, 128], P(('groups', 'row'), None, 'col'), parts along dimension 0, may hold values from -200 to 200
- value_cache: bfloat16 [32, 1536, 4, 128], P(('groups', 'row'), None, 'col'), parts along dimension 0, may hold values from -6 to 6
- cache_len: int32 [32], P('groups'), parts along dimension 0, may hold values from 1 to 1536, 12288 in all
- slot_seq: int32 [32], P('groups'), parts along dimension 0, may hold values from 0 to 15, each once
Outputs:
- layer_out: bfloat16 [512, 16384], P(('groups', 'col'), 'row'), parts along dimension 0
There are 2 independent parts, one for each index of `groups`. A program takes and returns all parts, laid end to end along the dimension named above; an argument that names none is the same for every part. Nothing has to cross between parts.
Inputs may be any that keep to these rules, and one draw needn't show every extreme that they name: `cache_len`: every sequence has at least one cached token and at most 1536; some sequence has exactly 1536. `slot_seq`: each sequence stands in exactly one slot.
All inputs are finite; a program needn't handle non-finite values.
Results may differ from a plain program's by a relative error of at most 0.038.
Values may be sent and summed in bfloat16 or wider, within the bound.
No kernel may reach another device: no remote copies, remote signals or barrier semaphores. Data moves between devices by JAX's collectives and lax.ppermute only.
A program may use at most 128 MiB of HBM per device.

v0:
```python
import math

import jax
import jax.numpy as jnp
from jax import lax
from jax.sharding import PartitionSpec as P

ROPE_BASE = 500000.0


def apply_turning(values, token_places):
    half_dim = values.shape[-1] // 2
    frequency = ROPE_BASE ** (-(2.0 * jnp.arange(half_dim, dtype=jnp.float32)) / values.shape[-1])
    angles = token_places[:, None] * frequency[None, :]
    cosine = jnp.cos(angles)[:, None, :]
    sine_part = jnp.sin(angles)[:, None, :]
    leading = values[..., :half_dim]
    trailing = values[..., half_dim:]
    return jnp.concatenate(
        [leading * cosine - trailing * sine_part, trailing * cosine + leading * sine_part], axis=-1
    )


def attend(queries, incoming_keys, incoming_values, cached_keys, cached_values, length):
    tokens_new, kv_heads, head_dim = incoming_keys.shape
    grouped = queries.reshape(tokens_new, kv_heads, -1, head_dim)
    scale_factor = 1.0 / math.sqrt(head_dim)
    cache_scores = (
        jnp.einsum("nkgd,ckd->kgnc", grouped, cached_keys, preferred_element_type=jnp.float32)
        * scale_factor
    )
    valid_cache = jnp.arange(cached_keys.shape[0]) < length
    cache_scores = jnp.where(valid_cache, cache_scores, -jnp.inf)
    fresh_scores = (
        jnp.einsum("nkgd,mkd->kgnm", grouped, incoming_keys, preferred_element_type=jnp.float32)
        * scale_factor
    )
    causal = jnp.arange(tokens_new)[None, :] <= jnp.arange(tokens_new)[:, None]
    fresh_scores = jnp.where(causal, fresh_scores, -jnp.inf)
    highest = jnp.maximum(jnp.max(cache_scores, axis=-1), jnp.max(fresh_scores, axis=-1))
    cache_weights = jnp.exp(cache_scores - highest[..., None])
    fresh_weights = jnp.exp(fresh_scores - highest[..., None])
    totals = jnp.sum(cache_weights, axis=-1) + jnp.sum(fresh_weights, axis=-1)
    weighted = jnp.einsum(
        "kgnc,ckd->nkgd",
        cache_weights.astype(jnp.bfloat16),
        cached_values,
        preferred_element_type=jnp.float32,
    )
    weighted = weighted + jnp.einsum(
        "kgnm,mkd->nkgd",
        fresh_weights.astype(jnp.bfloat16),
        incoming_values,
        preferred_element_type=jnp.float32,
    )
    normed = weighted / jnp.transpose(totals, (2, 0, 1))[..., None]
    return normed.reshape(tokens_new, -1).astype(jnp.bfloat16)


def body(
    tokens, q_weight, key_matrix, value_matrix, o_weight, k_cache, value_cache, cache_len, slot_seq
):
    row_index = lax.axis_index("row")
    seq_dev = k_cache.shape[0]
    head_dim = k_cache.shape[3]
    slot_total = slot_seq.shape[0]
    gathered = lax.all_gather(tokens, "col", axis=0, tiled=True)
    new_len = gathered.shape[0] // slot_total
    slot_list = jnp.arange(slot_total)
    sequences = slot_seq[slot_list]
    row_ids = (sequences[:, None] * new_len + jnp.arange(new_len)[None, :]).reshape(-1)
    chosen = gathered[row_ids]
    q_part = jnp.dot(chosen, q_weight, preferred_element_type=jnp.float32)
    k_part = jnp.dot(chosen, key_matrix, preferred_element_type=jnp.float32)
    v_part = jnp.dot(chosen, value_matrix, preferred_element_type=jnp.float32)
    q_part, k_part, v_part = (q_part, k_part, v_part)
    q_sum = lax.psum_scatter(
        q_part.astype(jnp.bfloat16), "row", scatter_dimension=0, tiled=True
    ).astype(jnp.float32)
    key_total_sum = lax.psum_scatter(
        k_part.astype(jnp.bfloat16), "row", scatter_dimension=0, tiled=True
    ).astype(jnp.float32)
    value_total_sum = lax.psum_scatter(
        v_part.astype(jnp.bfloat16), "row", scatter_dimension=0, tiled=True
    ).astype(jnp.float32)
    local_slots = row_index * seq_dev + jnp.arange(seq_dev)
    sequences = slot_seq[local_slots]
    starts = cache_len[sequences]
    token_places = (starts[:, None] + jnp.arange(new_len)[None, :]).reshape(-1).astype(jnp.float32)
    row_total = q_sum.shape[0]
    queries = apply_turning(q_sum.reshape(row_total, -1, head_dim), token_places).astype(
        jnp.bfloat16
    )
    rotated_keys = apply_turning(
        key_total_sum.reshape(row_total, -1, head_dim), token_places
    ).astype(jnp.bfloat16)
    values = value_total_sum.reshape(row_total, -1, head_dim).astype(jnp.bfloat16)
    results = jax.vmap(attend)(
        queries.reshape(seq_dev, new_len, -1, head_dim),
        rotated_keys.reshape(seq_dev, new_len, -1, head_dim),
        values.reshape(seq_dev, new_len, -1, head_dim),
        k_cache,
        value_cache,
        starts,
    )
    attended = results.reshape(seq_dev * new_len, -1)
    products = jnp.dot(
        lax.all_gather(attended, "row", axis=0, tiled=True),
        o_weight,
        preferred_element_type=jnp.float32,
    )
    matches = (slot_seq[:, None] == jnp.arange(slot_total)[None, :]).astype(jnp.int32)
    slot_of = jnp.sum(matches * jnp.arange(slot_total)[:, None], axis=0)
    row_order = (slot_of[:, None] * new_len + jnp.arange(new_len)[None, :]).reshape(-1)
    ordered = products[row_order]
    return lax.psum_scatter(ordered.astype(jnp.bfloat16), "col", scatter_dimension=0, tiled=True)


def solution(mesh):
    return jax.shard_map(
        body,
        mesh=mesh,
        in_specs=(
            P(("groups", "col"), "row"),
            P("row", "col"),
            P("row", "col"),
            P("row", "col"),
            P("col", "row"),
            P(("groups", "row"), None, "col", None),
            P(("groups", "row"), None, "col", None),
            P("groups"),
            P("groups"),
        ),
        out_specs=P(("groups", "col"), "row"),
        check_vma=False,
    )
```

profile of v0, /device:TPU:0, one launch (start us, length us, event | category | flops | bytes accessed | tf_op | source)
XLA Modules:
  0.0 308.8 jit_solution(259567492452346959)
XLA Ops:
  6.5 0.7 all-gather.3.cloned.1.call-update
  7.3 1.3 gather_fusion.2
  8.8 11.8 %all-gather.3.cloned.1.call-done = bf16[256,2048]{1,0:T(8,128)(2,1)} async-done(((bf16[128,2048]{1,0:T(8,128)(2,1)}), bf16[256,2048]{1,0:T(8,128)(2,1)}) %all-gather.3.cloned.1.call-update) | async-done | bytes 1048592 | tf_op jit(solution)/shard_map/all_gather | solution.py:67
  20.7 3.7 %gather_fusion.3 = bf16[256,2048]{1,0:T(8,128)(2,1)S(1)} fusion(bf16[256,2048]{1,0:T(8,128)(2,1)} %all-gather.3.cloned.1.call-done, s32[1024]{0:T(1024)S(1)} %pad_clamp_fusion.1), kind=kCustom, calls=%fused_computation.3 | custom fusion | bytes 2098176 | tf_op jit(solution)/shard_map/gather | solution.py:72
  24.4 2.3 convolution_convert_fusion.2
  26.8 2.3 convolution_convert_fusion.1
  29.3 11.5 %convolution_convert_fusion = bf16[256,4096]{1,0:T(8,128)(2,1)} fusion(bf16[256,2048]{1,0:T(8,128)(2,1)S(1)} %gather_fusion.3, bf16[2048,4096]{1,0:T(8,128)(2,1)} %param.10), kind=kOutput, calls=%fused_computation.9 | convolution fusion | flops 4296015872 | bytes 19922944 | tf_op jit(solution)/shard_map/dot_general | solution.py:73
  40.9 0.6 gather_fusion
  41.6 0.6 gather_fusion.1
  42.4 0.1 multiply_cosine_fusion
  42.6 47.7 %reduce-scatter.7.cloned.1.call-done = bf16[32,256]{1,0:T(8,128)(2,1)} async-done(((bf16[256,256]{1,0:T(8,128)(2,1)}), bf16[32,256]{1,0:T(8,128)(2,1)}) %reduce-scatter.7.cloned.1.call-update) | async-done | bytes 16400 | tf_op jit(solution)/shard_map/reduce_scatter | solution.py:80
  90.3 0.7 reshape.210
  91.1 63.5 %reduce-scatter.9.cloned.1.call-done = bf16[32,256]{1,0:T(8,128)(2,1)} async-done(((bf16[256,256]{1,0:T(8,128)(2,1)}), bf16[32,256]{1,0:T(8,128)(2,1)}) %reduce-scatter.9.cloned.1.call-update) | async-done | bytes 16400 | tf_op jit(solution)/shard_map/reduce_scatter | solution.py:83
  154.6 0.7 convert_element_type.54
  155.3 0.1 fusion.31
  155.4 69.9 %reduce-scatter.5.cloned.1.call-done = bf16[32,4096]{1,0:T(8,128)(2,1)} async-done(((bf16[256,4096]{1,0:T(8,128)(2,1)}), bf16[32,4096]{1,0:T(8,128)(2,1)}) %reduce-scatter.5.cloned.1.call-update) | async-done | bytes 262160 | tf_op jit(solution)/shard_map/reduce_scatter | solution.py:77
  225.3 1.0 convert_bitcast_fusion
  226.3 0.1 copy.67
  226.4 0.2 subtract_convert_fusion
  226.6 1.3 bitcast_reduce_fusion
  227.9 0.8 fusion.32
  228.8 0.2 fusion.19
  228.9 1.4 fusion.1
  230.3 1.8 fusion.9
  232.1 0.3 fusion.18
  232.5 0.8 convert_element_type.57
  233.3 0.2 reduce-scatter.11.cloned.1.call-start
  233.5 0.1 select_reduce_fusion
  233.8 47.8 %all-gather.5.cloned.1.call-done = bf16[256,4096]{1,0:T(8,128)(2,1)} async-done(((bf16[32,4096]{1,0:T(8,128)(2,1)}), bf16[256,4096]{1,0:T(8,128)(2,1)}) %all-gather.5.cloned.1.call-update) | async-done | bytes 2097168 | tf_op jit(solution)/shard_map/all_gather | solution.py:108
  281.6 10.9 %fusion.33 = bf16[256,2048]{1,0:T(8,128)(2,1)S(1)} fusion(bf16[256,4096]{1,0:T(8,128)(2,1)} %all-gather.5.cloned.1.call-done, bf16[4096,2048]{1,0:T(8,128)(2,1)} %param.13), kind=kOutput, calls=%fused_computation.70 | convolution fusion | flops 4294967296 | bytes 19922944 | tf_op jit(solution)/shard_map/dot_general | solution.py:107
  292.5 2.3 gather_fusion.4
  294.9 7.1 %reduce-scatter.11.cloned.1.call-done = bf16[128,2048]{1,0:T(8,128)(2,1)} async-done(((bf16[256,2048]{1,0:T(8,128)(2,1)}), bf16[128,2048]{1,0:T(8,128)(2,1)}) %reduce-scatter.11.cloned.1.call-update) | async-done | bytes 524304 | tf_op jit(solution)/shard_map/reduce_scatter | solution.py:116
  (43 shorter events, 1.0 us)
Async XLA Ops:
  6.5 220.1 %copy-start = (bf16[2,1536,2,128]{3,2,1,0:T(2,128)(2,1)S(1)}, bf16[2,1536,2,128]{3,2,1,0:T(2,128)(2,1)}, u32[]{:S(2)}) copy-start(bf16[2,1536,2,128]{3,2,1,0:T(2,128)(2,1)} %param.14) | copy-start | bytes 4718596
  6.5 14.1 %all-gather.3.cloned.1.call-start = ((), (), s32[]{:S(2)}) async-start(), calls=%async_computation.4 | async-start | bytes 1572864 | tf_op jit(solution)/shard_map/all_gather | solution.py:67
  7.3 83.1 %reduce-scatter.7.cloned.1.call-start = ((), (), s32[]{:S(2)}) async-start(), calls=%async_computation.6 | async-start | bytes 147456 | tf_op jit(solution)/shard_map/reduce_scatter | solution.py:80
  26.8 127.8 %reduce-scatter.9.cloned.1.call-start = ((), (), s32[]{:S(2)}) async-start(), calls=%async_computation.7 | async-start | bytes 147456 | tf_op jit(solution)/shard_map/reduce_scatter | solution.py:83
  29.2 11.7 %copy-start.1 = (s32[16]{0:T(128)S(1)}, s32[16]{0:T(128)}, u32[]{:S(2)}) copy-start(s32[16]{0:T(128)} %param.17) | copy-start | bytes 196
  29.2 12.4 %copy-start.2 = (s32[16]{0:T(128)S(1)}, s32[16]{0:T(128)}, u32[]{:S(2)}) copy-start(s32[16]{0:T(128)} %param.16) | copy-start | bytes 196
  29.2 196.1 %reduce-scatter.5.cloned.1.call-start = ((), (), s32[]{:S(2)}) async-start(), calls=%async_computation.5 | async-start | bytes 2359296 | tf_op jit(solution)/shard_map/reduce_scatter | solution.py:77
  40.8 240.8 %all-gather.5.cloned.1.call-start = ((), (), s32[]{:S(2)}) async-start(), calls=%async_computation.8 | async-start | bytes 2359296 | tf_op jit(solution)/shard_map/all_gather | solution.py:108
  226.6 3.7 %copy-start.3 = (bf16[2,1536,2,128]{3,2,1,0:T(2,128)(2,1)S(1)}, bf16[2,1536,2,128]{3,2,1,0:T(2,128)(2,1)}, u32[]{:S(2)}) copy-start(bf16[2,1536,2,128]{3,2,1,0:T(2,128)(2,1)} %param.15) | copy-start | bytes 4718596
  233.3 68.6 %reduce-scatter.11.cloned.1.call-start = ((), (), s32[]{:S(2)}) async-start(), calls=%async_computation.9 | async-start | bytes 1572864 | tf_op jit(solution)/shard_map/reduce_scatter | solution.py:116
Sparse Core Ops, SparseCore 0:
  8.9 11.7 all-gather.2
  26.9 63.3 reduce-scatter.6
  93.6 60.8 reduce-scatter.8
  158.0 67.2 reduce-scatter.4
  233.4 48.1 all-gather.4
  295.0 6.8 reduce-scatter.10
where the time goes:
time: 309 us
  waiting for transfers between devices  249 us (81%)
  matrix products  31.3 us (10%)
  between operations  13.7 us (4%)
  local copies, waits for them, and re-layouts  11.4 us (4%)
  other arithmetic  3.41 us (1%)
    reduce_scatter x1, waiting for transfers between devices, body(): lax.psum_scatter(q_part.astype(jnp.bfloat16), 'row', scatter_dimension=0,...  69.9 us
    reduce_scatter x1, waiting for transfers between devices, body(): lax.psum_scatter(v_part.astype(jnp.bfloat16), 'row', scatter_dimension=0,...  63.5 us
    all_gather x1, waiting for transfers between devices, body(): lax.all_gather(attended, 'row', axis=0, tiled=True)  47.8 us
    reduce_scatter x1, waiting for transfers between devices, body(): lax.psum_scatter(k_part.astype(jnp.bfloat16), 'row', scatter_dimension=0,...  47.7 us
    all_gather x1, waiting for transfers between devices, body(): gathered = lax.all_gather(tokens, 'col', axis=0, tiled=True)  11.8 us
    dot_general x1, matrix products, body(): q_part = jnp.dot(chosen, q_weight, preferred_element_type=jnp.float32)  11.5 us
    dot_general x1, matrix products, body(): jnp.dot(lax.all_gather(attended, 'row', axis=0, tiled=True), o_weight, pr...  10.9 us
    reduce_scatter x1, waiting for transfers between devices, body(): lax.psum_scatter(ordered.astype(jnp.bfloat16), 'col', scatter_dimension=0...  7.07 us
  transfers between devices with their start and end apart: 6, of which 6 were waited for; matrix products, arithmetic and copies ran while one was open for 6% of the time, Pallas kernels for 0%

commit v1 on v0

--- a/solution.py
+++ b/solution.py
@@ -74,15 +74,16 @@
     k_part = jnp.dot(chosen, key_matrix, preferred_element_type=jnp.float32)
     v_part = jnp.dot(chosen, value_matrix, preferred_element_type=jnp.float32)
     q_part, k_part, v_part = (q_part, k_part, v_part)
-    q_sum = lax.psum_scatter(
-        q_part.astype(jnp.bfloat16), "row", scatter_dimension=0, tiled=True
-    ).astype(jnp.float32)
-    key_total_sum = lax.psum_scatter(
-        k_part.astype(jnp.bfloat16), "row", scatter_dimension=0, tiled=True
-    ).astype(jnp.float32)
-    value_total_sum = lax.psum_scatter(
-        v_part.astype(jnp.bfloat16), "row", scatter_dimension=0, tiled=True
-    ).astype(jnp.float32)
+    q_width = q_part.shape[1]
+    k_width = k_part.shape[1]
+    joined = jnp.concatenate(
+        [q_part.astype(jnp.bfloat16), k_part.astype(jnp.bfloat16), v_part.astype(jnp.bfloat16)],
+        axis=1,
+    )
+    summed = lax.psum_scatter(joined, "row", scatter_dimension=0, tiled=True).astype(jnp.float32)
+    q_sum = summed[:, :q_width]
+    key_total_sum = summed[:, q_width : q_width + k_width]
+    value_total_sum = summed[:, q_width + k_width :]
     local_slots = row_index * seq_dev + jnp.arange(seq_dev)
     sequences = slot_seq[local_slots]
     starts = cache_len[sequences]

time: 309 us -> 194 us (0.63)
  waiting for transfers between devices: 249 us -> 137 us
  matrix products: 31.3 us -> 26.9 us
    reduce_scatter x3 -> x1, waiting for transfers between devices: 181 us -> 69.2 us  [body(): lax.psum_scatter(joined, 'row', scatter_dimension=0, tiled=True)]
    dot_general x1, matrix products: 11.5 us -> 8.43 us  [body(): q_part = jnp.dot(chosen, q_weight, preferred_element_type=jnp.float32)]
  transfers between devices with their start and end apart: 6 -> 4, of which waited for: 6 -> 4; matrix products, arithmetic and copies ran while one was open for 6% -> 2% of each run, Pallas kernels for 0% -> 0%
where the time goes in v1:
time: 194 us
  waiting for transfers between devices  137 us (71%)
  matrix products  26.9 us (14%)
  between operations  13.4 us (7%)
  local copies, waits for them, and re-layouts  11.5 us (6%)
  other arithmetic  5.03 us (3%)
    reduce_scatter x1, waiting for transfers between devices, body(): lax.psum_scatter(joined, 'row', scatter_dimension=0, tiled=True)  69.2 us
    all_gather x1, waiting for transfers between devices, body(): lax.all_gather(attended, 'row', axis=0, tiled=True)  48 us
    all_gather x1, waiting for transfers between devices, body(): gathered = lax.all_gather(tokens, 'col', axis=0, tiled=True)  11.8 us
    dot_general x1, matrix products, body(): jnp.dot(lax.all_gather(attended, 'row', axis=0, tiled=True), o_weight, pr...  10.9 us
    dot_general x1, matrix products, body(): q_part = jnp.dot(chosen, q_weight, preferred_element_type=jnp.float32)  8.43 us
    reduce_scatter x1, waiting for transfers between devices, body(): lax.psum_scatter(ordered.astype(jnp.bfloat16), 'col', scatter_dimension=0...  7.07 us
  transfers between devices with their start and end apart: 4, of which 4 were waited for; matrix products, arithmetic and copies ran while one was open for 2% of the time, Pallas kernels for 0%

profile of v1, /device:TPU:0, one launch (start us, length us, event | category | flops | bytes accessed | tf_op | source)
XLA Modules:
  0.0 193.8 jit_solution(1497433566667456908)
XLA Ops:
  6.5 0.7 all-gather.3.cloned.1.call-update
  7.3 1.3 gather_fusion.2
  8.8 11.8 %all-gather.3.cloned.1.call-done = bf16[256,2048]{1,0:T(8,128)(2,1)} async-done(((bf16[128,2048]{1,0:T(8,128)(2,1)}), bf16[256,2048]{1,0:T(8,128)(2,1)}) %all-gather.3.cloned.1.call-update) | async-done | bytes 1048592 | tf_op jit(solution)/shard_map/all_gather | solution.py:67
  20.7 3.7 %gather_fusion.3 = bf16[256,2048]{1,0:T(8,128)(2,1)S(1)} fusion(bf16[256,2048]{1,0:T(8,128)(2,1)} %all-gather.3.cloned.1.call-done, s32[1024]{0:T(1024)S(1)} %pad_clamp_fusion.1), kind=kCustom, calls=%fused_computation.3 | custom fusion | bytes 2098176 | tf_op jit(solution)/shard_map/gather | solution.py:72
  24.4 1.7 convolution_convert_fusion.2
  26.1 1.7 convolution_convert_fusion.1
  27.8 8.4 %convolution_convert_fusion = bf16[256,4096]{1,0:T(8,128)(2,1)S(1)} fusion(bf16[256,2048]{1,0:T(8,128)(2,1)S(1)} %gather_fusion.3, bf16[2048,4096]{1,0:T(8,128)(2,1)} %param.10), kind=kOutput, calls=%fused_computation.9 | convolution fusion | flops 4296015872 | bytes 19922944 | tf_op jit(solution)/shard_map/dot_general | solution.py:73
  36.2 1.6 pad_maximum_fusion
  37.9 0.6 gather_fusion
  38.6 0.6 gather_fusion.1
  39.3 0.1 convert_element_type.53
  39.4 0.1 multiply_cosine_fusion
  39.7 69.2 %reduce-scatter.3.cloned.1.call-done = bf16[32,4608]{1,0:T(8,128)(2,1)} async-done(((bf16[256,4608]{1,0:T(8,128)(2,1)}), bf16[32,4608]{1,0:T(8,128)(2,1)}) %reduce-scatter.3.cloned.1.call-update) | async-done | bytes 294928 | tf_op jit(solution)/shard_map/reduce_scatter | solution.py:83
  108.8 0.7 slice.45
  109.6 0.7 slice.42
  110.3 0.1 fusion.31
  110.4 1.0 convert_element_type.51
  111.5 0.1 copy.77
  111.6 0.2 subtract_convert_fusion
  111.8 1.3 bitcast_reduce_fusion
  113.1 0.8 fusion.32
  114.0 0.2 fusion.19
  114.1 1.4 fusion.1
  115.5 1.8 fusion.9
  117.3 0.3 fusion.18
  117.7 0.8 convert_element_type.58
  118.5 0.2 reduce-scatter.5.cloned.1.call-start
  118.7 0.1 select_reduce_fusion
  119.0 48.0 %all-gather.5.cloned.1.call-done = bf16[256,4096]{1,0:T(8,128)(2,1)} async-done(((bf16[32,4096]{1,0:T(8,128)(2,1)}), bf16[256,4096]{1,0:T(8,128)(2,1)}) %all-gather.5.cloned.1.call-update) | async-done | bytes 2097168 | tf_op jit(solution)/shard_map/all_gather | solution.py:109
  167.0 10.9 %fusion.33 = bf16[256,2048]{1,0:T(8,128)(2,1)S(1)} fusion(bf16[256,4096]{1,0:T(8,128)(2,1)} %all-gather.5.cloned.1.call-done, bf16[4096,2048]{1,0:T(8,128)(2,1)} %param.13), kind=kOutput, calls=%fused_computation.71 | convolution fusion | flops 4294967296 | bytes 19922944 | tf_op jit(solution)/shard_map/dot_general | solution.py:108
  177.9 2.3 %gather_fusion.4 = bf16[256,2048]{1,0:T(8,128)(2,1)} fusion(bf16[256,2048]{1,0:T(8,128)(2,1)S(1)} %fusion.33, s32[1024]{0:T(1024)S(1)} %pad_clamp_fusion), kind=kCustom, calls=%fused_computation.4 | custom fusion | bytes 2098176 | tf_op jit(solution)/shard_map/gather | solution.py:116
  180.2 7.1 %reduce-scatter.5.cloned.1.call-done = bf16[128,2048]{1,0:T(8,128)(2,1)} async-done(((bf16[256,2048]{1,0:T(8,128)(2,1)}), bf16[128,2048]{1,0:T(8,128)(2,1)}) %reduce-scatter.5.cloned.1.call-update) | async-done | bytes 524304 | tf_op jit(solution)/shard_map/reduce_scatter | solution.py:117
  (41 shorter events, 0.8 us)
Async XLA Ops:
  6.5 105.3 %copy-start = (bf16[2,1536,2,128]{3,2,1,0:T(2,128)(2,1)S(1)}, bf16[2,1536,2,128]{3,2,1,0:T(2,128)(2,1)}, u32[]{:S(2)}) copy-start(bf16[2,1536,2,128]{3,2,1,0:T(2,128)(2,1)} %param.14) | copy-start | bytes 4718596
  6.5 14.1 %all-gather.3.cloned.1.call-start = ((), (), s32[]{:S(2)}) async-start(), calls=%async_computation.2 | async-start | bytes 1572864 | tf_op jit(solution)/shard_map/all_gather | solution.py:67
  7.3 101.6 %reduce-scatter.3.cloned.1.call-start = ((), (), s32[]{:S(2)}) async-start(), calls=%async_computation.3 | async-start | bytes 2654208 | tf_op jit(solution)/shard_map/reduce_scatter | solution.py:83
  36.2 1.7 copy-start.1
  36.2 2.4 %copy-start.2 = (s32[16]{0:T(128)S(1)}, s32[16]{0:T(128)}, u32[]{:S(2)}) copy-start(s32[16]{0:T(128)} %param.16) | copy-start | bytes 196
  37.9 129.1 %all-gather.5.cloned.1.call-start = ((), (), s32[]{:S(2)}) async-start(), calls=%async_computation.4 | async-start | bytes 2359296 | tf_op jit(solution)/shard_map/all_gather | solution.py:109
  113.1 2.4 %copy-start.3 = (bf16[2,1536,2,128]{3,2,1,0:T(2,128)(2,1)S(1)}, bf16[2,1536,2,128]{3,2,1,0:T(2,128)(2,1)}, u32[]{:S(2)}) copy-start(bf16[2,1536,2,128]{3,2,1,0:T(2,128)(2,1)} %param.15) | copy-start | bytes 4718596
  118.5 68.8 %reduce-scatter.5.cloned.1.call-start = ((), (), s32[]{:S(2)}) async-start(), calls=%async_computation.5 | async-start | bytes 1572864 | tf_op jit(solution)/shard_map/reduce_scatter | solution.py:117
Sparse Core Ops, SparseCore 0:
  8.9 11.7 all-gather.2
  38.0 70.7 reduce-scatter.2
  118.6 48.3 all-gather.4
  180.4 6.8 reduce-scatter.4

commit v2 on v0

v2 whole, which is shorter than its diff:
```python
import math

import jax
import jax.numpy as jnp
import numpy as np
from jax import lax
from jax.sharding import PartitionSpec as P

ROPE_BASE = 500000.0


def apply_turning(values, token_places):
    half_dim = values.shape[-1] // 2
    frequency = ROPE_BASE ** (-(2.0 * jnp.arange(half_dim, dtype=jnp.float32)) / values.shape[-1])
    angles = token_places[:, None] * frequency[None, :]
    cosine = jnp.cos(angles)[:, None, :]
    sine_part = jnp.sin(angles)[:, None, :]
    leading = values[..., :half_dim]
    trailing = values[..., half_dim:]
    return jnp.concatenate(
        [leading * cosine - trailing * sine_part, trailing * cosine + leading * sine_part], axis=-1
    )


def attend(queries, incoming_keys, incoming_values, cached_keys, cached_values, length):
    tokens_new, kv_heads, head_dim = incoming_keys.shape
    grouped = queries.reshape(tokens_new, kv_heads, -1, head_dim)
    scale_factor = 1.0 / math.sqrt(head_dim)
    cache_scores = (
        jnp.einsum("nkgd,ckd->kgnc", grouped, cached_keys, preferred_element_type=jnp.float32)
        * scale_factor
    )
    valid_cache = jnp.arange(cached_keys.shape[0]) < length
    cache_scores = jnp.where(valid_cache, cache_scores, -jnp.inf)
    fresh_scores = (
        jnp.einsum("nkgd,mkd->kgnm", grouped, incoming_keys, preferred_element_type=jnp.float32)
        * scale_factor
    )
    causal = jnp.arange(tokens_new)[None, :] <= jnp.arange(tokens_new)[:, None]
    fresh_scores = jnp.where(causal, fresh_scores, -jnp.inf)
    highest = jnp.maximum(jnp.max(cache_scores, axis=-1), jnp.max(fresh_scores, axis=-1))
    cache_weights = jnp.exp(cache_scores - highest[..., None])
    fresh_weights = jnp.exp(fresh_scores - highest[..., None])
    totals = jnp.sum(cache_weights, axis=-1) + jnp.sum(fresh_weights, axis=-1)
    weighted = jnp.einsum(
        "kgnc,ckd->nkgd",
        cache_weights.astype(jnp.bfloat16),
        cached_values,
        preferred_element_type=jnp.float32,
    )
    weighted = weighted + jnp.einsum(
        "kgnm,mkd->nkgd",
        fresh_weights.astype(jnp.bfloat16),
        incoming_values,
        preferred_element_type=jnp.float32,
    )
    normed = weighted / jnp.transpose(totals, (2, 0, 1))[..., None]
    return normed.reshape(tokens_new, -1).astype(jnp.bfloat16)


def row_ring(mesh):
    n_row = mesh.shape["row"]
    natural = list(range(n_row))
    try:
        names = list(mesh.axis_names)
        picked = np.moveaxis(np.asarray(mesh.devices), names.index("row"), 0).reshape(n_row, -1)[:, 0]
        coords = [tuple(d.coords) for d in picked]
    except Exception:
        return natural
    varying = [a for a in range(len(coords[0])) if len({c[a] for c in coords}) > 1]
    if len(varying) != 2:
        return natural
    sizes = {a: len({c[a] for c in coords}) for a in varying}
    inner = [a for a in varying if sizes[a] == 2]
    if not inner or sizes[varying[0]] * sizes[varying[1]] != n_row:
        return natural
    inner = inner[-1]
    outer = [a for a in varying if a != inner][0]
    lo, hi = min(c[inner] for c in coords), max(c[inner] for c in coords)
    first = sorted([i for i in natural if coords[i][inner] == lo], key=lambda i: coords[i][outer])
    second = sorted([i for i in natural if coords[i][inner] == hi], key=lambda i: -coords[i][outer])
    return first + second


def make_body(ring):
    n_row = len(ring)
    position_of = [ring.index(i) for i in range(n_row)]
    forward_hops = n_row // 2
    backward_hops = n_row - 1 - forward_hops
    forward_pairs = [(ring[i], ring[(i + 1) % n_row]) for i in range(n_row)]
    backward_pairs = [(ring[i], ring[(i - 1) % n_row]) for i in range(n_row)]
    gather_offsets = [0]
    for s in range(forward_hops):
        gather_offsets.append(-(s + 1) % n_row)
        if s < backward_hops:
            gather_offsets.append((s + 1) % n_row)
    stacked_of_offset = [gather_offsets.index(d) for d in range(n_row)]

    def add_bf16(a, b):
        return (a.astype(jnp.float32) + b.astype(jnp.float32)).astype(jnp.bfloat16)

    def ring_reduce_scatter(blocks):
        if n_row == 1:
            return blocks[0].astype(jnp.float32)
        forward = blocks[forward_hops % n_row]
        backward = blocks[(n_row - backward_hops) % n_row] if backward_hops else None
        got_forward = got_backward = None
        for s in range(forward_hops):
            got_forward = lax.ppermute(forward, "row", forward_pairs)
            if s < backward_hops:
                got_backward = lax.ppermute(backward, "row", backward_pairs)
            if s < forward_hops - 1:
                forward = add_bf16(got_forward, blocks[(forward_hops - s - 1) % n_row])
            if s < backward_hops - 1:
                backward = add_bf16(got_backward, blocks[(s + 1 - backward_hops) % n_row])
        total = got_forward.astype(jnp.float32) + blocks[0].astype(jnp.float32)
        if got_backward is not None:
            total = total + got_backward.astype(jnp.float32)
        return total

    def ring_all_gather(own):
        got = [own]
        forward = backward = own
        for s in range(forward_hops):
            forward = lax.ppermute(forward, "row", forward_pairs)
            got.append(forward)
            if s < backward_hops:
                backward = lax.ppermute(backward, "row", backward_pairs)
                got.append(backward)
        return jnp.concatenate(got, axis=0)

    def body(
        tokens, q_weight, key_matrix, value_matrix, o_weight, k_cache, value_cache, cache_len, slot_seq
    ):
        row_index = lax.axis_index("row")
        col_index = lax.axis_index("col")
        n_col = 2
        seq_dev = k_cache.shape[0]
        head_dim = k_cache.shape[3]
        slot_total = slot_seq.shape[0]
        own_rows = tokens.shape[0]
        other_tokens = lax.ppermute(tokens, "col", [(0, 1), (1, 0)])
        both = jnp.concatenate([tokens, other_tokens], axis=0)
        new_len = own_rows * n_col // slot_total
        my_pos = jnp.asarray(position_of, jnp.int32)[row_index]
        ring_arr = jnp.asarray(ring, jnp.int32)
        block_dev = ring_arr[(my_pos + jnp.arange(n_row)) % n_row]
        slots = (block_dev[:, None] * seq_dev + jnp.arange(seq_dev)[None, :]).reshape(-1)
        sequences = slot_seq[slots]
        token_rows = (sequences[:, None] * new_len + jnp.arange(new_len)[None, :]).reshape(-1)
        local_rows = jnp.where(
            token_rows // own_rows == col_index, token_rows % own_rows, own_rows + token_rows % own_rows
        )
        chosen = both[local_rows]
        q_part = jnp.dot(chosen, q_weight, preferred_element_type=jnp.float32)
        k_part = jnp.dot(chosen, key_matrix, preferred_element_type=jnp.float32)
        v_part = jnp.dot(chosen, value_matrix, preferred_element_type=jnp.float32)
        q_width = q_part.shape[1]
        k_width = k_part.shape[1]
        joined = jnp.concatenate(
            [q_part.astype(jnp.bfloat16), k_part.astype(jnp.bfloat16), v_part.astype(jnp.bfloat16)],
            axis=1,
        )
        block_rows = seq_dev * new_len
        blocks = [joined[k * block_rows : (k + 1) * block_rows] for k in range(n_row)]
        summed = ring_reduce_scatter(blocks)
        q_sum = summed[:, :q_width]
        key_total_sum = summed[:, q_width : q_width + k_width]
        value_total_sum = summed[:, q_width + k_width :]
        local_slots = row_index * seq_dev + jnp.arange(seq_dev)
        starts = cache_len[slot_seq[local_slots]]
        token_places = (starts[:, None] + jnp.arange(new_len)[None, :]).reshape(-1).astype(jnp.float32)
        row_total = q_sum.shape[0]
        queries = apply_turning(q_sum.reshape(row_total, -1, head_dim), token_places).astype(
            jnp.bfloat16
        )
        rotated_keys = apply_turning(
            key_total_sum.reshape(row_total, -1, head_dim), token_places
        ).astype(jnp.bfloat16)
        values = value_total_sum.reshape(row_total, -1, head_dim).astype(jnp.bfloat16)
        results = jax.vmap(attend)(
            queries.reshape(seq_dev, new_len, -1, head_dim),
            rotated_keys.reshape(seq_dev, new_len, -1, head_dim),
            values.reshape(seq_dev, new_len, -1, head_dim),
            k_cache,
            value_cache,
            starts,
        )
        attended = results.reshape(seq_dev * new_len, -1)
        products = jnp.dot(ring_all_gather(attended), o_weight, preferred_element_type=jnp.float32)
        matches = (slot_seq[:, None] == jnp.arange(slot_total)[None, :]).astype(jnp.int32)
        slot_of = jnp.sum(matches * jnp.arange(slot_total)[:, None], axis=0)
        span = jnp.arange(own_rows * n_col)
        seq_of = span // new_len
        slot_t = slot_of[seq_of]
        offset = (jnp.asarray(position_of, jnp.int32)[slot_t // seq_dev] - my_pos) % n_row
        stacked = jnp.asarray(stacked_of_offset, jnp.int32)[offset]
        product_rows = stacked * block_rows + (slot_t % seq_dev) * new_len + span % new_len
        product_rows = product_rows.reshape(n_col, own_rows)
        mine = products[lax.dynamic_index_in_dim(product_rows, col_index, 0, keepdims=False)]
        theirs = products[lax.dynamic_index_in_dim(product_rows, 1 - col_index, 0, keepdims=False)]
        received = lax.ppermute(theirs.astype(jnp.bfloat16), "col", [(0, 1), (1, 0)])
        return (mine + received.astype(jnp.float32)).astype(jnp.bfloat16)

    return body


def solution(mesh):
    return jax.shard_map(
        make_body(row_ring(mesh)),
        mesh=mesh,
        in_specs=(
            P(("groups", "col"), "row"),
            P("row", "col"),
            P("row", "col"),
            P("row", "col"),
            P("col", "row"),
            P(("groups", "row"), None, "col", None),
            P(("groups", "row"), None, "col", None),
            P("groups"),
            P("groups"),
        ),
        out_specs=P(("groups", "col"), "row"),
        check_vma=False,
    )
```

time: 309 us -> 129 us (0.42)
  waiting for transfers between devices: 249 us -> 51.4 us
  starting transfers between devices: 0.39 us -> 16.9 us
  other arithmetic: 3.41 us -> 18.5 us
  between operations: 13.7 us -> 0.46 us
  matrix products: 31.3 us -> 24.8 us
  local copies, waits for them, and re-layouts: 11.4 us -> 16.6 us
    reduce_scatter x4 -> x0, waiting for transfers between devices: 188 us -> none  [the longest x1 69.9 us: body(): lax.psum_scatter(q_part.astype(jnp.bfloat16), 'row', scatter_dimension=0,...]
    all_gather x2 -> x0, waiting for transfers between devices: 59.6 us -> none  [the longest x1 47.8 us: body(): lax.all_gather(attended, 'row', axis=0, tiled=True)]
    ppermute x0 -> x16, waiting for transfers between devices: none -> 51.4 us  [the longest x4 24.9 us: ring_reduce_scatter(): got_forward = lax.ppermute(forward, 'row', forward_pairs)]
    ppermute x0 -> x16, starting transfers between devices: none -> 16.9 us  [the longest x4 7.68 us: ring_reduce_scatter(): got_forward = lax.ppermute(forward, 'row', forward_pairs)]
    gather x5 -> x21, other arithmetic: 0.03 us -> 10.3 us  [the longest x11 10.2 us: body(): slot_t = slot_of[seq_of]]
    gather x5 -> x8, local copies, waits for them, and re-layouts: 8.65 us -> 14.5 us  [the longest x1 3.16 us: body(): products[lax.dynamic_index_in_dim(product_rows, col_index, 0, keepdims=Fa...]
    dot_general x1, matrix products: 11.5 us -> 8.41 us  [body(): q_part = jnp.dot(chosen, q_weight, preferred_element_type=jnp.float32)]
  transfers between devices with their start and end apart: 6 -> 16, of which waited for: 6 -> 11; matrix products, arithmetic and copies ran while one was open for 6% -> 18% of each run, Pallas kernels for 0% -> 0%
where the time goes in v2:
time: 129 us
  waiting for transfers between devices  51.4 us (40%)
  matrix products  24.8 us (19%)
  other arithmetic  18.5 us (14%)
  starting transfers between devices  16.9 us (13%)
  local copies, waits for them, and re-layouts  16.6 us (13%)
    ppermute x4, waiting for transfers between devices, ring_reduce_scatter(): got_forward = lax.ppermute(forward, 'row', forward_pairs)  24.9 us
    ppermute x3, waiting for transfers between devices, ring_all_gather(): backward = lax.ppermute(backward, 'row', backward_pairs)  13.1 us
    ppermute x4, waiting for transfers between devices, ring_all_gather(): forward = lax.ppermute(forward, 'row', forward_pairs)  10.9 us
    gather x11, other arithmetic, body(): slot_t = slot_of[seq_of]  10.2 us
    dot_general x1, matrix products, body(): jnp.dot(ring_all_gather(attended), o_weight, preferred_element_type=jnp.f...  9.5 us
    dot_general x1, matrix products, body(): q_part = jnp.dot(chosen, q_weight, preferred_element_type=jnp.float32)  8.41 us
    ppermute x4, starting transfers between devices, ring_reduce_scatter(): got_forward = lax.ppermute(forward, 'row', forward_pairs)  7.68 us
    ppermute x4, starting transfers between devices, ring_all_gather(): forward = lax.ppermute(forward, 'row', forward_pairs)  6.24 us
  transfers between devices with their start and end apart: 16, of which 11 were waited for; matrix products, arithmetic and copies ran while one was open for 18% of the time, Pallas kernels for 0%

profile of v2, /device:TPU:0, one launch (start us, length us, event | category | flops | bytes accessed | tf_op | source)
XLA Modules:
  0.0 128.6 jit_solution(9122350091393945438)
XLA Ops:
  3.5 1.3 %gather_fusion.2 = s32[8]{0:T(128)S(1)} fusion(s32[8]{0:T(128)} %constant.146.clone, s32[1024]{0:T(1024)S(1)} %pad_clamp_fusion.4), kind=kCustom, calls=%fused_computation.2 | custom fusion | bytes 96 | tf_op jit(solution)/shard_map/gather | solution.py:147
  5.0 1.3 %gather_fusion = s32[2]{0:T(128)S(1)} fusion(s32[16]{0:T(128)} %param.21, s32[1024]{0:T(1024)S(1)} %pad_clamp_fusion.6), kind=kCustom, calls=%fused_computation | custom fusion | bytes 24 | tf_op jit(solution)/shard_map/gather | solution.py:171
  6.3 1.3 %gather_fusion.3 = s32[16]{0:T(128)S(1)} fusion(s32[16]{0:T(128)} %param.21, s32[1024]{0:T(1024)S(1)} %get-tuple-element.45), kind=kCustom, calls=%fused_computation.3 | custom fusion | bytes 192 | tf_op jit(solution)/shard_map/gather | solution.py:149
  7.6 1.3 %gather_fusion.1 = s32[2]{0:T(128)S(1)} fusion(s32[16]{0:T(128)} %param.20, s32[1024]{0:T(1024)S(1)} %get-tuple-element.46), kind=kCustom, calls=%fused_computation.1 | custom fusion | bytes 24 | tf_op jit(solution)/shard_map/gather | solution.py:171
  9.9 4.3 %compare_select_fusion.18 = s32[256,1]{0,1:T(1,128)S(1)} fusion(s32[]{:T(128)} %bitcast.29, s32[]{:T(128)} %bitcast.30, s32[]{:T(128)} %bitcast.31, s32[]{:T(128)} %bitcast.32, s32[]{:T(128)} %bitcast.33, s32[]{:T(128)} %bitcast.35, s32[]{:T(128)} %bitcast.34), kind=kLoop, calls=%fused_computation.107 | loop fusion | flops 5888 | bytes 1052 | tf_op jit(solution)/shard_map/gather | solution.py:195
  14.2 5.6 %select_select_fusion = s32[256]{0:T(256)S(1)} fusion(pred[256]{0:T(512)(128)(4,1)S(1)} %compare_reduce_fusion.2, pred[256]{0:T(512)(128)(4,1)S(1)} %compare_reduce_fusion.3, pred[256]{0:T(512)(128)(4,1)S(1)} %compare_reduce_fusion.4, pred[256]{0:T(512)(128)(4,1)S(1)} %compare_reduce_fusion.5, pred[256]{0:T(512)(128)(4,1)S(1)} %compare_reduce_fusion.6, ...), kind=kLoop, calls=%fused_computation.151 | loop fusion | flops 2304 | bytes 4388 | tf_op jit(solution)/shard_map/gather | solution.py:195
  21.7 2.4 %gather_fusion.4 = bf16[256,2048]{1,0:T(8,128)(2,1)} fusion(bf16[256,2048]{1,0:T(8,128)(2,1)S(1)} %pad_maximum_fusion.1, s32[1024]{0:T(1024)S(1)} %pad_clamp_fusion.2), kind=kCustom, calls=%fused_computation.4 | custom fusion | bytes 2098176 | tf_op jit(solution)/shard_map/gather | solution.py:154
  24.1 2.1 %convolution_convert_fusion.2 = bf16[256,256]{1,0:T(8,128)(2,1)S(1)} fusion(bf16[256,2048]{1,0:T(8,128)(2,1)} %gather_fusion.4, bf16[2048,256]{1,0:T(8,128)(2,1)} %param.15), kind=kOutput, calls=%fused_computation.29 | convolution fusion | flops 268500992 | bytes 2228224 | tf_op jit(solution)/shard_map/dot_general | solution.py:156
  26.7 8.4 %convolution_convert_fusion = bf16[256,4096]{1,0:T(8,128)(2,1)S(1)} fusion(bf16[256,2048]{1,0:T(8,128)(2,1)S(1)} %copy-done.2, bf16[2048,4096]{1,0:T(8,128)(2,1)} %param.14), kind=kOutput, calls=%fused_computation.11 | convolution fusion | flops 4296015872 | bytes 19922944 | tf_op jit(solution)/shard_map/dot_general | solution.py:155
  35.3 2.6 %collective-permute-start.1 = (bf16[32,4608]{1,0:T(8,128)(2,1)S(1)}, bf16[32,4608]{1,0:T(8,128)(2,1)S(1)}, u32[]{:S(2)}, u32[]{:S(2)}) collective-permute-start(bf16[32,4608]{1,0:T(8,128)(2,1)S(1)} %get-tuple-element.13), channel_id=1, source_target_pairs={{0,4},{4,8},{8,12},{12,14},{14,10},{10,6},{6,2},{2,0},{1,5},{5,9},... | collective-permute-start | bytes 884744 | tf_op jit(solution)/shard_map/ppermute | solution.py:109
  38.1 7.5 %collective-permute-done.1 = bf16[32,4608]{1,0:T(8,128)(2,1)S(1)} collective-permute-done((bf16[32,4608]{1,0:T(8,128)(2,1)S(1)}, bf16[32,4608]{1,0:T(8,128)(2,1)S(1)}, u32[]{:S(2)}, u32[]{:S(2)}) %collective-permute-start.1) | collective-permute-done | bytes 294944 | tf_op jit(solution)/shard_map/ppermute | solution.py:109
  45.7 1.8 %collective-permute-start.2 = (bf16[32,4608]{1,0:T(8,128)(2,1)S(1)}, bf16[32,4608]{1,0:T(8,128)(2,1)S(1)}, u32[]{:S(2)}, u32[]{:S(2)}) collective-permute-start(bf16[32,4608]{1,0:T(8,128)(2,1)S(1)} %add_convert_fusion.5), channel_id=1, source_target_pairs={{0,4},{4,8},{8,12},{12,14},{14,10},{10,6},{6,2},{2,0},{1,5},{5,9},... | collective-permute-start | bytes 884744 | tf_op jit(solution)/shard_map/ppermute | solution.py:109
  47.6 7.0 %collective-permute-done.2 = bf16[32,4608]{1,0:T(8,128)(2,1)S(1)} collective-permute-done((bf16[32,4608]{1,0:T(8,128)(2,1)S(1)}, bf16[32,4608]{1,0:T(8,128)(2,1)S(1)}, u32[]{:S(2)}, u32[]{:S(2)}) %collective-permute-start.2) | collective-permute-done | bytes 294944 | tf_op jit(solution)/shard_map/ppermute | solution.py:109
  54.7 1.6 %collective-permute-start.3 = (bf16[32,4608]{1,0:T(8,128)(2,1)S(1)}, bf16[32,4608]{1,0:T(8,128)(2,1)S(1)}, u32[]{:S(2)}, u32[]{:S(2)}) collective-permute-start(bf16[32,4608]{1,0:T(8,128)(2,1)S(1)} %get-tuple-element.11), channel_id=1, source_target_pairs={{0,4},{4,8},{8,12},{12,14},{14,10},{10,6},{6,2},{2,0},{1,5},{5,9},... | collective-permute-start | bytes 884744 | tf_op jit(solution)/shard_map/ppermute | solution.py:109
  56.9 5.9 %collective-permute-done.3 = bf16[32,4608]{1,0:T(8,128)(2,1)S(1)} collective-permute-done((bf16[32,4608]{1,0:T(8,128)(2,1)S(1)}, bf16[32,4608]{1,0:T(8,128)(2,1)S(1)}, u32[]{:S(2)}, u32[]{:S(2)}) %collective-permute-start.3) | collective-permute-done | bytes 294944 | tf_op jit(solution)/shard_map/ppermute | solution.py:109
  63.8 1.6 %collective-permute-start.4 = (bf16[32,4608]{1,0:T(8,128)(2,1)S(1)}, bf16[32,4608]{1,0:T(8,128)(2,1)S(1)}, u32[]{:S(2)}, u32[]{:S(2)}) collective-permute-start(bf16[32,4608]{1,0:T(8,128)(2,1)S(1)} %get-tuple-element.9), channel_id=1, source_target_pairs={{0,4},{4,8},{8,12},{12,14},{14,10},{10,6},{6,2},{2,0},{1,5},{5,9},... | collective-permute-start | bytes 884744 | tf_op jit(solution)/shard_map/ppermute | solution.py:109
  66.1 4.5 %collective-permute-done.4 = bf16[32,4608]{1,0:T(8,128)(2,1)S(1)} collective-permute-done((bf16[32,4608]{1,0:T(8,128)(2,1)S(1)}, bf16[32,4608]{1,0:T(8,128)(2,1)S(1)}, u32[]{:S(2)}, u32[]{:S(2)}) %collective-permute-start.4) | collective-permute-done | bytes 294944 | tf_op jit(solution)/shard_map/ppermute | solution.py:109
  70.6 1.6 %collective-permute-done.7 = bf16[32,4608]{1,0:T(8,128)(2,1)S(1)} collective-permute-done((bf16[32,4608]{1,0:T(8,128)(2,1)S(1)}, bf16[32,4608]{1,0:T(8,128)(2,1)S(1)}, u32[]{:S(2)}, u32[]{:S(2)}) %collective-permute-start.7) | collective-permute-done | bytes 294944 | tf_op jit(solution)/shard_map/ppermute | solution.py:111
  75.2 1.4 %fusion.1 = f32[2,2,16,16]{2,3,1,0:T(8,128)S(1)} fusion(f32[2,2,16,16,1536]{4,3,2,1,0:T(8,128)S(1)} %get-tuple-element.42, f32[2,2,16,16]{2,3,1,0:T(8,128)S(1)} %max.7, pred[2,1536]{1,0:T(4,128)(4,1)S(1)} %iota_compare_fusion), kind=kLoop, calls=%fused_computation.12 | loop fusion | flops 6290432 | bytes 6302720 | tf_op jit(solution)/shard_map/vmap()/reduce_sum | solution.py:44
  76.6 1.9 %fusion.9 = f32[2,16,2,16,128]{4,3,1,2,0:T(8,128)S(1)} fusion(bf16[2,1536,2,128,1]{3,2,1,0,4:T(2,128)(2,1)S(1)} %bitcast.112, f32[2,2,16,16,1536]{4,3,2,1,0:T(8,128)S(1)} %get-tuple-element.42, f32[2,2,16,16]{2,3,1,0:T(8,128)S(1)} %max.7, pred[2,1536]{1,0:T(4,128)(4,1)S(1)} %iota_compare_fusion), kind=kOutput, calls=%fused_computation.20 | convolution fusion | flops 408944640 | bytes 8395776 | tf_op jit(solution)/shard_map/vmap(kgnc,ckd->nkgd)/dot_general | solution.py:45
  79.5 1.6 %collective-permute-start.8 = (bf16[32,4096]{1,0:T(8,128)(2,1)S(1)}, bf16[32,4096]{1,0:T(8,128)(2,1)S(1)}, u32[]{:S(2)}, u32[]{:S(2)}) collective-permute-start(bf16[32,4096]{1,0:T(8,128)(2,1)S(1)} %convert_element_type.132), channel_id=1, source_target_pairs={{0,4},{4,8},{8,12},{12,14},{14,10},{10,6},{6,2},{2,0},{1,5},{5,9},... | collective-permute-start | bytes 786440 | tf_op jit(solution)/shard_map/ppermute | solution.py:125
  81.1 6.4 %collective-permute-done.9 = bf16[32,4096]{1,0:T(8,128)(2,1)S(1)} collective-permute-done((bf16[32,4096]{1,0:T(8,128)(2,1)S(1)}, bf16[32,4096]{1,0:T(8,128)(2,1)S(1)}, u32[]{:S(2)}, u32[]{:S(2)}) %collective-permute-start.9) | collective-permute-done | bytes 262176 | tf_op jit(solution)/shard_map/ppermute | solution.py:128
  88.2 1.6 %collective-permute-start.10 = (bf16[32,4096]{1,0:T(8,128)(2,1)S(1)}, bf16[32,4096]{1,0:T(8,128)(2,1)S(1)}, u32[]{:S(2)}, u32[]{:S(2)}) collective-permute-start(bf16[32,4096]{1,0:T(8,128)(2,1)S(1)} %collective-permute-done.8), channel_id=1, source_target_pairs={{0,4},{4,8},{8,12},{12,14},{14,10},{10,6},{6,2},{2,0},{1,5},{5,9},... | collective-permute-start | bytes 786440 | tf_op jit(solution)/shard_map/ppermute | solution.py:125
  89.8 6.7 %collective-permute-done.11 = bf16[32,4096]{1,0:T(8,128)(2,1)S(1)} collective-permute-done((bf16[32,4096]{1,0:T(8,128)(2,1)S(1)}, bf16[32,4096]{1,0:T(8,128)(2,1)S(1)}, u32[]{:S(2)}, u32[]{:S(2)}) %collective-permute-start.11) | collective-permute-done | bytes 262176 | tf_op jit(solution)/shard_map/ppermute | solution.py:128
  97.0 1.5 %collective-permute-start.12 = (bf16[32,4096]{1,0:T(8,128)(2,1)S(1)}, bf16[32,4096]{1,0:T(8,128)(2,1)S(1)}, u32[]{:S(2)}, u32[]{:S(2)}) collective-permute-start(bf16[32,4096]{1,0:T(8,128)(2,1)S(1)} %collective-permute-done.10), channel_id=1, source_target_pairs={{0,4},{4,8},{8,12},{12,14},{14,10},{10,6},{6,2},{2,0},{1,5},{5,9},... | collective-permute-start | bytes 786440 | tf_op jit(solution)/shard_map/ppermute | solution.py:125
  98.6 5.8 %collective-permute-done.12 = bf16[32,4096]{1,0:T(8,128)(2,1)S(1)} collective-permute-done((bf16[32,4096]{1,0:T(8,128)(2,1)S(1)}, bf16[32,4096]{1,0:T(8,128)(2,1)S(1)}, u32[]{:S(2)}, u32[]{:S(2)}) %collective-permute-start.12) | collective-permute-done | bytes 262176 | tf_op jit(solution)/shard_map/ppermute | solution.py:125
  104.4 1.5 %collective-permute-start.14 = (bf16[32,4096]{1,0:T(8,128)(2,1)S(1)}, bf16[32,4096]{1,0:T(8,128)(2,1)S(1)}, u32[]{:S(2)}, u32[]{:S(2)}) collective-permute-start(bf16[32,4096]{1,0:T(8,128)(2,1)S(1)} %collective-permute-done.12), channel_id=1, source_target_pairs={{0,4},{4,8},{8,12},{12,14},{14,10},{10,6},{6,2},{2,0},{1,5},{5,9},... | collective-permute-start | bytes 786440 | tf_op jit(solution)/shard_map/ppermute | solution.py:125
  106.0 4.8 %collective-permute-done.14 = bf16[32,4096]{1,0:T(8,128)(2,1)S(1)} collective-permute-done((bf16[32,4096]{1,0:T(8,128)(2,1)S(1)}, bf16[32,4096]{1,0:T(8,128)(2,1)S(1)}, u32[]{:S(2)}, u32[]{:S(2)}) %collective-permute-start.14) | collective-permute-done | bytes 262176 | tf_op jit(solution)/shard_map/ppermute | solution.py:125
  110.8 9.5 %fusion.46 = f32[256,2048]{1,0:T(8,128)} fusion(bf16[256,4096]{1,0:T(8,128)(2,1)S(1)} %constant_dynamic-update-slice_fusion, bf16[4096,2048]{1,0:T(8,128)(2,1)} %param.17), kind=kOutput, calls=%fused_computation.169 | convolution fusion | flops 4294967296 | bytes 20971520 | tf_op jit(solution)/shard_map/dot_general | solution.py:190
  120.3 3.0 %gather_fusion.6 = bf16[128,2048]{1,0:T(8,128)(2,1)S(1)} fusion(f32[256,2048]{1,0:T(8,128)} %fusion.46, s32[1024]{0:T(1024)S(1)} %pad_clamp_fusion), kind=kCustom, calls=%fused_computation.6 | custom fusion | bytes 1049088 | tf_op jit(solution)/shard_map/gather | solution.py:201
  123.4 3.2 %gather_fusion.5 = f32[128,2048]{1,0:T(8,128)S(1)} fusion(f32[256,2048]{1,0:T(8,128)} %fusion.46, s32[1024]{0:T(1024)S(1)} %pad_clamp_fusion.1), kind=kCustom, calls=%fused_computation.5 | custom fusion | bytes 2097664 | tf_op jit(solution)/shard_map/gather | solution.py:200
  126.6 2.0 %add_convert_fusion = bf16[128,2048]{1,0:T(8,128)(2,1)} fusion(f32[128,2048]{1,0:T(8,128)S(1)} %gather_fusion.5, bf16[128,2048]{1,0:T(8,128)(2,1)} %collective-permute-done.15), kind=kLoop, calls=%fused_computation.31 | loop fusion | flops 786432 | bytes 2097152 | tf_op jit(solution)/shard_map/convert_element_type | solution.py:203
  (102 shorter events, 15.2 us)
Async XLA Ops:
  0.0 72.9 %copy-start = (bf16[2,1536,2,128]{3,2,1,0:T(2,128)(2,1)S(1)}, bf16[2,1536,2,128]{3,2,1,0:T(2,128)(2,1)}, u32[]{:S(2)}) copy-start(bf16[2,1536,2,128]{3,2,1,0:T(2,128)(2,1)} %param.18) | copy-start | bytes 4718596
  0.0 20.6 %copy-start.4 = (bf16[128,2048]{1,0:T(8,128)(2,1)S(1)}, bf16[128,2048]{1,0:T(8,128)(2,1)}, u32[]{:S(2)}) copy-start(bf16[128,2048]{1,0:T(8,128)(2,1)} %param.13) | copy-start | bytes 1572868
  0.0 20.6 %collective-permute-start = (bf16[128,2048]{1,0:T(8,128)(2,1)}, bf16[128,2048]{1,0:T(8,128)(2,1)}, u32[]{:S(2)}, u32[]{:S(2)}) collective-permute-start(bf16[128,2048]{1,0:T(8,128)(2,1)} %param.13), channel_id=1, source_target_pairs={{0,1},{1,0},{2,3},{3,2},{4,5},{5,4},{6,7},{7,6},{8,9},{9,8},{10,11... | collective-permute-start | bytes 1572872 | tf_op jit(solution)/shard_map/ppermute | solution.py:142
  24.1 2.1 %copy-start.2 = (bf16[256,2048]{1,0:T(8,128)(2,1)S(1)}, bf16[256,2048]{1,0:T(8,128)(2,1)}, u32[]{:S(2)}) copy-start(bf16[256,2048]{1,0:T(8,128)(2,1)} %gather_fusion.4) | copy-start | bytes 3145732
  24.1 2.2 %copy-start.3 = (bf16[2048,256]{1,0:T(8,128)(2,1)S(1)}, bf16[2048,256]{1,0:T(8,128)(2,1)}, u32[]{:S(2)}) copy-start(bf16[2048,256]{1,0:T(8,128)(2,1)} %param.16) | copy-start | bytes 3145732
  35.3 10.2 %collective-permute-start.1 = (bf16[32,4608]{1,0:T(8,128)(2,1)S(1)}, bf16[32,4608]{1,0:T(8,128)(2,1)S(1)}, u32[]{:S(2)}, u32[]{:S(2)}) collective-permute-start(bf16[32,4608]{1,0:T(8,128)(2,1)S(1)} %get-tuple-element.13), channel_id=1, source_target_pairs={{0,4},{4,8},{8,12},{12,14},{14,10},{10,6},{6,2},{2,0},{1,5},{5,9},... | collective-permute-start | bytes 884744 | tf_op jit(solution)/shard_map/ppermute | solution.py:109
  38.0 9.5 %collective-permute-start.5 = (bf16[32,4608]{1,0:T(8,128)(2,1)S(1)}, bf16[32,4608]{1,0:T(8,128)(2,1)S(1)}, u32[]{:S(2)}, u32[]{:S(2)}) collective-permute-start(bf16[32,4608]{1,0:T(8,128)(2,1)S(1)} %get-tuple-element.14), channel_id=1, source_target_pairs={{0,2},{4,0},{8,4},{12,8},{14,12},{10,14},{6,10},{2,6},{1,3},{5,1},... | collective-permute-start | bytes 884744 | tf_op jit(solution)/shard_map/ppermute | solution.py:111
  45.7 8.9 %collective-permute-start.2 = (bf16[32,4608]{1,0:T(8,128)(2,1)S(1)}, bf16[32,4608]{1,0:T(8,128)(2,1)S(1)}, u32[]{:S(2)}, u32[]{:S(2)}) collective-permute-start(bf16[32,4608]{1,0:T(8,128)(2,1)S(1)} %add_convert_fusion.5), channel_id=1, source_target_pairs={{0,4},{4,8},{8,12},{12,14},{14,10},{10,6},{6,2},{2,0},{1,5},{5,9},... | collective-permute-start | bytes 884744 | tf_op jit(solution)/shard_map/ppermute | solution.py:109
  54.7 8.0 %collective-permute-start.3 = (bf16[32,4608]{1,0:T(8,128)(2,1)S(1)}, bf16[32,4608]{1,0:T(8,128)(2,1)S(1)}, u32[]{:S(2)}, u32[]{:S(2)}) collective-permute-start(bf16[32,4608]{1,0:T(8,128)(2,1)S(1)} %get-tuple-element.11), channel_id=1, source_target_pairs={{0,4},{4,8},{8,12},{12,14},{14,10},{10,6},{6,2},{2,0},{1,5},{5,9},... | collective-permute-start | bytes 884744 | tf_op jit(solution)/shard_map/ppermute | solution.py:109
  56.3 7.4 %collective-permute-start.6 = (bf16[32,4608]{1,0:T(8,128)(2,1)S(1)}, bf16[32,4608]{1,0:T(8,128)(2,1)S(1)}, u32[]{:S(2)}, u32[]{:S(2)}) collective-permute-start(bf16[32,4608]{1,0:T(8,128)(2,1)S(1)} %get-tuple-element.12), channel_id=1, source_target_pairs={{0,2},{4,0},{8,4},{12,8},{14,12},{10,14},{6,10},{2,6},{1,3},{5,1},... | collective-permute-start | bytes 884744 | tf_op jit(solution)/shard_map/ppermute | solution.py:111
  63.8 6.8 %collective-permute-start.4 = (bf16[32,4608]{1,0:T(8,128)(2,1)S(1)}, bf16[32,4608]{1,0:T(8,128)(2,1)S(1)}, u32[]{:S(2)}, u32[]{:S(2)}) collective-permute-start(bf16[32,4608]{1,0:T(8,128)(2,1)S(1)} %get-tuple-element.9), channel_id=1, source_target_pairs={{0,4},{4,8},{8,12},{12,14},{14,10},{10,6},{6,2},{2,0},{1,5},{5,9},... | collective-permute-start | bytes 884744 | tf_op jit(solution)/shard_map/ppermute | solution.py:109
  65.5 6.7 %collective-permute-start.7 = (bf16[32,4608]{1,0:T(8,128)(2,1)S(1)}, bf16[32,4608]{1,0:T(8,128)(2,1)S(1)}, u32[]{:S(2)}, u32[]{:S(2)}) collective-permute-start(bf16[32,4608]{1,0:T(8,128)(2,1)S(1)} %get-tuple-element.10), channel_id=1, source_target_pairs={{0,2},{4,0},{8,4},{12,8},{14,12},{10,14},{6,10},{2,6},{1,3},{5,1},... | collective-permute-start | bytes 884744 | tf_op jit(solution)/shard_map/ppermute | solution.py:111
  75.2 1.4 %copy-start.5 = (bf16[2,1536,2,128]{3,2,1,0:T(2,128)(2,1)S(1)}, bf16[2,1536,2,128]{3,2,1,0:T(2,128)(2,1)}, u32[]{:S(2)}) copy-start(bf16[2,1536,2,128]{3,2,1,0:T(2,128)(2,1)} %param.19) | copy-start | bytes 4718596
  79.0 8.5 %collective-permute-start.9 = (bf16[32,4096]{1,0:T(8,128)(2,1)S(1)}, bf16[32,4096]{1,0:T(8,128)(2,1)S(1)}, u32[]{:S(2)}, u32[]{:S(2)}) collective-permute-start(bf16[32,4096]{1,0:T(8,128)(2,1)S(1)} %convert_element_type.132), channel_id=1, source_target_pairs={{0,2},{4,0},{8,4},{12,8},{14,12},{10,14},{6,10},{2,6},{1,3},{5,1},... | collective-permute-start | bytes 786440 | tf_op jit(solution)/shard_map/ppermute | solution.py:128
  79.5 8.7 %collective-permute-start.8 = (bf16[32,4096]{1,0:T(8,128)(2,1)S(1)}, bf16[32,4096]{1,0:T(8,128)(2,1)S(1)}, u32[]{:S(2)}, u32[]{:S(2)}) collective-permute-start(bf16[32,4096]{1,0:T(8,128)(2,1)S(1)} %convert_element_type.132), channel_id=1, source_target_pairs={{0,4},{4,8},{8,12},{12,14},{14,10},{10,6},{6,2},{2,0},{1,5},{5,9},... | collective-permute-start | bytes 786440 | tf_op jit(solution)/shard_map/ppermute | solution.py:125
  87.5 9.1 %collective-permute-start.11 = (bf16[32,4096]{1,0:T(8,128)(2,1)S(1)}, bf16[32,4096]{1,0:T(8,128)(2,1)S(1)}, u32[]{:S(2)}, u32[]{:S(2)}) collective-permute-start(bf16[32,4096]{1,0:T(8,128)(2,1)S(1)} %collective-permute-done.9), channel_id=1, source_target_pairs={{0,2},{4,0},{8,4},{12,8},{14,12},{10,14},{6,10},{2,6},{1,3},{5,1},... | collective-permute-start | bytes 786440 | tf_op jit(solution)/shard_map/ppermute | solution.py:128
  88.2 8.8 %collective-permute-start.10 = (bf16[32,4096]{1,0:T(8,128)(2,1)S(1)}, bf16[32,4096]{1,0:T(8,128)(2,1)S(1)}, u32[]{:S(2)}, u32[]{:S(2)}) collective-permute-start(bf16[32,4096]{1,0:T(8,128)(2,1)S(1)} %collective-permute-done.8), channel_id=1, source_target_pairs={{0,4},{4,8},{8,12},{12,14},{14,10},{10,6},{6,2},{2,0},{1,5},{5,9},... | collective-permute-start | bytes 786440 | tf_op jit(solution)/shard_map/ppermute | solution.py:125
  96.5 9.4 %collective-permute-start.13 = (bf16[32,4096]{1,0:T(8,128)(2,1)S(1)}, bf16[32,4096]{1,0:T(8,128)(2,1)S(1)}, u32[]{:S(2)}, u32[]{:S(2)}) collective-permute-start(bf16[32,4096]{1,0:T(8,128)(2,1)S(1)} %collective-permute-done.11), channel_id=1, source_target_pairs={{0,2},{4,0},{8,4},{12,8},{14,12},{10,14},{6,10},{2,6},{1,3},{5,1},... | collective-permute-start | bytes 786440 | tf_op jit(solution)/shard_map/ppermute | solution.py:128
  97.0 7.4 %collective-permute-start.12 = (bf16[32,4096]{1,0:T(8,128)(2,1)S(1)}, bf16[32,4096]{1,0:T(8,128)(2,1)S(1)}, u32[]{:S(2)}, u32[]{:S(2)}) collective-permute-start(bf16[32,4096]{1,0:T(8,128)(2,1)S(1)} %collective-permute-done.10), channel_id=1, source_target_pairs={{0,4},{4,8},{8,12},{12,14},{14,10},{10,6},{6,2},{2,0},{1,5},{5,9},... | collective-permute-start | bytes 786440 | tf_op jit(solution)/shard_map/ppermute | solution.py:125
  104.4 6.4 %collective-permute-start.14 = (bf16[32,4096]{1,0:T(8,128)(2,1)S(1)}, bf16[32,4096]{1,0:T(8,128)(2,1)S(1)}, u32[]{:S(2)}, u32[]{:S(2)}) collective-permute-start(bf16[32,4096]{1,0:T(8,128)(2,1)S(1)} %collective-permute-done.12), channel_id=1, source_target_pairs={{0,4},{4,8},{8,12},{12,14},{14,10},{10,6},{6,2},{2,0},{1,5},{5,9},... | collective-permute-start | bytes 786440 | tf_op jit(solution)/shard_map/ppermute | solution.py:125
  123.3 3.3 %collective-permute-start.15 = (bf16[128,2048]{1,0:T(8,128)(2,1)S(1)}, bf16[128,2048]{1,0:T(8,128)(2,1)}, u32[]{:S(2)}, u32[]{:S(2)}) collective-permute-start(bf16[128,2048]{1,0:T(8,128)(2,1)S(1)} %gather_fusion.6), channel_id=1, source_target_pairs={{0,1},{1,0},{2,3},{3,2},{4,5},{5,4},{6,7},{7,6},{8,9},{9,8},{10,11... | collective-permute-start | bytes 1572872 | tf_op jit(solution)/shard_map/ppermute | solution.py:202
  123.4 5.2 %copy-start.1 = (bf16[2,1536,2,128]{3,2,1,0:T(2,128)(2,1)S(1)}, bf16[2,1536,2,128]{3,2,1,0:T(2,128)(2,1)}, u32[]{:S(2)}) copy-start(bf16[2,1536,2,128]{3,2,1,0:T(2,128)(2,1)} %param.18) | copy-start | bytes 4718596

commit v3 on v2

--- a/solution.py
+++ b/solution.py
@@ -129,29 +129,42 @@
                 got.append(backward)
         return jnp.concatenate(got, axis=0)
 
+    def lookup(table, index):
+        table = jnp.asarray(table, jnp.int32)
+        hit = index[..., None] == jnp.arange(table.shape[0], dtype=jnp.int32)
+        return jnp.sum(jnp.where(hit, table, 0), axis=-1)
+
+    def one_hot(rows, width):
+        return (rows[:, None] == jnp.arange(width, dtype=jnp.int32)[None, :]).astype(jnp.bfloat16)
+
     def body(
         tokens, q_weight, key_matrix, value_matrix, o_weight, k_cache, value_cache, cache_len, slot_seq
     ):
-        row_index = lax.axis_index("row")
-        col_index = lax.axis_index("col")
+        row_index = lax.axis_index("row").astype(jnp.int32)
+        col_index = lax.axis_index("col").astype(jnp.int32)
         n_col = 2
         seq_dev = k_cache.shape[0]
         head_dim = k_cache.shape[3]
         slot_total = slot_seq.shape[0]
         own_rows = tokens.shape[0]
+        span_rows = own_rows * n_col
+        new_len = span_rows // slot_total
+        block_rows = seq_dev * new_len
         other_tokens = lax.ppermute(tokens, "col", [(0, 1), (1, 0)])
-        both = jnp.concatenate([tokens, other_tokens], axis=0)
-        new_len = own_rows * n_col // slot_total
-        my_pos = jnp.asarray(position_of, jnp.int32)[row_index]
-        ring_arr = jnp.asarray(ring, jnp.int32)
-        block_dev = ring_arr[(my_pos + jnp.arange(n_row)) % n_row]
-        slots = (block_dev[:, None] * seq_dev + jnp.arange(seq_dev)[None, :]).reshape(-1)
-        sequences = slot_seq[slots]
-        token_rows = (sequences[:, None] * new_len + jnp.arange(new_len)[None, :]).reshape(-1)
-        local_rows = jnp.where(
-            token_rows // own_rows == col_index, token_rows % own_rows, own_rows + token_rows % own_rows
-        )
-        chosen = both[local_rows]
+        my_pos = lookup(position_of, row_index)
+        block_dev = lookup(ring, (my_pos + jnp.arange(n_row, dtype=jnp.int32)) % n_row)
+        slots = (block_dev[:, None] * seq_dev + jnp.arange(seq_dev, dtype=jnp.int32)[None, :]).reshape(-1)
+        sequences = lookup(slot_seq, slots)
+        local = jnp.arange(span_rows, dtype=jnp.int32)
+        token_rows = jnp.repeat(sequences, new_len) * new_len + local % new_len
+        from_own = token_rows // own_rows == col_index
+        in_half = token_rows % own_rows
+        pick_own = one_hot(jnp.where(from_own, in_half, -1), own_rows)
+        pick_other = one_hot(jnp.where(from_own, -1, in_half), own_rows)
+        chosen = (
+            jnp.dot(pick_own, tokens, preferred_element_type=jnp.float32)
+            + jnp.dot(pick_other, other_tokens, preferred_element_type=jnp.float32)
+        ).astype(jnp.bfloat16)
         q_part = jnp.dot(chosen, q_weight, preferred_element_type=jnp.float32)
         k_part = jnp.dot(chosen, key_matrix, preferred_element_type=jnp.float32)
         v_part = jnp.dot(chosen, value_matrix, preferred_element_type=jnp.float32)
@@ -161,14 +174,12 @@
             [q_part.astype(jnp.bfloat16), k_part.astype(jnp.bfloat16), v_part.astype(jnp.bfloat16)],
             axis=1,
         )
-        block_rows = seq_dev * new_len
         blocks = [joined[k * block_rows : (k + 1) * block_rows] for k in range(n_row)]
         summed = ring_reduce_scatter(blocks)
         q_sum = summed[:, :q_width]
         key_total_sum = summed[:, q_width : q_width + k_width]
         value_total_sum = summed[:, q_width + k_width :]
-        local_slots = row_index * seq_dev + jnp.arange(seq_dev)
-        starts = cache_len[slot_seq[local_slots]]
+        starts = lookup(cache_len, sequences[:seq_dev])
         token_places = (starts[:, None] + jnp.arange(new_len)[None, :]).reshape(-1).astype(jnp.float32)
         row_total = q_sum.shape[0]
         queries = apply_turning(q_sum.reshape(row_total, -1, head_dim), token_places).astype(
@@ -187,19 +198,25 @@
             starts,
         )
         attended = results.reshape(seq_dev * new_len, -1)
-        products = jnp.dot(ring_all_gather(attended), o_weight, preferred_element_type=jnp.float32)
-        matches = (slot_seq[:, None] == jnp.arange(slot_total)[None, :]).astype(jnp.int32)
-        slot_of = jnp.sum(matches * jnp.arange(slot_total)[:, None], axis=0)
-        span = jnp.arange(own_rows * n_col)
-        seq_of = span // new_len
-        slot_t = slot_of[seq_of]
-        offset = (jnp.asarray(position_of, jnp.int32)[slot_t // seq_dev] - my_pos) % n_row
-        stacked = jnp.asarray(stacked_of_offset, jnp.int32)[offset]
-        product_rows = stacked * block_rows + (slot_t % seq_dev) * new_len + span % new_len
-        product_rows = product_rows.reshape(n_col, own_rows)
-        mine = products[lax.dynamic_index_in_dim(product_rows, col_index, 0, keepdims=False)]
-        theirs = products[lax.dynamic_index_in_dim(product_rows, 1 - col_index, 0, keepdims=False)]
+        stacked = ring_all_gather(attended)
+        slot_ids = jnp.arange(slot_total, dtype=jnp.int32)
+        slot_of = jnp.sum(jnp.where(slot_seq[:, None] == slot_ids[None, :], slot_ids[:, None], 0), axis=0)
+        offset = (lookup(position_of, slot_ids // seq_dev) - my_pos) % n_row
+        stacked_row_of_slot = lookup(stacked_of_offset, offset) * block_rows + (slot_ids % seq_dev) * new_len
+        seq_base = lookup(stacked_row_of_slot, slot_of)
+        span = jnp.arange(own_rows, dtype=jnp.int32)
+        def half_rows(half):
+            t = half * own_rows + span
+            return lookup(seq_base, t // new_len) + t % new_len
+        theirs_att = jnp.dot(
+            one_hot(half_rows(1 - col_index), span_rows), stacked, preferred_element_type=jnp.float32
+        ).astype(jnp.bfloat16)
+        theirs = jnp.dot(theirs_att, o_weight, preferred_element_type=jnp.float32)
         received = lax.ppermute(theirs.astype(jnp.bfloat16), "col", [(0, 1), (1, 0)])
+        mine_att = jnp.dot(
+            one_hot(half_rows(col_index), span_rows), stacked, preferred_element_type=jnp.float32
+        ).astype(jnp.bfloat16)
+        mine = jnp.dot(mine_att, o_weight, preferred_element_type=jnp.float32)
         return (mine + received.astype(jnp.float32)).astype(jnp.bfloat16)
 
     return body

time: 129 us -> 117 us (0.907)
  matrix products: 24.8 us -> 34.6 us
  local copies, waits for them, and re-layouts: 16.6 us -> 7.28 us
  other arithmetic: 18.5 us -> 9.9 us
  waiting for transfers between devices: 51.4 us -> 47.7 us
    gather x8 -> x0, local copies, waits for them, and re-layouts: 14.5 us -> none  [the longest x1 3.16 us: body(): products[lax.dynamic_index_in_dim(product_rows, col_index, 0, keepdims=Fa...]
    dot_general x1 -> x4, matrix products: 9.5 us -> 21 us  [the longest x1 9.96 us: body(): mine = jnp.dot(mine_att, o_weight, preferred_element_type=jnp.float32)]
    gather x21 -> x0, other arithmetic: 10.3 us -> none  [the longest x11 10.2 us: body(): slot_t = slot_of[seq_of]]
    unnamed x21 -> x19, local copies, waits for them, and re-layouts: 0.32 us -> 5.93 us
    reduce_sum x1 -> x8, other arithmetic: 0.74 us -> 5.65 us  [the longest x7 4.72 us: lookup(): return jnp.sum(jnp.where(hit, table, 0), axis=-1)]
    ppermute x4, waiting for transfers between devices: 10.9 us -> 7.84 us  [ring_all_gather(): forward = lax.ppermute(forward, 'row', forward_pairs)]
    ppermute x3, waiting for transfers between devices: 13.1 us -> 11 us  [ring_all_gather(): backward = lax.ppermute(backward, 'row', backward_pairs)]
    convert_element_type x1 -> x0, other arithmetic: 1.97 us -> none  [body(): return (mine + received.astype(jnp.float32)).astype(jnp.bfloat16)]
  transfers between devices with their start and end apart: 16 -> 16, of which waited for: 11 -> 12; matrix products, arithmetic and copies ran while one was open for 18% -> 12% of each run, Pallas kernels for 0% -> 0%
where the time goes in v3:
time: 117 us
  waiting for transfers between devices  47.7 us (41%)
  matrix products  34.6 us (30%)
  starting transfers between devices  17 us (15%)
  other arithmetic  9.9 us (8%)
  local copies, waits for them, and re-layouts  7.28 us (6%)
    ppermute x4, waiting for transfers between devices, ring_reduce_scatter(): got_forward = lax.ppermute(forward, 'row', forward_pairs)  24.4 us
    ppermute x3, waiting for transfers between devices, ring_all_gather(): backward = lax.ppermute(backward, 'row', backward_pairs)  11 us
    dot_general x1, matrix products, body(): mine = jnp.dot(mine_att, o_weight, preferred_element_type=jnp.float32)  9.96 us
    dot_general x1, matrix products, body(): theirs = jnp.dot(theirs_att, o_weight, preferred_element_type=jnp.float32)  9.05 us
    dot_general x1, matrix products, body(): q_part = jnp.dot(chosen, q_weight, preferred_element_type=jnp.float32)  8.41 us
    ppermute x4, waiting for transfers between devices, ring_all_gather(): forward = lax.ppermute(forward, 'row', forward_pairs)  7.84 us
    ppermute x4, starting transfers between devices, ring_reduce_scatter(): got_forward = lax.ppermute(forward, 'row', forward_pairs)  7.8 us
    ppermute x4, starting transfers between devices, ring_all_gather(): forward = lax.ppermute(forward, 'row', forward_pairs)  6.31 us
  transfers between devices with their start and end apart: 16, of which 12 were waited for; matrix products, arithmetic and copies ran while one was open for 12% of the time, Pallas kernels for 0%

profile of v3, /device:TPU:0, one launch (start us, length us, event | category | flops | bytes accessed | tf_op | source)
XLA Modules:
  0.0 116.8 jit_solution(7642353825415892166)
XLA Ops:
  0.5 1.3 %fusion.45 = s32[]{:T(128)} fusion(s32[8]{0:T(128)} %constant.149.clone, s32[]{:T(128)S(6)} %axis_index.25), kind=kLoop, calls=%fused_computation.129 | loop fusion | flops 23 | bytes 40 | tf_op jit(solution)/shard_map/reduce_sum | solution.py:135
  2.5 0.8 select_reduce_fusion.5
  4.7 0.7 select_reduce_fusion.6
  5.6 0.9 select_reduce_fusion.4
  6.5 0.8 fusion.39
  7.7 1.5 %fusion.29 = f32[256,2048]{1,0:T(8,128)S(1)} fusion(bf16[128,2048]{1,0:T(8,128)(2,1)} %param.13, s32[256]{0:T(256)S(1)} %broadcast_select_fusion.1), kind=kOutput, calls=%fused_computation.51 | convolution fusion | flops 134250496 | bytes 2622464 | tf_op jit(solution)/shard_map/dot_general | solution.py:165
  11.4 8.4 %convolution_convert_fusion = bf16[256,4096]{1,0:T(8,128)(2,1)S(1)} fusion(bf16[256,2048]{1,0:T(8,128)(2,1)S(1)} %fusion.6, bf16[2048,4096]{1,0:T(8,128)(2,1)} %param.14), kind=kOutput, calls=%fused_computation.4 | convolution fusion | flops 4296015872 | bytes 19922944 | tf_op jit(solution)/shard_map/dot_general | solution.py:168
  20.0 2.8 %collective-permute-start.1 = (bf16[32,4608]{1,0:T(8,128)(2,1)S(1)}, bf16[32,4608]{1,0:T(8,128)(2,1)S(1)}, u32[]{:S(2)}, u32[]{:S(2)}) collective-permute-start(bf16[32,4608]{1,0:T(8,128)(2,1)S(1)} %get-tuple-element.16), channel_id=1, source_target_pairs={{0,4},{4,8},{8,12},{12,14},{14,10},{10,6},{6,2},{2,0},{1,5},{5,9},... | collective-permute-start | bytes 884744 | tf_op jit(solution)/shard_map/ppermute | solution.py:109
  23.0 7.2 %collective-permute-done.1 = bf16[32,4608]{1,0:T(8,128)(2,1)S(1)} collective-permute-done((bf16[32,4608]{1,0:T(8,128)(2,1)S(1)}, bf16[32,4608]{1,0:T(8,128)(2,1)S(1)}, u32[]{:S(2)}, u32[]{:S(2)}) %collective-permute-start.1) | collective-permute-done | bytes 294944 | tf_op jit(solution)/shard_map/ppermute | solution.py:109
  30.3 1.8 %collective-permute-start.2 = (bf16[32,4608]{1,0:T(8,128)(2,1)S(1)}, bf16[32,4608]{1,0:T(8,128)(2,1)S(1)}, u32[]{:S(2)}, u32[]{:S(2)}) collective-permute-start(bf16[32,4608]{1,0:T(8,128)(2,1)S(1)} %add_convert_fusion.4), channel_id=1, source_target_pairs={{0,4},{4,8},{8,12},{12,14},{14,10},{10,6},{6,2},{2,0},{1,5},{5,9},... | collective-permute-start | bytes 884744 | tf_op jit(solution)/shard_map/ppermute | solution.py:109
  32.2 6.8 %collective-permute-done.2 = bf16[32,4608]{1,0:T(8,128)(2,1)S(1)} collective-permute-done((bf16[32,4608]{1,0:T(8,128)(2,1)S(1)}, bf16[32,4608]{1,0:T(8,128)(2,1)S(1)}, u32[]{:S(2)}, u32[]{:S(2)}) %collective-permute-start.2) | collective-permute-done | bytes 294944 | tf_op jit(solution)/shard_map/ppermute | solution.py:109
  39.2 1.6 %collective-permute-start.3 = (bf16[32,4608]{1,0:T(8,128)(2,1)S(1)}, bf16[32,4608]{1,0:T(8,128)(2,1)S(1)}, u32[]{:S(2)}, u32[]{:S(2)}) collective-permute-start(bf16[32,4608]{1,0:T(8,128)(2,1)S(1)} %get-tuple-element.14), channel_id=1, source_target_pairs={{0,4},{4,8},{8,12},{12,14},{14,10},{10,6},{6,2},{2,0},{1,5},{5,9},... | collective-permute-start | bytes 884744 | tf_op jit(solution)/shard_map/ppermute | solution.py:109
  41.3 5.8 %collective-permute-done.3 = bf16[32,4608]{1,0:T(8,128)(2,1)S(1)} collective-permute-done((bf16[32,4608]{1,0:T(8,128)(2,1)S(1)}, bf16[32,4608]{1,0:T(8,128)(2,1)S(1)}, u32[]{:S(2)}, u32[]{:S(2)}) %collective-permute-start.3) | collective-permute-done | bytes 294944 | tf_op jit(solution)/shard_map/ppermute | solution.py:109
  47.1 1.0 collective-permute-done.6
  48.2 1.6 %collective-permute-start.4 = (bf16[32,4608]{1,0:T(8,128)(2,1)S(1)}, bf16[32,4608]{1,0:T(8,128)(2,1)S(1)}, u32[]{:S(2)}, u32[]{:S(2)}) collective-permute-start(bf16[32,4608]{1,0:T(8,128)(2,1)S(1)} %get-tuple-element.12), channel_id=1, source_target_pairs={{0,4},{4,8},{8,12},{12,14},{14,10},{10,6},{6,2},{2,0},{1,5},{5,9},... | collective-permute-start | bytes 884744 | tf_op jit(solution)/shard_map/ppermute | solution.py:109
  50.5 4.5 %collective-permute-done.4 = bf16[32,4608]{1,0:T(8,128)(2,1)S(1)} collective-permute-done((bf16[32,4608]{1,0:T(8,128)(2,1)S(1)}, bf16[32,4608]{1,0:T(8,128)(2,1)S(1)}, u32[]{:S(2)}, u32[]{:S(2)}) %collective-permute-start.4) | collective-permute-done | bytes 294944 | tf_op jit(solution)/shard_map/ppermute | solution.py:109
  55.0 1.6 %collective-permute-done.7 = bf16[32,4608]{1,0:T(8,128)(2,1)S(1)} collective-permute-done((bf16[32,4608]{1,0:T(8,128)(2,1)S(1)}, bf16[32,4608]{1,0:T(8,128)(2,1)S(1)}, u32[]{:S(2)}, u32[]{:S(2)}) %collective-permute-start.7) | collective-permute-done | bytes 294944 | tf_op jit(solution)/shard_map/ppermute | solution.py:111
  57.3 1.3 %bitcast_reduce_fusion = (f32[2,2,16,16]{2,3,1,0:T(8,128)S(1)}, f32[2,2,16,16,1536]{4,3,2,1,0:T(8,128)S(1)}) fusion(pred[2,1536]{1,0:T(4,128)(4,1)S(1)} %iota_compare_fusion.10, bf16[2,1536,2,128,1]{3,2,1,0,4:T(2,128)(2,1)S(1)} %bitcast.57, bf16[2,16,2,16,64]{4,3,2,1,0:T(8,128)(2,1)S(1)} %bitcast.61, bf16[2,16,2,16,64]{4,3,2,1,0:T(8,128)(2,1)S(1)} %bitcast.59), kind=kOutput, calls=%fused_computation.1 | convolution fusion | flops 407895040 | bytes 8133632 | tf_op jit(solution)/shard_map/vmap(nkgd,ckd->kgnc)/dot_general | solution.py:30
  58.6 0.8 fusion.53
  59.6 1.4 %fusion.1 = f32[2,2,16,16]{2,3,1,0:T(8,128)S(1)} fusion(f32[2,2,16,16,1536]{4,3,2,1,0:T(8,128)S(1)} %get-tuple-element.27, f32[2,2,16,16]{2,3,1,0:T(8,128)S(1)} %max.7, pred[2,1536]{1,0:T(4,128)(4,1)S(1)} %iota_compare_fusion.10), kind=kLoop, calls=%fused_computation.7 | loop fusion | flops 6290432 | bytes 6302720 | tf_op jit(solution)/shard_map/vmap()/reduce_sum | solution.py:44
  61.0 1.9 %fusion.13 = f32[2,16,2,16,128]{4,3,1,2,0:T(8,128)S(1)} fusion(bf16[2,1536,2,128,1]{3,2,1,0,4:T(2,128)(2,1)S(1)} %bitcast.67, f32[2,2,16,16,1536]{4,3,2,1,0:T(8,128)S(1)} %get-tuple-element.27, f32[2,2,16,16]{2,3,1,0:T(8,128)S(1)} %max.7, pred[2,1536]{1,0:T(4,128)(4,1)S(1)} %iota_compare_fusion.10), kind=kOutput, calls=%fused_computation.21 | convolution fusion | flops 408944640 | bytes 8395776 | tf_op jit(solution)/shard_map/vmap(kgnc,ckd->nkgd)/dot_general | solution.py:45
  63.9 1.6 %collective-permute-start.8 = (bf16[32,4096]{1,0:T(8,128)(2,1)S(1)}, bf16[32,4096]{1,0:T(8,128)(2,1)S(1)}, u32[]{:S(2)}, u32[]{:S(2)}) collective-permute-start(bf16[32,4096]{1,0:T(8,128)(2,1)S(1)} %convert_element_type.145), channel_id=1, source_target_pairs={{0,4},{4,8},{8,12},{12,14},{14,10},{10,6},{6,2},{2,0},{1,5},{5,9},... | collective-permute-start | bytes 786440 | tf_op jit(solution)/shard_map/ppermute | solution.py:125
  66.2 5.8 %collective-permute-done.9 = bf16[32,4096]{1,0:T(8,128)(2,1)S(1)} collective-permute-done((bf16[32,4096]{1,0:T(8,128)(2,1)S(1)}, bf16[32,4096]{1,0:T(8,128)(2,1)S(1)}, u32[]{:S(2)}, u32[]{:S(2)}) %collective-permute-start.9) | collective-permute-done | bytes 262176 | tf_op jit(solution)/shard_map/ppermute | solution.py:128
  72.7 1.6 %collective-permute-start.10 = (bf16[32,4096]{1,0:T(8,128)(2,1)S(1)}, bf16[32,4096]{1,0:T(8,128)(2,1)S(1)}, u32[]{:S(2)}, u32[]{:S(2)}) collective-permute-start(bf16[32,4096]{1,0:T(8,128)(2,1)S(1)} %collective-permute-done.8), channel_id=1, source_target_pairs={{0,4},{4,8},{8,12},{12,14},{14,10},{10,6},{6,2},{2,0},{1,5},{5,9},... | collective-permute-start | bytes 786440 | tf_op jit(solution)/shard_map/ppermute | solution.py:125
  75.7 5.2 %collective-permute-done.11 = bf16[32,4096]{1,0:T(8,128)(2,1)S(1)} collective-permute-done((bf16[32,4096]{1,0:T(8,128)(2,1)S(1)}, bf16[32,4096]{1,0:T(8,128)(2,1)S(1)}, u32[]{:S(2)}, u32[]{:S(2)}) %collective-permute-start.11) | collective-permute-done | bytes 262176 | tf_op jit(solution)/shard_map/ppermute | solution.py:128
  81.4 1.6 %collective-permute-start.12 = (bf16[32,4096]{1,0:T(8,128)(2,1)S(1)}, bf16[32,4096]{1,0:T(8,128)(2,1)S(1)}, u32[]{:S(2)}, u32[]{:S(2)}) collective-permute-start(bf16[32,4096]{1,0:T(8,128)(2,1)S(1)} %collective-permute-done.10), channel_id=1, source_target_pairs={{0,4},{4,8},{8,12},{12,14},{14,10},{10,6},{6,2},{2,0},{1,5},{5,9},... | collective-permute-start | bytes 786440 | tf_op jit(solution)/shard_map/ppermute | solution.py:125
  84.5 4.2 %collective-permute-done.12 = bf16[32,4096]{1,0:T(8,128)(2,1)S(1)} collective-permute-done((bf16[32,4096]{1,0:T(8,128)(2,1)S(1)}, bf16[32,4096]{1,0:T(8,128)(2,1)S(1)}, u32[]{:S(2)}, u32[]{:S(2)}) %collective-permute-start.12) | collective-permute-done | bytes 262176 | tf_op jit(solution)/shard_map/ppermute | solution.py:125
  88.7 1.6 %collective-permute-start.14 = (bf16[32,4096]{1,0:T(8,128)(2,1)S(1)}, bf16[32,4096]{1,0:T(8,128)(2,1)S(1)}, u32[]{:S(2)}, u32[]{:S(2)}) collective-permute-start(bf16[32,4096]{1,0:T(8,128)(2,1)S(1)} %collective-permute-done.12), channel_id=1, source_target_pairs={{0,4},{4,8},{8,12},{12,14},{14,10},{10,6},{6,2},{2,0},{1,5},{5,9},... | collective-permute-start | bytes 786440 | tf_op jit(solution)/shard_map/ppermute | solution.py:125
  91.7 3.3 %collective-permute-done.14 = bf16[32,4096]{1,0:T(8,128)(2,1)S(1)} collective-permute-done((bf16[32,4096]{1,0:T(8,128)(2,1)S(1)}, bf16[32,4096]{1,0:T(8,128)(2,1)S(1)}, u32[]{:S(2)}, u32[]{:S(2)}) %collective-permute-start.14) | collective-permute-done | bytes 262176 | tf_op jit(solution)/shard_map/ppermute | solution.py:125
  95.8 9.1 %convolution_convert_fusion.3 = bf16[128,2048]{1,0:T(8,128)(2,1)S(1)} fusion(bf16[4096,2048]{1,0:T(8,128)(2,1)} %param.17, bf16[256,4096]{1,0:T(8,128)(2,1)} %constant_dynamic-update-slice_fusion, s32[128]{0:T(128)S(1)} %fusion.44), kind=kOutput, calls=%fused_computation.13 | convolution fusion | flops 2416738304 | bytes 19399168 | tf_op jit(solution)/shard_map/dot_general | solution.py:214
  104.9 1.9 %collective-permute-done.15 = bf16[128,2048]{1,0:T(8,128)(2,1)S(1)} collective-permute-done((bf16[128,2048]{1,0:T(8,128)(2,1)S(1)}, bf16[128,2048]{1,0:T(8,128)(2,1)S(1)}, u32[]{:S(2)}, u32[]{:S(2)}) %collective-permute-start.15) | collective-permute-done | bytes 524320 | tf_op jit(solution)/shard_map/ppermute | solution.py:215
  106.8 10.0 %fusion.12 = bf16[128,2048]{1,0:T(8,128)(2,1)} fusion(bf16[4096,2048]{1,0:T(8,128)(2,1)} %param.17, bf16[256,4096]{1,0:T(8,128)(2,1)} %constant_dynamic-update-slice_fusion, bf16[128,2048]{1,0:T(8,128)(2,1)S(1)} %collective-permute-done.15, s32[128]{0:T(128)S(1)} %fusion.43), kind=kOutput, calls=%fused_computation.20 | convolution fusion | flops 2417262592 | bytes 19923456 | tf_op jit(solution)/shard_map/dot_general | solution.py:219
  (79 shorter events, 16.0 us)
Async XLA Ops:
  0.0 57.3 %copy-start = (bf16[2,1536,2,128]{3,2,1,0:T(2,128)(2,1)S(1)}, bf16[2,1536,2,128]{3,2,1,0:T(2,128)(2,1)}, u32[]{:S(2)}) copy-start(bf16[2,1536,2,128]{3,2,1,0:T(2,128)(2,1)} %param.18) | copy-start | bytes 4718596
  0.0 9.2 %collective-permute-start = (bf16[128,2048]{1,0:T(8,128)(2,1)}, bf16[128,2048]{1,0:T(8,128)(2,1)S(1)}, u32[]{:S(2)}, u32[]{:S(2)}) collective-permute-start(bf16[128,2048]{1,0:T(8,128)(2,1)} %param.13), channel_id=1, source_target_pairs={{0,1},{1,0},{2,3},{3,2},{4,5},{5,4},{6,7},{7,6},{8,9},{9,8},{10,11... | collective-permute-start | bytes 1572872 | tf_op jit(solution)/shard_map/ppermute | solution.py:153
  9.2 1.2 %copy-start.2 = (bf16[2048,256]{1,0:T(8,128)(2,1)S(1)}, bf16[2048,256]{1,0:T(8,128)(2,1)}, u32[]{:S(2)}) copy-start(bf16[2048,256]{1,0:T(8,128)(2,1)} %param.16) | copy-start | bytes 3145732
  9.3 1.7 %copy-start.3 = (bf16[2048,256]{1,0:T(8,128)(2,1)S(1)}, bf16[2048,256]{1,0:T(8,128)(2,1)}, u32[]{:S(2)}) copy-start(bf16[2048,256]{1,0:T(8,128)(2,1)} %param.15) | copy-start | bytes 3145732
  20.0 10.2 %collective-permute-start.1 = (bf16[32,4608]{1,0:T(8,128)(2,1)S(1)}, bf16[32,4608]{1,0:T(8,128)(2,1)S(1)}, u32[]{:S(2)}, u32[]{:S(2)}) collective-permute-start(bf16[32,4608]{1,0:T(8,128)(2,1)S(1)} %get-tuple-element.16), channel_id=1, source_target_pairs={{0,4},{4,8},{8,12},{12,14},{14,10},{10,6},{6,2},{2,0},{1,5},{5,9},... | collective-permute-start | bytes 884744 | tf_op jit(solution)/shard_map/ppermute | solution.py:109
  23.0 9.2 %collective-permute-start.5 = (bf16[32,4608]{1,0:T(8,128)(2,1)S(1)}, bf16[32,4608]{1,0:T(8,128)(2,1)S(1)}, u32[]{:S(2)}, u32[]{:S(2)}) collective-permute-start(bf16[32,4608]{1,0:T(8,128)(2,1)S(1)} %get-tuple-element.17), channel_id=1, source_target_pairs={{0,2},{4,0},{8,4},{12,8},{14,12},{10,14},{6,10},{2,6},{1,3},{5,1},... | collective-permute-start | bytes 884744 | tf_op jit(solution)/shard_map/ppermute | solution.py:111
  30.3 8.8 %collective-permute-start.2 = (bf16[32,4608]{1,0:T(8,128)(2,1)S(1)}, bf16[32,4608]{1,0:T(8,128)(2,1)S(1)}, u32[]{:S(2)}, u32[]{:S(2)}) collective-permute-start(bf16[32,4608]{1,0:T(8,128)(2,1)S(1)} %add_convert_fusion.4), channel_id=1, source_target_pairs={{0,4},{4,8},{8,12},{12,14},{14,10},{10,6},{6,2},{2,0},{1,5},{5,9},... | collective-permute-start | bytes 884744 | tf_op jit(solution)/shard_map/ppermute | solution.py:109
  39.2 7.9 %collective-permute-start.3 = (bf16[32,4608]{1,0:T(8,128)(2,1)S(1)}, bf16[32,4608]{1,0:T(8,128)(2,1)S(1)}, u32[]{:S(2)}, u32[]{:S(2)}) collective-permute-start(bf16[32,4608]{1,0:T(8,128)(2,1)S(1)} %get-tuple-element.14), channel_id=1, source_target_pairs={{0,4},{4,8},{8,12},{12,14},{14,10},{10,6},{6,2},{2,0},{1,5},{5,9},... | collective-permute-start | bytes 884744 | tf_op jit(solution)/shard_map/ppermute | solution.py:109
  40.8 7.3 %collective-permute-start.6 = (bf16[32,4608]{1,0:T(8,128)(2,1)S(1)}, bf16[32,4608]{1,0:T(8,128)(2,1)S(1)}, u32[]{:S(2)}, u32[]{:S(2)}) collective-permute-start(bf16[32,4608]{1,0:T(8,128)(2,1)S(1)} %get-tuple-element.15), channel_id=1, source_target_pairs={{0,2},{4,0},{8,4},{12,8},{14,12},{10,14},{6,10},{2,6},{1,3},{5,1},... | collective-permute-start | bytes 884744 | tf_op jit(solution)/shard_map/ppermute | solution.py:111
  48.2 6.8 %collective-permute-start.4 = (bf16[32,4608]{1,0:T(8,128)(2,1)S(1)}, bf16[32,4608]{1,0:T(8,128)(2,1)S(1)}, u32[]{:S(2)}, u32[]{:S(2)}) collective-permute-start(bf16[32,4608]{1,0:T(8,128)(2,1)S(1)} %get-tuple-element.12), channel_id=1, source_target_pairs={{0,4},{4,8},{8,12},{12,14},{14,10},{10,6},{6,2},{2,0},{1,5},{5,9},... | collective-permute-start | bytes 884744 | tf_op jit(solution)/shard_map/ppermute | solution.py:109
  49.9 6.7 %collective-permute-start.7 = (bf16[32,4608]{1,0:T(8,128)(2,1)S(1)}, bf16[32,4608]{1,0:T(8,128)(2,1)S(1)}, u32[]{:S(2)}, u32[]{:S(2)}) collective-permute-start(bf16[32,4608]{1,0:T(8,128)(2,1)S(1)} %get-tuple-element.13), channel_id=1, source_target_pairs={{0,2},{4,0},{8,4},{12,8},{14,12},{10,14},{6,10},{2,6},{1,3},{5,1},... | collective-permute-start | bytes 884744 | tf_op jit(solution)/shard_map/ppermute | solution.py:111
  59.6 1.4 %copy-start.4 = (bf16[2,1536,2,128]{3,2,1,0:T(2,128)(2,1)S(1)}, bf16[2,1536,2,128]{3,2,1,0:T(2,128)(2,1)}, u32[]{:S(2)}) copy-start(bf16[2,1536,2,128]{3,2,1,0:T(2,128)(2,1)} %param.19) | copy-start | bytes 4718596
  63.4 8.6 %collective-permute-start.9 = (bf16[32,4096]{1,0:T(8,128)(2,1)S(1)}, bf16[32,4096]{1,0:T(8,128)(2,1)S(1)}, u32[]{:S(2)}, u32[]{:S(2)}) collective-permute-start(bf16[32,4096]{1,0:T(8,128)(2,1)S(1)} %convert_element_type.145), channel_id=1, source_target_pairs={{0,2},{4,0},{8,4},{12,8},{14,12},{10,14},{6,10},{2,6},{1,3},{5,1},... | collective-permute-start | bytes 786440 | tf_op jit(solution)/shard_map/ppermute | solution.py:128
  63.9 8.8 %collective-permute-start.8 = (bf16[32,4096]{1,0:T(8,128)(2,1)S(1)}, bf16[32,4096]{1,0:T(8,128)(2,1)S(1)}, u32[]{:S(2)}, u32[]{:S(2)}) collective-permute-start(bf16[32,4096]{1,0:T(8,128)(2,1)S(1)} %convert_element_type.145), channel_id=1, source_target_pairs={{0,4},{4,8},{8,12},{12,14},{14,10},{10,6},{6,2},{2,0},{1,5},{5,9},... | collective-permute-start | bytes 786440 | tf_op jit(solution)/shard_map/ppermute | solution.py:125
  72.0 9.0 %collective-permute-start.11 = (bf16[32,4096]{1,0:T(8,128)(2,1)S(1)}, bf16[32,4096]{1,0:T(8,128)(2,1)S(1)}, u32[]{:S(2)}, u32[]{:S(2)}) collective-permute-start(bf16[32,4096]{1,0:T(8,128)(2,1)S(1)} %collective-permute-done.9), channel_id=1, source_target_pairs={{0,2},{4,0},{8,4},{12,8},{14,12},{10,14},{6,10},{2,6},{1,3},{5,1},... | collective-permute-start | bytes 786440 | tf_op jit(solution)/shard_map/ppermute | solution.py:128
  72.7 8.7 %collective-permute-start.10 = (bf16[32,4096]{1,0:T(8,128)(2,1)S(1)}, bf16[32,4096]{1,0:T(8,128)(2,1)S(1)}, u32[]{:S(2)}, u32[]{:S(2)}) collective-permute-start(bf16[32,4096]{1,0:T(8,128)(2,1)S(1)} %collective-permute-done.8), channel_id=1, source_target_pairs={{0,4},{4,8},{8,12},{12,14},{14,10},{10,6},{6,2},{2,0},{1,5},{5,9},... | collective-permute-start | bytes 786440 | tf_op jit(solution)/shard_map/ppermute | solution.py:125
  81.0 10.0 %collective-permute-start.13 = (bf16[32,4096]{1,0:T(8,128)(2,1)S(1)}, bf16[32,4096]{1,0:T(8,128)(2,1)S(1)}, u32[]{:S(2)}, u32[]{:S(2)}) collective-permute-start(bf16[32,4096]{1,0:T(8,128)(2,1)S(1)} %collective-permute-done.11), channel_id=1, source_target_pairs={{0,2},{4,0},{8,4},{12,8},{14,12},{10,14},{6,10},{2,6},{1,3},{5,1},... | collective-permute-start | bytes 786440 | tf_op jit(solution)/shard_map/ppermute | solution.py:128
  81.4 7.3 %collective-permute-start.12 = (bf16[32,4096]{1,0:T(8,128)(2,1)S(1)}, bf16[32,4096]{1,0:T(8,128)(2,1)S(1)}, u32[]{:S(2)}, u32[]{:S(2)}) collective-permute-start(bf16[32,4096]{1,0:T(8,128)(2,1)S(1)} %collective-permute-done.10), channel_id=1, source_target_pairs={{0,4},{4,8},{8,12},{12,14},{14,10},{10,6},{6,2},{2,0},{1,5},{5,9},... | collective-permute-start | bytes 786440 | tf_op jit(solution)/shard_map/ppermute | solution.py:125
  88.7 6.4 %collective-permute-start.14 = (bf16[32,4096]{1,0:T(8,128)(2,1)S(1)}, bf16[32,4096]{1,0:T(8,128)(2,1)S(1)}, u32[]{:S(2)}, u32[]{:S(2)}) collective-permute-start(bf16[32,4096]{1,0:T(8,128)(2,1)S(1)} %collective-permute-done.12), channel_id=1, source_target_pairs={{0,4},{4,8},{8,12},{12,14},{14,10},{10,6},{6,2},{2,0},{1,5},{5,9},... | collective-permute-start | bytes 786440 | tf_op jit(solution)/shard_map/ppermute | solution.py:125
  104.8 2.0 %collective-permute-start.15 = (bf16[128,2048]{1,0:T(8,128)(2,1)S(1)}, bf16[128,2048]{1,0:T(8,128)(2,1)S(1)}, u32[]{:S(2)}, u32[]{:S(2)}) collective-permute-start(bf16[128,2048]{1,0:T(8,128)(2,1)S(1)} %convolution_convert_fusion.3), channel_id=1, source_target_pairs={{0,1},{1,0},{2,3},{3,2},{4,5},{5,4},{6,7},{7,6},{8,9},{9,8},{10,11... | collective-permute-start | bytes 1572872 | tf_op jit(solution)/shard_map/ppermute | solution.py:215
  106.8 10.0 %copy-start.1 = (bf16[2,1536,2,128]{3,2,1,0:T(2,128)(2,1)S(1)}, bf16[2,1536,2,128]{3,2,1,0:T(2,128)(2,1)}, u32[]{:S(2)}) copy-start(bf16[2,1536,2,128]{3,2,1,0:T(2,128)(2,1)} %param.18) | copy-start | bytes 4718596

commit v4 on v3

--- a/solution.py
+++ b/solution.py
@@ -96,6 +96,19 @@
             gather_offsets.append((s + 1) % n_row)
     stacked_of_offset = [gather_offsets.index(d) for d in range(n_row)]
 
+    def tables(seq_dev, new_len):
+        slots = np.zeros((n_row, n_row * seq_dev), np.int32)
+        stacked_row = np.zeros((n_row, n_row * seq_dev), np.int32)
+        for r in range(n_row):
+            p = position_of[r]
+            for k in range(n_row):
+                for j in range(seq_dev):
+                    slots[r, k * seq_dev + j] = ring[(p + k) % n_row] * seq_dev + j
+            for slot in range(n_row * seq_dev):
+                offset = (position_of[slot // seq_dev] - p) % n_row
+                stacked_row[r, slot] = (stacked_of_offset[offset] * seq_dev + slot % seq_dev) * new_len
+        return slots, stacked_row
+
     def add_bf16(a, b):
         return (a.astype(jnp.float32) + b.astype(jnp.float32)).astype(jnp.bfloat16)
 
@@ -151,9 +164,9 @@
         new_len = span_rows // slot_total
         block_rows = seq_dev * new_len
         other_tokens = lax.ppermute(tokens, "col", [(0, 1), (1, 0)])
-        my_pos = lookup(position_of, row_index)
-        block_dev = lookup(ring, (my_pos + jnp.arange(n_row, dtype=jnp.int32)) % n_row)
-        slots = (block_dev[:, None] * seq_dev + jnp.arange(seq_dev, dtype=jnp.int32)[None, :]).reshape(-1)
+        slots_table, stacked_table = tables(seq_dev, new_len)
+        mine_of_row = jnp.arange(n_row, dtype=jnp.int32)[:, None] == row_index
+        slots = jnp.sum(jnp.where(mine_of_row, jnp.asarray(slots_table), 0), axis=0)
         sequences = lookup(slot_seq, slots)
         local = jnp.arange(span_rows, dtype=jnp.int32)
         token_rows = jnp.repeat(sequences, new_len) * new_len + local % new_len
@@ -176,6 +189,7 @@
         )
         blocks = [joined[k * block_rows : (k + 1) * block_rows] for k in range(n_row)]
         summed = ring_reduce_scatter(blocks)
+        summed, late_slot_seq, late_row = lax.optimization_barrier((summed, slot_seq, row_index))
         q_sum = summed[:, :q_width]
         key_total_sum = summed[:, q_width : q_width + k_width]
         value_total_sum = summed[:, q_width + k_width :]
@@ -199,25 +213,31 @@
         )
         attended = results.reshape(seq_dev * new_len, -1)
         stacked = ring_all_gather(attended)
-        slot_ids = jnp.arange(slot_total, dtype=jnp.int32)
-        slot_of = jnp.sum(jnp.where(slot_seq[:, None] == slot_ids[None, :], slot_ids[:, None], 0), axis=0)
-        offset = (lookup(position_of, slot_ids // seq_dev) - my_pos) % n_row
-        stacked_row_of_slot = lookup(stacked_of_offset, offset) * block_rows + (slot_ids % seq_dev) * new_len
-        seq_base = lookup(stacked_row_of_slot, slot_of)
-        span = jnp.arange(own_rows, dtype=jnp.int32)
-        def half_rows(half):
-            t = half * own_rows + span
-            return lookup(seq_base, t // new_len) + t % new_len
-        theirs_att = jnp.dot(
-            one_hot(half_rows(1 - col_index), span_rows), stacked, preferred_element_type=jnp.float32
+        late_mine = jnp.arange(n_row, dtype=jnp.int32)[:, None] == late_row
+        row_of_slot = jnp.sum(jnp.where(late_mine, jnp.asarray(stacked_table), 0), axis=0)
+        seq_ids = jnp.arange(slot_total, dtype=jnp.int32)
+        seq_base = jnp.sum(
+            jnp.where(late_slot_seq[None, :] == seq_ids[:, None], row_of_slot[None, :], 0), axis=1
+        )
+        half = jnp.where(local < own_rows, 1 - col_index, col_index)
+        t = half * own_rows + local % own_rows
+        span_order = lookup(seq_base, t // new_len) + t % new_len
+        arranged = jnp.dot(
+            one_hot(span_order, span_rows), stacked, preferred_element_type=jnp.float32
         ).astype(jnp.bfloat16)
-        theirs = jnp.dot(theirs_att, o_weight, preferred_element_type=jnp.float32)
-        received = lax.ppermute(theirs.astype(jnp.bfloat16), "col", [(0, 1), (1, 0)])
-        mine_att = jnp.dot(
-            one_hot(half_rows(col_index), span_rows), stacked, preferred_element_type=jnp.float32
-        ).astype(jnp.bfloat16)
-        mine = jnp.dot(mine_att, o_weight, preferred_element_type=jnp.float32)
-        return (mine + received.astype(jnp.float32)).astype(jnp.bfloat16)
+        out_width = o_weight.shape[1]
+        n_chunks = 2 if out_width % 256 == 0 else 1
+        chunk = out_width // n_chunks
+        pieces = []
+        for i in range(n_chunks):
+            products = jnp.dot(
+                arranged, o_weight[:, i * chunk : (i + 1) * chunk], preferred_element_type=jnp.float32
+            )
+            received = lax.ppermute(
+                products[:own_rows].astype(jnp.bfloat16), "col", [(0, 1), (1, 0)]
+            )
+            pieces.append((products[own_rows:] + received.astype(jnp.float32)).astype(jnp.bfloat16))
+        return jnp.concatenate(pieces, axis=1)
 
     return body
 

time: 117 us -> 108 us (0.923)
  matrix products: 34.6 us -> 28 us
  local copies, waits for them, and re-layouts: 7.28 us -> 1.65 us
  waiting for transfers between devices: 47.7 us -> 51.1 us
    dot_general x2 -> x3, matrix products: 19 us -> 12.4 us  [the longest x2 11.7 us: body(): jnp.dot(arranged, o_weight[:, i * chunk:(i + 1) * chunk], preferred_eleme...]
    unnamed x19 -> x27, local copies, waits for them, and re-layouts: 5.93 us -> 1.02 us
    reduce_sum x7 -> x3, other arithmetic: 4.72 us -> 1.11 us  [lookup(): return jnp.sum(jnp.where(hit, table, 0), axis=-1)]
    ppermute x4, waiting for transfers between devices: 7.84 us -> 10.7 us  [ring_all_gather(): forward = lax.ppermute(forward, 'row', forward_pairs)]
    convert_element_type x3, other arithmetic: 0.38 us -> 2.46 us  [add_bf16(): return (a.astype(jnp.float32) + b.astype(jnp.float32)).astype(jnp.bfloat16)]
    ppermute x3, waiting for transfers between devices: 11 us -> 12.8 us  [ring_all_gather(): backward = lax.ppermute(backward, 'row', backward_pairs)]
    select_n x4 -> x1, other arithmetic: 1.32 us -> 0.01 us  [body(): span_order = lookup(seq_base, t // new_len) + t % new_len]
  transfers between devices with their start and end apart: 16 -> 17, of which waited for: 12 -> 12; matrix products, arithmetic and copies ran while one was open for 12% -> 10% of each run, Pallas kernels for 0% -> 0%
where the time goes in v4:
time: 108 us
  waiting for transfers between devices  51.1 us (47%)
  matrix products  28 us (26%)
  starting transfers between devices  17.9 us (17%)
  other arithmetic  8.93 us (8%)
  local copies, waits for them, and re-layouts  1.65 us (2%)
    ppermute x4, waiting for transfers between devices, ring_reduce_scatter(): got_forward = lax.ppermute(forward, 'row', forward_pairs)  24 us
    ppermute x3, waiting for transfers between devices, ring_all_gather(): backward = lax.ppermute(backward, 'row', backward_pairs)  12.8 us
    dot_general x2, matrix products, body(): jnp.dot(arranged, o_weight[:, i * chunk:(i + 1) * chunk], preferred_eleme...  11.7 us
    ppermute x4, waiting for transfers between devices, ring_all_gather(): forward = lax.ppermute(forward, 'row', forward_pairs)  10.7 us
    dot_general x1, matrix products, body(): q_part = jnp.dot(chosen, q_weight, preferred_element_type=jnp.float32)  8.4 us
    ppermute x4, starting transfers between devices, ring_reduce_scatter(): got_forward = lax.ppermute(forward, 'row', forward_pairs)  7.8 us
    ppermute x4, starting transfers between devices, ring_all_gather(): forward = lax.ppermute(forward, 'row', forward_pairs)  6.21 us
    ppermute x3, waiting for transfers between devices, ring_reduce_scatter(): got_backward = lax.ppermute(backward, 'row', backward_pairs)  2.53 us
  transfers between devices with their start and end apart: 17, of which 12 were waited for; matrix products, arithmetic and copies ran while one was open for 10% of the time, Pallas kernels for 0%

profile of v4, /device:TPU:0, one launch (start us, length us, event | category | flops | bytes accessed | tf_op | source)
XLA Modules:
  0.0 108.0 jit_solution(11667534865664352673)
XLA Ops:
  1.3 0.8 select_reduce_fusion.2
  2.3 1.5 %fusion.33 = f32[256,2048]{1,0:T(8,128)S(1)} fusion(bf16[128,2048]{1,0:T(8,128)(2,1)} %param.11, s32[256]{0:T(256)S(1)} %broadcast_select_fusion.1), kind=kOutput, calls=%fused_computation.57 | convolution fusion | flops 134250496 | bytes 2622464 | tf_op jit(solution)/shard_map/dot_general | solution.py:178
  6.0 8.4 %convolution_convert_fusion.1 = bf16[256,4096]{1,0:T(8,128)(2,1)S(1)} fusion(bf16[256,2048]{1,0:T(8,128)(2,1)S(1)} %fusion.10, bf16[2048,4096]{1,0:T(8,128)(2,1)} %param.12), kind=kOutput, calls=%fused_computation.9 | convolution fusion | flops 4296015872 | bytes 19922944 | tf_op jit(solution)/shard_map/dot_general | solution.py:181
  14.6 2.8 %collective-permute-start.1 = (bf16[32,4608]{1,0:T(8,128)(2,1)S(1)}, bf16[32,4608]{1,0:T(8,128)(2,1)S(1)}, u32[]{:S(2)}, u32[]{:S(2)}) collective-permute-start(bf16[32,4608]{1,0:T(8,128)(2,1)S(1)} %get-tuple-element.18), channel_id=1, source_target_pairs={{0,4},{4,8},{8,12},{12,14},{14,10},{10,6},{6,2},{2,0},{1,5},{5,9},... | collective-permute-start | bytes 884744 | tf_op jit(solution)/shard_map/ppermute | solution.py:122
  17.9 7.0 %collective-permute-done.1 = bf16[32,4608]{1,0:T(8,128)(2,1)S(1)} collective-permute-done((bf16[32,4608]{1,0:T(8,128)(2,1)S(1)}, bf16[32,4608]{1,0:T(8,128)(2,1)S(1)}, u32[]{:S(2)}, u32[]{:S(2)}) %collective-permute-start.1) | collective-permute-done | bytes 294944 | tf_op jit(solution)/shard_map/ppermute | solution.py:122
  24.9 1.9 %collective-permute-start.2 = (bf16[32,4608]{1,0:T(8,128)(2,1)S(1)}, bf16[32,4608]{1,0:T(8,128)(2,1)S(1)}, u32[]{:S(2)}, u32[]{:S(2)}) collective-permute-start(bf16[32,4608]{1,0:T(8,128)(2,1)S(1)} %add_convert_fusion.4), channel_id=1, source_target_pairs={{0,4},{4,8},{8,12},{12,14},{14,10},{10,6},{6,2},{2,0},{1,5},{5,9},... | collective-permute-start | bytes 884744 | tf_op jit(solution)/shard_map/ppermute | solution.py:122
  27.0 6.7 %collective-permute-done.2 = bf16[32,4608]{1,0:T(8,128)(2,1)S(1)} collective-permute-done((bf16[32,4608]{1,0:T(8,128)(2,1)S(1)}, bf16[32,4608]{1,0:T(8,128)(2,1)S(1)}, u32[]{:S(2)}, u32[]{:S(2)}) %collective-permute-start.2) | collective-permute-done | bytes 294944 | tf_op jit(solution)/shard_map/ppermute | solution.py:122
  33.7 1.2 %add_convert_fusion.3 = (bf16[32,4608]{1,0:T(8,128)(2,1)S(1)}, bf16[32,4608]{1,0:T(8,128)(2,1)S(1)}) fusion(bf16[32,4608]{1,0:T(8,128)(2,1)S(1)} %collective-permute-done.2, bf16[256,4608]{1,0:T(8,128)(2,1)} %copy-done.2, bf16[32,4608]{1,0:T(8,128)(2,1)S(1)} %collective-permute-done.5), kind=kLoop, calls=%fused_computation.34 | loop fusion | flops 1179648 | bytes 1769472 | tf_op jit(solution)/shard_map/convert_element_type | solution.py:113
  34.9 1.6 %collective-permute-start.3 = (bf16[32,4608]{1,0:T(8,128)(2,1)S(1)}, bf16[32,4608]{1,0:T(8,128)(2,1)S(1)}, u32[]{:S(2)}, u32[]{:S(2)}) collective-permute-start(bf16[32,4608]{1,0:T(8,128)(2,1)S(1)} %get-tuple-element.16), channel_id=1, source_target_pairs={{0,4},{4,8},{8,12},{12,14},{14,10},{10,6},{6,2},{2,0},{1,5},{5,9},... | collective-permute-start | bytes 884744 | tf_op jit(solution)/shard_map/ppermute | solution.py:122
  37.1 5.8 %collective-permute-done.3 = bf16[32,4608]{1,0:T(8,128)(2,1)S(1)} collective-permute-done((bf16[32,4608]{1,0:T(8,128)(2,1)S(1)}, bf16[32,4608]{1,0:T(8,128)(2,1)S(1)}, u32[]{:S(2)}, u32[]{:S(2)}) %collective-permute-start.3) | collective-permute-done | bytes 294944 | tf_op jit(solution)/shard_map/ppermute | solution.py:122
  42.8 1.0 collective-permute-done.6
  43.8 1.2 %add_convert_fusion.2 = (bf16[32,4608]{1,0:T(8,128)(2,1)S(1)}, bf16[32,4608]{1,0:T(8,128)(2,1)S(1)}) fusion(bf16[32,4608]{1,0:T(8,128)(2,1)S(1)} %collective-permute-done.3, bf16[256,4608]{1,0:T(8,128)(2,1)} %copy-done.2, bf16[32,4608]{1,0:T(8,128)(2,1)S(1)} %collective-permute-done.6), kind=kLoop, calls=%fused_computation.33 | loop fusion | flops 1179648 | bytes 1769472 | tf_op jit(solution)/shard_map/convert_element_type | solution.py:113
  45.0 1.6 %collective-permute-start.4 = (bf16[32,4608]{1,0:T(8,128)(2,1)S(1)}, bf16[32,4608]{1,0:T(8,128)(2,1)S(1)}, u32[]{:S(2)}, u32[]{:S(2)}) collective-permute-start(bf16[32,4608]{1,0:T(8,128)(2,1)S(1)} %get-tuple-element.14), channel_id=1, source_target_pairs={{0,4},{4,8},{8,12},{12,14},{14,10},{10,6},{6,2},{2,0},{1,5},{5,9},... | collective-permute-start | bytes 884744 | tf_op jit(solution)/shard_map/ppermute | solution.py:122
  47.2 4.5 %collective-permute-done.4 = bf16[32,4608]{1,0:T(8,128)(2,1)S(1)} collective-permute-done((bf16[32,4608]{1,0:T(8,128)(2,1)S(1)}, bf16[32,4608]{1,0:T(8,128)(2,1)S(1)}, u32[]{:S(2)}, u32[]{:S(2)}) %collective-permute-start.4) | collective-permute-done | bytes 294944 | tf_op jit(solution)/shard_map/ppermute | solution.py:122
  51.8 1.6 %collective-permute-done.7 = bf16[32,4608]{1,0:T(8,128)(2,1)S(1)} collective-permute-done((bf16[32,4608]{1,0:T(8,128)(2,1)S(1)}, bf16[32,4608]{1,0:T(8,128)(2,1)S(1)}, u32[]{:S(2)}, u32[]{:S(2)}) %collective-permute-start.7) | collective-permute-done | bytes 294944 | tf_op jit(solution)/shard_map/ppermute | solution.py:124
  53.3 1.1 convert_add_fusion
  55.0 1.3 %bitcast_reduce_fusion = (f32[2,2,16,16]{2,3,1,0:T(8,128)S(1)}, f32[2,2,16,16,1536]{4,3,2,1,0:T(8,128)S(1)}) fusion(pred[2,1536]{1,0:T(4,128)(4,1)S(1)} %iota_compare_fusion.7, bf16[2,1536,2,128,1]{3,2,1,0,4:T(2,128)(2,1)S(1)} %bitcast.56, bf16[2,16,2,16,64]{4,3,2,1,0:T(8,128)(2,1)S(1)} %bitcast.60, bf16[2,16,2,16,64]{4,3,2,1,0:T(8,128)(2,1)S(1)} %bitcast.58), kind=kOutput, calls=%fused_computation.5 | convolution fusion | flops 407895040 | bytes 8133632 | tf_op jit(solution)/shard_map/vmap(nkgd,ckd->kgnc)/dot_general | solution.py:30
  56.2 0.8 fusion.49
  57.3 1.4 %fusion.5 = f32[2,2,16,16]{2,3,1,0:T(8,128)S(1)} fusion(f32[2,2,16,16,1536]{4,3,2,1,0:T(8,128)S(1)} %get-tuple-element.29, f32[2,2,16,16]{2,3,1,0:T(8,128)S(1)} %max.7, pred[2,1536]{1,0:T(4,128)(4,1)S(1)} %iota_compare_fusion.7), kind=kLoop, calls=%fused_computation.10 | loop fusion | flops 6290432 | bytes 6302720 | tf_op jit(solution)/shard_map/vmap()/reduce_sum | solution.py:44
  58.7 1.9 %fusion.14 = f32[2,16,2,16,128]{4,3,1,2,0:T(8,128)S(1)} fusion(bf16[2,1536,2,128,1]{3,2,1,0,4:T(2,128)(2,1)S(1)} %bitcast.65, f32[2,2,16,16,1536]{4,3,2,1,0:T(8,128)S(1)} %get-tuple-element.29, f32[2,2,16,16]{2,3,1,0:T(8,128)S(1)} %max.7, pred[2,1536]{1,0:T(4,128)(4,1)S(1)} %iota_compare_fusion.7), kind=kOutput, calls=%fused_computation.20 | convolution fusion | flops 408944640 | bytes 8395776 | tf_op jit(solution)/shard_map/vmap(kgnc,ckd->nkgd)/dot_general | solution.py:45
  61.6 1.6 %collective-permute-start.8 = (bf16[32,4096]{1,0:T(8,128)(2,1)S(1)}, bf16[32,4096]{1,0:T(8,128)(2,1)S(1)}, u32[]{:S(2)}, u32[]{:S(2)}) collective-permute-start(bf16[32,4096]{1,0:T(8,128)(2,1)S(1)} %convert_element_type.146), channel_id=1, source_target_pairs={{0,4},{4,8},{8,12},{12,14},{14,10},{10,6},{6,2},{2,0},{1,5},{5,9},... | collective-permute-start | bytes 786440 | tf_op jit(solution)/shard_map/ppermute | solution.py:138
  63.5 6.1 %collective-permute-done.9 = bf16[32,4096]{1,0:T(8,128)(2,1)S(1)} collective-permute-done((bf16[32,4096]{1,0:T(8,128)(2,1)S(1)}, bf16[32,4096]{1,0:T(8,128)(2,1)S(1)}, u32[]{:S(2)}, u32[]{:S(2)}) %collective-permute-start.9) | collective-permute-done | bytes 262176 | tf_op jit(solution)/shard_map/ppermute | solution.py:141
  70.4 1.6 %collective-permute-start.10 = (bf16[32,4096]{1,0:T(8,128)(2,1)S(1)}, bf16[32,4096]{1,0:T(8,128)(2,1)S(1)}, u32[]{:S(2)}, u32[]{:S(2)}) collective-permute-start(bf16[32,4096]{1,0:T(8,128)(2,1)S(1)} %collective-permute-done.8), channel_id=1, source_target_pairs={{0,4},{4,8},{8,12},{12,14},{14,10},{10,6},{6,2},{2,0},{1,5},{5,9},... | collective-permute-start | bytes 786440 | tf_op jit(solution)/shard_map/ppermute | solution.py:138
  72.0 6.6 %collective-permute-done.11 = bf16[32,4096]{1,0:T(8,128)(2,1)S(1)} collective-permute-done((bf16[32,4096]{1,0:T(8,128)(2,1)S(1)}, bf16[32,4096]{1,0:T(8,128)(2,1)S(1)}, u32[]{:S(2)}, u32[]{:S(2)}) %collective-permute-start.11) | collective-permute-done | bytes 262176 | tf_op jit(solution)/shard_map/ppermute | solution.py:141
  79.1 1.6 %collective-permute-start.12 = (bf16[32,4096]{1,0:T(8,128)(2,1)S(1)}, bf16[32,4096]{1,0:T(8,128)(2,1)S(1)}, u32[]{:S(2)}, u32[]{:S(2)}) collective-permute-start(bf16[32,4096]{1,0:T(8,128)(2,1)S(1)} %collective-permute-done.10), channel_id=1, source_target_pairs={{0,4},{4,8},{8,12},{12,14},{14,10},{10,6},{6,2},{2,0},{1,5},{5,9},... | collective-permute-start | bytes 786440 | tf_op jit(solution)/shard_map/ppermute | solution.py:138
  80.7 5.7 %collective-permute-done.12 = bf16[32,4096]{1,0:T(8,128)(2,1)S(1)} collective-permute-done((bf16[32,4096]{1,0:T(8,128)(2,1)S(1)}, bf16[32,4096]{1,0:T(8,128)(2,1)S(1)}, u32[]{:S(2)}, u32[]{:S(2)}) %collective-permute-start.12) | collective-permute-done | bytes 262176 | tf_op jit(solution)/shard_map/ppermute | solution.py:138
  86.4 1.5 %collective-permute-start.14 = (bf16[32,4096]{1,0:T(8,128)(2,1)S(1)}, bf16[32,4096]{1,0:T(8,128)(2,1)S(1)}, u32[]{:S(2)}, u32[]{:S(2)}) collective-permute-start(bf16[32,4096]{1,0:T(8,128)(2,1)S(1)} %collective-permute-done.12), channel_id=1, source_target_pairs={{0,4},{4,8},{8,12},{12,14},{14,10},{10,6},{6,2},{2,0},{1,5},{5,9},... | collective-permute-start | bytes 786440 | tf_op jit(solution)/shard_map/ppermute | solution.py:138
  88.0 4.8 %collective-permute-done.14 = bf16[32,4096]{1,0:T(8,128)(2,1)S(1)} collective-permute-done((bf16[32,4096]{1,0:T(8,128)(2,1)S(1)}, bf16[32,4096]{1,0:T(8,128)(2,1)S(1)}, u32[]{:S(2)}, u32[]{:S(2)}) %collective-permute-start.14) | collective-permute-done | bytes 262176 | tf_op jit(solution)/shard_map/ppermute | solution.py:138
  93.6 5.8 %fusion = f32[256,1024]{1,0:T(8,128)S(1)} fusion(bf16[256,4096]{1,0:T(8,128)(2,1)S(1)} %convolution_convert_fusion, bf16[4096,2048]{1,0:T(8,128)(2,1)} %param.15), kind=kOutput, calls=%fused_computation | convolution fusion | flops 2147483648 | bytes 11534336 | tf_op jit(solution)/shard_map/dot_general | solution.py:233
  99.5 5.9 %fusion.2 = f32[256,1024]{1,0:T(8,128)S(1)} fusion(bf16[256,4096]{1,0:T(8,128)(2,1)S(1)} %convolution_convert_fusion, bf16[4096,2048]{1,0:T(8,128)(2,1)} %param.15), kind=kOutput, calls=%fused_computation.2 | convolution fusion | flops 2147483648 | bytes 11534336 | tf_op jit(solution)/shard_map/dot_general | solution.py:233
  106.0 1.1 %collective-permute-done.15 = bf16[128,1024]{1,0:T(8,128)(2,1)S(1)} collective-permute-done((bf16[128,1024]{1,0:T(8,128)(2,1)S(1)}, bf16[128,1024]{1,0:T(8,128)(2,1)S(1)}, u32[]{:S(2)}, u32[]{:S(2)}) %collective-permute-start.15) | collective-permute-done | bytes 262176 | tf_op jit(solution)/shard_map/ppermute | solution.py:236
  107.2 0.8 pad_maximum_fusion.1
  (87 shorter events, 10.7 us)
Async XLA Ops:
  0.0 55.0 %copy-start = (bf16[2,1536,2,128]{3,2,1,0:T(2,128)(2,1)S(1)}, bf16[2,1536,2,128]{3,2,1,0:T(2,128)(2,1)}, u32[]{:S(2)}) copy-start(bf16[2,1536,2,128]{3,2,1,0:T(2,128)(2,1)} %param.16) | copy-start | bytes 4718596
  0.0 3.8 %collective-permute-start = (bf16[128,2048]{1,0:T(8,128)(2,1)}, bf16[128,2048]{1,0:T(8,128)(2,1)S(1)}, u32[]{:S(2)}, u32[]{:S(2)}) collective-permute-start(bf16[128,2048]{1,0:T(8,128)(2,1)} %param.11), channel_id=1, source_target_pairs={{0,1},{1,0},{2,3},{3,2},{4,5},{5,4},{6,7},{7,6},{8,9},{9,8},{10,11... | collective-permute-start | bytes 1572872 | tf_op jit(solution)/shard_map/ppermute | solution.py:166
  3.8 1.2 %copy-start.3 = (bf16[2048,256]{1,0:T(8,128)(2,1)S(1)}, bf16[2048,256]{1,0:T(8,128)(2,1)}, u32[]{:S(2)}) copy-start(bf16[2048,256]{1,0:T(8,128)(2,1)} %param.14) | copy-start | bytes 3145732
  3.9 1.7 %copy-start.4 = (bf16[2048,256]{1,0:T(8,128)(2,1)S(1)}, bf16[2048,256]{1,0:T(8,128)(2,1)}, u32[]{:S(2)}) copy-start(bf16[2048,256]{1,0:T(8,128)(2,1)} %param.13) | copy-start | bytes 3145732
  14.4 3.0 %copy-start.7 = (s32[16]{0:T(128)S(1)}, s32[16]{0:T(128)}, u32[]{:S(2)}) copy-start(s32[16]{0:T(128)} %param.18) | copy-start | bytes 196
  14.6 10.3 %copy-start.2 = (bf16[256,4608]{1,0:T(8,128)(2,1)}, bf16[256,4608]{1,0:T(8,128)(2,1)S(1)}, u32[]{:S(2)}) copy-start(bf16[256,4608]{1,0:T(8,128)(2,1)S(1)} %pad_maximum_fusion) | copy-start | bytes 7077892
  14.6 10.2 %collective-permute-start.1 = (bf16[32,4608]{1,0:T(8,128)(2,1)S(1)}, bf16[32,4608]{1,0:T(8,128)(2,1)S(1)}, u32[]{:S(2)}, u32[]{:S(2)}) collective-permute-start(bf16[32,4608]{1,0:T(8,128)(2,1)S(1)} %get-tuple-element.18), channel_id=1, source_target_pairs={{0,4},{4,8},{8,12},{12,14},{14,10},{10,6},{6,2},{2,0},{1,5},{5,9},... | collective-permute-start | bytes 884744 | tf_op jit(solution)/shard_map/ppermute | solution.py:122
  17.6 9.4 %collective-permute-start.5 = (bf16[32,4608]{1,0:T(8,128)(2,1)S(1)}, bf16[32,4608]{1,0:T(8,128)(2,1)S(1)}, u32[]{:S(2)}, u32[]{:S(2)}) collective-permute-start(bf16[32,4608]{1,0:T(8,128)(2,1)S(1)} %get-tuple-element.19), channel_id=1, source_target_pairs={{0,2},{4,0},{8,4},{12,8},{14,12},{10,14},{6,10},{2,6},{1,3},{5,1},... | collective-permute-start | bytes 884744 | tf_op jit(solution)/shard_map/ppermute | solution.py:124
  24.9 8.8 %collective-permute-start.2 = (bf16[32,4608]{1,0:T(8,128)(2,1)S(1)}, bf16[32,4608]{1,0:T(8,128)(2,1)S(1)}, u32[]{:S(2)}, u32[]{:S(2)}) collective-permute-start(bf16[32,4608]{1,0:T(8,128)(2,1)S(1)} %add_convert_fusion.4), channel_id=1, source_target_pairs={{0,4},{4,8},{8,12},{12,14},{14,10},{10,6},{6,2},{2,0},{1,5},{5,9},... | collective-permute-start | bytes 884744 | tf_op jit(solution)/shard_map/ppermute | solution.py:122
  34.9 7.9 %collective-permute-start.3 = (bf16[32,4608]{1,0:T(8,128)(2,1)S(1)}, bf16[32,4608]{1,0:T(8,128)(2,1)S(1)}, u32[]{:S(2)}, u32[]{:S(2)}) collective-permute-start(bf16[32,4608]{1,0:T(8,128)(2,1)S(1)} %get-tuple-element.16), channel_id=1, source_target_pairs={{0,4},{4,8},{8,12},{12,14},{14,10},{10,6},{6,2},{2,0},{1,5},{5,9},... | collective-permute-start | bytes 884744 | tf_op jit(solution)/shard_map/ppermute | solution.py:122
  36.5 7.3 %collective-permute-start.6 = (bf16[32,4608]{1,0:T(8,128)(2,1)S(1)}, bf16[32,4608]{1,0:T(8,128)(2,1)S(1)}, u32[]{:S(2)}, u32[]{:S(2)}) collective-permute-start(bf16[32,4608]{1,0:T(8,128)(2,1)S(1)} %get-tuple-element.17), channel_id=1, source_target_pairs={{0,2},{4,0},{8,4},{12,8},{14,12},{10,14},{6,10},{2,6},{1,3},{5,1},... | collective-permute-start | bytes 884744 | tf_op jit(solution)/shard_map/ppermute | solution.py:124
  45.0 6.8 %collective-permute-start.4 = (bf16[32,4608]{1,0:T(8,128)(2,1)S(1)}, bf16[32,4608]{1,0:T(8,128)(2,1)S(1)}, u32[]{:S(2)}, u32[]{:S(2)}) collective-permute-start(bf16[32,4608]{1,0:T(8,128)(2,1)S(1)} %get-tuple-element.14), channel_id=1, source_target_pairs={{0,4},{4,8},{8,12},{12,14},{14,10},{10,6},{6,2},{2,0},{1,5},{5,9},... | collective-permute-start | bytes 884744 | tf_op jit(solution)/shard_map/ppermute | solution.py:122
  46.6 6.7 %collective-permute-start.7 = (bf16[32,4608]{1,0:T(8,128)(2,1)S(1)}, bf16[32,4608]{1,0:T(8,128)(2,1)S(1)}, u32[]{:S(2)}, u32[]{:S(2)}) collective-permute-start(bf16[32,4608]{1,0:T(8,128)(2,1)S(1)} %get-tuple-element.15), channel_id=1, source_target_pairs={{0,2},{4,0},{8,4},{12,8},{14,12},{10,14},{6,10},{2,6},{1,3},{5,1},... | collective-permute-start | bytes 884744 | tf_op jit(solution)/shard_map/ppermute | solution.py:124
  57.2 1.4 %copy-start.6 = (bf16[2,1536,2,128]{3,2,1,0:T(2,128)(2,1)S(1)}, bf16[2,1536,2,128]{3,2,1,0:T(2,128)(2,1)}, u32[]{:S(2)}) copy-start(bf16[2,1536,2,128]{3,2,1,0:T(2,128)(2,1)} %param.17) | copy-start | bytes 4718596
  60.6 2.6 %copy-start.5 = (s32[8,16]{1,0:T(8,128)S(1)}, s32[8,16]{1,0:T(8,128)}, u32[]{:S(2)}) copy-start(s32[8,16]{1,0:T(8,128)} %constant.92.clone) | copy-start | bytes 1540
  60.6 2.7 %copy-start.8 = (s32[16]{0:T(128)S(1)}, s32[16]{0:T(128)}, u32[]{:S(2)}) copy-start(s32[16]{0:T(128)} %param.19) | copy-start | bytes 196
  61.1 8.6 %collective-permute-start.9 = (bf16[32,4096]{1,0:T(8,128)(2,1)S(1)}, bf16[32,4096]{1,0:T(8,128)(2,1)S(1)}, u32[]{:S(2)}, u32[]{:S(2)}) collective-permute-start(bf16[32,4096]{1,0:T(8,128)(2,1)S(1)} %convert_element_type.146), channel_id=1, source_target_pairs={{0,2},{4,0},{8,4},{12,8},{14,12},{10,14},{6,10},{2,6},{1,3},{5,1},... | collective-permute-start | bytes 786440 | tf_op jit(solution)/shard_map/ppermute | solution.py:141
  61.6 8.8 %collective-permute-start.8 = (bf16[32,4096]{1,0:T(8,128)(2,1)S(1)}, bf16[32,4096]{1,0:T(8,128)(2,1)S(1)}, u32[]{:S(2)}, u32[]{:S(2)}) collective-permute-start(bf16[32,4096]{1,0:T(8,128)(2,1)S(1)} %convert_element_type.146), channel_id=1, source_target_pairs={{0,4},{4,8},{8,12},{12,14},{14,10},{10,6},{6,2},{2,0},{1,5},{5,9},... | collective-permute-start | bytes 786440 | tf_op jit(solution)/shard_map/ppermute | solution.py:138
  69.7 9.0 %collective-permute-start.11 = (bf16[32,4096]{1,0:T(8,128)(2,1)S(1)}, bf16[32,4096]{1,0:T(8,128)(2,1)S(1)}, u32[]{:S(2)}, u32[]{:S(2)}) collective-permute-start(bf16[32,4096]{1,0:T(8,128)(2,1)S(1)} %collective-permute-done.9), channel_id=1, source_target_pairs={{0,2},{4,0},{8,4},{12,8},{14,12},{10,14},{6,10},{2,6},{1,3},{5,1},... | collective-permute-start | bytes 786440 | tf_op jit(solution)/shard_map/ppermute | solution.py:141
  70.4 8.7 %collective-permute-start.10 = (bf16[32,4096]{1,0:T(8,128)(2,1)S(1)}, bf16[32,4096]{1,0:T(8,128)(2,1)S(1)}, u32[]{:S(2)}, u32[]{:S(2)}) collective-permute-start(bf16[32,4096]{1,0:T(8,128)(2,1)S(1)} %collective-permute-done.8), channel_id=1, source_target_pairs={{0,4},{4,8},{8,12},{12,14},{14,10},{10,6},{6,2},{2,0},{1,5},{5,9},... | collective-permute-start | bytes 786440 | tf_op jit(solution)/shard_map/ppermute | solution.py:138
  78.6 9.3 %collective-permute-start.13 = (bf16[32,4096]{1,0:T(8,128)(2,1)S(1)}, bf16[32,4096]{1,0:T(8,128)(2,1)S(1)}, u32[]{:S(2)}, u32[]{:S(2)}) collective-permute-start(bf16[32,4096]{1,0:T(8,128)(2,1)S(1)} %collective-permute-done.11), channel_id=1, source_target_pairs={{0,2},{4,0},{8,4},{12,8},{14,12},{10,14},{6,10},{2,6},{1,3},{5,1},... | collective-permute-start | bytes 786440 | tf_op jit(solution)/shard_map/ppermute | solution.py:141
  79.1 7.3 %collective-permute-start.12 = (bf16[32,4096]{1,0:T(8,128)(2,1)S(1)}, bf16[32,4096]{1,0:T(8,128)(2,1)S(1)}, u32[]{:S(2)}, u32[]{:S(2)}) collective-permute-start(bf16[32,4096]{1,0:T(8,128)(2,1)S(1)} %collective-permute-done.10), channel_id=1, source_target_pairs={{0,4},{4,8},{8,12},{12,14},{14,10},{10,6},{6,2},{2,0},{1,5},{5,9},... | collective-permute-start | bytes 786440 | tf_op jit(solution)/shard_map/ppermute | solution.py:138
  86.4 6.4 %collective-permute-start.14 = (bf16[32,4096]{1,0:T(8,128)(2,1)S(1)}, bf16[32,4096]{1,0:T(8,128)(2,1)S(1)}, u32[]{:S(2)}, u32[]{:S(2)}) collective-permute-start(bf16[32,4096]{1,0:T(8,128)(2,1)S(1)} %collective-permute-done.12), channel_id=1, source_target_pairs={{0,4},{4,8},{8,12},{12,14},{14,10},{10,6},{6,2},{2,0},{1,5},{5,9},... | collective-permute-start | bytes 786440 | tf_op jit(solution)/shard_map/ppermute | solution.py:138
  99.4 6.6 %collective-permute-start.16 = (bf16[128,1024]{1,0:T(8,128)(2,1)S(1)}, bf16[128,1024]{1,0:T(8,128)(2,1)S(1)}, u32[]{:S(2)}, u32[]{:S(2)}) collective-permute-start(bf16[128,1024]{1,0:T(8,128)(2,1)S(1)} %slice.132), channel_id=1, source_target_pairs={{0,1},{1,0},{2,3},{3,2},{4,5},{5,4},{6,7},{7,6},{8,9},{9,8},{10,11... | collective-permute-start | bytes 786440 | tf_op jit(solution)/shard_map/ppermute | solution.py:236
  99.5 8.6 %copy-start.1 = (bf16[2,1536,2,128]{3,2,1,0:T(2,128)(2,1)S(1)}, bf16[2,1536,2,128]{3,2,1,0:T(2,128)(2,1)}, u32[]{:S(2)}) copy-start(bf16[2,1536,2,128]{3,2,1,0:T(2,128)(2,1)} %param.16) | copy-start | bytes 4718596
  105.4 1.7 %collective-permute-start.15 = (bf16[128,1024]{1,0:T(8,128)(2,1)S(1)}, bf16[128,1024]{1,0:T(8,128)(2,1)S(1)}, u32[]{:S(2)}, u32[]{:S(2)}) collective-permute-start(bf16[128,1024]{1,0:T(8,128)(2,1)S(1)} %slice.133), channel_id=1, source_target_pairs={{0,1},{1,0},{2,3},{3,2},{4,5},{5,4},{6,7},{7,6},{8,9},{9,8},{10,11... | collective-permute-start | bytes 786440 | tf_op jit(solution)/shard_map/ppermute | solution.py:236

commit v5 on v4

--- a/solution.py
+++ b/solution.py
@@ -178,41 +178,53 @@
             jnp.dot(pick_own, tokens, preferred_element_type=jnp.float32)
             + jnp.dot(pick_other, other_tokens, preferred_element_type=jnp.float32)
         ).astype(jnp.bfloat16)
-        q_part = jnp.dot(chosen, q_weight, preferred_element_type=jnp.float32)
-        k_part = jnp.dot(chosen, key_matrix, preferred_element_type=jnp.float32)
-        v_part = jnp.dot(chosen, value_matrix, preferred_element_type=jnp.float32)
-        q_width = q_part.shape[1]
-        k_width = k_part.shape[1]
-        joined = jnp.concatenate(
-            [q_part.astype(jnp.bfloat16), k_part.astype(jnp.bfloat16), v_part.astype(jnp.bfloat16)],
-            axis=1,
-        )
-        blocks = [joined[k * block_rows : (k + 1) * block_rows] for k in range(n_row)]
-        summed = ring_reduce_scatter(blocks)
-        summed, late_slot_seq, late_row = lax.optimization_barrier((summed, slot_seq, row_index))
-        q_sum = summed[:, :q_width]
-        key_total_sum = summed[:, q_width : q_width + k_width]
-        value_total_sum = summed[:, q_width + k_width :]
+        n_kv = k_cache.shape[2]
+        q_cols = q_weight.shape[1] // n_kv
+        k_cols = key_matrix.shape[1] // n_kv
         starts = lookup(cache_len, sequences[:seq_dev])
         token_places = (starts[:, None] + jnp.arange(new_len)[None, :]).reshape(-1).astype(jnp.float32)
-        row_total = q_sum.shape[0]
-        queries = apply_turning(q_sum.reshape(row_total, -1, head_dim), token_places).astype(
-            jnp.bfloat16
-        )
-        rotated_keys = apply_turning(
-            key_total_sum.reshape(row_total, -1, head_dim), token_places
-        ).astype(jnp.bfloat16)
-        values = value_total_sum.reshape(row_total, -1, head_dim).astype(jnp.bfloat16)
-        results = jax.vmap(attend)(
-            queries.reshape(seq_dev, new_len, -1, head_dim),
-            rotated_keys.reshape(seq_dev, new_len, -1, head_dim),
-            values.reshape(seq_dev, new_len, -1, head_dim),
-            k_cache,
-            value_cache,
-            starts,
-        )
-        attended = results.reshape(seq_dev * new_len, -1)
-        stacked = ring_all_gather(attended)
+        late = None
+        arranged_parts = []
+        for h in range(n_kv):
+            q_part = jnp.dot(
+                chosen, q_weight[:, h * q_cols : (h + 1) * q_cols], preferred_element_type=jnp.float32
+            )
+            k_part = jnp.dot(
+                chosen, key_matrix[:, h * k_cols : (h + 1) * k_cols], preferred_element_type=jnp.float32
+            )
+            v_part = jnp.dot(
+                chosen, value_matrix[:, h * k_cols : (h + 1) * k_cols], preferred_element_type=jnp.float32
+            )
+            joined = jnp.concatenate(
+                [q_part.astype(jnp.bfloat16), k_part.astype(jnp.bfloat16), v_part.astype(jnp.bfloat16)],
+                axis=1,
+            )
+            blocks = [joined[k * block_rows : (k + 1) * block_rows] for k in range(n_row)]
+            summed = ring_reduce_scatter(blocks)
+            if late is None:
+                summed, late_slot_seq, late_row = lax.optimization_barrier((summed, slot_seq, row_index))
+                late = True
+            q_sum = summed[:, :q_cols]
+            key_total_sum = summed[:, q_cols : q_cols + k_cols]
+            value_total_sum = summed[:, q_cols + k_cols :]
+            row_total = q_sum.shape[0]
+            queries = apply_turning(q_sum.reshape(row_total, -1, head_dim), token_places).astype(
+                jnp.bfloat16
+            )
+            rotated_keys = apply_turning(
+                key_total_sum.reshape(row_total, -1, head_dim), token_places
+            ).astype(jnp.bfloat16)
+            values = value_total_sum.reshape(row_total, -1, head_dim).astype(jnp.bfloat16)
+            results = jax.vmap(attend)(
+                queries.reshape(seq_dev, new_len, -1, head_dim),
+                rotated_keys.reshape(seq_dev, new_len, -1, head_dim),
+                values.reshape(seq_dev, new_len, -1, head_dim),
+                k_cache[:, :, h : h + 1, :],
+                value_cache[:, :, h : h + 1, :],
+                starts,
+            )
+            attended = results.reshape(seq_dev * new_len, -1)
+            arranged_parts.append(ring_all_gather(attended))
         late_mine = jnp.arange(n_row, dtype=jnp.int32)[:, None] == late_row
         row_of_slot = jnp.sum(jnp.where(late_mine, jnp.asarray(stacked_table), 0), axis=0)
         seq_ids = jnp.arange(slot_total, dtype=jnp.int32)
@@ -222,22 +234,18 @@
         half = jnp.where(local < own_rows, 1 - col_index, col_index)
         t = half * own_rows + local % own_rows
         span_order = lookup(seq_base, t // new_len) + t % new_len
-        arranged = jnp.dot(
-            one_hot(span_order, span_rows), stacked, preferred_element_type=jnp.float32
-        ).astype(jnp.bfloat16)
-        out_width = o_weight.shape[1]
-        n_chunks = 2 if out_width % 256 == 0 else 1
-        chunk = out_width // n_chunks
-        pieces = []
-        for i in range(n_chunks):
-            products = jnp.dot(
-                arranged, o_weight[:, i * chunk : (i + 1) * chunk], preferred_element_type=jnp.float32
-            )
-            received = lax.ppermute(
-                products[:own_rows].astype(jnp.bfloat16), "col", [(0, 1), (1, 0)]
-            )
-            pieces.append((products[own_rows:] + received.astype(jnp.float32)).astype(jnp.bfloat16))
-        return jnp.concatenate(pieces, axis=1)
+        order_matrix = one_hot(span_order, span_rows)
+        products = None
+        for h in range(n_kv):
+            arranged = jnp.dot(
+                order_matrix, arranged_parts[h], preferred_element_type=jnp.float32
+            ).astype(jnp.bfloat16)
+            term = jnp.dot(
+                arranged, o_weight[h * q_cols : (h + 1) * q_cols], preferred_element_type=jnp.float32
+            )
+            products = term if products is None else products + term
+        received = lax.ppermute(products[:own_rows].astype(jnp.bfloat16), "col", [(0, 1), (1, 0)])
+        return (products[own_rows:] + received.astype(jnp.float32)).astype(jnp.bfloat16)
 
     return body
 

time: 108 us -> 104 us (0.963)
  waiting for transfers between devices: 51.1 us -> 21.4 us
  starting transfers between devices: 17.9 us -> 33.8 us
  local copies, waits for them, and re-layouts: 1.65 us -> 11.3 us
  other arithmetic: 8.93 us -> 6.35 us
  matrix products: 28 us -> 30.3 us
    ppermute x4 -> x8, waiting for transfers between devices: 24 us -> 7.36 us  [ring_reduce_scatter(): got_forward = lax.ppermute(forward, 'row', forward_pairs)]
    ppermute x3 -> x6, waiting for transfers between devices: 12.8 us -> 0.38 us  [ring_all_gather(): backward = lax.ppermute(backward, 'row', backward_pairs)]
    slice x3 -> x4, local copies, waits for them, and re-layouts: 0.1 us -> 10.6 us  [the longest x1 5.67 us: body(): k_cache[:, :, h:h + 1, :]]
    ppermute x4 -> x8, starting transfers between devices: 7.8 us -> 17.1 us  [ring_reduce_scatter(): got_forward = lax.ppermute(forward, 'row', forward_pairs)]
    ppermute x4 -> x8, starting transfers between devices: 6.21 us -> 14.4 us  [ring_all_gather(): forward = lax.ppermute(forward, 'row', forward_pairs)]
    ppermute x4 -> x8, waiting for transfers between devices: 10.7 us -> 5.44 us  [ring_all_gather(): forward = lax.ppermute(forward, 'row', forward_pairs)]
    ppermute x3 -> x6, waiting for transfers between devices: 2.53 us -> 6.29 us  [ring_reduce_scatter(): got_backward = lax.ppermute(backward, 'row', backward_pairs)]
    dot_general x6 -> x8, matrix products: 21.7 us -> 24.9 us  [the longest x2 14 us: body(): jnp.dot(arranged, o_weight[h * q_cols:(h + 1) * q_cols], preferred_elemen...]
  transfers between devices with their start and end apart: 17 -> 30, of which waited for: 12 -> 19; matrix products, arithmetic and copies ran while one was open for 10% -> 24% of each run, Pallas kernels for 0% -> 0%
where the time goes in v5:
time: 104 us
  starting transfers between devices  33.8 us (32%)
  matrix products  30.3 us (29%)
  waiting for transfers between devices  21.4 us (21%)
  local copies, waits for them, and re-layouts  11.3 us (11%)
  other arithmetic  6.35 us (6%)
    ppermute x8, starting transfers between devices, ring_reduce_scatter(): got_forward = lax.ppermute(forward, 'row', forward_pairs)  17.1 us
    ppermute x8, starting transfers between devices, ring_all_gather(): forward = lax.ppermute(forward, 'row', forward_pairs)  14.4 us
    dot_general x2, matrix products, body(): jnp.dot(arranged, o_weight[h * q_cols:(h + 1) * q_cols], preferred_elemen...  14 us
    ppermute x8, waiting for transfers between devices, ring_reduce_scatter(): got_forward = lax.ppermute(forward, 'row', forward_pairs)  7.36 us
    ppermute x6, waiting for transfers between devices, ring_reduce_scatter(): got_backward = lax.ppermute(backward, 'row', backward_pairs)  6.29 us
    slice x1, local copies, waits for them, and re-layouts, body(): k_cache[:, :, h:h + 1, :]  5.67 us
    ppermute x8, waiting for transfers between devices, ring_all_gather(): forward = lax.ppermute(forward, 'row', forward_pairs)  5.44 us
    slice x1, local copies, waits for them, and re-layouts, body(): value_cache[:, :, h:h + 1, :]  4.88 us
  transfers between devices with their start and end apart: 30, of which 19 were waited for; matrix products, arithmetic and copies ran while one was open for 24% of the time, Pallas kernels for 0%

profile of v5, /device:TPU:0, one launch (start us, length us, event | category | flops | bytes accessed | tf_op | source)
XLA Modules:
  0.0 103.8 jit_solution(3746766217278143547)
XLA Ops:
  3.1 5.7 %fusion.106 = (bf16[2,1536,1,128]{3,2,1,0:T(2,128)(2,1)}, bf16[2,1536,1,128]{3,2,1,0:T(2,128)(2,1)}) fusion(bf16[2,1536,2,128]{3,2,1,0:T(2,128)(2,1)} %param.16), kind=kLoop, calls=%fused_computation.204 | loop fusion | bytes 3145728 | tf_op jit(solution)/shard_map/slice | solution.py:222
  9.7 4.9 %fusion.105 = (bf16[2,1536,1,128]{3,2,1,0:T(2,128)(2,1)S(1)}, bf16[2,1536,1,128]{3,2,1,0:T(2,128)(2,1)S(1)}) fusion(bf16[2,1536,2,128]{3,2,1,0:T(2,128)(2,1)} %param.17), kind=kLoop, calls=%fused_computation.203 | loop fusion | bytes 3145728 | tf_op jit(solution)/shard_map/slice | solution.py:223
  15.1 1.8 %convolution_convert_fusion.4 = bf16[256,128]{1,0:T(8,128)(2,1)S(1)} fusion(bf16[256,2048]{1,0:T(8,128)(2,1)S(1)} %fusion.21, bf16[2048,256]{1,0:T(8,128)(2,1)} %param.14), kind=kOutput, calls=%fused_computation.53 | convolution fusion | flops 134250496 | bytes 1638400 | tf_op jit(solution)/shard_map/dot_general | solution.py:195
  16.9 1.5 %convolution_convert_fusion.2 = bf16[256,128]{1,0:T(8,128)(2,1)S(1)} fusion(bf16[256,2048]{1,0:T(8,128)(2,1)S(1)} %fusion.21, bf16[2048,256]{1,0:T(8,128)(2,1)} %param.14), kind=kOutput, calls=%fused_computation.51 | convolution fusion | flops 134250496 | bytes 1638400 | tf_op jit(solution)/shard_map/dot_general | solution.py:195
  18.4 1.5 %convolution_convert_fusion.5 = bf16[256,128]{1,0:T(8,128)(2,1)S(1)} fusion(bf16[256,2048]{1,0:T(8,128)(2,1)S(1)} %fusion.21, bf16[2048,256]{1,0:T(8,128)(2,1)} %param.13), kind=kOutput, calls=%fused_computation.54 | convolution fusion | flops 134250496 | bytes 1638400 | tf_op jit(solution)/shard_map/dot_general | solution.py:192
  19.9 1.5 %convolution_convert_fusion.3 = bf16[256,128]{1,0:T(8,128)(2,1)S(1)} fusion(bf16[256,2048]{1,0:T(8,128)(2,1)S(1)} %fusion.21, bf16[2048,256]{1,0:T(8,128)(2,1)} %param.13), kind=kOutput, calls=%fused_computation.52 | convolution fusion | flops 134250496 | bytes 1638400 | tf_op jit(solution)/shard_map/dot_general | solution.py:192
  21.4 2.4 %fusion.22 = bf16[256,2048]{1,0:T(8,128)(2,1)S(1)} fusion(bf16[256,2048]{1,0:T(8,128)(2,1)S(1)} %fusion.21, bf16[2048,4096]{1,0:T(8,128)(2,1)S(1)} %copy-done.4), kind=kOutput, calls=%fused_computation.29 | convolution fusion | flops 2148007936 | bytes 10485760 | tf_op jit(solution)/shard_map/dot_general | solution.py:189
  23.7 2.4 %fusion.25 = bf16[256,2048]{1,0:T(8,128)(2,1)S(1)} fusion(bf16[256,2048]{1,0:T(8,128)(2,1)S(1)} %fusion.21, bf16[2048,4096]{1,0:T(8,128)(2,1)S(1)} %copy-done.4), kind=kOutput, calls=%fused_computation.30 | convolution fusion | flops 2148007936 | bytes 10485760 | tf_op jit(solution)/shard_map/dot_general | solution.py:189
  26.2 2.6 %collective-permute-start.1 = (bf16[32,2304]{1,0:T(8,128)(2,1)S(1)}, bf16[32,2304]{1,0:T(8,128)(2,1)S(1)}, u32[]{:S(2)}, u32[]{:S(2)}) collective-permute-start(bf16[32,2304]{1,0:T(8,128)(2,1)S(1)} %get-tuple-element.22), channel_id=1, source_target_pairs={{0,4},{4,8},{8,12},{12,14},{14,10},{10,6},{6,2},{2,0},{1,5},{5,9},... | collective-permute-start | bytes 442376 | tf_op jit(solution)/shard_map/ppermute | solution.py:122
  29.0 2.1 %collective-permute-start.15 = (bf16[32,2304]{1,0:T(8,128)(2,1)S(1)}, bf16[32,2304]{1,0:T(8,128)(2,1)S(1)}, u32[]{:S(2)}, u32[]{:S(2)}) collective-permute-start(bf16[32,2304]{1,0:T(8,128)(2,1)S(1)} %get-tuple-element.28), channel_id=1, source_target_pairs={{0,4},{4,8},{8,12},{12,14},{14,10},{10,6},{6,2},{2,0},{1,5},{5,9},... | collective-permute-start | bytes 442376 | tf_op jit(solution)/shard_map/ppermute | solution.py:122
  31.1 2.4 %collective-permute-done.1 = bf16[32,2304]{1,0:T(8,128)(2,1)S(1)} collective-permute-done((bf16[32,2304]{1,0:T(8,128)(2,1)S(1)}, bf16[32,2304]{1,0:T(8,128)(2,1)S(1)}, u32[]{:S(2)}, u32[]{:S(2)}) %collective-permute-start.1) | collective-permute-done | bytes 147488 | tf_op jit(solution)/shard_map/ppermute | solution.py:122
  33.5 2.1 %collective-permute-start.2 = (bf16[32,2304]{1,0:T(8,128)(2,1)S(1)}, bf16[32,2304]{1,0:T(8,128)(2,1)S(1)}, u32[]{:S(2)}, u32[]{:S(2)}) collective-permute-start(bf16[32,2304]{1,0:T(8,128)(2,1)S(1)} %add_convert_fusion.9), channel_id=1, source_target_pairs={{0,4},{4,8},{8,12},{12,14},{14,10},{10,6},{6,2},{2,0},{1,5},{5,9},... | collective-permute-start | bytes 442376 | tf_op jit(solution)/shard_map/ppermute | solution.py:122
  36.7 2.1 %collective-permute-start.16 = (bf16[32,2304]{1,0:T(8,128)(2,1)S(1)}, bf16[32,2304]{1,0:T(8,128)(2,1)S(1)}, u32[]{:S(2)}, u32[]{:S(2)}) collective-permute-start(bf16[32,2304]{1,0:T(8,128)(2,1)S(1)} %add_convert_fusion.4), channel_id=1, source_target_pairs={{0,4},{4,8},{8,12},{12,14},{14,10},{10,6},{6,2},{2,0},{1,5},{5,9},... | collective-permute-start | bytes 442376 | tf_op jit(solution)/shard_map/ppermute | solution.py:122
  40.3 2.1 %collective-permute-start.3 = (bf16[32,2304]{1,0:T(8,128)(2,1)S(1)}, bf16[32,2304]{1,0:T(8,128)(2,1)S(1)}, u32[]{:S(2)}, u32[]{:S(2)}) collective-permute-start(bf16[32,2304]{1,0:T(8,128)(2,1)S(1)} %get-tuple-element.20), channel_id=1, source_target_pairs={{0,4},{4,8},{8,12},{12,14},{14,10},{10,6},{6,2},{2,0},{1,5},{5,9},... | collective-permute-start | bytes 442376 | tf_op jit(solution)/shard_map/ppermute | solution.py:122
  43.6 2.1 %collective-permute-start.17 = (bf16[32,2304]{1,0:T(8,128)(2,1)S(1)}, bf16[32,2304]{1,0:T(8,128)(2,1)S(1)}, u32[]{:S(2)}, u32[]{:S(2)}) collective-permute-start(bf16[32,2304]{1,0:T(8,128)(2,1)S(1)} %get-tuple-element.26), channel_id=1, source_target_pairs={{0,4},{4,8},{8,12},{12,14},{14,10},{10,6},{6,2},{2,0},{1,5},{5,9},... | collective-permute-start | bytes 442376 | tf_op jit(solution)/shard_map/ppermute | solution.py:122
  47.0 1.9 %collective-permute-done.6 = bf16[32,2304]{1,0:T(8,128)(2,1)S(1)} collective-permute-done((bf16[32,2304]{1,0:T(8,128)(2,1)S(1)}, bf16[32,2304]{1,0:T(8,128)(2,1)S(1)}, u32[]{:S(2)}, u32[]{:S(2)}) %collective-permute-start.6) | collective-permute-done | bytes 147488 | tf_op jit(solution)/shard_map/ppermute | solution.py:124
  49.1 1.9 %collective-permute-start.4 = (bf16[32,2304]{1,0:T(8,128)(2,1)S(1)}, bf16[32,2304]{1,0:T(8,128)(2,1)S(1)}, u32[]{:S(2)}, u32[]{:S(2)}) collective-permute-start(bf16[32,2304]{1,0:T(8,128)(2,1)S(1)} %get-tuple-element.18), channel_id=1, source_target_pairs={{0,4},{4,8},{8,12},{12,14},{14,10},{10,6},{6,2},{2,0},{1,5},{5,9},... | collective-permute-start | bytes 442376 | tf_op jit(solution)/shard_map/ppermute | solution.py:122
  51.0 1.4 %collective-permute-done.20 = bf16[32,2304]{1,0:T(8,128)(2,1)S(1)} collective-permute-done((bf16[32,2304]{1,0:T(8,128)(2,1)S(1)}, bf16[32,2304]{1,0:T(8,128)(2,1)S(1)}, u32[]{:S(2)}, u32[]{:S(2)}) %collective-permute-start.20) | collective-permute-done | bytes 147488 | tf_op jit(solution)/shard_map/ppermute | solution.py:124
  52.6 2.0 %collective-permute-start.18 = (bf16[32,2304]{1,0:T(8,128)(2,1)S(1)}, bf16[32,2304]{1,0:T(8,128)(2,1)S(1)}, u32[]{:S(2)}, u32[]{:S(2)}) collective-permute-start(bf16[32,2304]{1,0:T(8,128)(2,1)S(1)} %get-tuple-element.24), channel_id=1, source_target_pairs={{0,4},{4,8},{8,12},{12,14},{14,10},{10,6},{6,2},{2,0},{1,5},{5,9},... | collective-permute-start | bytes 442376 | tf_op jit(solution)/shard_map/ppermute | solution.py:122
  55.5 2.1 %collective-permute-done.21 = bf16[32,2304]{1,0:T(8,128)(2,1)S(1)} collective-permute-done((bf16[32,2304]{1,0:T(8,128)(2,1)S(1)}, bf16[32,2304]{1,0:T(8,128)(2,1)S(1)}, u32[]{:S(2)}, u32[]{:S(2)}) %collective-permute-start.21) | collective-permute-done | bytes 147488 | tf_op jit(solution)/shard_map/ppermute | solution.py:124
  61.6 1.8 %collective-permute-start.22 = (bf16[32,2048]{1,0:T(8,128)(2,1)S(1)}, bf16[32,2048]{1,0:T(8,128)(2,1)S(1)}, u32[]{:S(2)}, u32[]{:S(2)}) collective-permute-start(bf16[32,2048]{1,0:T(8,128)(2,1)S(1)} %bitcast.213), channel_id=1, source_target_pairs={{0,4},{4,8},{8,12},{12,14},{14,10},{10,6},{6,2},{2,0},{1,5},{5,9},... | collective-permute-start | bytes 393224 | tf_op jit(solution)/shard_map/ppermute | solution.py:138
  66.7 1.8 %collective-permute-start.8 = (bf16[32,2048]{1,0:T(8,128)(2,1)S(1)}, bf16[32,2048]{1,0:T(8,128)(2,1)S(1)}, u32[]{:S(2)}, u32[]{:S(2)}) collective-permute-start(bf16[32,2048]{1,0:T(8,128)(2,1)S(1)} %bitcast.215), channel_id=1, source_target_pairs={{0,4},{4,8},{8,12},{12,14},{14,10},{10,6},{6,2},{2,0},{1,5},{5,9},... | collective-permute-start | bytes 393224 | tf_op jit(solution)/shard_map/ppermute | solution.py:138
  69.1 1.8 %collective-permute-start.24 = (bf16[32,2048]{1,0:T(8,128)(2,1)S(1)}, bf16[32,2048]{1,0:T(8,128)(2,1)S(1)}, u32[]{:S(2)}, u32[]{:S(2)}) collective-permute-start(bf16[32,2048]{1,0:T(8,128)(2,1)S(1)} %collective-permute-done.22), channel_id=1, source_target_pairs={{0,4},{4,8},{8,12},{12,14},{14,10},{10,6},{6,2},{2,0},{1,5},{5,9},... | collective-permute-start | bytes 393224 | tf_op jit(solution)/shard_map/ppermute | solution.py:138
  71.2 1.4 %collective-permute-done.8 = bf16[32,2048]{1,0:T(8,128)(2,1)S(1)} collective-permute-done((bf16[32,2048]{1,0:T(8,128)(2,1)S(1)}, bf16[32,2048]{1,0:T(8,128)(2,1)S(1)}, u32[]{:S(2)}, u32[]{:S(2)}) %collective-permute-start.8) | collective-permute-done | bytes 131104 | tf_op jit(solution)/shard_map/ppermute | solution.py:138
  72.7 1.8 %collective-permute-start.10 = (bf16[32,2048]{1,0:T(8,128)(2,1)S(1)}, bf16[32,2048]{1,0:T(8,128)(2,1)S(1)}, u32[]{:S(2)}, u32[]{:S(2)}) collective-permute-start(bf16[32,2048]{1,0:T(8,128)(2,1)S(1)} %collective-permute-done.8), channel_id=1, source_target_pairs={{0,4},{4,8},{8,12},{12,14},{14,10},{10,6},{6,2},{2,0},{1,5},{5,9},... | collective-permute-start | bytes 393224 | tf_op jit(solution)/shard_map/ppermute | solution.py:138
  75.5 1.8 %collective-permute-start.26 = (bf16[32,2048]{1,0:T(8,128)(2,1)S(1)}, bf16[32,2048]{1,0:T(8,128)(2,1)S(1)}, u32[]{:S(2)}, u32[]{:S(2)}) collective-permute-start(bf16[32,2048]{1,0:T(8,128)(2,1)S(1)} %collective-permute-done.24), channel_id=1, source_target_pairs={{0,4},{4,8},{8,12},{12,14},{14,10},{10,6},{6,2},{2,0},{1,5},{5,9},... | collective-permute-start | bytes 393224 | tf_op jit(solution)/shard_map/ppermute | solution.py:138
  79.0 1.8 %collective-permute-start.12 = (bf16[32,2048]{1,0:T(8,128)(2,1)S(1)}, bf16[32,2048]{1,0:T(8,128)(2,1)S(1)}, u32[]{:S(2)}, u32[]{:S(2)}) collective-permute-start(bf16[32,2048]{1,0:T(8,128)(2,1)S(1)} %collective-permute-done.10), channel_id=1, source_target_pairs={{0,4},{4,8},{8,12},{12,14},{14,10},{10,6},{6,2},{2,0},{1,5},{5,9},... | collective-permute-start | bytes 393224 | tf_op jit(solution)/shard_map/ppermute | solution.py:138
  81.9 1.8 %collective-permute-start.28 = (bf16[32,2048]{1,0:T(8,128)(2,1)S(1)}, bf16[32,2048]{1,0:T(8,128)(2,1)S(1)}, u32[]{:S(2)}, u32[]{:S(2)}) collective-permute-start(bf16[32,2048]{1,0:T(8,128)(2,1)S(1)} %collective-permute-done.26), channel_id=1, source_target_pairs={{0,4},{4,8},{8,12},{12,14},{14,10},{10,6},{6,2},{2,0},{1,5},{5,9},... | collective-permute-start | bytes 393224 | tf_op jit(solution)/shard_map/ppermute | solution.py:138
  84.6 1.8 %collective-permute-start.14 = (bf16[32,2048]{1,0:T(8,128)(2,1)S(1)}, bf16[32,2048]{1,0:T(8,128)(2,1)S(1)}, u32[]{:S(2)}, u32[]{:S(2)}) collective-permute-start(bf16[32,2048]{1,0:T(8,128)(2,1)S(1)} %collective-permute-done.12), channel_id=1, source_target_pairs={{0,4},{4,8},{8,12},{12,14},{14,10},{10,6},{6,2},{2,0},{1,5},{5,9},... | collective-permute-start | bytes 393224 | tf_op jit(solution)/shard_map/ppermute | solution.py:138
  86.9 7.4 %fusion = f32[256,2048]{1,0:T(8,128)} fusion(bf16[4096,2048]{1,0:T(8,128)(2,1)} %param.15, bf16[256,2048]{1,0:T(8,128)(2,1)S(1)} %constant_dynamic-update-slice_fusion.8, s32[256]{0:T(256)S(1)} %fusion.97), kind=kOutput, calls=%fused_computation | convolution fusion | flops 2416508928 | bytes 11535360 | tf_op jit(solution)/shard_map/dot_general | solution.py:243
  94.2 6.6 %fusion.18 = f32[256,2048]{1,0:T(8,128)S(1)} fusion(f32[256,2048]{1,0:T(8,128)} %fusion, bf16[4096,2048]{1,0:T(8,128)(2,1)} %param.15, bf16[256,2048]{1,0:T(8,128)(2,1)S(1)} %constant_dynamic-update-slice_fusion, s32[256]{0:T(256)S(1)} %fusion.97), kind=kOutput, calls=%fused_computation.25 | convolution fusion | flops 2417033216 | bytes 13632512 | tf_op jit(solution)/shard_map/dot_general | solution.py:243
  101.0 1.9 %collective-permute-done.29 = bf16[128,2048]{1,0:T(8,128)(2,1)S(1)} collective-permute-done((bf16[128,2048]{1,0:T(8,128)(2,1)S(1)}, bf16[128,2048]{1,0:T(8,128)(2,1)S(1)}, u32[]{:S(2)}, u32[]{:S(2)}) %collective-permute-start.29) | collective-permute-done | bytes 524320 | tf_op jit(solution)/shard_map/ppermute | solution.py:247
  (131 shorter events, 25.1 us)
Async XLA Ops:
  0.0 14.6 %collective-permute-start = (bf16[128,2048]{1,0:T(8,128)(2,1)}, bf16[128,2048]{1,0:T(8,128)(2,1)S(1)}, u32[]{:S(2)}, u32[]{:S(2)}) collective-permute-start(bf16[128,2048]{1,0:T(8,128)(2,1)} %param.11), channel_id=1, source_target_pairs={{0,1},{1,0},{2,3},{3,2},{4,5},{5,4},{6,7},{7,6},{8,9},{9,8},{10,11... | collective-permute-start | bytes 1572872 | tf_op jit(solution)/shard_map/ppermute | solution.py:166
  3.1 5.9 %copy-start.2 = (bf16[128,2048]{1,0:T(8,128)(2,1)S(1)}, bf16[128,2048]{1,0:T(8,128)(2,1)}, u32[]{:S(2)}) copy-start(bf16[128,2048]{1,0:T(8,128)(2,1)} %param.11) | copy-start | bytes 1572868
  9.7 11.6 %copy-start.4 = (bf16[2048,4096]{1,0:T(8,128)(2,1)S(1)}, bf16[2048,4096]{1,0:T(8,128)(2,1)}, u32[]{:S(2)}) copy-start(bf16[2048,4096]{1,0:T(8,128)(2,1)} %param.12) | copy-start | bytes 50331652
  26.2 7.3 %collective-permute-start.1 = (bf16[32,2304]{1,0:T(8,128)(2,1)S(1)}, bf16[32,2304]{1,0:T(8,128)(2,1)S(1)}, u32[]{:S(2)}, u32[]{:S(2)}) collective-permute-start(bf16[32,2304]{1,0:T(8,128)(2,1)S(1)} %get-tuple-element.22), channel_id=1, source_target_pairs={{0,4},{4,8},{8,12},{12,14},{14,10},{10,6},{6,2},{2,0},{1,5},{5,9},... | collective-permute-start | bytes 442376 | tf_op jit(solution)/shard_map/ppermute | solution.py:122
  28.9 10.0 %collective-permute-start.5 = (bf16[32,2304]{1,0:T(8,128)(2,1)S(1)}, bf16[32,2304]{1,0:T(8,128)(2,1)S(1)}, u32[]{:S(2)}, u32[]{:S(2)}) collective-permute-start(bf16[32,2304]{1,0:T(8,128)(2,1)S(1)} %get-tuple-element.23), channel_id=1, source_target_pairs={{0,2},{4,0},{8,4},{12,8},{14,12},{10,14},{6,10},{2,6},{1,3},{5,1},... | collective-permute-start | bytes 442376 | tf_op jit(solution)/shard_map/ppermute | solution.py:124
  29.0 7.7 %collective-permute-start.15 = (bf16[32,2304]{1,0:T(8,128)(2,1)S(1)}, bf16[32,2304]{1,0:T(8,128)(2,1)S(1)}, u32[]{:S(2)}, u32[]{:S(2)}) collective-permute-start(bf16[32,2304]{1,0:T(8,128)(2,1)S(1)} %get-tuple-element.28), channel_id=1, source_target_pairs={{0,4},{4,8},{8,12},{12,14},{14,10},{10,6},{6,2},{2,0},{1,5},{5,9},... | collective-permute-start | bytes 442376 | tf_op jit(solution)/shard_map/ppermute | solution.py:122
  31.1 11.3 %collective-permute-start.19 = (bf16[32,2304]{1,0:T(8,128)(2,1)S(1)}, bf16[32,2304]{1,0:T(8,128)(2,1)S(1)}, u32[]{:S(2)}, u32[]{:S(2)}) collective-permute-start(bf16[32,2304]{1,0:T(8,128)(2,1)S(1)} %get-tuple-element.29), channel_id=1, source_target_pairs={{0,2},{4,0},{8,4},{12,8},{14,12},{10,14},{6,10},{2,6},{1,3},{5,1},... | collective-permute-start | bytes 442376 | tf_op jit(solution)/shard_map/ppermute | solution.py:124
  33.5 6.6 %collective-permute-start.2 = (bf16[32,2304]{1,0:T(8,128)(2,1)S(1)}, bf16[32,2304]{1,0:T(8,128)(2,1)S(1)}, u32[]{:S(2)}, u32[]{:S(2)}) collective-permute-start(bf16[32,2304]{1,0:T(8,128)(2,1)S(1)} %add_convert_fusion.9), channel_id=1, source_target_pairs={{0,4},{4,8},{8,12},{12,14},{14,10},{10,6},{6,2},{2,0},{1,5},{5,9},... | collective-permute-start | bytes 442376 | tf_op jit(solution)/shard_map/ppermute | solution.py:122
  36.7 6.8 %collective-permute-start.16 = (bf16[32,2304]{1,0:T(8,128)(2,1)S(1)}, bf16[32,2304]{1,0:T(8,128)(2,1)S(1)}, u32[]{:S(2)}, u32[]{:S(2)}) collective-permute-start(bf16[32,2304]{1,0:T(8,128)(2,1)S(1)} %add_convert_fusion.4), channel_id=1, source_target_pairs={{0,4},{4,8},{8,12},{12,14},{14,10},{10,6},{6,2},{2,0},{1,5},{5,9},... | collective-permute-start | bytes 442376 | tf_op jit(solution)/shard_map/ppermute | solution.py:122
  40.3 6.7 %collective-permute-start.3 = (bf16[32,2304]{1,0:T(8,128)(2,1)S(1)}, bf16[32,2304]{1,0:T(8,128)(2,1)S(1)}, u32[]{:S(2)}, u32[]{:S(2)}) collective-permute-start(bf16[32,2304]{1,0:T(8,128)(2,1)S(1)} %get-tuple-element.20), channel_id=1, source_target_pairs={{0,4},{4,8},{8,12},{12,14},{14,10},{10,6},{6,2},{2,0},{1,5},{5,9},... | collective-permute-start | bytes 442376 | tf_op jit(solution)/shard_map/ppermute | solution.py:122
  42.4 6.5 %collective-permute-start.6 = (bf16[32,2304]{1,0:T(8,128)(2,1)S(1)}, bf16[32,2304]{1,0:T(8,128)(2,1)S(1)}, u32[]{:S(2)}, u32[]{:S(2)}) collective-permute-start(bf16[32,2304]{1,0:T(8,128)(2,1)S(1)} %get-tuple-element.21), channel_id=1, source_target_pairs={{0,2},{4,0},{8,4},{12,8},{14,12},{10,14},{6,10},{2,6},{1,3},{5,1},... | collective-permute-start | bytes 442376 | tf_op jit(solution)/shard_map/ppermute | solution.py:124
  43.6 7.5 %collective-permute-start.17 = (bf16[32,2304]{1,0:T(8,128)(2,1)S(1)}, bf16[32,2304]{1,0:T(8,128)(2,1)S(1)}, u32[]{:S(2)}, u32[]{:S(2)}) collective-permute-start(bf16[32,2304]{1,0:T(8,128)(2,1)S(1)} %get-tuple-element.26), channel_id=1, source_target_pairs={{0,4},{4,8},{8,12},{12,14},{14,10},{10,6},{6,2},{2,0},{1,5},{5,9},... | collective-permute-start | bytes 442376 | tf_op jit(solution)/shard_map/ppermute | solution.py:122
  45.7 6.7 %collective-permute-start.20 = (bf16[32,2304]{1,0:T(8,128)(2,1)S(1)}, bf16[32,2304]{1,0:T(8,128)(2,1)S(1)}, u32[]{:S(2)}, u32[]{:S(2)}) collective-permute-start(bf16[32,2304]{1,0:T(8,128)(2,1)S(1)} %get-tuple-element.27), channel_id=1, source_target_pairs={{0,2},{4,0},{8,4},{12,8},{14,12},{10,14},{6,10},{2,6},{1,3},{5,1},... | collective-permute-start | bytes 442376 | tf_op jit(solution)/shard_map/ppermute | solution.py:124
  49.0 6.5 %collective-permute-start.7 = (bf16[32,2304]{1,0:T(8,128)(2,1)S(1)}, bf16[32,2304]{1,0:T(8,128)(2,1)S(1)}, u32[]{:S(2)}, u32[]{:S(2)}) collective-permute-start(bf16[32,2304]{1,0:T(8,128)(2,1)S(1)} %get-tuple-element.19), channel_id=1, source_target_pairs={{0,2},{4,0},{8,4},{12,8},{14,12},{10,14},{6,10},{2,6},{1,3},{5,1},... | collective-permute-start | bytes 442376 | tf_op jit(solution)/shard_map/ppermute | solution.py:124
  49.1 6.3 %collective-permute-start.4 = (bf16[32,2304]{1,0:T(8,128)(2,1)S(1)}, bf16[32,2304]{1,0:T(8,128)(2,1)S(1)}, u32[]{:S(2)}, u32[]{:S(2)}) collective-permute-start(bf16[32,2304]{1,0:T(8,128)(2,1)S(1)} %get-tuple-element.18), channel_id=1, source_target_pairs={{0,4},{4,8},{8,12},{12,14},{14,10},{10,6},{6,2},{2,0},{1,5},{5,9},... | collective-permute-start | bytes 442376 | tf_op jit(solution)/shard_map/ppermute | solution.py:122
  52.5 5.2 %collective-permute-start.21 = (bf16[32,2304]{1,0:T(8,128)(2,1)S(1)}, bf16[32,2304]{1,0:T(8,128)(2,1)S(1)}, u32[]{:S(2)}, u32[]{:S(2)}) collective-permute-start(bf16[32,2304]{1,0:T(8,128)(2,1)S(1)} %get-tuple-element.25), channel_id=1, source_target_pairs={{0,2},{4,0},{8,4},{12,8},{14,12},{10,14},{6,10},{2,6},{1,3},{5,1},... | collective-permute-start | bytes 442376 | tf_op jit(solution)/shard_map/ppermute | solution.py:124
  52.6 5.4 %collective-permute-start.18 = (bf16[32,2304]{1,0:T(8,128)(2,1)S(1)}, bf16[32,2304]{1,0:T(8,128)(2,1)S(1)}, u32[]{:S(2)}, u32[]{:S(2)}) collective-permute-start(bf16[32,2304]{1,0:T(8,128)(2,1)S(1)} %get-tuple-element.24), channel_id=1, source_target_pairs={{0,4},{4,8},{8,12},{12,14},{14,10},{10,6},{6,2},{2,0},{1,5},{5,9},... | collective-permute-start | bytes 442376 | tf_op jit(solution)/shard_map/ppermute | solution.py:122
  61.6 7.5 %collective-permute-start.22 = (bf16[32,2048]{1,0:T(8,128)(2,1)S(1)}, bf16[32,2048]{1,0:T(8,128)(2,1)S(1)}, u32[]{:S(2)}, u32[]{:S(2)}) collective-permute-start(bf16[32,2048]{1,0:T(8,128)(2,1)S(1)} %bitcast.213), channel_id=1, source_target_pairs={{0,4},{4,8},{8,12},{12,14},{14,10},{10,6},{6,2},{2,0},{1,5},{5,9},... | collective-permute-start | bytes 393224 | tf_op jit(solution)/shard_map/ppermute | solution.py:138
  63.4 7.5 %collective-permute-start.23 = (bf16[32,2048]{1,0:T(8,128)(2,1)S(1)}, bf16[32,2048]{1,0:T(8,128)(2,1)S(1)}, u32[]{:S(2)}, u32[]{:S(2)}) collective-permute-start(bf16[32,2048]{1,0:T(8,128)(2,1)S(1)} %bitcast.214), channel_id=1, source_target_pairs={{0,2},{4,0},{8,4},{12,8},{14,12},{10,14},{6,10},{2,6},{1,3},{5,1},... | collective-permute-start | bytes 393224 | tf_op jit(solution)/shard_map/ppermute | solution.py:141
  66.7 6.0 %collective-permute-start.8 = (bf16[32,2048]{1,0:T(8,128)(2,1)S(1)}, bf16[32,2048]{1,0:T(8,128)(2,1)S(1)}, u32[]{:S(2)}, u32[]{:S(2)}) collective-permute-start(bf16[32,2048]{1,0:T(8,128)(2,1)S(1)} %bitcast.215), channel_id=1, source_target_pairs={{0,4},{4,8},{8,12},{12,14},{14,10},{10,6},{6,2},{2,0},{1,5},{5,9},... | collective-permute-start | bytes 393224 | tf_op jit(solution)/shard_map/ppermute | solution.py:138
  68.5 6.2 %collective-permute-start.9 = (bf16[32,2048]{1,0:T(8,128)(2,1)S(1)}, bf16[32,2048]{1,0:T(8,128)(2,1)S(1)}, u32[]{:S(2)}, u32[]{:S(2)}) collective-permute-start(bf16[32,2048]{1,0:T(8,128)(2,1)S(1)} %bitcast.216), channel_id=1, source_target_pairs={{0,2},{4,0},{8,4},{12,8},{14,12},{10,14},{6,10},{2,6},{1,3},{5,1},... | collective-permute-start | bytes 393224 | tf_op jit(solution)/shard_map/ppermute | solution.py:141
  69.1 6.4 %collective-permute-start.24 = (bf16[32,2048]{1,0:T(8,128)(2,1)S(1)}, bf16[32,2048]{1,0:T(8,128)(2,1)S(1)}, u32[]{:S(2)}, u32[]{:S(2)}) collective-permute-start(bf16[32,2048]{1,0:T(8,128)(2,1)S(1)} %collective-permute-done.22), channel_id=1, source_target_pairs={{0,4},{4,8},{8,12},{12,14},{14,10},{10,6},{6,2},{2,0},{1,5},{5,9},... | collective-permute-start | bytes 393224 | tf_op jit(solution)/shard_map/ppermute | solution.py:138
  70.9 6.5 %collective-permute-start.25 = (bf16[32,2048]{1,0:T(8,128)(2,1)S(1)}, bf16[32,2048]{1,0:T(8,128)(2,1)S(1)}, u32[]{:S(2)}, u32[]{:S(2)}) collective-permute-start(bf16[32,2048]{1,0:T(8,128)(2,1)S(1)} %collective-permute-done.23), channel_id=1, source_target_pairs={{0,2},{4,0},{8,4},{12,8},{14,12},{10,14},{6,10},{2,6},{1,3},{5,1},... | collective-permute-start | bytes 393224 | tf_op jit(solution)/shard_map/ppermute | solution.py:141
  72.7 6.4 %collective-permute-start.10 = (bf16[32,2048]{1,0:T(8,128)(2,1)S(1)}, bf16[32,2048]{1,0:T(8,128)(2,1)S(1)}, u32[]{:S(2)}, u32[]{:S(2)}) collective-permute-start(bf16[32,2048]{1,0:T(8,128)(2,1)S(1)} %collective-permute-done.8), channel_id=1, source_target_pairs={{0,4},{4,8},{8,12},{12,14},{14,10},{10,6},{6,2},{2,0},{1,5},{5,9},... | collective-permute-start | bytes 393224 | tf_op jit(solution)/shard_map/ppermute | solution.py:138
  74.7 6.2 %collective-permute-start.11 = (bf16[32,2048]{1,0:T(8,128)(2,1)S(1)}, bf16[32,2048]{1,0:T(8,128)(2,1)S(1)}, u32[]{:S(2)}, u32[]{:S(2)}) collective-permute-start(bf16[32,2048]{1,0:T(8,128)(2,1)S(1)} %collective-permute-done.9), channel_id=1, source_target_pairs={{0,2},{4,0},{8,4},{12,8},{14,12},{10,14},{6,10},{2,6},{1,3},{5,1},... | collective-permute-start | bytes 393224 | tf_op jit(solution)/shard_map/ppermute | solution.py:141
  75.5 6.4 %collective-permute-start.26 = (bf16[32,2048]{1,0:T(8,128)(2,1)S(1)}, bf16[32,2048]{1,0:T(8,128)(2,1)S(1)}, u32[]{:S(2)}, u32[]{:S(2)}) collective-permute-start(bf16[32,2048]{1,0:T(8,128)(2,1)S(1)} %collective-permute-done.24), channel_id=1, source_target_pairs={{0,4},{4,8},{8,12},{12,14},{14,10},{10,6},{6,2},{2,0},{1,5},{5,9},... | collective-permute-start | bytes 393224 | tf_op jit(solution)/shard_map/ppermute | solution.py:138
  77.5 9.0 %collective-permute-start.27 = (bf16[32,2048]{1,0:T(8,128)(2,1)S(1)}, bf16[32,2048]{1,0:T(8,128)(2,1)S(1)}, u32[]{:S(2)}, u32[]{:S(2)}) collective-permute-start(bf16[32,2048]{1,0:T(8,128)(2,1)S(1)} %collective-permute-done.25), channel_id=1, source_target_pairs={{0,2},{4,0},{8,4},{12,8},{14,12},{10,14},{6,10},{2,6},{1,3},{5,1},... | collective-permute-start | bytes 393224 | tf_op jit(solution)/shard_map/ppermute | solution.py:141
  79.0 5.6 %collective-permute-start.12 = (bf16[32,2048]{1,0:T(8,128)(2,1)S(1)}, bf16[32,2048]{1,0:T(8,128)(2,1)S(1)}, u32[]{:S(2)}, u32[]{:S(2)}) collective-permute-start(bf16[32,2048]{1,0:T(8,128)(2,1)S(1)} %collective-permute-done.10), channel_id=1, source_target_pairs={{0,4},{4,8},{8,12},{12,14},{14,10},{10,6},{6,2},{2,0},{1,5},{5,9},... | collective-permute-start | bytes 393224 | tf_op jit(solution)/shard_map/ppermute | solution.py:138
  80.8 5.6 %collective-permute-start.13 = (bf16[32,2048]{1,0:T(8,128)(2,1)S(1)}, bf16[32,2048]{1,0:T(8,128)(2,1)S(1)}, u32[]{:S(2)}, u32[]{:S(2)}) collective-permute-start(bf16[32,2048]{1,0:T(8,128)(2,1)S(1)} %collective-permute-done.11), channel_id=1, source_target_pairs={{0,2},{4,0},{8,4},{12,8},{14,12},{10,14},{6,10},{2,6},{1,3},{5,1},... | collective-permute-start | bytes 393224 | tf_op jit(solution)/shard_map/ppermute | solution.py:141
  81.9 5.0 %collective-permute-start.28 = (bf16[32,2048]{1,0:T(8,128)(2,1)S(1)}, bf16[32,2048]{1,0:T(8,128)(2,1)S(1)}, u32[]{:S(2)}, u32[]{:S(2)}) collective-permute-start(bf16[32,2048]{1,0:T(8,128)(2,1)S(1)} %collective-permute-done.26), channel_id=1, source_target_pairs={{0,4},{4,8},{8,12},{12,14},{14,10},{10,6},{6,2},{2,0},{1,5},{5,9},... | collective-permute-start | bytes 393224 | tf_op jit(solution)/shard_map/ppermute | solution.py:138
  84.6 9.6 %collective-permute-start.14 = (bf16[32,2048]{1,0:T(8,128)(2,1)S(1)}, bf16[32,2048]{1,0:T(8,128)(2,1)S(1)}, u32[]{:S(2)}, u32[]{:S(2)}) collective-permute-start(bf16[32,2048]{1,0:T(8,128)(2,1)S(1)} %collective-permute-done.12), channel_id=1, source_target_pairs={{0,4},{4,8},{8,12},{12,14},{14,10},{10,6},{6,2},{2,0},{1,5},{5,9},... | collective-permute-start | bytes 393224 | tf_op jit(solution)/shard_map/ppermute | solution.py:138
  100.9 2.0 %collective-permute-start.29 = (bf16[128,2048]{1,0:T(8,128)(2,1)S(1)}, bf16[128,2048]{1,0:T(8,128)(2,1)S(1)}, u32[]{:S(2)}, u32[]{:S(2)}) collective-permute-start(bf16[128,2048]{1,0:T(8,128)(2,1)S(1)} %slice.273), channel_id=1, source_target_pairs={{0,1},{1,0},{2,3},{3,2},{4,5},{5,4},{6,7},{7,6},{8,9},{9,8},{10,11... | collective-permute-start | bytes 1572872 | tf_op jit(solution)/shard_map/ppermute | solution.py:247
  (4 other events, 12.9 us)

commit v6 on v4

--- a/solution.py
+++ b/solution.py
@@ -178,21 +178,29 @@
             jnp.dot(pick_own, tokens, preferred_element_type=jnp.float32)
             + jnp.dot(pick_other, other_tokens, preferred_element_type=jnp.float32)
         ).astype(jnp.bfloat16)
-        q_part = jnp.dot(chosen, q_weight, preferred_element_type=jnp.float32)
-        k_part = jnp.dot(chosen, key_matrix, preferred_element_type=jnp.float32)
-        v_part = jnp.dot(chosen, value_matrix, preferred_element_type=jnp.float32)
-        q_width = q_part.shape[1]
-        k_width = k_part.shape[1]
-        joined = jnp.concatenate(
-            [q_part.astype(jnp.bfloat16), k_part.astype(jnp.bfloat16), v_part.astype(jnp.bfloat16)],
-            axis=1,
-        )
-        blocks = [joined[k * block_rows : (k + 1) * block_rows] for k in range(n_row)]
-        summed = ring_reduce_scatter(blocks)
-        summed, late_slot_seq, late_row = lax.optimization_barrier((summed, slot_seq, row_index))
-        q_sum = summed[:, :q_width]
-        key_total_sum = summed[:, q_width : q_width + k_width]
-        value_total_sum = summed[:, q_width + k_width :]
+        n_kv = k_cache.shape[2]
+        q_cols = q_weight.shape[1] // n_kv
+        k_cols = key_matrix.shape[1] // n_kv
+        k_part = jnp.dot(chosen, key_matrix, preferred_element_type=jnp.float32).astype(jnp.bfloat16)
+        v_part = jnp.dot(chosen, value_matrix, preferred_element_type=jnp.float32).astype(jnp.bfloat16)
+        q_sums, k_sums, v_sums = [], [], []
+        for h in range(n_kv):
+            q_part = jnp.dot(
+                chosen, q_weight[:, h * q_cols : (h + 1) * q_cols], preferred_element_type=jnp.float32
+            ).astype(jnp.bfloat16)
+            joined = jnp.concatenate(
+                [q_part, k_part[:, h * k_cols : (h + 1) * k_cols], v_part[:, h * k_cols : (h + 1) * k_cols]],
+                axis=1,
+            )
+            blocks = [joined[k * block_rows : (k + 1) * block_rows] for k in range(n_row)]
+            summed = ring_reduce_scatter(blocks)
+            q_sums.append(summed[:, :q_cols])
+            k_sums.append(summed[:, q_cols : q_cols + k_cols])
+            v_sums.append(summed[:, q_cols + k_cols :])
+        q_sum = jnp.concatenate(q_sums, axis=1)
+        key_total_sum = jnp.concatenate(k_sums, axis=1)
+        value_total_sum = jnp.concatenate(v_sums, axis=1)
+        q_sum, late_slot_seq, late_row = lax.optimization_barrier((q_sum, slot_seq, row_index))
         starts = lookup(cache_len, sequences[:seq_dev])
         token_places = (starts[:, None] + jnp.arange(new_len)[None, :]).reshape(-1).astype(jnp.float32)
         row_total = q_sum.shape[0]
@@ -212,7 +220,9 @@
             starts,
         )
         attended = results.reshape(seq_dev * new_len, -1)
-        stacked = ring_all_gather(attended)
+        stacked = jnp.concatenate(
+            [ring_all_gather(attended[:, h * q_cols : (h + 1) * q_cols]) for h in range(n_kv)], axis=1
+        )
         late_mine = jnp.arange(n_row, dtype=jnp.int32)[:, None] == late_row
         row_of_slot = jnp.sum(jnp.where(late_mine, jnp.asarray(stacked_table), 0), axis=0)
         seq_ids = jnp.arange(slot_total, dtype=jnp.int32)
@@ -225,19 +235,10 @@
         arranged = jnp.dot(
             one_hot(span_order, span_rows), stacked, preferred_element_type=jnp.float32
         ).astype(jnp.bfloat16)
-        out_width = o_weight.shape[1]
-        n_chunks = 2 if out_width % 256 == 0 else 1
-        chunk = out_width // n_chunks
-        pieces = []
-        for i in range(n_chunks):
-            products = jnp.dot(
-                arranged, o_weight[:, i * chunk : (i + 1) * chunk], preferred_element_type=jnp.float32
-            )
-            received = lax.ppermute(
-                products[:own_rows].astype(jnp.bfloat16), "col", [(0, 1), (1, 0)]
-            )
-            pieces.append((products[own_rows:] + received.astype(jnp.float32)).astype(jnp.bfloat16))
-        return jnp.concatenate(pieces, axis=1)
+        arranged = lax.optimization_barrier(arranged)
+        products = jnp.dot(arranged, o_weight, preferred_element_type=jnp.float32)
+        received = lax.ppermute(products[:own_rows].astype(jnp.bfloat16), "col", [(0, 1), (1, 0)])
+        return (products[own_rows:] + received.astype(jnp.float32)).astype(jnp.bfloat16)
 
     return body
 

time: 108 us -> 95 us (0.88)
  waiting for transfers between devices: 51.1 us -> 26.9 us
  starting transfers between devices: 17.9 us -> 33.5 us
  matrix products: 28 us -> 24.6 us
  other arithmetic: 8.93 us -> 6.56 us
    ppermute x4 -> x8, waiting for transfers between devices: 24 us -> 8.82 us  [ring_reduce_scatter(): got_forward = lax.ppermute(forward, 'row', forward_pairs)]
    ppermute x4 -> x8, starting transfers between devices: 7.8 us -> 16.6 us  [ring_reduce_scatter(): got_forward = lax.ppermute(forward, 'row', forward_pairs)]
    ppermute x3 -> x6, waiting for transfers between devices: 12.8 us -> 4.07 us  [ring_all_gather(): backward = lax.ppermute(backward, 'row', backward_pairs)]
    ppermute x4 -> x8, starting transfers between devices: 6.21 us -> 12.7 us  [ring_all_gather(): forward = lax.ppermute(forward, 'row', forward_pairs)]
    ppermute x4 -> x8, waiting for transfers between devices: 10.7 us -> 6.05 us  [ring_all_gather(): forward = lax.ppermute(forward, 'row', forward_pairs)]
    ppermute x3 -> x6, waiting for transfers between devices: 2.53 us -> 6.01 us  [ring_reduce_scatter(): got_backward = lax.ppermute(backward, 'row', backward_pairs)]
    dot_general x5, matrix products: 21 us -> 17.5 us  [the longest x2 8.35 us: body(): jnp.dot(chosen, q_weight[:, h * q_cols:(h + 1) * q_cols], preferred_eleme...]
    convert_element_type x3 -> x6, other arithmetic: 2.46 us -> 0.37 us  [add_bf16(): return (a.astype(jnp.float32) + b.astype(jnp.float32)).astype(jnp.bfloat16)]
  transfers between devices with their start and end apart: 17 -> 30, of which waited for: 12 -> 20; matrix products, arithmetic and copies ran while one was open for 10% -> 6% of each run, Pallas kernels for 0% -> 0%
where the time goes in v6:
time: 95 us; the launch traced here: 94.7 us
  starting transfers between devices  33.5 us (35%)
  waiting for transfers between devices  26.9 us (28%)
  matrix products  24.6 us (26%)
  other arithmetic  6.56 us (7%)
  local copies, waits for them, and re-layouts  2.71 us (3%)
    ppermute x8, starting transfers between devices, ring_reduce_scatter(): got_forward = lax.ppermute(forward, 'row', forward_pairs)  16.6 us
    ppermute x8, starting transfers between devices, ring_all_gather(): forward = lax.ppermute(forward, 'row', forward_pairs)  12.7 us
    ppermute x8, waiting for transfers between devices, ring_reduce_scatter(): got_forward = lax.ppermute(forward, 'row', forward_pairs)  8.82 us
    dot_general x2, matrix products, body(): jnp.dot(chosen, q_weight[:, h * q_cols:(h + 1) * q_cols], preferred_eleme...  8.35 us
    dot_general x1, matrix products, body(): products = jnp.dot(arranged, o_weight, preferred_element_type=jnp.float32)  8.31 us
    ppermute x8, waiting for transfers between devices, ring_all_gather(): forward = lax.ppermute(forward, 'row', forward_pairs)  6.05 us
    ppermute x6, waiting for transfers between devices, ring_reduce_scatter(): got_backward = lax.ppermute(backward, 'row', backward_pairs)  6.01 us
    ppermute x6, waiting for transfers between devices, ring_all_gather(): backward = lax.ppermute(backward, 'row', backward_pairs)  4.07 us
  transfers between devices with their start and end apart: 30, of which 20 were waited for; matrix products, arithmetic and copies ran while one was open for 6% of the time, Pallas kernels for 0%

profile of v6, /device:TPU:0, one launch (start us, length us, event | category | flops | bytes accessed | tf_op | source)
XLA Modules:
  0.0 94.7 jit_solution(9343316380006700250)
XLA Ops:
  3.3 1.5 %fusion.41 = f32[256,2048]{1,0:T(8,128)S(1)} fusion(bf16[128,2048]{1,0:T(8,128)(2,1)} %param.11, s32[256]{0:T(256)S(1)} %broadcast_select_fusion.1), kind=kOutput, calls=%fused_computation.64 | convolution fusion | flops 134250496 | bytes 2622464 | tf_op jit(solution)/shard_map/dot_general | solution.py:178
  5.6 6.0 %fusion.14 = bf16[256,2048]{1,0:T(8,128)(2,1)S(1)} fusion(bf16[256,2048]{1,0:T(8,128)(2,1)S(1)} %fusion.10, bf16[2048,4096]{1,0:T(8,128)(2,1)} %param.12), kind=kOutput, calls=%fused_computation.16 | convolution fusion | flops 2148007936 | bytes 10485760 | tf_op jit(solution)/shard_map/dot_general | solution.py:188
  11.6 1.7 %copy-done.5 = bf16[2048,4096]{1,0:T(8,128)(2,1)S(1)} copy-done((bf16[2048,4096]{1,0:T(8,128)(2,1)S(1)}, bf16[2048,4096]{1,0:T(8,128)(2,1)}, u32[]{:S(2)}) %copy-start.5) | copy-done | bytes 16777240
  13.3 2.4 %fusion.11 = bf16[256,2048]{1,0:T(8,128)(2,1)S(1)} fusion(bf16[256,2048]{1,0:T(8,128)(2,1)S(1)} %fusion.10, bf16[2048,4096]{1,0:T(8,128)(2,1)S(1)} %copy-done.5), kind=kOutput, calls=%fused_computation.15 | convolution fusion | flops 2148007936 | bytes 10485760 | tf_op jit(solution)/shard_map/dot_general | solution.py:188
  16.8 2.7 %collective-permute-start.1 = (bf16[32,2304]{1,0:T(8,128)(2,1)S(1)}, bf16[32,2304]{1,0:T(8,128)(2,1)S(1)}, u32[]{:S(2)}, u32[]{:S(2)}) collective-permute-start(bf16[32,2304]{1,0:T(8,128)(2,1)S(1)} %get-tuple-element.18), channel_id=1, source_target_pairs={{0,4},{4,8},{8,12},{12,14},{14,10},{10,6},{6,2},{2,0},{1,5},{5,9},... | collective-permute-start | bytes 442376 | tf_op jit(solution)/shard_map/ppermute | solution.py:122
  19.6 2.1 %collective-permute-start.8 = (bf16[32,2304]{1,0:T(8,128)(2,1)S(1)}, bf16[32,2304]{1,0:T(8,128)(2,1)S(1)}, u32[]{:S(2)}, u32[]{:S(2)}) collective-permute-start(bf16[32,2304]{1,0:T(8,128)(2,1)S(1)} %get-tuple-element.24), channel_id=1, source_target_pairs={{0,4},{4,8},{8,12},{12,14},{14,10},{10,6},{6,2},{2,0},{1,5},{5,9},... | collective-permute-start | bytes 442376 | tf_op jit(solution)/shard_map/ppermute | solution.py:122
  21.7 2.4 %collective-permute-done.1 = bf16[32,2304]{1,0:T(8,128)(2,1)S(1)} collective-permute-done((bf16[32,2304]{1,0:T(8,128)(2,1)S(1)}, bf16[32,2304]{1,0:T(8,128)(2,1)S(1)}, u32[]{:S(2)}, u32[]{:S(2)}) %collective-permute-start.1) | collective-permute-done | bytes 147488 | tf_op jit(solution)/shard_map/ppermute | solution.py:122
  24.2 2.1 %collective-permute-start.2 = (bf16[32,2304]{1,0:T(8,128)(2,1)S(1)}, bf16[32,2304]{1,0:T(8,128)(2,1)S(1)}, u32[]{:S(2)}, u32[]{:S(2)}) collective-permute-start(bf16[32,2304]{1,0:T(8,128)(2,1)S(1)} %add_convert_fusion.10), channel_id=1, source_target_pairs={{0,4},{4,8},{8,12},{12,14},{14,10},{10,6},{6,2},{2,0},{1,5},{5,9},... | collective-permute-start | bytes 442376 | tf_op jit(solution)/shard_map/ppermute | solution.py:122
  27.3 2.1 %collective-permute-start.9 = (bf16[32,2304]{1,0:T(8,128)(2,1)S(1)}, bf16[32,2304]{1,0:T(8,128)(2,1)S(1)}, u32[]{:S(2)}, u32[]{:S(2)}) collective-permute-start(bf16[32,2304]{1,0:T(8,128)(2,1)S(1)} %add_convert_fusion.5), channel_id=1, source_target_pairs={{0,4},{4,8},{8,12},{12,14},{14,10},{10,6},{6,2},{2,0},{1,5},{5,9},... | collective-permute-start | bytes 442376 | tf_op jit(solution)/shard_map/ppermute | solution.py:122
  29.5 1.3 %collective-permute-done.2 = bf16[32,2304]{1,0:T(8,128)(2,1)S(1)} collective-permute-done((bf16[32,2304]{1,0:T(8,128)(2,1)S(1)}, bf16[32,2304]{1,0:T(8,128)(2,1)S(1)}, u32[]{:S(2)}, u32[]{:S(2)}) %collective-permute-start.2) | collective-permute-done | bytes 147488 | tf_op jit(solution)/shard_map/ppermute | solution.py:122
  30.9 2.1 %collective-permute-start.3 = (bf16[32,2304]{1,0:T(8,128)(2,1)S(1)}, bf16[32,2304]{1,0:T(8,128)(2,1)S(1)}, u32[]{:S(2)}, u32[]{:S(2)}) collective-permute-start(bf16[32,2304]{1,0:T(8,128)(2,1)S(1)} %get-tuple-element.16), channel_id=1, source_target_pairs={{0,4},{4,8},{8,12},{12,14},{14,10},{10,6},{6,2},{2,0},{1,5},{5,9},... | collective-permute-start | bytes 442376 | tf_op jit(solution)/shard_map/ppermute | solution.py:122
  34.2 2.1 %collective-permute-start.10 = (bf16[32,2304]{1,0:T(8,128)(2,1)S(1)}, bf16[32,2304]{1,0:T(8,128)(2,1)S(1)}, u32[]{:S(2)}, u32[]{:S(2)}) collective-permute-start(bf16[32,2304]{1,0:T(8,128)(2,1)S(1)} %get-tuple-element.22), channel_id=1, source_target_pairs={{0,4},{4,8},{8,12},{12,14},{14,10},{10,6},{6,2},{2,0},{1,5},{5,9},... | collective-permute-start | bytes 442376 | tf_op jit(solution)/shard_map/ppermute | solution.py:122
  37.6 2.1 %collective-permute-done.6 = bf16[32,2304]{1,0:T(8,128)(2,1)S(1)} collective-permute-done((bf16[32,2304]{1,0:T(8,128)(2,1)S(1)}, bf16[32,2304]{1,0:T(8,128)(2,1)S(1)}, u32[]{:S(2)}, u32[]{:S(2)}) %collective-permute-start.6) | collective-permute-done | bytes 147488 | tf_op jit(solution)/shard_map/ppermute | solution.py:124
  39.8 1.6 %collective-permute-start.4 = (bf16[32,2304]{1,0:T(8,128)(2,1)S(1)}, bf16[32,2304]{1,0:T(8,128)(2,1)S(1)}, u32[]{:S(2)}, u32[]{:S(2)}) collective-permute-start(bf16[32,2304]{1,0:T(8,128)(2,1)S(1)} %get-tuple-element.14), channel_id=1, source_target_pairs={{0,4},{4,8},{8,12},{12,14},{14,10},{10,6},{6,2},{2,0},{1,5},{5,9},... | collective-permute-start | bytes 442376 | tf_op jit(solution)/shard_map/ppermute | solution.py:122
  43.0 1.6 %collective-permute-start.11 = (bf16[32,2304]{1,0:T(8,128)(2,1)S(1)}, bf16[32,2304]{1,0:T(8,128)(2,1)S(1)}, u32[]{:S(2)}, u32[]{:S(2)}) collective-permute-start(bf16[32,2304]{1,0:T(8,128)(2,1)S(1)} %get-tuple-element.20), channel_id=1, source_target_pairs={{0,4},{4,8},{8,12},{12,14},{14,10},{10,6},{6,2},{2,0},{1,5},{5,9},... | collective-permute-start | bytes 442376 | tf_op jit(solution)/shard_map/ppermute | solution.py:122
  45.7 1.3 %collective-permute-done.7 = bf16[32,2304]{1,0:T(8,128)(2,1)S(1)} collective-permute-done((bf16[32,2304]{1,0:T(8,128)(2,1)S(1)}, bf16[32,2304]{1,0:T(8,128)(2,1)S(1)}, u32[]{:S(2)}, u32[]{:S(2)}) %collective-permute-start.7) | collective-permute-done | bytes 147488 | tf_op jit(solution)/shard_map/ppermute | solution.py:124
  48.2 1.6 %collective-permute-done.14 = bf16[32,2304]{1,0:T(8,128)(2,1)S(1)} collective-permute-done((bf16[32,2304]{1,0:T(8,128)(2,1)S(1)}, bf16[32,2304]{1,0:T(8,128)(2,1)S(1)}, u32[]{:S(2)}, u32[]{:S(2)}) %collective-permute-start.14) | collective-permute-done | bytes 147488 | tf_op jit(solution)/shard_map/ppermute | solution.py:124
  52.7 1.4 %fusion.5 = f32[2,2,16,16]{2,3,1,0:T(8,128)S(1)} fusion(f32[2,2,16,16,1536]{4,3,2,1,0:T(8,128)S(1)} %get-tuple-element.43, f32[2,2,16,16]{2,3,1,0:T(8,128)S(1)} %max.7, pred[2,1536]{1,0:T(4,128)(4,1)S(1)} %iota_compare_fusion.7), kind=kLoop, calls=%fused_computation.9 | loop fusion | flops 6290432 | bytes 6302720 | tf_op jit(solution)/shard_map/vmap()/reduce_sum | solution.py:44
  54.1 1.9 %fusion.23 = f32[2,16,2,16,128]{4,3,1,2,0:T(8,128)S(1)} fusion(bf16[2,1536,2,128,1]{3,2,1,0,4:T(2,128)(2,1)S(1)} %bitcast.64, f32[2,2,16,16,1536]{4,3,2,1,0:T(8,128)S(1)} %get-tuple-element.43, f32[2,2,16,16]{2,3,1,0:T(8,128)S(1)} %max.7, pred[2,1536]{1,0:T(4,128)(4,1)S(1)} %iota_compare_fusion.7), kind=kOutput, calls=%fused_computation.23 | convolution fusion | flops 408944640 | bytes 8395776 | tf_op jit(solution)/shard_map/vmap(kgnc,ckd->nkgd)/dot_general | solution.py:45
  57.1 1.6 %collective-permute-start.15 = (bf16[32,2048]{1,0:T(8,128)(2,1)S(1)}, bf16[32,2048]{1,0:T(8,128)(2,1)S(1)}, u32[]{:S(2)}, u32[]{:S(2)}) collective-permute-start(bf16[32,2048]{1,0:T(8,128)(2,1)S(1)} %get-tuple-element.28), channel_id=1, source_target_pairs={{0,4},{4,8},{8,12},{12,14},{14,10},{10,6},{6,2},{2,0},{1,5},{5,9},... | collective-permute-start | bytes 393224 | tf_op jit(solution)/shard_map/ppermute | solution.py:138
  59.1 1.6 %collective-permute-start.22 = (bf16[32,2048]{1,0:T(8,128)(2,1)S(1)}, bf16[32,2048]{1,0:T(8,128)(2,1)S(1)}, u32[]{:S(2)}, u32[]{:S(2)}) collective-permute-start(bf16[32,2048]{1,0:T(8,128)(2,1)S(1)} %get-tuple-element.31), channel_id=1, source_target_pairs={{0,4},{4,8},{8,12},{12,14},{14,10},{10,6},{6,2},{2,0},{1,5},{5,9},... | collective-permute-start | bytes 393224 | tf_op jit(solution)/shard_map/ppermute | solution.py:138
  61.0 2.0 %collective-permute-done.16 = bf16[32,2048]{1,0:T(8,128)(2,1)S(1)} collective-permute-done((bf16[32,2048]{1,0:T(8,128)(2,1)S(1)}, bf16[32,2048]{1,0:T(8,128)(2,1)S(1)}, u32[]{:S(2)}, u32[]{:S(2)}) %collective-permute-start.16) | collective-permute-done | bytes 131104 | tf_op jit(solution)/shard_map/ppermute | solution.py:141
  63.5 1.6 %collective-permute-start.17 = (bf16[32,2048]{1,0:T(8,128)(2,1)S(1)}, bf16[32,2048]{1,0:T(8,128)(2,1)S(1)}, u32[]{:S(2)}, u32[]{:S(2)}) collective-permute-start(bf16[32,2048]{1,0:T(8,128)(2,1)S(1)} %collective-permute-done.15), channel_id=1, source_target_pairs={{0,4},{4,8},{8,12},{12,14},{14,10},{10,6},{6,2},{2,0},{1,5},{5,9},... | collective-permute-start | bytes 393224 | tf_op jit(solution)/shard_map/ppermute | solution.py:138
  66.3 1.6 %collective-permute-start.24 = (bf16[32,2048]{1,0:T(8,128)(2,1)S(1)}, bf16[32,2048]{1,0:T(8,128)(2,1)S(1)}, u32[]{:S(2)}, u32[]{:S(2)}) collective-permute-start(bf16[32,2048]{1,0:T(8,128)(2,1)S(1)} %collective-permute-done.22), channel_id=1, source_target_pairs={{0,4},{4,8},{8,12},{12,14},{14,10},{10,6},{6,2},{2,0},{1,5},{5,9},... | collective-permute-start | bytes 393224 | tf_op jit(solution)/shard_map/ppermute | solution.py:138
  68.0 1.3 %collective-permute-done.18 = bf16[32,2048]{1,0:T(8,128)(2,1)S(1)} collective-permute-done((bf16[32,2048]{1,0:T(8,128)(2,1)S(1)}, bf16[32,2048]{1,0:T(8,128)(2,1)S(1)}, u32[]{:S(2)}, u32[]{:S(2)}) %collective-permute-start.18) | collective-permute-done | bytes 131104 | tf_op jit(solution)/shard_map/ppermute | solution.py:141
  69.7 1.7 %collective-permute-start.19 = (bf16[32,2048]{1,0:T(8,128)(2,1)S(1)}, bf16[32,2048]{1,0:T(8,128)(2,1)S(1)}, u32[]{:S(2)}, u32[]{:S(2)}) collective-permute-start(bf16[32,2048]{1,0:T(8,128)(2,1)S(1)} %collective-permute-done.17), channel_id=1, source_target_pairs={{0,4},{4,8},{8,12},{12,14},{14,10},{10,6},{6,2},{2,0},{1,5},{5,9},... | collective-permute-start | bytes 393224 | tf_op jit(solution)/shard_map/ppermute | solution.py:138
  72.7 1.6 %collective-permute-start.26 = (bf16[32,2048]{1,0:T(8,128)(2,1)S(1)}, bf16[32,2048]{1,0:T(8,128)(2,1)S(1)}, u32[]{:S(2)}, u32[]{:S(2)}) collective-permute-start(bf16[32,2048]{1,0:T(8,128)(2,1)S(1)} %collective-permute-done.24), channel_id=1, source_target_pairs={{0,4},{4,8},{8,12},{12,14},{14,10},{10,6},{6,2},{2,0},{1,5},{5,9},... | collective-permute-start | bytes 393224 | tf_op jit(solution)/shard_map/ppermute | solution.py:138
  75.5 1.5 %collective-permute-start.21 = (bf16[32,2048]{1,0:T(8,128)(2,1)S(1)}, bf16[32,2048]{1,0:T(8,128)(2,1)S(1)}, u32[]{:S(2)}, u32[]{:S(2)}) collective-permute-start(bf16[32,2048]{1,0:T(8,128)(2,1)S(1)} %collective-permute-done.19), channel_id=1, source_target_pairs={{0,4},{4,8},{8,12},{12,14},{14,10},{10,6},{6,2},{2,0},{1,5},{5,9},... | collective-permute-start | bytes 393224 | tf_op jit(solution)/shard_map/ppermute | solution.py:138
  77.7 1.6 %collective-permute-start.28 = (bf16[32,2048]{1,0:T(8,128)(2,1)S(1)}, bf16[32,2048]{1,0:T(8,128)(2,1)S(1)}, u32[]{:S(2)}, u32[]{:S(2)}) collective-permute-start(bf16[32,2048]{1,0:T(8,128)(2,1)S(1)} %collective-permute-done.26), channel_id=1, source_target_pairs={{0,4},{4,8},{8,12},{12,14},{14,10},{10,6},{6,2},{2,0},{1,5},{5,9},... | collective-permute-start | bytes 393224 | tf_op jit(solution)/shard_map/ppermute | solution.py:138
  80.5 2.2 %collective-permute-done.28 = bf16[32,2048]{1,0:T(8,128)(2,1)S(1)} collective-permute-done((bf16[32,2048]{1,0:T(8,128)(2,1)S(1)}, bf16[32,2048]{1,0:T(8,128)(2,1)S(1)}, u32[]{:S(2)}, u32[]{:S(2)}) %collective-permute-start.28) | collective-permute-done | bytes 131104 | tf_op jit(solution)/shard_map/ppermute | solution.py:138
  83.5 8.3 %fusion.63 = f32[256,2048]{1,0:T(8,128)S(1)} fusion(bf16[256,4096]{1,0:T(8,128)(2,1)S(1)} %convolution_convert_fusion, bf16[4096,2048]{1,0:T(8,128)(2,1)} %param.15), kind=kOutput, calls=%fused_computation.146 | convolution fusion | flops 4294967296 | bytes 20971520 | tf_op jit(solution)/shard_map/dot_general | solution.py:239
  91.9 1.9 %collective-permute-done.29 = bf16[128,2048]{1,0:T(8,128)(2,1)S(1)} collective-permute-done((bf16[128,2048]{1,0:T(8,128)(2,1)S(1)}, bf16[128,2048]{1,0:T(8,128)(2,1)S(1)}, u32[]{:S(2)}, u32[]{:S(2)}) %collective-permute-start.29) | collective-permute-done | bytes 524320 | tf_op jit(solution)/shard_map/ppermute | solution.py:240
  (128 shorter events, 25.6 us)
Async XLA Ops:
  0.0 50.4 %copy-start = (bf16[2,1536,2,128]{3,2,1,0:T(2,128)(2,1)S(1)}, bf16[2,1536,2,128]{3,2,1,0:T(2,128)(2,1)}, u32[]{:S(2)}) copy-start(bf16[2,1536,2,128]{3,2,1,0:T(2,128)(2,1)} %param.16) | copy-start | bytes 4718596
  0.0 5.1 %collective-permute-start = (bf16[128,2048]{1,0:T(8,128)(2,1)}, bf16[128,2048]{1,0:T(8,128)(2,1)S(1)}, u32[]{:S(2)}, u32[]{:S(2)}) collective-permute-start(bf16[128,2048]{1,0:T(8,128)(2,1)} %param.11), channel_id=1, source_target_pairs={{0,1},{1,0},{2,3},{3,2},{4,5},{5,4},{6,7},{7,6},{8,9},{9,8},{10,11... | collective-permute-start | bytes 1572872 | tf_op jit(solution)/shard_map/ppermute | solution.py:166
  16.8 7.4 %collective-permute-start.1 = (bf16[32,2304]{1,0:T(8,128)(2,1)S(1)}, bf16[32,2304]{1,0:T(8,128)(2,1)S(1)}, u32[]{:S(2)}, u32[]{:S(2)}) collective-permute-start(bf16[32,2304]{1,0:T(8,128)(2,1)S(1)} %get-tuple-element.18), channel_id=1, source_target_pairs={{0,4},{4,8},{8,12},{12,14},{14,10},{10,6},{6,2},{2,0},{1,5},{5,9},... | collective-permute-start | bytes 442376 | tf_op jit(solution)/shard_map/ppermute | solution.py:122
  19.5 10.0 %collective-permute-start.5 = (bf16[32,2304]{1,0:T(8,128)(2,1)S(1)}, bf16[32,2304]{1,0:T(8,128)(2,1)S(1)}, u32[]{:S(2)}, u32[]{:S(2)}) collective-permute-start(bf16[32,2304]{1,0:T(8,128)(2,1)S(1)} %get-tuple-element.19), channel_id=1, source_target_pairs={{0,2},{4,0},{8,4},{12,8},{14,12},{10,14},{6,10},{2,6},{1,3},{5,1},... | collective-permute-start | bytes 442376 | tf_op jit(solution)/shard_map/ppermute | solution.py:124
  19.6 7.7 %collective-permute-start.8 = (bf16[32,2304]{1,0:T(8,128)(2,1)S(1)}, bf16[32,2304]{1,0:T(8,128)(2,1)S(1)}, u32[]{:S(2)}, u32[]{:S(2)}) collective-permute-start(bf16[32,2304]{1,0:T(8,128)(2,1)S(1)} %get-tuple-element.24), channel_id=1, source_target_pairs={{0,4},{4,8},{8,12},{12,14},{14,10},{10,6},{6,2},{2,0},{1,5},{5,9},... | collective-permute-start | bytes 442376 | tf_op jit(solution)/shard_map/ppermute | solution.py:122
  21.7 11.3 %collective-permute-start.12 = (bf16[32,2304]{1,0:T(8,128)(2,1)S(1)}, bf16[32,2304]{1,0:T(8,128)(2,1)S(1)}, u32[]{:S(2)}, u32[]{:S(2)}) collective-permute-start(bf16[32,2304]{1,0:T(8,128)(2,1)S(1)} %get-tuple-element.25), channel_id=1, source_target_pairs={{0,2},{4,0},{8,4},{12,8},{14,12},{10,14},{6,10},{2,6},{1,3},{5,1},... | collective-permute-start | bytes 442376 | tf_op jit(solution)/shard_map/ppermute | solution.py:124
  24.2 6.6 %collective-permute-start.2 = (bf16[32,2304]{1,0:T(8,128)(2,1)S(1)}, bf16[32,2304]{1,0:T(8,128)(2,1)S(1)}, u32[]{:S(2)}, u32[]{:S(2)}) collective-permute-start(bf16[32,2304]{1,0:T(8,128)(2,1)S(1)} %add_convert_fusion.10), channel_id=1, source_target_pairs={{0,4},{4,8},{8,12},{12,14},{14,10},{10,6},{6,2},{2,0},{1,5},{5,9},... | collective-permute-start | bytes 442376 | tf_op jit(solution)/shard_map/ppermute | solution.py:122
  27.3 6.8 %collective-permute-start.9 = (bf16[32,2304]{1,0:T(8,128)(2,1)S(1)}, bf16[32,2304]{1,0:T(8,128)(2,1)S(1)}, u32[]{:S(2)}, u32[]{:S(2)}) collective-permute-start(bf16[32,2304]{1,0:T(8,128)(2,1)S(1)} %add_convert_fusion.5), channel_id=1, source_target_pairs={{0,4},{4,8},{8,12},{12,14},{14,10},{10,6},{6,2},{2,0},{1,5},{5,9},... | collective-permute-start | bytes 442376 | tf_op jit(solution)/shard_map/ppermute | solution.py:122
  30.9 6.7 %collective-permute-start.3 = (bf16[32,2304]{1,0:T(8,128)(2,1)S(1)}, bf16[32,2304]{1,0:T(8,128)(2,1)S(1)}, u32[]{:S(2)}, u32[]{:S(2)}) collective-permute-start(bf16[32,2304]{1,0:T(8,128)(2,1)S(1)} %get-tuple-element.16), channel_id=1, source_target_pairs={{0,4},{4,8},{8,12},{12,14},{14,10},{10,6},{6,2},{2,0},{1,5},{5,9},... | collective-permute-start | bytes 442376 | tf_op jit(solution)/shard_map/ppermute | solution.py:122
  33.0 6.7 %collective-permute-start.6 = (bf16[32,2304]{1,0:T(8,128)(2,1)S(1)}, bf16[32,2304]{1,0:T(8,128)(2,1)S(1)}, u32[]{:S(2)}, u32[]{:S(2)}) collective-permute-start(bf16[32,2304]{1,0:T(8,128)(2,1)S(1)} %get-tuple-element.17), channel_id=1, source_target_pairs={{0,2},{4,0},{8,4},{12,8},{14,12},{10,14},{6,10},{2,6},{1,3},{5,1},... | collective-permute-start | bytes 442376 | tf_op jit(solution)/shard_map/ppermute | solution.py:124
  34.2 7.7 %collective-permute-start.10 = (bf16[32,2304]{1,0:T(8,128)(2,1)S(1)}, bf16[32,2304]{1,0:T(8,128)(2,1)S(1)}, u32[]{:S(2)}, u32[]{:S(2)}) collective-permute-start(bf16[32,2304]{1,0:T(8,128)(2,1)S(1)} %get-tuple-element.22), channel_id=1, source_target_pairs={{0,4},{4,8},{8,12},{12,14},{14,10},{10,6},{6,2},{2,0},{1,5},{5,9},... | collective-permute-start | bytes 442376 | tf_op jit(solution)/shard_map/ppermute | solution.py:122
  36.3 6.6 %collective-permute-start.13 = (bf16[32,2304]{1,0:T(8,128)(2,1)S(1)}, bf16[32,2304]{1,0:T(8,128)(2,1)S(1)}, u32[]{:S(2)}, u32[]{:S(2)}) collective-permute-start(bf16[32,2304]{1,0:T(8,128)(2,1)S(1)} %get-tuple-element.23), channel_id=1, source_target_pairs={{0,2},{4,0},{8,4},{12,8},{14,12},{10,14},{6,10},{2,6},{1,3},{5,1},... | collective-permute-start | bytes 442376 | tf_op jit(solution)/shard_map/ppermute | solution.py:124
  39.8 5.9 %collective-permute-start.4 = (bf16[32,2304]{1,0:T(8,128)(2,1)S(1)}, bf16[32,2304]{1,0:T(8,128)(2,1)S(1)}, u32[]{:S(2)}, u32[]{:S(2)}) collective-permute-start(bf16[32,2304]{1,0:T(8,128)(2,1)S(1)} %get-tuple-element.14), channel_id=1, source_target_pairs={{0,4},{4,8},{8,12},{12,14},{14,10},{10,6},{6,2},{2,0},{1,5},{5,9},... | collective-permute-start | bytes 442376 | tf_op jit(solution)/shard_map/ppermute | solution.py:122
  41.5 5.6 %collective-permute-start.7 = (bf16[32,2304]{1,0:T(8,128)(2,1)S(1)}, bf16[32,2304]{1,0:T(8,128)(2,1)S(1)}, u32[]{:S(2)}, u32[]{:S(2)}) collective-permute-start(bf16[32,2304]{1,0:T(8,128)(2,1)S(1)} %get-tuple-element.15), channel_id=1, source_target_pairs={{0,2},{4,0},{8,4},{12,8},{14,12},{10,14},{6,10},{2,6},{1,3},{5,1},... | collective-permute-start | bytes 442376 | tf_op jit(solution)/shard_map/ppermute | solution.py:124
  43.0 5.2 %collective-permute-start.11 = (bf16[32,2304]{1,0:T(8,128)(2,1)S(1)}, bf16[32,2304]{1,0:T(8,128)(2,1)S(1)}, u32[]{:S(2)}, u32[]{:S(2)}) collective-permute-start(bf16[32,2304]{1,0:T(8,128)(2,1)S(1)} %get-tuple-element.20), channel_id=1, source_target_pairs={{0,4},{4,8},{8,12},{12,14},{14,10},{10,6},{6,2},{2,0},{1,5},{5,9},... | collective-permute-start | bytes 442376 | tf_op jit(solution)/shard_map/ppermute | solution.py:122
  44.6 5.1 %collective-permute-start.14 = (bf16[32,2304]{1,0:T(8,128)(2,1)S(1)}, bf16[32,2304]{1,0:T(8,128)(2,1)S(1)}, u32[]{:S(2)}, u32[]{:S(2)}) collective-permute-start(bf16[32,2304]{1,0:T(8,128)(2,1)S(1)} %get-tuple-element.21), channel_id=1, source_target_pairs={{0,2},{4,0},{8,4},{12,8},{14,12},{10,14},{6,10},{2,6},{1,3},{5,1},... | collective-permute-start | bytes 442376 | tf_op jit(solution)/shard_map/ppermute | solution.py:124
  56.6 6.4 %collective-permute-start.16 = (bf16[32,2048]{1,0:T(8,128)(2,1)S(1)}, bf16[32,2048]{1,0:T(8,128)(2,1)S(1)}, u32[]{:S(2)}, u32[]{:S(2)}) collective-permute-start(bf16[32,2048]{1,0:T(8,128)(2,1)S(1)} %get-tuple-element.28), channel_id=1, source_target_pairs={{0,2},{4,0},{8,4},{12,8},{14,12},{10,14},{6,10},{2,6},{1,3},{5,1},... | collective-permute-start | bytes 393224 | tf_op jit(solution)/shard_map/ppermute | solution.py:141
  57.1 6.4 %collective-permute-start.15 = (bf16[32,2048]{1,0:T(8,128)(2,1)S(1)}, bf16[32,2048]{1,0:T(8,128)(2,1)S(1)}, u32[]{:S(2)}, u32[]{:S(2)}) collective-permute-start(bf16[32,2048]{1,0:T(8,128)(2,1)S(1)} %get-tuple-element.28), channel_id=1, source_target_pairs={{0,4},{4,8},{8,12},{12,14},{14,10},{10,6},{6,2},{2,0},{1,5},{5,9},... | collective-permute-start | bytes 393224 | tf_op jit(solution)/shard_map/ppermute | solution.py:138
  58.7 7.2 %collective-permute-start.23 = (bf16[32,2048]{1,0:T(8,128)(2,1)S(1)}, bf16[32,2048]{1,0:T(8,128)(2,1)S(1)}, u32[]{:S(2)}, u32[]{:S(2)}) collective-permute-start(bf16[32,2048]{1,0:T(8,128)(2,1)S(1)} %get-tuple-element.31), channel_id=1, source_target_pairs={{0,2},{4,0},{8,4},{12,8},{14,12},{10,14},{6,10},{2,6},{1,3},{5,1},... | collective-permute-start | bytes 393224 | tf_op jit(solution)/shard_map/ppermute | solution.py:141
  59.1 7.2 %collective-permute-start.22 = (bf16[32,2048]{1,0:T(8,128)(2,1)S(1)}, bf16[32,2048]{1,0:T(8,128)(2,1)S(1)}, u32[]{:S(2)}, u32[]{:S(2)}) collective-permute-start(bf16[32,2048]{1,0:T(8,128)(2,1)S(1)} %get-tuple-element.31), channel_id=1, source_target_pairs={{0,4},{4,8},{8,12},{12,14},{14,10},{10,6},{6,2},{2,0},{1,5},{5,9},... | collective-permute-start | bytes 393224 | tf_op jit(solution)/shard_map/ppermute | solution.py:138
  63.0 6.2 %collective-permute-start.18 = (bf16[32,2048]{1,0:T(8,128)(2,1)S(1)}, bf16[32,2048]{1,0:T(8,128)(2,1)S(1)}, u32[]{:S(2)}, u32[]{:S(2)}) collective-permute-start(bf16[32,2048]{1,0:T(8,128)(2,1)S(1)} %collective-permute-done.16), channel_id=1, source_target_pairs={{0,2},{4,0},{8,4},{12,8},{14,12},{10,14},{6,10},{2,6},{1,3},{5,1},... | collective-permute-start | bytes 393224 | tf_op jit(solution)/shard_map/ppermute | solution.py:141
  63.5 6.3 %collective-permute-start.17 = (bf16[32,2048]{1,0:T(8,128)(2,1)S(1)}, bf16[32,2048]{1,0:T(8,128)(2,1)S(1)}, u32[]{:S(2)}, u32[]{:S(2)}) collective-permute-start(bf16[32,2048]{1,0:T(8,128)(2,1)S(1)} %collective-permute-done.15), channel_id=1, source_target_pairs={{0,4},{4,8},{8,12},{12,14},{14,10},{10,6},{6,2},{2,0},{1,5},{5,9},... | collective-permute-start | bytes 393224 | tf_op jit(solution)/shard_map/ppermute | solution.py:138
  65.8 5.6 %collective-permute-start.25 = (bf16[32,2048]{1,0:T(8,128)(2,1)S(1)}, bf16[32,2048]{1,0:T(8,128)(2,1)S(1)}, u32[]{:S(2)}, u32[]{:S(2)}) collective-permute-start(bf16[32,2048]{1,0:T(8,128)(2,1)S(1)} %collective-permute-done.23), channel_id=1, source_target_pairs={{0,2},{4,0},{8,4},{12,8},{14,12},{10,14},{6,10},{2,6},{1,3},{5,1},... | collective-permute-start | bytes 393224 | tf_op jit(solution)/shard_map/ppermute | solution.py:141
  66.3 6.4 %collective-permute-start.24 = (bf16[32,2048]{1,0:T(8,128)(2,1)S(1)}, bf16[32,2048]{1,0:T(8,128)(2,1)S(1)}, u32[]{:S(2)}, u32[]{:S(2)}) collective-permute-start(bf16[32,2048]{1,0:T(8,128)(2,1)S(1)} %collective-permute-done.22), channel_id=1, source_target_pairs={{0,4},{4,8},{8,12},{12,14},{14,10},{10,6},{6,2},{2,0},{1,5},{5,9},... | collective-permute-start | bytes 393224 | tf_op jit(solution)/shard_map/ppermute | solution.py:138
  69.3 10.0 %collective-permute-start.20 = (bf16[32,2048]{1,0:T(8,128)(2,1)S(1)}, bf16[32,2048]{1,0:T(8,128)(2,1)S(1)}, u32[]{:S(2)}, u32[]{:S(2)}) collective-permute-start(bf16[32,2048]{1,0:T(8,128)(2,1)S(1)} %collective-permute-done.18), channel_id=1, source_target_pairs={{0,2},{4,0},{8,4},{12,8},{14,12},{10,14},{6,10},{2,6},{1,3},{5,1},... | collective-permute-start | bytes 393224 | tf_op jit(solution)/shard_map/ppermute | solution.py:141
  69.7 5.7 %collective-permute-start.19 = (bf16[32,2048]{1,0:T(8,128)(2,1)S(1)}, bf16[32,2048]{1,0:T(8,128)(2,1)S(1)}, u32[]{:S(2)}, u32[]{:S(2)}) collective-permute-start(bf16[32,2048]{1,0:T(8,128)(2,1)S(1)} %collective-permute-done.17), channel_id=1, source_target_pairs={{0,4},{4,8},{8,12},{12,14},{14,10},{10,6},{6,2},{2,0},{1,5},{5,9},... | collective-permute-start | bytes 393224 | tf_op jit(solution)/shard_map/ppermute | solution.py:138
  71.4 7.9 %collective-permute-start.27 = (bf16[32,2048]{1,0:T(8,128)(2,1)S(1)}, bf16[32,2048]{1,0:T(8,128)(2,1)S(1)}, u32[]{:S(2)}, u32[]{:S(2)}) collective-permute-start(bf16[32,2048]{1,0:T(8,128)(2,1)S(1)} %collective-permute-done.25), channel_id=1, source_target_pairs={{0,2},{4,0},{8,4},{12,8},{14,12},{10,14},{6,10},{2,6},{1,3},{5,1},... | collective-permute-start | bytes 393224 | tf_op jit(solution)/shard_map/ppermute | solution.py:141
  72.7 5.0 %collective-permute-start.26 = (bf16[32,2048]{1,0:T(8,128)(2,1)S(1)}, bf16[32,2048]{1,0:T(8,128)(2,1)S(1)}, u32[]{:S(2)}, u32[]{:S(2)}) collective-permute-start(bf16[32,2048]{1,0:T(8,128)(2,1)S(1)} %collective-permute-done.24), channel_id=1, source_target_pairs={{0,4},{4,8},{8,12},{12,14},{14,10},{10,6},{6,2},{2,0},{1,5},{5,9},... | collective-permute-start | bytes 393224 | tf_op jit(solution)/shard_map/ppermute | solution.py:138
  75.5 5.0 %collective-permute-start.21 = (bf16[32,2048]{1,0:T(8,128)(2,1)S(1)}, bf16[32,2048]{1,0:T(8,128)(2,1)S(1)}, u32[]{:S(2)}, u32[]{:S(2)}) collective-permute-start(bf16[32,2048]{1,0:T(8,128)(2,1)S(1)} %collective-permute-done.19), channel_id=1, source_target_pairs={{0,4},{4,8},{8,12},{12,14},{14,10},{10,6},{6,2},{2,0},{1,5},{5,9},... | collective-permute-start | bytes 393224 | tf_op jit(solution)/shard_map/ppermute | solution.py:138
  77.7 5.0 %collective-permute-start.28 = (bf16[32,2048]{1,0:T(8,128)(2,1)S(1)}, bf16[32,2048]{1,0:T(8,128)(2,1)S(1)}, u32[]{:S(2)}, u32[]{:S(2)}) collective-permute-start(bf16[32,2048]{1,0:T(8,128)(2,1)S(1)} %collective-permute-done.26), channel_id=1, source_target_pairs={{0,4},{4,8},{8,12},{12,14},{14,10},{10,6},{6,2},{2,0},{1,5},{5,9},... | collective-permute-start | bytes 393224 | tf_op jit(solution)/shard_map/ppermute | solution.py:138
  83.4 11.3 %copy-start.1 = (bf16[2,1536,2,128]{3,2,1,0:T(2,128)(2,1)S(1)}, bf16[2,1536,2,128]{3,2,1,0:T(2,128)(2,1)}, u32[]{:S(2)}) copy-start(bf16[2,1536,2,128]{3,2,1,0:T(2,128)(2,1)} %param.16) | copy-start | bytes 4718596
  91.8 2.0 %collective-permute-start.29 = (bf16[128,2048]{1,0:T(8,128)(2,1)S(1)}, bf16[128,2048]{1,0:T(8,128)(2,1)S(1)}, u32[]{:S(2)}, u32[]{:S(2)}) collective-permute-start(bf16[128,2048]{1,0:T(8,128)(2,1)S(1)} %slice.217), channel_id=1, source_target_pairs={{0,1},{1,0},{2,3},{3,2},{4,5},{5,4},{6,7},{7,6},{8,9},{9,8},{10,11... | collective-permute-start | bytes 1572872 | tf_op jit(solution)/shard_map/ppermute | solution.py:240
  (6 other events, 24.2 us)

commit v7 on v6

--- a/solution.py
+++ b/solution.py
@@ -89,11 +89,19 @@
     backward_hops = n_row - 1 - forward_hops
     forward_pairs = [(ring[i], ring[(i + 1) % n_row]) for i in range(n_row)]
     backward_pairs = [(ring[i], ring[(i - 1) % n_row]) for i in range(n_row)]
+    balanced = n_row % 2 == 0
+    if balanced:
+        forward_hops = backward_hops = n_row // 2
     gather_offsets = [0]
-    for s in range(forward_hops):
-        gather_offsets.append(-(s + 1) % n_row)
-        if s < backward_hops:
+    full_forward = forward_hops - 1 if balanced else forward_hops
+    full_backward = backward_hops - 1 if balanced else backward_hops
+    for s in range(max(full_forward, full_backward)):
+        if s < full_forward:
+            gather_offsets.append(-(s + 1) % n_row)
+        if s < full_backward:
             gather_offsets.append((s + 1) % n_row)
+    if balanced and n_row > 1:
+        gather_offsets.append(n_row // 2)
     stacked_of_offset = [gather_offsets.index(d) for d in range(n_row)]
 
     def tables(seq_dev, new_len):
@@ -115,31 +123,57 @@
     def ring_reduce_scatter(blocks):
         if n_row == 1:
             return blocks[0].astype(jnp.float32)
-        forward = blocks[forward_hops % n_row]
-        backward = blocks[(n_row - backward_hops) % n_row] if backward_hops else None
+        width = blocks[0].shape[1]
+        split = width // 2
+        if balanced:
+            forward = blocks[forward_hops][:, :split]
+            backward = blocks[forward_hops][:, split:]
+        else:
+            forward = blocks[forward_hops % n_row]
+            backward = blocks[(n_row - backward_hops) % n_row] if backward_hops else None
         got_forward = got_backward = None
-        for s in range(forward_hops):
-            got_forward = lax.ppermute(forward, "row", forward_pairs)
+        for s in range(max(forward_hops, backward_hops)):
+            if s < forward_hops:
+                got_forward = lax.ppermute(forward, "row", forward_pairs)
             if s < backward_hops:
                 got_backward = lax.ppermute(backward, "row", backward_pairs)
             if s < forward_hops - 1:
-                forward = add_bf16(got_forward, blocks[(forward_hops - s - 1) % n_row])
+                own = blocks[(forward_hops - s - 1) % n_row]
+                if balanced and s == 0:
+                    forward = jnp.concatenate([add_bf16(got_forward, own[:, :split]), own[:, split:]], axis=1)
+                else:
+                    forward = add_bf16(got_forward, own)
             if s < backward_hops - 1:
-                backward = add_bf16(got_backward, blocks[(s + 1 - backward_hops) % n_row])
-        total = got_forward.astype(jnp.float32) + blocks[0].astype(jnp.float32)
+                own = blocks[(s + 1 - backward_hops) % n_row]
+                if balanced and s == 0:
+                    backward = jnp.concatenate([own[:, :split], add_bf16(got_backward, own[:, split:])], axis=1)
+                else:
+                    backward = add_bf16(got_backward, own)
+        total = blocks[0].astype(jnp.float32)
+        if balanced and forward_hops == 1:
+            return total + jnp.concatenate([got_forward, got_backward], axis=1).astype(jnp.float32)
+        total = total + got_forward.astype(jnp.float32)
         if got_backward is not None:
             total = total + got_backward.astype(jnp.float32)
         return total
 
     def ring_all_gather(own):
+        if n_row == 1:
+            return own
+        split = own.shape[1] // 2
         got = [own]
         forward = backward = own
-        for s in range(forward_hops):
-            forward = lax.ppermute(forward, "row", forward_pairs)
-            got.append(forward)
-            if s < backward_hops:
+        for s in range(max(full_forward, full_backward)):
+            if s < full_forward:
+                forward = lax.ppermute(forward, "row", forward_pairs)
+                got.append(forward)
+            if s < full_backward:
                 backward = lax.ppermute(backward, "row", backward_pairs)
                 got.append(backward)
+        if balanced:
+            first = lax.ppermute(forward[:, :split], "row", forward_pairs)
+            second = lax.ppermute(backward[:, split:], "row", backward_pairs)
+            got.append(jnp.concatenate([first, second], axis=1))
         return jnp.concatenate(got, axis=0)
 
     def lookup(table, index):

time: 95 us -> 99.2 us (1.044)
  starting transfers between devices: 33.5 us -> 37.9 us
  matrix products: 24.6 us -> 27.9 us
  waiting for transfers between devices: 26.9 us -> 24.5 us
    ppermute x8 -> x6, starting transfers between devices: 12.7 us -> 3.14 us  [ring_all_gather(): forward = lax.ppermute(forward, 'row', forward_pairs)]
    ppermute x6 -> x8, starting transfers between devices: 0.93 us -> 9.54 us  [ring_reduce_scatter(): got_backward = lax.ppermute(backward, 'row', backward_pairs)]
    ppermute x6, starting transfers between devices: 2.7 us -> 8.99 us  [ring_all_gather(): backward = lax.ppermute(backward, 'row', backward_pairs)]
    ppermute x8, starting transfers between devices: 16.6 us -> 11.7 us  [ring_reduce_scatter(): got_forward = lax.ppermute(forward, 'row', forward_pairs)]
    ppermute x0 -> x4, starting transfers between devices: none -> 3.96 us  [the longest x2 3.2 us: ring_all_gather(): second = lax.ppermute(backward[:, split:], 'row', backward_pairs)]
    ppermute x6, waiting for transfers between devices: 4.07 us -> 0.54 us  [ring_all_gather(): backward = lax.ppermute(backward, 'row', backward_pairs)]
    ppermute x8, waiting for transfers between devices: 8.82 us -> 6.08 us  [ring_reduce_scatter(): got_forward = lax.ppermute(forward, 'row', forward_pairs)]
    ppermute x6 -> x8, waiting for transfers between devices: 6.01 us -> 8.55 us  [ring_reduce_scatter(): got_backward = lax.ppermute(backward, 'row', backward_pairs)]
  transfers between devices with their start and end apart: 30 -> 34, of which waited for: 20 -> 22; matrix products, arithmetic and copies ran while one was open for 6% -> 7% of each run, Pallas kernels for 0% -> 0%
where the time goes in v7:
time: 99.2 us; the launch traced here: 99 us
  starting transfers between devices  37.9 us (38%)
  matrix products  27.9 us (28%)
  waiting for transfers between devices  24.5 us (25%)
  other arithmetic  6.06 us (6%)
  local copies, waits for them, and re-layouts  2.07 us (2%)
    ppermute x8, starting transfers between devices, ring_reduce_scatter(): got_forward = lax.ppermute(forward, 'row', forward_pairs)  11.7 us
    ppermute x8, starting transfers between devices, ring_reduce_scatter(): got_backward = lax.ppermute(backward, 'row', backward_pairs)  9.54 us
    ppermute x6, starting transfers between devices, ring_all_gather(): backward = lax.ppermute(backward, 'row', backward_pairs)  8.99 us
    dot_general x2, matrix products, body(): jnp.dot(chosen, q_weight[:, h * q_cols:(h + 1) * q_cols], preferred_eleme...  8.58 us
    ppermute x8, waiting for transfers between devices, ring_reduce_scatter(): got_backward = lax.ppermute(backward, 'row', backward_pairs)  8.55 us
    dot_general x1, matrix products, body(): products = jnp.dot(arranged, o_weight, preferred_element_type=jnp.float32)  8.31 us
    ppermute x8, waiting for transfers between devices, ring_reduce_scatter(): got_forward = lax.ppermute(forward, 'row', forward_pairs)  6.08 us
    ppermute x6, waiting for transfers between devices, ring_all_gather(): forward = lax.ppermute(forward, 'row', forward_pairs)  4.87 us
  transfers between devices with their start and end apart: 34, of which 22 were waited for; matrix products, arithmetic and copies ran while one was open for 7% of the time, Pallas kernels for 0%

profile of v7, /device:TPU:0, one launch (start us, length us, event | category | flops | bytes accessed | tf_op | source)
XLA Modules:
  0.0 99.0 jit_solution(2091765810041564339)
XLA Ops:
  2.3 2.9 %fusion.49 = f32[256,2048]{1,0:T(8,128)} fusion(bf16[128,2048]{1,0:T(8,128)(2,1)} %param.11, s32[256]{0:T(256)S(1)} %broadcast_select_fusion.1), kind=kOutput, calls=%fused_computation.79 | convolution fusion | flops 134250496 | bytes 2622464 | tf_op jit(solution)/shard_map/dot_general | solution.py:212
  5.8 2.2 %fusion.10 = bf16[256,2048]{1,0:T(8,128)(2,1)S(1)} fusion(f32[256,2048]{1,0:T(8,128)} %fusion.49, bf16[128,2048]{1,0:T(8,128)(2,1)S(1)} %collective-permute-done, s32[256]{0:T(256)S(1)} %get-tuple-element.11), kind=kOutput, calls=%fused_computation.14 | convolution fusion | flops 135299072 | bytes 3671040 | tf_op jit(solution)/shard_map/dot_general | solution.py:213
  8.0 6.2 %fusion.11 = bf16[256,2048]{1,0:T(8,128)(2,1)S(1)} fusion(bf16[256,2048]{1,0:T(8,128)(2,1)S(1)} %fusion.10, bf16[2048,4096]{1,0:T(8,128)(2,1)} %param.12), kind=kOutput, calls=%fused_computation.15 | convolution fusion | flops 2148007936 | bytes 10485760 | tf_op jit(solution)/shard_map/dot_general | solution.py:222
  14.6 2.4 %fusion.14 = bf16[256,2048]{1,0:T(8,128)(2,1)S(1)} fusion(bf16[256,2048]{1,0:T(8,128)(2,1)S(1)} %fusion.10, bf16[2048,4096]{1,0:T(8,128)(2,1)S(1)} %copy-done.5), kind=kOutput, calls=%fused_computation.16 | convolution fusion | flops 2148007936 | bytes 10485760 | tf_op jit(solution)/shard_map/dot_general | solution.py:222
  18.7 2.7 %collective-permute-start.1 = (bf16[32,1152]{1,0:T(8,128)(2,1)S(1)}, bf16[32,1152]{1,0:T(8,128)(2,1)S(1)}, u32[]{:S(2)}, u32[]{:S(2)}) collective-permute-start(bf16[32,1152]{1,0:T(8,128)(2,1)S(1)} %get-tuple-element.20), channel_id=1, source_target_pairs={{0,4},{4,8},{8,12},{12,14},{14,10},{10,6},{6,2},{2,0},{1,5},{5,9},... | collective-permute-start | bytes 221192 | tf_op jit(solution)/shard_map/ppermute | solution.py:137
  21.7 2.0 %collective-permute-start.13 = (bf16[32,1152]{1,0:T(8,128)(2,1)S(1)}, bf16[32,1152]{1,0:T(8,128)(2,1)S(1)}, u32[]{:S(2)}, u32[]{:S(2)}) collective-permute-start(bf16[32,1152]{1,0:T(8,128)(2,1)S(1)} %get-tuple-element.26), channel_id=1, source_target_pairs={{0,2},{4,0},{8,4},{12,8},{14,12},{10,14},{6,10},{2,6},{1,3},{5,1},... | collective-permute-start | bytes 221192 | tf_op jit(solution)/shard_map/ppermute | solution.py:139
  24.2 2.3 %collective-permute-done.5 = bf16[32,1152]{1,0:T(8,128)(2,1)S(1)} collective-permute-done((bf16[32,1152]{1,0:T(8,128)(2,1)S(1)}, bf16[32,1152]{1,0:T(8,128)(2,1)S(1)}, u32[]{:S(2)}, u32[]{:S(2)}) %collective-permute-start.5) | collective-permute-done | bytes 73760 | tf_op jit(solution)/shard_map/ppermute | solution.py:139
  26.7 2.1 %collective-permute-start.2 = (bf16[32,2304]{1,0:T(8,128)(2,1)S(1)}, bf16[32,2304]{1,0:T(8,128)(2,1)S(1)}, u32[]{:S(2)}, u32[]{:S(2)}) collective-permute-start(bf16[32,2304]{1,0:T(8,128)(2,1)S(1)} %fusion.44), channel_id=1, source_target_pairs={{0,4},{4,8},{8,12},{12,14},{14,10},{10,6},{6,2},{2,0},{1,5},{5,9},... | collective-permute-start | bytes 442376 | tf_op jit(solution)/shard_map/ppermute | solution.py:137
  31.0 2.1 %collective-permute-done.2 = bf16[32,2304]{1,0:T(8,128)(2,1)S(1)} collective-permute-done((bf16[32,2304]{1,0:T(8,128)(2,1)S(1)}, bf16[32,2304]{1,0:T(8,128)(2,1)S(1)}, u32[]{:S(2)}, u32[]{:S(2)}) %collective-permute-start.2) | collective-permute-done | bytes 147488 | tf_op jit(solution)/shard_map/ppermute | solution.py:137
  33.1 2.4 %collective-permute-start.3 = (bf16[32,2304]{1,0:T(8,128)(2,1)S(1)}, bf16[32,2304]{1,0:T(8,128)(2,1)S(1)}, u32[]{:S(2)}, u32[]{:S(2)}) collective-permute-start(bf16[32,2304]{1,0:T(8,128)(2,1)S(1)} %add_convert_fusion.8), channel_id=1, source_target_pairs={{0,4},{4,8},{8,12},{12,14},{14,10},{10,6},{6,2},{2,0},{1,5},{5,9},... | collective-permute-start | bytes 442376 | tf_op jit(solution)/shard_map/ppermute | solution.py:137
  36.7 2.0 %collective-permute-start.11 = (bf16[32,2304]{1,0:T(8,128)(2,1)S(1)}, bf16[32,2304]{1,0:T(8,128)(2,1)S(1)}, u32[]{:S(2)}, u32[]{:S(2)}) collective-permute-start(bf16[32,2304]{1,0:T(8,128)(2,1)S(1)} %add_convert_fusion.4), channel_id=1, source_target_pairs={{0,4},{4,8},{8,12},{12,14},{14,10},{10,6},{6,2},{2,0},{1,5},{5,9},... | collective-permute-start | bytes 442376 | tf_op jit(solution)/shard_map/ppermute | solution.py:137
  39.9 1.4 %collective-permute-start.7 = (bf16[32,2304]{1,0:T(8,128)(2,1)S(1)}, bf16[32,2304]{1,0:T(8,128)(2,1)S(1)}, u32[]{:S(2)}, u32[]{:S(2)}) collective-permute-start(bf16[32,2304]{1,0:T(8,128)(2,1)S(1)} %get-tuple-element.15), channel_id=1, source_target_pairs={{0,2},{4,0},{8,4},{12,8},{14,12},{10,14},{6,10},{2,6},{1,3},{5,1},... | collective-permute-start | bytes 442376 | tf_op jit(solution)/shard_map/ppermute | solution.py:139
  42.0 1.4 %collective-permute-done.11 = bf16[32,2304]{1,0:T(8,128)(2,1)S(1)} collective-permute-done((bf16[32,2304]{1,0:T(8,128)(2,1)S(1)}, bf16[32,2304]{1,0:T(8,128)(2,1)S(1)}, u32[]{:S(2)}, u32[]{:S(2)}) %collective-permute-start.11) | collective-permute-done | bytes 147488 | tf_op jit(solution)/shard_map/ppermute | solution.py:137
  43.5 1.6 %collective-permute-start.15 = (bf16[32,2304]{1,0:T(8,128)(2,1)S(1)}, bf16[32,2304]{1,0:T(8,128)(2,1)S(1)}, u32[]{:S(2)}, u32[]{:S(2)}) collective-permute-start(bf16[32,2304]{1,0:T(8,128)(2,1)S(1)} %get-tuple-element.17), channel_id=1, source_target_pairs={{0,2},{4,0},{8,4},{12,8},{14,12},{10,14},{6,10},{2,6},{1,3},{5,1},... | collective-permute-start | bytes 442376 | tf_op jit(solution)/shard_map/ppermute | solution.py:139
  46.7 1.4 %collective-permute-start.8 = (bf16[32,2304]{1,0:T(8,128)(2,1)S(1)}, bf16[32,2304]{1,0:T(8,128)(2,1)S(1)}, u32[]{:S(2)}, u32[]{:S(2)}) collective-permute-start(bf16[32,2304]{1,0:T(8,128)(2,1)S(1)} %add_convert_fusion.5), channel_id=1, source_target_pairs={{0,2},{4,0},{8,4},{12,8},{14,12},{10,14},{6,10},{2,6},{1,3},{5,1},... | collective-permute-start | bytes 442376 | tf_op jit(solution)/shard_map/ppermute | solution.py:139
  48.1 1.9 %collective-permute-done.15 = bf16[32,2304]{1,0:T(8,128)(2,1)S(1)} collective-permute-done((bf16[32,2304]{1,0:T(8,128)(2,1)S(1)}, bf16[32,2304]{1,0:T(8,128)(2,1)S(1)}, u32[]{:S(2)}, u32[]{:S(2)}) %collective-permute-start.15) | collective-permute-done | bytes 147488 | tf_op jit(solution)/shard_map/ppermute | solution.py:139
  50.0 2.1 %collective-permute-start.16 = (bf16[32,2304]{1,0:T(8,128)(2,1)S(1)}, bf16[32,2304]{1,0:T(8,128)(2,1)S(1)}, u32[]{:S(2)}, u32[]{:S(2)}) collective-permute-start(bf16[32,2304]{1,0:T(8,128)(2,1)S(1)} %add_convert_fusion.1), channel_id=1, source_target_pairs={{0,2},{4,0},{8,4},{12,8},{14,12},{10,14},{6,10},{2,6},{1,3},{5,1},... | collective-permute-start | bytes 442376 | tf_op jit(solution)/shard_map/ppermute | solution.py:139
  52.2 3.2 %collective-permute-done.16 = bf16[32,2304]{1,0:T(8,128)(2,1)S(1)} collective-permute-done((bf16[32,2304]{1,0:T(8,128)(2,1)S(1)}, bf16[32,2304]{1,0:T(8,128)(2,1)S(1)}, u32[]{:S(2)}, u32[]{:S(2)}) %collective-permute-start.16) | collective-permute-done | bytes 147488 | tf_op jit(solution)/shard_map/ppermute | solution.py:139
  58.4 1.4 %fusion.5 = f32[2,2,16,16]{2,3,1,0:T(8,128)S(1)} fusion(f32[2,2,16,16,1536]{4,3,2,1,0:T(8,128)S(1)} %get-tuple-element.45, f32[2,2,16,16]{2,3,1,0:T(8,128)S(1)} %max.7, pred[2,1536]{1,0:T(4,128)(4,1)S(1)} %iota_compare_fusion.8), kind=kLoop, calls=%fused_computation.9 | loop fusion | flops 6290432 | bytes 6302720 | tf_op jit(solution)/shard_map/vmap()/reduce_sum | solution.py:44
  59.8 1.9 %fusion.23 = f32[2,16,2,16,128]{4,3,1,2,0:T(8,128)S(1)} fusion(bf16[2,1536,2,128,1]{3,2,1,0,4:T(2,128)(2,1)S(1)} %bitcast.64, f32[2,2,16,16,1536]{4,3,2,1,0:T(8,128)S(1)} %get-tuple-element.45, f32[2,2,16,16]{2,3,1,0:T(8,128)S(1)} %max.7, pred[2,1536]{1,0:T(4,128)(4,1)S(1)} %iota_compare_fusion.8), kind=kOutput, calls=%fused_computation.23 | convolution fusion | flops 408944640 | bytes 8395776 | tf_op jit(solution)/shard_map/vmap(kgnc,ckd->nkgd)/dot_general | solution.py:45
  63.0 1.3 %collective-permute-start.18 = (bf16[32,2048]{1,0:T(8,128)(2,1)S(1)}, bf16[32,2048]{1,0:T(8,128)(2,1)S(1)}, u32[]{:S(2)}, u32[]{:S(2)}) collective-permute-start(bf16[32,2048]{1,0:T(8,128)(2,1)S(1)} %get-tuple-element.30), channel_id=1, source_target_pairs={{0,2},{4,0},{8,4},{12,8},{14,12},{10,14},{6,10},{2,6},{1,3},{5,1},... | collective-permute-start | bytes 393224 | tf_op jit(solution)/shard_map/ppermute | solution.py:171
  65.1 1.3 %collective-permute-start.26 = (bf16[32,2048]{1,0:T(8,128)(2,1)S(1)}, bf16[32,2048]{1,0:T(8,128)(2,1)S(1)}, u32[]{:S(2)}, u32[]{:S(2)}) collective-permute-start(bf16[32,2048]{1,0:T(8,128)(2,1)S(1)} %get-tuple-element.33), channel_id=1, source_target_pairs={{0,2},{4,0},{8,4},{12,8},{14,12},{10,14},{6,10},{2,6},{1,3},{5,1},... | collective-permute-start | bytes 393224 | tf_op jit(solution)/shard_map/ppermute | solution.py:171
  66.7 2.0 %collective-permute-done.17 = bf16[32,2048]{1,0:T(8,128)(2,1)S(1)} collective-permute-done((bf16[32,2048]{1,0:T(8,128)(2,1)S(1)}, bf16[32,2048]{1,0:T(8,128)(2,1)S(1)}, u32[]{:S(2)}, u32[]{:S(2)}) %collective-permute-start.17) | collective-permute-done | bytes 131104 | tf_op jit(solution)/shard_map/ppermute | solution.py:168
  69.3 1.5 %collective-permute-start.20 = (bf16[32,2048]{1,0:T(8,128)(2,1)S(1)}, bf16[32,2048]{1,0:T(8,128)(2,1)S(1)}, u32[]{:S(2)}, u32[]{:S(2)}) collective-permute-start(bf16[32,2048]{1,0:T(8,128)(2,1)S(1)} %collective-permute-done.18), channel_id=1, source_target_pairs={{0,2},{4,0},{8,4},{12,8},{14,12},{10,14},{6,10},{2,6},{1,3},{5,1},... | collective-permute-start | bytes 393224 | tf_op jit(solution)/shard_map/ppermute | solution.py:171
  71.9 1.7 %collective-permute-start.28 = (bf16[32,2048]{1,0:T(8,128)(2,1)S(1)}, bf16[32,2048]{1,0:T(8,128)(2,1)S(1)}, u32[]{:S(2)}, u32[]{:S(2)}) collective-permute-start(bf16[32,2048]{1,0:T(8,128)(2,1)S(1)} %collective-permute-done.26), channel_id=1, source_target_pairs={{0,2},{4,0},{8,4},{12,8},{14,12},{10,14},{6,10},{2,6},{1,3},{5,1},... | collective-permute-start | bytes 393224 | tf_op jit(solution)/shard_map/ppermute | solution.py:171
  75.0 1.6 %collective-permute-start.22 = (bf16[32,2048]{1,0:T(8,128)(2,1)S(1)}, bf16[32,2048]{1,0:T(8,128)(2,1)S(1)}, u32[]{:S(2)}, u32[]{:S(2)}) collective-permute-start(bf16[32,2048]{1,0:T(8,128)(2,1)S(1)} %collective-permute-done.20), channel_id=1, source_target_pairs={{0,2},{4,0},{8,4},{12,8},{14,12},{10,14},{6,10},{2,6},{1,3},{5,1},... | collective-permute-start | bytes 393224 | tf_op jit(solution)/shard_map/ppermute | solution.py:171
  77.7 1.6 %collective-permute-start.30 = (bf16[32,2048]{1,0:T(8,128)(2,1)S(1)}, bf16[32,2048]{1,0:T(8,128)(2,1)S(1)}, u32[]{:S(2)}, u32[]{:S(2)}) collective-permute-start(bf16[32,2048]{1,0:T(8,128)(2,1)S(1)} %collective-permute-done.28), channel_id=1, source_target_pairs={{0,2},{4,0},{8,4},{12,8},{14,12},{10,14},{6,10},{2,6},{1,3},{5,1},... | collective-permute-start | bytes 393224 | tf_op jit(solution)/shard_map/ppermute | solution.py:171
  79.9 1.6 %collective-permute-start.24 = (bf16[32,1024]{1,0:T(8,128)(2,1)S(1)}, bf16[32,1024]{1,0:T(8,128)(2,1)S(1)}, u32[]{:S(2)}, u32[]{:S(2)}) collective-permute-start(bf16[32,1024]{1,0:T(8,128)(2,1)S(1)} %slice.239), channel_id=1, source_target_pairs={{0,2},{4,0},{8,4},{12,8},{14,12},{10,14},{6,10},{2,6},{1,3},{5,1},... | collective-permute-start | bytes 196616 | tf_op jit(solution)/shard_map/ppermute | solution.py:175
  82.6 1.6 %collective-permute-start.32 = (bf16[32,1024]{1,0:T(8,128)(2,1)S(1)}, bf16[32,1024]{1,0:T(8,128)(2,1)S(1)}, u32[]{:S(2)}, u32[]{:S(2)}) collective-permute-start(bf16[32,1024]{1,0:T(8,128)(2,1)S(1)} %slice.242), channel_id=1, source_target_pairs={{0,2},{4,0},{8,4},{12,8},{14,12},{10,14},{6,10},{2,6},{1,3},{5,1},... | collective-permute-start | bytes 196616 | tf_op jit(solution)/shard_map/ppermute | solution.py:175
  84.4 2.1 %collective-permute-done.31 = bf16[32,1024]{1,0:T(8,128)(2,1)S(1)} collective-permute-done((bf16[32,1024]{1,0:T(8,128)(2,1)S(1)}, bf16[32,1024]{1,0:T(8,128)(2,1)S(1)}, u32[]{:S(2)}, u32[]{:S(2)}) %collective-permute-start.31) | collective-permute-done | bytes 65568 | tf_op jit(solution)/shard_map/ppermute | solution.py:174
  87.7 8.3 %fusion.71 = f32[256,2048]{1,0:T(8,128)S(1)} fusion(bf16[256,4096]{1,0:T(8,128)(2,1)S(1)} %convolution_convert_fusion, bf16[4096,2048]{1,0:T(8,128)(2,1)} %param.15), kind=kOutput, calls=%fused_computation.161 | convolution fusion | flops 4294967296 | bytes 20971520 | tf_op jit(solution)/shard_map/dot_general | solution.py:273
  96.2 1.9 %collective-permute-done.33 = bf16[128,2048]{1,0:T(8,128)(2,1)S(1)} collective-permute-done((bf16[128,2048]{1,0:T(8,128)(2,1)S(1)}, bf16[128,2048]{1,0:T(8,128)(2,1)S(1)}, u32[]{:S(2)}, u32[]{:S(2)}) %collective-permute-start.33) | collective-permute-done | bytes 524320 | tf_op jit(solution)/shard_map/ppermute | solution.py:274
  (148 shorter events, 26.2 us)
Async XLA Ops:
  0.0 5.8 %collective-permute-start = (bf16[128,2048]{1,0:T(8,128)(2,1)}, bf16[128,2048]{1,0:T(8,128)(2,1)S(1)}, u32[]{:S(2)}, u32[]{:S(2)}) collective-permute-start(bf16[128,2048]{1,0:T(8,128)(2,1)} %param.11), channel_id=1, source_target_pairs={{0,1},{1,0},{2,3},{3,2},{4,5},{5,4},{6,7},{7,6},{8,9},{9,8},{10,11... | collective-permute-start | bytes 1572872 | tf_op jit(solution)/shard_map/ppermute | solution.py:200
  18.7 5.5 %collective-permute-start.1 = (bf16[32,1152]{1,0:T(8,128)(2,1)S(1)}, bf16[32,1152]{1,0:T(8,128)(2,1)S(1)}, u32[]{:S(2)}, u32[]{:S(2)}) collective-permute-start(bf16[32,1152]{1,0:T(8,128)(2,1)S(1)} %get-tuple-element.20), channel_id=1, source_target_pairs={{0,4},{4,8},{8,12},{12,14},{14,10},{10,6},{6,2},{2,0},{1,5},{5,9},... | collective-permute-start | bytes 221192 | tf_op jit(solution)/shard_map/ppermute | solution.py:137
  21.5 5.1 %collective-permute-start.5 = (bf16[32,1152]{1,0:T(8,128)(2,1)S(1)}, bf16[32,1152]{1,0:T(8,128)(2,1)S(1)}, u32[]{:S(2)}, u32[]{:S(2)}) collective-permute-start(bf16[32,1152]{1,0:T(8,128)(2,1)S(1)} %get-tuple-element.21), channel_id=1, source_target_pairs={{0,2},{4,0},{8,4},{12,8},{14,12},{10,14},{6,10},{2,6},{1,3},{5,1},... | collective-permute-start | bytes 221192 | tf_op jit(solution)/shard_map/ppermute | solution.py:139
  21.7 7.0 %collective-permute-start.13 = (bf16[32,1152]{1,0:T(8,128)(2,1)S(1)}, bf16[32,1152]{1,0:T(8,128)(2,1)S(1)}, u32[]{:S(2)}, u32[]{:S(2)}) collective-permute-start(bf16[32,1152]{1,0:T(8,128)(2,1)S(1)} %get-tuple-element.26), channel_id=1, source_target_pairs={{0,2},{4,0},{8,4},{12,8},{14,12},{10,14},{6,10},{2,6},{1,3},{5,1},... | collective-permute-start | bytes 221192 | tf_op jit(solution)/shard_map/ppermute | solution.py:139
  23.7 5.0 %collective-permute-start.9 = (bf16[32,1152]{1,0:T(8,128)(2,1)S(1)}, bf16[32,1152]{1,0:T(8,128)(2,1)S(1)}, u32[]{:S(2)}, u32[]{:S(2)}) collective-permute-start(bf16[32,1152]{1,0:T(8,128)(2,1)S(1)} %get-tuple-element.25), channel_id=1, source_target_pairs={{0,4},{4,8},{8,12},{12,14},{14,10},{10,6},{6,2},{2,0},{1,5},{5,9},... | collective-permute-start | bytes 221192 | tf_op jit(solution)/shard_map/ppermute | solution.py:137
  26.6 12.1 %collective-permute-start.6 = (bf16[32,2304]{1,0:T(8,128)(2,1)S(1)}, bf16[32,2304]{1,0:T(8,128)(2,1)S(1)}, u32[]{:S(2)}, u32[]{:S(2)}) collective-permute-start(bf16[32,2304]{1,0:T(8,128)(2,1)S(1)} %pad_maximum_fusion.4), channel_id=1, source_target_pairs={{0,2},{4,0},{8,4},{12,8},{14,12},{10,14},{6,10},{2,6},{1,3},{5,1},... | collective-permute-start | bytes 442376 | tf_op jit(solution)/shard_map/ppermute | solution.py:139
  26.7 6.4 %collective-permute-start.2 = (bf16[32,2304]{1,0:T(8,128)(2,1)S(1)}, bf16[32,2304]{1,0:T(8,128)(2,1)S(1)}, u32[]{:S(2)}, u32[]{:S(2)}) collective-permute-start(bf16[32,2304]{1,0:T(8,128)(2,1)S(1)} %fusion.44), channel_id=1, source_target_pairs={{0,4},{4,8},{8,12},{12,14},{14,10},{10,6},{6,2},{2,0},{1,5},{5,9},... | collective-permute-start | bytes 442376 | tf_op jit(solution)/shard_map/ppermute | solution.py:137
  28.8 13.1 %collective-permute-start.14 = (bf16[32,2304]{1,0:T(8,128)(2,1)S(1)}, bf16[32,2304]{1,0:T(8,128)(2,1)S(1)}, u32[]{:S(2)}, u32[]{:S(2)}) collective-permute-start(bf16[32,2304]{1,0:T(8,128)(2,1)S(1)} %pad_maximum_fusion.5), channel_id=1, source_target_pairs={{0,2},{4,0},{8,4},{12,8},{14,12},{10,14},{6,10},{2,6},{1,3},{5,1},... | collective-permute-start | bytes 442376 | tf_op jit(solution)/shard_map/ppermute | solution.py:139
  29.9 6.8 %collective-permute-start.10 = (bf16[32,2304]{1,0:T(8,128)(2,1)S(1)}, bf16[32,2304]{1,0:T(8,128)(2,1)S(1)}, u32[]{:S(2)}, u32[]{:S(2)}) collective-permute-start(bf16[32,2304]{1,0:T(8,128)(2,1)S(1)} %fusion.47), channel_id=1, source_target_pairs={{0,4},{4,8},{8,12},{12,14},{14,10},{10,6},{6,2},{2,0},{1,5},{5,9},... | collective-permute-start | bytes 442376 | tf_op jit(solution)/shard_map/ppermute | solution.py:137
  33.1 6.7 %collective-permute-start.3 = (bf16[32,2304]{1,0:T(8,128)(2,1)S(1)}, bf16[32,2304]{1,0:T(8,128)(2,1)S(1)}, u32[]{:S(2)}, u32[]{:S(2)}) collective-permute-start(bf16[32,2304]{1,0:T(8,128)(2,1)S(1)} %add_convert_fusion.8), channel_id=1, source_target_pairs={{0,4},{4,8},{8,12},{12,14},{14,10},{10,6},{6,2},{2,0},{1,5},{5,9},... | collective-permute-start | bytes 442376 | tf_op jit(solution)/shard_map/ppermute | solution.py:137
  36.7 6.7 %collective-permute-start.11 = (bf16[32,2304]{1,0:T(8,128)(2,1)S(1)}, bf16[32,2304]{1,0:T(8,128)(2,1)S(1)}, u32[]{:S(2)}, u32[]{:S(2)}) collective-permute-start(bf16[32,2304]{1,0:T(8,128)(2,1)S(1)} %add_convert_fusion.4), channel_id=1, source_target_pairs={{0,4},{4,8},{8,12},{12,14},{14,10},{10,6},{6,2},{2,0},{1,5},{5,9},... | collective-permute-start | bytes 442376 | tf_op jit(solution)/shard_map/ppermute | solution.py:137
  39.9 6.8 %collective-permute-start.7 = (bf16[32,2304]{1,0:T(8,128)(2,1)S(1)}, bf16[32,2304]{1,0:T(8,128)(2,1)S(1)}, u32[]{:S(2)}, u32[]{:S(2)}) collective-permute-start(bf16[32,2304]{1,0:T(8,128)(2,1)S(1)} %get-tuple-element.15), channel_id=1, source_target_pairs={{0,2},{4,0},{8,4},{12,8},{14,12},{10,14},{6,10},{2,6},{1,3},{5,1},... | collective-permute-start | bytes 442376 | tf_op jit(solution)/shard_map/ppermute | solution.py:139
  41.2 10.8 %collective-permute-start.4 = (bf16[32,2304]{1,0:T(8,128)(2,1)S(1)}, bf16[32,2304]{1,0:T(8,128)(2,1)S(1)}, u32[]{:S(2)}, u32[]{:S(2)}) collective-permute-start(bf16[32,2304]{1,0:T(8,128)(2,1)S(1)} %get-tuple-element.14), channel_id=1, source_target_pairs={{0,4},{4,8},{8,12},{12,14},{14,10},{10,6},{6,2},{2,0},{1,5},{5,9},... | collective-permute-start | bytes 442376 | tf_op jit(solution)/shard_map/ppermute | solution.py:137
  43.5 6.5 %collective-permute-start.15 = (bf16[32,2304]{1,0:T(8,128)(2,1)S(1)}, bf16[32,2304]{1,0:T(8,128)(2,1)S(1)}, u32[]{:S(2)}, u32[]{:S(2)}) collective-permute-start(bf16[32,2304]{1,0:T(8,128)(2,1)S(1)} %get-tuple-element.17), channel_id=1, source_target_pairs={{0,2},{4,0},{8,4},{12,8},{14,12},{10,14},{6,10},{2,6},{1,3},{5,1},... | collective-permute-start | bytes 442376 | tf_op jit(solution)/shard_map/ppermute | solution.py:139
  45.1 7.1 %collective-permute-start.12 = (bf16[32,2304]{1,0:T(8,128)(2,1)S(1)}, bf16[32,2304]{1,0:T(8,128)(2,1)S(1)}, u32[]{:S(2)}, u32[]{:S(2)}) collective-permute-start(bf16[32,2304]{1,0:T(8,128)(2,1)S(1)} %get-tuple-element.16), channel_id=1, source_target_pairs={{0,4},{4,8},{8,12},{12,14},{14,10},{10,6},{6,2},{2,0},{1,5},{5,9},... | collective-permute-start | bytes 442376 | tf_op jit(solution)/shard_map/ppermute | solution.py:137
  46.7 5.4 %collective-permute-start.8 = (bf16[32,2304]{1,0:T(8,128)(2,1)S(1)}, bf16[32,2304]{1,0:T(8,128)(2,1)S(1)}, u32[]{:S(2)}, u32[]{:S(2)}) collective-permute-start(bf16[32,2304]{1,0:T(8,128)(2,1)S(1)} %add_convert_fusion.5), channel_id=1, source_target_pairs={{0,2},{4,0},{8,4},{12,8},{14,12},{10,14},{6,10},{2,6},{1,3},{5,1},... | collective-permute-start | bytes 442376 | tf_op jit(solution)/shard_map/ppermute | solution.py:139
  50.0 5.4 %collective-permute-start.16 = (bf16[32,2304]{1,0:T(8,128)(2,1)S(1)}, bf16[32,2304]{1,0:T(8,128)(2,1)S(1)}, u32[]{:S(2)}, u32[]{:S(2)}) collective-permute-start(bf16[32,2304]{1,0:T(8,128)(2,1)S(1)} %add_convert_fusion.1), channel_id=1, source_target_pairs={{0,2},{4,0},{8,4},{12,8},{14,12},{10,14},{6,10},{2,6},{1,3},{5,1},... | collective-permute-start | bytes 442376 | tf_op jit(solution)/shard_map/ppermute | solution.py:139
  62.3 6.4 %collective-permute-start.17 = (bf16[32,2048]{1,0:T(8,128)(2,1)S(1)}, bf16[32,2048]{1,0:T(8,128)(2,1)S(1)}, u32[]{:S(2)}, u32[]{:S(2)}) collective-permute-start(bf16[32,2048]{1,0:T(8,128)(2,1)S(1)} %get-tuple-element.30), channel_id=1, source_target_pairs={{0,4},{4,8},{8,12},{12,14},{14,10},{10,6},{6,2},{2,0},{1,5},{5,9},... | collective-permute-start | bytes 393224 | tf_op jit(solution)/shard_map/ppermute | solution.py:168
  63.0 6.3 %collective-permute-start.18 = (bf16[32,2048]{1,0:T(8,128)(2,1)S(1)}, bf16[32,2048]{1,0:T(8,128)(2,1)S(1)}, u32[]{:S(2)}, u32[]{:S(2)}) collective-permute-start(bf16[32,2048]{1,0:T(8,128)(2,1)S(1)} %get-tuple-element.30), channel_id=1, source_target_pairs={{0,2},{4,0},{8,4},{12,8},{14,12},{10,14},{6,10},{2,6},{1,3},{5,1},... | collective-permute-start | bytes 393224 | tf_op jit(solution)/shard_map/ppermute | solution.py:171
  64.4 7.2 %collective-permute-start.25 = (bf16[32,2048]{1,0:T(8,128)(2,1)S(1)}, bf16[32,2048]{1,0:T(8,128)(2,1)S(1)}, u32[]{:S(2)}, u32[]{:S(2)}) collective-permute-start(bf16[32,2048]{1,0:T(8,128)(2,1)S(1)} %get-tuple-element.33), channel_id=1, source_target_pairs={{0,4},{4,8},{8,12},{12,14},{14,10},{10,6},{6,2},{2,0},{1,5},{5,9},... | collective-permute-start | bytes 393224 | tf_op jit(solution)/shard_map/ppermute | solution.py:168
  65.1 6.9 %collective-permute-start.26 = (bf16[32,2048]{1,0:T(8,128)(2,1)S(1)}, bf16[32,2048]{1,0:T(8,128)(2,1)S(1)}, u32[]{:S(2)}, u32[]{:S(2)}) collective-permute-start(bf16[32,2048]{1,0:T(8,128)(2,1)S(1)} %get-tuple-element.33), channel_id=1, source_target_pairs={{0,2},{4,0},{8,4},{12,8},{14,12},{10,14},{6,10},{2,6},{1,3},{5,1},... | collective-permute-start | bytes 393224 | tf_op jit(solution)/shard_map/ppermute | solution.py:171
  68.7 5.7 %collective-permute-start.19 = (bf16[32,2048]{1,0:T(8,128)(2,1)S(1)}, bf16[32,2048]{1,0:T(8,128)(2,1)S(1)}, u32[]{:S(2)}, u32[]{:S(2)}) collective-permute-start(bf16[32,2048]{1,0:T(8,128)(2,1)S(1)} %collective-permute-done.17), channel_id=1, source_target_pairs={{0,4},{4,8},{8,12},{12,14},{14,10},{10,6},{6,2},{2,0},{1,5},{5,9},... | collective-permute-start | bytes 393224 | tf_op jit(solution)/shard_map/ppermute | solution.py:168
  69.3 5.6 %collective-permute-start.20 = (bf16[32,2048]{1,0:T(8,128)(2,1)S(1)}, bf16[32,2048]{1,0:T(8,128)(2,1)S(1)}, u32[]{:S(2)}, u32[]{:S(2)}) collective-permute-start(bf16[32,2048]{1,0:T(8,128)(2,1)S(1)} %collective-permute-done.18), channel_id=1, source_target_pairs={{0,2},{4,0},{8,4},{12,8},{14,12},{10,14},{6,10},{2,6},{1,3},{5,1},... | collective-permute-start | bytes 393224 | tf_op jit(solution)/shard_map/ppermute | solution.py:171
  71.5 5.7 %collective-permute-start.27 = (bf16[32,2048]{1,0:T(8,128)(2,1)S(1)}, bf16[32,2048]{1,0:T(8,128)(2,1)S(1)}, u32[]{:S(2)}, u32[]{:S(2)}) collective-permute-start(bf16[32,2048]{1,0:T(8,128)(2,1)S(1)} %collective-permute-done.25), channel_id=1, source_target_pairs={{0,4},{4,8},{8,12},{12,14},{14,10},{10,6},{6,2},{2,0},{1,5},{5,9},... | collective-permute-start | bytes 393224 | tf_op jit(solution)/shard_map/ppermute | solution.py:168
  71.9 5.7 %collective-permute-start.28 = (bf16[32,2048]{1,0:T(8,128)(2,1)S(1)}, bf16[32,2048]{1,0:T(8,128)(2,1)S(1)}, u32[]{:S(2)}, u32[]{:S(2)}) collective-permute-start(bf16[32,2048]{1,0:T(8,128)(2,1)S(1)} %collective-permute-done.26), channel_id=1, source_target_pairs={{0,2},{4,0},{8,4},{12,8},{14,12},{10,14},{6,10},{2,6},{1,3},{5,1},... | collective-permute-start | bytes 393224 | tf_op jit(solution)/shard_map/ppermute | solution.py:171
  74.4 5.0 %collective-permute-start.21 = (bf16[32,2048]{1,0:T(8,128)(2,1)S(1)}, bf16[32,2048]{1,0:T(8,128)(2,1)S(1)}, u32[]{:S(2)}, u32[]{:S(2)}) collective-permute-start(bf16[32,2048]{1,0:T(8,128)(2,1)S(1)} %collective-permute-done.19), channel_id=1, source_target_pairs={{0,4},{4,8},{8,12},{12,14},{14,10},{10,6},{6,2},{2,0},{1,5},{5,9},... | collective-permute-start | bytes 393224 | tf_op jit(solution)/shard_map/ppermute | solution.py:168
  75.0 5.0 %collective-permute-start.22 = (bf16[32,2048]{1,0:T(8,128)(2,1)S(1)}, bf16[32,2048]{1,0:T(8,128)(2,1)S(1)}, u32[]{:S(2)}, u32[]{:S(2)}) collective-permute-start(bf16[32,2048]{1,0:T(8,128)(2,1)S(1)} %collective-permute-done.20), channel_id=1, source_target_pairs={{0,2},{4,0},{8,4},{12,8},{14,12},{10,14},{6,10},{2,6},{1,3},{5,1},... | collective-permute-start | bytes 393224 | tf_op jit(solution)/shard_map/ppermute | solution.py:171
  77.2 5.0 %collective-permute-start.29 = (bf16[32,2048]{1,0:T(8,128)(2,1)S(1)}, bf16[32,2048]{1,0:T(8,128)(2,1)S(1)}, u32[]{:S(2)}, u32[]{:S(2)}) collective-permute-start(bf16[32,2048]{1,0:T(8,128)(2,1)S(1)} %collective-permute-done.27), channel_id=1, source_target_pairs={{0,4},{4,8},{8,12},{12,14},{14,10},{10,6},{6,2},{2,0},{1,5},{5,9},... | collective-permute-start | bytes 393224 | tf_op jit(solution)/shard_map/ppermute | solution.py:168
  77.7 5.0 %collective-permute-start.30 = (bf16[32,2048]{1,0:T(8,128)(2,1)S(1)}, bf16[32,2048]{1,0:T(8,128)(2,1)S(1)}, u32[]{:S(2)}, u32[]{:S(2)}) collective-permute-start(bf16[32,2048]{1,0:T(8,128)(2,1)S(1)} %collective-permute-done.28), channel_id=1, source_target_pairs={{0,2},{4,0},{8,4},{12,8},{14,12},{10,14},{6,10},{2,6},{1,3},{5,1},... | collective-permute-start | bytes 393224 | tf_op jit(solution)/shard_map/ppermute | solution.py:171
  79.4 4.9 %collective-permute-start.23 = (bf16[32,1024]{1,0:T(8,128)(2,1)S(1)}, bf16[32,1024]{1,0:T(8,128)(2,1)S(1)}, u32[]{:S(2)}, u32[]{:S(2)}) collective-permute-start(bf16[32,1024]{1,0:T(8,128)(2,1)S(1)} %slice.238), channel_id=1, source_target_pairs={{0,4},{4,8},{8,12},{12,14},{14,10},{10,6},{6,2},{2,0},{1,5},{5,9},... | collective-permute-start | bytes 196616 | tf_op jit(solution)/shard_map/ppermute | solution.py:174
  79.9 4.4 %collective-permute-start.24 = (bf16[32,1024]{1,0:T(8,128)(2,1)S(1)}, bf16[32,1024]{1,0:T(8,128)(2,1)S(1)}, u32[]{:S(2)}, u32[]{:S(2)}) collective-permute-start(bf16[32,1024]{1,0:T(8,128)(2,1)S(1)} %slice.239), channel_id=1, source_target_pairs={{0,2},{4,0},{8,4},{12,8},{14,12},{10,14},{6,10},{2,6},{1,3},{5,1},... | collective-permute-start | bytes 196616 | tf_op jit(solution)/shard_map/ppermute | solution.py:175
  82.6 4.3 %collective-permute-start.32 = (bf16[32,1024]{1,0:T(8,128)(2,1)S(1)}, bf16[32,1024]{1,0:T(8,128)(2,1)S(1)}, u32[]{:S(2)}, u32[]{:S(2)}) collective-permute-start(bf16[32,1024]{1,0:T(8,128)(2,1)S(1)} %slice.242), channel_id=1, source_target_pairs={{0,2},{4,0},{8,4},{12,8},{14,12},{10,14},{6,10},{2,6},{1,3},{5,1},... | collective-permute-start | bytes 196616 | tf_op jit(solution)/shard_map/ppermute | solution.py:175
  (11 other events, 102.1 us)

commit v8 on v6

--- a/solution.py
+++ b/solution.py
@@ -192,8 +192,20 @@
                 [q_part, k_part[:, h * k_cols : (h + 1) * k_cols], v_part[:, h * k_cols : (h + 1) * k_cols]],
                 axis=1,
             )
-            blocks = [joined[k * block_rows : (k + 1) * block_rows] for k in range(n_row)]
-            summed = ring_reduce_scatter(blocks)
+            pieces = 2 if joined.shape[1] % 256 == 0 else 1
+            piece = joined.shape[1] // pieces
+            summed = jnp.concatenate(
+                [
+                    ring_reduce_scatter(
+                        [
+                            joined[k * block_rows : (k + 1) * block_rows, i * piece : (i + 1) * piece]
+                            for k in range(n_row)
+                        ]
+                    )
+                    for i in range(pieces)
+                ],
+                axis=1,
+            )
             q_sums.append(summed[:, :q_cols])
             k_sums.append(summed[:, q_cols : q_cols + k_cols])
             v_sums.append(summed[:, q_cols + k_cols :])
@@ -220,8 +232,14 @@
             starts,
         )
         attended = results.reshape(seq_dev * new_len, -1)
+        n_gather = 4 if attended.shape[1] % 512 == 0 else n_kv
+        gather_cols = attended.shape[1] // n_gather
         stacked = jnp.concatenate(
-            [ring_all_gather(attended[:, h * q_cols : (h + 1) * q_cols]) for h in range(n_kv)], axis=1
+            [
+                ring_all_gather(attended[:, i * gather_cols : (i + 1) * gather_cols])
+                for i in range(n_gather)
+            ],
+            axis=1,
         )
         late_mine = jnp.arange(n_row, dtype=jnp.int32)[:, None] == late_row
         row_of_slot = jnp.sum(jnp.where(late_mine, jnp.asarray(stacked_table), 0), axis=0)

time: 95 us -> 118 us (1.24)
  starting transfers between devices: 33.5 us -> 66.7 us
  waiting for transfers between devices: 26.9 us -> 17.3 us
    ppermute x8 -> x16, starting transfers between devices: 12.7 us -> 28.8 us  [ring_all_gather(): forward = lax.ppermute(forward, 'row', forward_pairs)]
    ppermute x8 -> x16, starting transfers between devices: 16.6 us -> 31 us  [ring_reduce_scatter(): got_forward = lax.ppermute(forward, 'row', forward_pairs)]
    ppermute x8 -> x16, waiting for transfers between devices: 8.82 us -> 3.03 us  [ring_reduce_scatter(): got_forward = lax.ppermute(forward, 'row', forward_pairs)]
    ppermute x6 -> x12, waiting for transfers between devices: 4.07 us -> 0.03 us  [ring_all_gather(): backward = lax.ppermute(backward, 'row', backward_pairs)]
    ppermute x6 -> x12, starting transfers between devices: 0.93 us -> 3.53 us  [ring_reduce_scatter(): got_backward = lax.ppermute(backward, 'row', backward_pairs)]
    ppermute x6 -> x12, waiting for transfers between devices: 6.01 us -> 8.29 us  [ring_reduce_scatter(): got_backward = lax.ppermute(backward, 'row', backward_pairs)]
    ppermute x8 -> x16, waiting for transfers between devices: 6.05 us -> 4.04 us  [ring_all_gather(): forward = lax.ppermute(forward, 'row', forward_pairs)]
    ppermute x6 -> x12, starting transfers between devices: 2.7 us -> 2.77 us  [ring_all_gather(): backward = lax.ppermute(backward, 'row', backward_pairs)]
  transfers between devices with their start and end apart: 30 -> 58, of which waited for: 20 -> 21; matrix products, arithmetic and copies ran while one was open for 6% -> 5% of each run, Pallas kernels for 0% -> 0%
where the time goes in v8:
time: 118 us
  starting transfers between devices  66.7 us (57%)
  matrix products  24.6 us (21%)
  waiting for transfers between devices  17.3 us (15%)
  other arithmetic  6.45 us (5%)
  local copies, waits for them, and re-layouts  2.64 us (2%)
    ppermute x16, starting transfers between devices, ring_reduce_scatter(): got_forward = lax.ppermute(forward, 'row', forward_pairs)  31 us
    ppermute x16, starting transfers between devices, ring_all_gather(): forward = lax.ppermute(forward, 'row', forward_pairs)  28.8 us
    dot_general x2, matrix products, body(): jnp.dot(chosen, q_weight[:, h * q_cols:(h + 1) * q_cols], preferred_eleme...  8.36 us
    ppermute x12, waiting for transfers between devices, ring_reduce_scatter(): got_backward = lax.ppermute(backward, 'row', backward_pairs)  8.29 us
    dot_general x1, matrix products, body(): products = jnp.dot(arranged, o_weight, preferred_element_type=jnp.float32)  8.29 us
    ppermute x16, waiting for transfers between devices, ring_all_gather(): forward = lax.ppermute(forward, 'row', forward_pairs)  4.04 us
    ppermute x12, starting transfers between devices, ring_reduce_scatter(): got_backward = lax.ppermute(backward, 'row', backward_pairs)  3.53 us
    ppermute x16, waiting for transfers between devices, ring_reduce_scatter(): got_forward = lax.ppermute(forward, 'row', forward_pairs)  3.03 us
  transfers between devices with their start and end apart: 58, of which 21 were waited for; matrix products, arithmetic and copies ran while one was open for 5% of the time, Pallas kernels for 0%

profile of v8, /device:TPU:0, one launch (start us, length us, event | category | flops | bytes accessed | tf_op | source)
XLA Modules:
  0.0 118.2 jit_solution(173284892943715374)
XLA Ops:
  5.6 6.0 %fusion.14 = bf16[256,2048]{1,0:T(8,128)(2,1)S(1)} fusion(bf16[256,2048]{1,0:T(8,128)(2,1)S(1)} %fusion.10, bf16[2048,4096]{1,0:T(8,128)(2,1)} %param.12), kind=kOutput, calls=%fused_computation.16 | convolution fusion | flops 2148007936 | bytes 10485760 | tf_op jit(solution)/shard_map/dot_general | solution.py:188
  11.6 1.7 %copy-done.5 = bf16[2048,4096]{1,0:T(8,128)(2,1)S(1)} copy-done((bf16[2048,4096]{1,0:T(8,128)(2,1)S(1)}, bf16[2048,4096]{1,0:T(8,128)(2,1)}, u32[]{:S(2)}) %copy-start.5) | copy-done | bytes 16777240
  13.3 2.4 %fusion.11 = bf16[256,2048]{1,0:T(8,128)(2,1)S(1)} fusion(bf16[256,2048]{1,0:T(8,128)(2,1)S(1)} %fusion.10, bf16[2048,4096]{1,0:T(8,128)(2,1)S(1)} %copy-done.5), kind=kOutput, calls=%fused_computation.15 | convolution fusion | flops 2148007936 | bytes 10485760 | tf_op jit(solution)/shard_map/dot_general | solution.py:188
  16.7 2.7 %collective-permute-start.8 = (bf16[32,1152]{1,0:T(8,128)(2,1)S(1)}, bf16[32,1152]{1,0:T(8,128)(2,1)S(1)}, u32[]{:S(2)}, u32[]{:S(2)}) collective-permute-start(bf16[32,1152]{1,0:T(8,128)(2,1)S(1)} %get-tuple-element.16), channel_id=1, source_target_pairs={{0,4},{4,8},{8,12},{12,14},{14,10},{10,6},{6,2},{2,0},{1,5},{5,9},... | collective-permute-start | bytes 221192 | tf_op jit(solution)/shard_map/ppermute | solution.py:122
  19.4 2.0 %collective-permute-start.1 = (bf16[32,1152]{1,0:T(8,128)(2,1)S(1)}, bf16[32,1152]{1,0:T(8,128)(2,1)S(1)}, u32[]{:S(2)}, u32[]{:S(2)}) collective-permute-start(bf16[32,1152]{1,0:T(8,128)(2,1)S(1)} %get-tuple-element.31), channel_id=1, source_target_pairs={{0,4},{4,8},{8,12},{12,14},{14,10},{10,6},{6,2},{2,0},{1,5},{5,9},... | collective-permute-start | bytes 221192 | tf_op jit(solution)/shard_map/ppermute | solution.py:122
  21.5 2.1 %collective-permute-start.22 = (bf16[32,1152]{1,0:T(8,128)(2,1)S(1)}, bf16[32,1152]{1,0:T(8,128)(2,1)S(1)}, u32[]{:S(2)}, u32[]{:S(2)}) collective-permute-start(bf16[32,1152]{1,0:T(8,128)(2,1)S(1)} %get-tuple-element.20), channel_id=1, source_target_pairs={{0,4},{4,8},{8,12},{12,14},{14,10},{10,6},{6,2},{2,0},{1,5},{5,9},... | collective-permute-start | bytes 221192 | tf_op jit(solution)/shard_map/ppermute | solution.py:122
  24.0 2.2 %collective-permute-start.15 = (bf16[32,1152]{1,0:T(8,128)(2,1)S(1)}, bf16[32,1152]{1,0:T(8,128)(2,1)S(1)}, u32[]{:S(2)}, u32[]{:S(2)}) collective-permute-start(bf16[32,1152]{1,0:T(8,128)(2,1)S(1)} %get-tuple-element.42), channel_id=1, source_target_pairs={{0,4},{4,8},{8,12},{12,14},{14,10},{10,6},{6,2},{2,0},{1,5},{5,9},... | collective-permute-start | bytes 221192 | tf_op jit(solution)/shard_map/ppermute | solution.py:122
  26.5 2.1 %collective-permute-start.2 = (bf16[32,1152]{1,0:T(8,128)(2,1)S(1)}, bf16[32,1152]{1,0:T(8,128)(2,1)S(1)}, u32[]{:S(2)}, u32[]{:S(2)}) collective-permute-start(bf16[32,1152]{1,0:T(8,128)(2,1)S(1)} %get-tuple-element.28), channel_id=1, source_target_pairs={{0,4},{4,8},{8,12},{12,14},{14,10},{10,6},{6,2},{2,0},{1,5},{5,9},... | collective-permute-start | bytes 221192 | tf_op jit(solution)/shard_map/ppermute | solution.py:122
  28.9 1.9 %collective-permute-start.9 = (bf16[32,1152]{1,0:T(8,128)(2,1)S(1)}, bf16[32,1152]{1,0:T(8,128)(2,1)S(1)}, u32[]{:S(2)}, u32[]{:S(2)}) collective-permute-start(bf16[32,1152]{1,0:T(8,128)(2,1)S(1)} %get-tuple-element.29), channel_id=1, source_target_pairs={{0,4},{4,8},{8,12},{12,14},{14,10},{10,6},{6,2},{2,0},{1,5},{5,9},... | collective-permute-start | bytes 221192 | tf_op jit(solution)/shard_map/ppermute | solution.py:122
  31.2 1.8 %collective-permute-start.16 = (bf16[32,1152]{1,0:T(8,128)(2,1)S(1)}, bf16[32,1152]{1,0:T(8,128)(2,1)S(1)}, u32[]{:S(2)}, u32[]{:S(2)}) collective-permute-start(bf16[32,1152]{1,0:T(8,128)(2,1)S(1)} %get-tuple-element.39), channel_id=1, source_target_pairs={{0,4},{4,8},{8,12},{12,14},{14,10},{10,6},{6,2},{2,0},{1,5},{5,9},... | collective-permute-start | bytes 221192 | tf_op jit(solution)/shard_map/ppermute | solution.py:122
  33.4 2.5 %collective-permute-start.23 = (bf16[32,1152]{1,0:T(8,128)(2,1)S(1)}, bf16[32,1152]{1,0:T(8,128)(2,1)S(1)}, u32[]{:S(2)}, u32[]{:S(2)}) collective-permute-start(bf16[32,1152]{1,0:T(8,128)(2,1)S(1)} %get-tuple-element.40), channel_id=1, source_target_pairs={{0,4},{4,8},{8,12},{12,14},{14,10},{10,6},{6,2},{2,0},{1,5},{5,9},... | collective-permute-start | bytes 221192 | tf_op jit(solution)/shard_map/ppermute | solution.py:122
  36.0 2.0 %collective-permute-start.3 = (bf16[32,1152]{1,0:T(8,128)(2,1)S(1)}, bf16[32,1152]{1,0:T(8,128)(2,1)S(1)}, u32[]{:S(2)}, u32[]{:S(2)}) collective-permute-start(bf16[32,1152]{1,0:T(8,128)(2,1)S(1)} %get-tuple-element.25), channel_id=1, source_target_pairs={{0,4},{4,8},{8,12},{12,14},{14,10},{10,6},{6,2},{2,0},{1,5},{5,9},... | collective-permute-start | bytes 221192 | tf_op jit(solution)/shard_map/ppermute | solution.py:122
  38.1 2.1 %collective-permute-start.10 = (bf16[32,1152]{1,0:T(8,128)(2,1)S(1)}, bf16[32,1152]{1,0:T(8,128)(2,1)S(1)}, u32[]{:S(2)}, u32[]{:S(2)}) collective-permute-start(bf16[32,1152]{1,0:T(8,128)(2,1)S(1)} %get-tuple-element.26), channel_id=1, source_target_pairs={{0,4},{4,8},{8,12},{12,14},{14,10},{10,6},{6,2},{2,0},{1,5},{5,9},... | collective-permute-start | bytes 221192 | tf_op jit(solution)/shard_map/ppermute | solution.py:122
  40.7 1.8 %collective-permute-start.17 = (bf16[32,1152]{1,0:T(8,128)(2,1)S(1)}, bf16[32,1152]{1,0:T(8,128)(2,1)S(1)}, u32[]{:S(2)}, u32[]{:S(2)}) collective-permute-start(bf16[32,1152]{1,0:T(8,128)(2,1)S(1)} %get-tuple-element.36), channel_id=1, source_target_pairs={{0,4},{4,8},{8,12},{12,14},{14,10},{10,6},{6,2},{2,0},{1,5},{5,9},... | collective-permute-start | bytes 221192 | tf_op jit(solution)/shard_map/ppermute | solution.py:122
  48.5 2.3 %collective-permute-done.13 = bf16[32,1152]{1,0:T(8,128)(2,1)S(1)} collective-permute-done((bf16[32,1152]{1,0:T(8,128)(2,1)S(1)}, bf16[32,1152]{1,0:T(8,128)(2,1)S(1)}, u32[]{:S(2)}, u32[]{:S(2)}) %collective-permute-start.13) | collective-permute-done | bytes 73760 | tf_op jit(solution)/shard_map/ppermute | solution.py:124
  51.3 3.8 %collective-permute-done.27 = bf16[32,1152]{1,0:T(8,128)(2,1)S(1)} collective-permute-done((bf16[32,1152]{1,0:T(8,128)(2,1)S(1)}, bf16[32,1152]{1,0:T(8,128)(2,1)S(1)}, u32[]{:S(2)}, u32[]{:S(2)}) %collective-permute-start.27) | collective-permute-done | bytes 73760 | tf_op jit(solution)/shard_map/ppermute | solution.py:124
  67.5 1.9 %fusion.27 = f32[2,16,2,16,128]{4,3,1,2,0:T(8,128)S(1)} fusion(bf16[2,1536,2,128,1]{3,2,1,0,4:T(2,128)(2,1)S(1)} %bitcast.64, f32[2,2,16,16,1536]{4,3,2,1,0:T(8,128)S(1)} %get-tuple-element.65, f32[2,2,16,16]{2,3,1,0:T(8,128)S(1)} %max.7, pred[2,1536]{1,0:T(4,128)(4,1)S(1)} %iota_compare_fusion.8), kind=kOutput, calls=%fused_computation.27 | convolution fusion | flops 408944640 | bytes 8395776 | tf_op jit(solution)/shard_map/vmap(kgnc,ckd->nkgd)/dot_general | solution.py:45
  70.5 2.2 %collective-permute-start.29 = (bf16[32,1024]{1,0:T(8,128)(2,1)S(1)}, bf16[32,1024]{1,0:T(8,128)(2,1)S(1)}, u32[]{:S(2)}, u32[]{:S(2)}) collective-permute-start(bf16[32,1024]{1,0:T(8,128)(2,1)S(1)} %get-tuple-element.46), channel_id=1, source_target_pairs={{0,4},{4,8},{8,12},{12,14},{14,10},{10,6},{6,2},{2,0},{1,5},{5,9},... | collective-permute-start | bytes 196616 | tf_op jit(solution)/shard_map/ppermute | solution.py:138
  72.7 2.0 %collective-permute-start.50 = (bf16[32,1024]{1,0:T(8,128)(2,1)S(1)}, bf16[32,1024]{1,0:T(8,128)(2,1)S(1)}, u32[]{:S(2)}, u32[]{:S(2)}) collective-permute-start(bf16[32,1024]{1,0:T(8,128)(2,1)S(1)} %get-tuple-element.51), channel_id=1, source_target_pairs={{0,4},{4,8},{8,12},{12,14},{14,10},{10,6},{6,2},{2,0},{1,5},{5,9},... | collective-permute-start | bytes 196616 | tf_op jit(solution)/shard_map/ppermute | solution.py:138
  75.4 2.1 %collective-permute-start.43 = (bf16[32,1024]{1,0:T(8,128)(2,1)S(1)}, bf16[32,1024]{1,0:T(8,128)(2,1)S(1)}, u32[]{:S(2)}, u32[]{:S(2)}) collective-permute-start(bf16[32,1024]{1,0:T(8,128)(2,1)S(1)} %get-tuple-element.52), channel_id=1, source_target_pairs={{0,4},{4,8},{8,12},{12,14},{14,10},{10,6},{6,2},{2,0},{1,5},{5,9},... | collective-permute-start | bytes 196616 | tf_op jit(solution)/shard_map/ppermute | solution.py:138
  77.6 2.0 %collective-permute-start.36 = (bf16[32,1024]{1,0:T(8,128)(2,1)S(1)}, bf16[32,1024]{1,0:T(8,128)(2,1)S(1)}, u32[]{:S(2)}, u32[]{:S(2)}) collective-permute-start(bf16[32,1024]{1,0:T(8,128)(2,1)S(1)} %get-tuple-element.53), channel_id=1, source_target_pairs={{0,4},{4,8},{8,12},{12,14},{14,10},{10,6},{6,2},{2,0},{1,5},{5,9},... | collective-permute-start | bytes 196616 | tf_op jit(solution)/shard_map/ppermute | solution.py:138
  79.8 2.2 %collective-permute-start.31 = (bf16[32,1024]{1,0:T(8,128)(2,1)S(1)}, bf16[32,1024]{1,0:T(8,128)(2,1)S(1)}, u32[]{:S(2)}, u32[]{:S(2)}) collective-permute-start(bf16[32,1024]{1,0:T(8,128)(2,1)S(1)} %collective-permute-done.29), channel_id=1, source_target_pairs={{0,4},{4,8},{8,12},{12,14},{14,10},{10,6},{6,2},{2,0},{1,5},{5,9},... | collective-permute-start | bytes 196616 | tf_op jit(solution)/shard_map/ppermute | solution.py:138
  82.0 2.1 %collective-permute-start.52 = (bf16[32,1024]{1,0:T(8,128)(2,1)S(1)}, bf16[32,1024]{1,0:T(8,128)(2,1)S(1)}, u32[]{:S(2)}, u32[]{:S(2)}) collective-permute-start(bf16[32,1024]{1,0:T(8,128)(2,1)S(1)} %collective-permute-done.50), channel_id=1, source_target_pairs={{0,4},{4,8},{8,12},{12,14},{14,10},{10,6},{6,2},{2,0},{1,5},{5,9},... | collective-permute-start | bytes 196616 | tf_op jit(solution)/shard_map/ppermute | solution.py:138
  86.9 2.1 %collective-permute-start.38 = (bf16[32,1024]{1,0:T(8,128)(2,1)S(1)}, bf16[32,1024]{1,0:T(8,128)(2,1)S(1)}, u32[]{:S(2)}, u32[]{:S(2)}) collective-permute-start(bf16[32,1024]{1,0:T(8,128)(2,1)S(1)} %collective-permute-done.36), channel_id=1, source_target_pairs={{0,4},{4,8},{8,12},{12,14},{14,10},{10,6},{6,2},{2,0},{1,5},{5,9},... | collective-permute-start | bytes 196616 | tf_op jit(solution)/shard_map/ppermute | solution.py:138
  91.6 1.7 %collective-permute-start.54 = (bf16[32,1024]{1,0:T(8,128)(2,1)S(1)}, bf16[32,1024]{1,0:T(8,128)(2,1)S(1)}, u32[]{:S(2)}, u32[]{:S(2)}) collective-permute-start(bf16[32,1024]{1,0:T(8,128)(2,1)S(1)} %collective-permute-done.52), channel_id=1, source_target_pairs={{0,4},{4,8},{8,12},{12,14},{14,10},{10,6},{6,2},{2,0},{1,5},{5,9},... | collective-permute-start | bytes 196616 | tf_op jit(solution)/shard_map/ppermute | solution.py:138
  93.8 1.7 %collective-permute-start.47 = (bf16[32,1024]{1,0:T(8,128)(2,1)S(1)}, bf16[32,1024]{1,0:T(8,128)(2,1)S(1)}, u32[]{:S(2)}, u32[]{:S(2)}) collective-permute-start(bf16[32,1024]{1,0:T(8,128)(2,1)S(1)} %collective-permute-done.45), channel_id=1, source_target_pairs={{0,4},{4,8},{8,12},{12,14},{14,10},{10,6},{6,2},{2,0},{1,5},{5,9},... | collective-permute-start | bytes 196616 | tf_op jit(solution)/shard_map/ppermute | solution.py:138
  95.9 1.7 %collective-permute-start.40 = (bf16[32,1024]{1,0:T(8,128)(2,1)S(1)}, bf16[32,1024]{1,0:T(8,128)(2,1)S(1)}, u32[]{:S(2)}, u32[]{:S(2)}) collective-permute-start(bf16[32,1024]{1,0:T(8,128)(2,1)S(1)} %collective-permute-done.38), channel_id=1, source_target_pairs={{0,4},{4,8},{8,12},{12,14},{14,10},{10,6},{6,2},{2,0},{1,5},{5,9},... | collective-permute-start | bytes 196616 | tf_op jit(solution)/shard_map/ppermute | solution.py:138
  97.6 1.9 %collective-permute-start.35 = (bf16[32,1024]{1,0:T(8,128)(2,1)S(1)}, bf16[32,1024]{1,0:T(8,128)(2,1)S(1)}, u32[]{:S(2)}, u32[]{:S(2)}) collective-permute-start(bf16[32,1024]{1,0:T(8,128)(2,1)S(1)} %collective-permute-done.33), channel_id=1, source_target_pairs={{0,4},{4,8},{8,12},{12,14},{14,10},{10,6},{6,2},{2,0},{1,5},{5,9},... | collective-permute-start | bytes 196616 | tf_op jit(solution)/shard_map/ppermute | solution.py:138
  101.9 1.9 %collective-permute-start.42 = (bf16[32,1024]{1,0:T(8,128)(2,1)S(1)}, bf16[32,1024]{1,0:T(8,128)(2,1)S(1)}, u32[]{:S(2)}, u32[]{:S(2)}) collective-permute-start(bf16[32,1024]{1,0:T(8,128)(2,1)S(1)} %collective-permute-done.40), channel_id=1, source_target_pairs={{0,4},{4,8},{8,12},{12,14},{14,10},{10,6},{6,2},{2,0},{1,5},{5,9},... | collective-permute-start | bytes 196616 | tf_op jit(solution)/shard_map/ppermute | solution.py:138
  104.6 1.6 %collective-permute-done.42 = bf16[32,1024]{1,0:T(8,128)(2,1)S(1)} collective-permute-done((bf16[32,1024]{1,0:T(8,128)(2,1)S(1)}, bf16[32,1024]{1,0:T(8,128)(2,1)S(1)}, u32[]{:S(2)}, u32[]{:S(2)}) %collective-permute-start.42) | collective-permute-done | bytes 65568 | tf_op jit(solution)/shard_map/ppermute | solution.py:138
  107.0 8.3 %fusion.66 = f32[256,2048]{1,0:T(8,128)S(1)} fusion(bf16[256,4096]{1,0:T(8,128)(2,1)S(1)} %convolution_convert_fusion, bf16[4096,2048]{1,0:T(8,128)(2,1)} %param.15), kind=kOutput, calls=%fused_computation.185 | convolution fusion | flops 4294967296 | bytes 20971520 | tf_op jit(solution)/shard_map/dot_general | solution.py:257
  115.4 1.9 %collective-permute-done.57 = bf16[128,2048]{1,0:T(8,128)(2,1)S(1)} collective-permute-done((bf16[128,2048]{1,0:T(8,128)(2,1)S(1)}, bf16[128,2048]{1,0:T(8,128)(2,1)S(1)}, u32[]{:S(2)}, u32[]{:S(2)}) %collective-permute-start.57) | collective-permute-done | bytes 524320 | tf_op jit(solution)/shard_map/ppermute | solution.py:258
  (196 shorter events, 40.9 us)
Async XLA Ops:
  0.0 5.1 %collective-permute-start = (bf16[128,2048]{1,0:T(8,128)(2,1)}, bf16[128,2048]{1,0:T(8,128)(2,1)S(1)}, u32[]{:S(2)}, u32[]{:S(2)}) collective-permute-start(bf16[128,2048]{1,0:T(8,128)(2,1)} %param.11), channel_id=1, source_target_pairs={{0,1},{1,0},{2,3},{3,2},{4,5},{5,4},{6,7},{7,6},{8,9},{9,8},{10,11... | collective-permute-start | bytes 1572872 | tf_op jit(solution)/shard_map/ppermute | solution.py:166
  16.7 6.9 %collective-permute-start.8 = (bf16[32,1152]{1,0:T(8,128)(2,1)S(1)}, bf16[32,1152]{1,0:T(8,128)(2,1)S(1)}, u32[]{:S(2)}, u32[]{:S(2)}) collective-permute-start(bf16[32,1152]{1,0:T(8,128)(2,1)S(1)} %get-tuple-element.16), channel_id=1, source_target_pairs={{0,4},{4,8},{8,12},{12,14},{14,10},{10,6},{6,2},{2,0},{1,5},{5,9},... | collective-permute-start | bytes 221192 | tf_op jit(solution)/shard_map/ppermute | solution.py:122
  19.4 21.2 %collective-permute-start.12 = (bf16[32,1152]{1,0:T(8,128)(2,1)S(1)}, bf16[32,1152]{1,0:T(8,128)(2,1)S(1)}, u32[]{:S(2)}, u32[]{:S(2)}) collective-permute-start(bf16[32,1152]{1,0:T(8,128)(2,1)S(1)} %get-tuple-element.17), channel_id=1, source_target_pairs={{0,2},{4,0},{8,4},{12,8},{14,12},{10,14},{6,10},{2,6},{1,3},{5,1},... | collective-permute-start | bytes 221192 | tf_op jit(solution)/shard_map/ppermute | solution.py:124
  21.4 5.0 %collective-permute-start.5 = (bf16[32,1152]{1,0:T(8,128)(2,1)S(1)}, bf16[32,1152]{1,0:T(8,128)(2,1)S(1)}, u32[]{:S(2)}, u32[]{:S(2)}) collective-permute-start(bf16[32,1152]{1,0:T(8,128)(2,1)S(1)} %get-tuple-element.32), channel_id=1, source_target_pairs={{0,2},{4,0},{8,4},{12,8},{14,12},{10,14},{6,10},{2,6},{1,3},{5,1},... | collective-permute-start | bytes 221192 | tf_op jit(solution)/shard_map/ppermute | solution.py:124
  21.5 5.0 %collective-permute-start.22 = (bf16[32,1152]{1,0:T(8,128)(2,1)S(1)}, bf16[32,1152]{1,0:T(8,128)(2,1)S(1)}, u32[]{:S(2)}, u32[]{:S(2)}) collective-permute-start(bf16[32,1152]{1,0:T(8,128)(2,1)S(1)} %get-tuple-element.20), channel_id=1, source_target_pairs={{0,4},{4,8},{8,12},{12,14},{14,10},{10,6},{6,2},{2,0},{1,5},{5,9},... | collective-permute-start | bytes 221192 | tf_op jit(solution)/shard_map/ppermute | solution.py:122
  23.6 21.1 %collective-permute-start.26 = (bf16[32,1152]{1,0:T(8,128)(2,1)S(1)}, bf16[32,1152]{1,0:T(8,128)(2,1)S(1)}, u32[]{:S(2)}, u32[]{:S(2)}) collective-permute-start(bf16[32,1152]{1,0:T(8,128)(2,1)S(1)} %get-tuple-element.21), channel_id=1, source_target_pairs={{0,2},{4,0},{8,4},{12,8},{14,12},{10,14},{6,10},{2,6},{1,3},{5,1},... | collective-permute-start | bytes 221192 | tf_op jit(solution)/shard_map/ppermute | solution.py:124
  24.0 4.9 %collective-permute-start.15 = (bf16[32,1152]{1,0:T(8,128)(2,1)S(1)}, bf16[32,1152]{1,0:T(8,128)(2,1)S(1)}, u32[]{:S(2)}, u32[]{:S(2)}) collective-permute-start(bf16[32,1152]{1,0:T(8,128)(2,1)S(1)} %get-tuple-element.42), channel_id=1, source_target_pairs={{0,4},{4,8},{8,12},{12,14},{14,10},{10,6},{6,2},{2,0},{1,5},{5,9},... | collective-permute-start | bytes 221192 | tf_op jit(solution)/shard_map/ppermute | solution.py:122
  30.9 5.0 %collective-permute-start.6 = (bf16[32,1152]{1,0:T(8,128)(2,1)S(1)}, bf16[32,1152]{1,0:T(8,128)(2,1)S(1)}, u32[]{:S(2)}, u32[]{:S(2)}) collective-permute-start(bf16[32,1152]{1,0:T(8,128)(2,1)S(1)} %get-tuple-element.30), channel_id=1, source_target_pairs={{0,2},{4,0},{8,4},{12,8},{14,12},{10,14},{6,10},{2,6},{1,3},{5,1},... | collective-permute-start | bytes 221192 | tf_op jit(solution)/shard_map/ppermute | solution.py:124
  36.0 6.4 %collective-permute-start.3 = (bf16[32,1152]{1,0:T(8,128)(2,1)S(1)}, bf16[32,1152]{1,0:T(8,128)(2,1)S(1)}, u32[]{:S(2)}, u32[]{:S(2)}) collective-permute-start(bf16[32,1152]{1,0:T(8,128)(2,1)S(1)} %get-tuple-element.25), channel_id=1, source_target_pairs={{0,4},{4,8},{8,12},{12,14},{14,10},{10,6},{6,2},{2,0},{1,5},{5,9},... | collective-permute-start | bytes 221192 | tf_op jit(solution)/shard_map/ppermute | solution.py:122
  38.1 5.9 %collective-permute-start.10 = (bf16[32,1152]{1,0:T(8,128)(2,1)S(1)}, bf16[32,1152]{1,0:T(8,128)(2,1)S(1)}, u32[]{:S(2)}, u32[]{:S(2)}) collective-permute-start(bf16[32,1152]{1,0:T(8,128)(2,1)S(1)} %get-tuple-element.26), channel_id=1, source_target_pairs={{0,4},{4,8},{8,12},{12,14},{14,10},{10,6},{6,2},{2,0},{1,5},{5,9},... | collective-permute-start | bytes 221192 | tf_op jit(solution)/shard_map/ppermute | solution.py:122
  40.3 15.3 %collective-permute-start.7 = (bf16[32,1152]{1,0:T(8,128)(2,1)S(1)}, bf16[32,1152]{1,0:T(8,128)(2,1)S(1)}, u32[]{:S(2)}, u32[]{:S(2)}) collective-permute-start(bf16[32,1152]{1,0:T(8,128)(2,1)S(1)} %get-tuple-element.27), channel_id=1, source_target_pairs={{0,2},{4,0},{8,4},{12,8},{14,12},{10,14},{6,10},{2,6},{1,3},{5,1},... | collective-permute-start | bytes 221192 | tf_op jit(solution)/shard_map/ppermute | solution.py:124
  40.7 5.5 %collective-permute-start.17 = (bf16[32,1152]{1,0:T(8,128)(2,1)S(1)}, bf16[32,1152]{1,0:T(8,128)(2,1)S(1)}, u32[]{:S(2)}, u32[]{:S(2)}) collective-permute-start(bf16[32,1152]{1,0:T(8,128)(2,1)S(1)} %get-tuple-element.36), channel_id=1, source_target_pairs={{0,4},{4,8},{8,12},{12,14},{14,10},{10,6},{6,2},{2,0},{1,5},{5,9},... | collective-permute-start | bytes 221192 | tf_op jit(solution)/shard_map/ppermute | solution.py:122
  44.0 15.5 %collective-permute-start.21 = (bf16[32,1152]{1,0:T(8,128)(2,1)S(1)}, bf16[32,1152]{1,0:T(8,128)(2,1)S(1)}, u32[]{:S(2)}, u32[]{:S(2)}) collective-permute-start(bf16[32,1152]{1,0:T(8,128)(2,1)S(1)} %get-tuple-element.38), channel_id=1, source_target_pairs={{0,2},{4,0},{8,4},{12,8},{14,12},{10,14},{6,10},{2,6},{1,3},{5,1},... | collective-permute-start | bytes 221192 | tf_op jit(solution)/shard_map/ppermute | solution.py:124
  44.6 12.6 %collective-permute-start.11 = (bf16[32,1152]{1,0:T(8,128)(2,1)S(1)}, bf16[32,1152]{1,0:T(8,128)(2,1)S(1)}, u32[]{:S(2)}, u32[]{:S(2)}) collective-permute-start(bf16[32,1152]{1,0:T(8,128)(2,1)S(1)} %get-tuple-element.14), channel_id=1, source_target_pairs={{0,4},{4,8},{8,12},{12,14},{14,10},{10,6},{6,2},{2,0},{1,5},{5,9},... | collective-permute-start | bytes 221192 | tf_op jit(solution)/shard_map/ppermute | solution.py:122
  46.9 11.9 %collective-permute-start.4 = (bf16[32,1152]{1,0:T(8,128)(2,1)S(1)}, bf16[32,1152]{1,0:T(8,128)(2,1)S(1)}, u32[]{:S(2)}, u32[]{:S(2)}) collective-permute-start(bf16[32,1152]{1,0:T(8,128)(2,1)S(1)} %get-tuple-element.24), channel_id=1, source_target_pairs={{0,4},{4,8},{8,12},{12,14},{14,10},{10,6},{6,2},{2,0},{1,5},{5,9},... | collective-permute-start | bytes 221192 | tf_op jit(solution)/shard_map/ppermute | solution.py:122
  70.0 7.5 %collective-permute-start.30 = (bf16[32,1024]{1,0:T(8,128)(2,1)S(1)}, bf16[32,1024]{1,0:T(8,128)(2,1)S(1)}, u32[]{:S(2)}, u32[]{:S(2)}) collective-permute-start(bf16[32,1024]{1,0:T(8,128)(2,1)S(1)} %get-tuple-element.46), channel_id=1, source_target_pairs={{0,2},{4,0},{8,4},{12,8},{14,12},{10,14},{6,10},{2,6},{1,3},{5,1},... | collective-permute-start | bytes 196616 | tf_op jit(solution)/shard_map/ppermute | solution.py:141
  70.5 4.9 %collective-permute-start.29 = (bf16[32,1024]{1,0:T(8,128)(2,1)S(1)}, bf16[32,1024]{1,0:T(8,128)(2,1)S(1)}, u32[]{:S(2)}, u32[]{:S(2)}) collective-permute-start(bf16[32,1024]{1,0:T(8,128)(2,1)S(1)} %get-tuple-element.46), channel_id=1, source_target_pairs={{0,4},{4,8},{8,12},{12,14},{14,10},{10,6},{6,2},{2,0},{1,5},{5,9},... | collective-permute-start | bytes 196616 | tf_op jit(solution)/shard_map/ppermute | solution.py:138
  72.7 7.0 %collective-permute-start.51 = (bf16[32,1024]{1,0:T(8,128)(2,1)S(1)}, bf16[32,1024]{1,0:T(8,128)(2,1)S(1)}, u32[]{:S(2)}, u32[]{:S(2)}) collective-permute-start(bf16[32,1024]{1,0:T(8,128)(2,1)S(1)} %get-tuple-element.51), channel_id=1, source_target_pairs={{0,2},{4,0},{8,4},{12,8},{14,12},{10,14},{6,10},{2,6},{1,3},{5,1},... | collective-permute-start | bytes 196616 | tf_op jit(solution)/shard_map/ppermute | solution.py:141
  72.7 4.9 %collective-permute-start.50 = (bf16[32,1024]{1,0:T(8,128)(2,1)S(1)}, bf16[32,1024]{1,0:T(8,128)(2,1)S(1)}, u32[]{:S(2)}, u32[]{:S(2)}) collective-permute-start(bf16[32,1024]{1,0:T(8,128)(2,1)S(1)} %get-tuple-element.51), channel_id=1, source_target_pairs={{0,4},{4,8},{8,12},{12,14},{14,10},{10,6},{6,2},{2,0},{1,5},{5,9},... | collective-permute-start | bytes 196616 | tf_op jit(solution)/shard_map/ppermute | solution.py:138
  75.0 6.9 %collective-permute-start.44 = (bf16[32,1024]{1,0:T(8,128)(2,1)S(1)}, bf16[32,1024]{1,0:T(8,128)(2,1)S(1)}, u32[]{:S(2)}, u32[]{:S(2)}) collective-permute-start(bf16[32,1024]{1,0:T(8,128)(2,1)S(1)} %get-tuple-element.52), channel_id=1, source_target_pairs={{0,2},{4,0},{8,4},{12,8},{14,12},{10,14},{6,10},{2,6},{1,3},{5,1},... | collective-permute-start | bytes 196616 | tf_op jit(solution)/shard_map/ppermute | solution.py:141
  77.5 6.6 %collective-permute-start.37 = (bf16[32,1024]{1,0:T(8,128)(2,1)S(1)}, bf16[32,1024]{1,0:T(8,128)(2,1)S(1)}, u32[]{:S(2)}, u32[]{:S(2)}) collective-permute-start(bf16[32,1024]{1,0:T(8,128)(2,1)S(1)} %get-tuple-element.53), channel_id=1, source_target_pairs={{0,2},{4,0},{8,4},{12,8},{14,12},{10,14},{6,10},{2,6},{1,3},{5,1},... | collective-permute-start | bytes 196616 | tf_op jit(solution)/shard_map/ppermute | solution.py:141
  79.7 6.6 %collective-permute-start.32 = (bf16[32,1024]{1,0:T(8,128)(2,1)S(1)}, bf16[32,1024]{1,0:T(8,128)(2,1)S(1)}, u32[]{:S(2)}, u32[]{:S(2)}) collective-permute-start(bf16[32,1024]{1,0:T(8,128)(2,1)S(1)} %collective-permute-done.30), channel_id=1, source_target_pairs={{0,2},{4,0},{8,4},{12,8},{14,12},{10,14},{6,10},{2,6},{1,3},{5,1},... | collective-permute-start | bytes 196616 | tf_op jit(solution)/shard_map/ppermute | solution.py:141
  79.8 5.0 %collective-permute-start.31 = (bf16[32,1024]{1,0:T(8,128)(2,1)S(1)}, bf16[32,1024]{1,0:T(8,128)(2,1)S(1)}, u32[]{:S(2)}, u32[]{:S(2)}) collective-permute-start(bf16[32,1024]{1,0:T(8,128)(2,1)S(1)} %collective-permute-done.29), channel_id=1, source_target_pairs={{0,4},{4,8},{8,12},{12,14},{14,10},{10,6},{6,2},{2,0},{1,5},{5,9},... | collective-permute-start | bytes 196616 | tf_op jit(solution)/shard_map/ppermute | solution.py:138
  81.9 7.1 %collective-permute-start.53 = (bf16[32,1024]{1,0:T(8,128)(2,1)S(1)}, bf16[32,1024]{1,0:T(8,128)(2,1)S(1)}, u32[]{:S(2)}, u32[]{:S(2)}) collective-permute-start(bf16[32,1024]{1,0:T(8,128)(2,1)S(1)} %collective-permute-done.51), channel_id=1, source_target_pairs={{0,2},{4,0},{8,4},{12,8},{14,12},{10,14},{6,10},{2,6},{1,3},{5,1},... | collective-permute-start | bytes 196616 | tf_op jit(solution)/shard_map/ppermute | solution.py:141
  84.1 7.1 %collective-permute-start.46 = (bf16[32,1024]{1,0:T(8,128)(2,1)S(1)}, bf16[32,1024]{1,0:T(8,128)(2,1)S(1)}, u32[]{:S(2)}, u32[]{:S(2)}) collective-permute-start(bf16[32,1024]{1,0:T(8,128)(2,1)S(1)} %collective-permute-done.44), channel_id=1, source_target_pairs={{0,2},{4,0},{8,4},{12,8},{14,12},{10,14},{6,10},{2,6},{1,3},{5,1},... | collective-permute-start | bytes 196616 | tf_op jit(solution)/shard_map/ppermute | solution.py:141
  86.3 7.1 %collective-permute-start.39 = (bf16[32,1024]{1,0:T(8,128)(2,1)S(1)}, bf16[32,1024]{1,0:T(8,128)(2,1)S(1)}, u32[]{:S(2)}, u32[]{:S(2)}) collective-permute-start(bf16[32,1024]{1,0:T(8,128)(2,1)S(1)} %collective-permute-done.37), channel_id=1, source_target_pairs={{0,2},{4,0},{8,4},{12,8},{14,12},{10,14},{6,10},{2,6},{1,3},{5,1},... | collective-permute-start | bytes 196616 | tf_op jit(solution)/shard_map/ppermute | solution.py:141
  89.0 6.5 %collective-permute-start.34 = (bf16[32,1024]{1,0:T(8,128)(2,1)S(1)}, bf16[32,1024]{1,0:T(8,128)(2,1)S(1)}, u32[]{:S(2)}, u32[]{:S(2)}) collective-permute-start(bf16[32,1024]{1,0:T(8,128)(2,1)S(1)} %collective-permute-done.32), channel_id=1, source_target_pairs={{0,2},{4,0},{8,4},{12,8},{14,12},{10,14},{6,10},{2,6},{1,3},{5,1},... | collective-permute-start | bytes 196616 | tf_op jit(solution)/shard_map/ppermute | solution.py:141
  91.2 6.5 %collective-permute-start.55 = (bf16[32,1024]{1,0:T(8,128)(2,1)S(1)}, bf16[32,1024]{1,0:T(8,128)(2,1)S(1)}, u32[]{:S(2)}, u32[]{:S(2)}) collective-permute-start(bf16[32,1024]{1,0:T(8,128)(2,1)S(1)} %collective-permute-done.53), channel_id=1, source_target_pairs={{0,2},{4,0},{8,4},{12,8},{14,12},{10,14},{6,10},{2,6},{1,3},{5,1},... | collective-permute-start | bytes 196616 | tf_op jit(solution)/shard_map/ppermute | solution.py:141
  93.3 8.6 %collective-permute-start.48 = (bf16[32,1024]{1,0:T(8,128)(2,1)S(1)}, bf16[32,1024]{1,0:T(8,128)(2,1)S(1)}, u32[]{:S(2)}, u32[]{:S(2)}) collective-permute-start(bf16[32,1024]{1,0:T(8,128)(2,1)S(1)} %collective-permute-done.46), channel_id=1, source_target_pairs={{0,2},{4,0},{8,4},{12,8},{14,12},{10,14},{6,10},{2,6},{1,3},{5,1},... | collective-permute-start | bytes 196616 | tf_op jit(solution)/shard_map/ppermute | solution.py:141
  93.8 5.7 %collective-permute-start.47 = (bf16[32,1024]{1,0:T(8,128)(2,1)S(1)}, bf16[32,1024]{1,0:T(8,128)(2,1)S(1)}, u32[]{:S(2)}, u32[]{:S(2)}) collective-permute-start(bf16[32,1024]{1,0:T(8,128)(2,1)S(1)} %collective-permute-done.45), channel_id=1, source_target_pairs={{0,4},{4,8},{8,12},{12,14},{14,10},{10,6},{6,2},{2,0},{1,5},{5,9},... | collective-permute-start | bytes 196616 | tf_op jit(solution)/shard_map/ppermute | solution.py:138
  95.5 8.3 %collective-permute-start.41 = (bf16[32,1024]{1,0:T(8,128)(2,1)S(1)}, bf16[32,1024]{1,0:T(8,128)(2,1)S(1)}, u32[]{:S(2)}, u32[]{:S(2)}) collective-permute-start(bf16[32,1024]{1,0:T(8,128)(2,1)S(1)} %collective-permute-done.39), channel_id=1, source_target_pairs={{0,2},{4,0},{8,4},{12,8},{14,12},{10,14},{6,10},{2,6},{1,3},{5,1},... | collective-permute-start | bytes 196616 | tf_op jit(solution)/shard_map/ppermute | solution.py:141
  97.6 6.2 %collective-permute-start.35 = (bf16[32,1024]{1,0:T(8,128)(2,1)S(1)}, bf16[32,1024]{1,0:T(8,128)(2,1)S(1)}, u32[]{:S(2)}, u32[]{:S(2)}) collective-permute-start(bf16[32,1024]{1,0:T(8,128)(2,1)S(1)} %collective-permute-done.33), channel_id=1, source_target_pairs={{0,4},{4,8},{8,12},{12,14},{14,10},{10,6},{6,2},{2,0},{1,5},{5,9},... | collective-permute-start | bytes 196616 | tf_op jit(solution)/shard_map/ppermute | solution.py:138
  (34 other events, 215.6 us)

commit v9 on v6

--- a/solution.py
+++ b/solution.py
@@ -183,11 +183,10 @@
         k_cols = key_matrix.shape[1] // n_kv
         k_part = jnp.dot(chosen, key_matrix, preferred_element_type=jnp.float32).astype(jnp.bfloat16)
         v_part = jnp.dot(chosen, value_matrix, preferred_element_type=jnp.float32).astype(jnp.bfloat16)
+        q_all = jnp.dot(chosen, q_weight, preferred_element_type=jnp.float32).astype(jnp.bfloat16)
         q_sums, k_sums, v_sums = [], [], []
         for h in range(n_kv):
-            q_part = jnp.dot(
-                chosen, q_weight[:, h * q_cols : (h + 1) * q_cols], preferred_element_type=jnp.float32
-            ).astype(jnp.bfloat16)
+            q_part = q_all[:, h * q_cols : (h + 1) * q_cols]
             joined = jnp.concatenate(
                 [q_part, k_part[:, h * k_cols : (h + 1) * k_cols], v_part[:, h * k_cols : (h + 1) * k_cols]],
                 axis=1,

time: 95 us -> 95.3 us (level)
  matrix products: 24.6 us -> 27.7 us
  local copies, waits for them, and re-layouts: 2.71 us -> 1.15 us
    ppermute x6, waiting for transfers between devices: 4.07 us -> 0.05 us  [ring_all_gather(): backward = lax.ppermute(backward, 'row', backward_pairs)]
    ppermute x8, waiting for transfers between devices: 6.05 us -> 9.39 us  [ring_all_gather(): forward = lax.ppermute(forward, 'row', forward_pairs)]
    unnamed x29, local copies, waits for them, and re-layouts: 1.95 us -> 0.25 us
    dot_general x1, matrix products: 0.48 us -> 2.15 us  [body(): jnp.dot(pick_other, other_tokens, preferred_element_type=jnp.float32)]
    dot_general x1, matrix products: 1.51 us -> 2.85 us  [body(): jnp.dot(pick_own, tokens, preferred_element_type=jnp.float32)]
    dot_general x2 -> x1, matrix products: 8.35 us -> 8.41 us  [body(): jnp.dot(chosen, q_weight, preferred_element_type=jnp.float32)]
  transfers between devices with their start and end apart: 30 -> 30, of which waited for: 20 -> 20; matrix products, arithmetic and copies ran while one was open for 6% -> 7% of each run, Pallas kernels for 0% -> 0%
where the time goes in v9:
time: 95.3 us; the launch traced here: 95.1 us
  starting transfers between devices  33.6 us (35%)
  matrix products  27.7 us (29%)
  waiting for transfers between devices  26.2 us (27%)
  other arithmetic  5.92 us (6%)
  local copies, waits for them, and re-layouts  1.15 us (1%)
    ppermute x8, starting transfers between devices, ring_reduce_scatter(): got_forward = lax.ppermute(forward, 'row', forward_pairs)  16.6 us
    ppermute x8, starting transfers between devices, ring_all_gather(): forward = lax.ppermute(forward, 'row', forward_pairs)  12.6 us
    ppermute x8, waiting for transfers between devices, ring_all_gather(): forward = lax.ppermute(forward, 'row', forward_pairs)  9.39 us
    ppermute x8, waiting for transfers between devices, ring_reduce_scatter(): got_forward = lax.ppermute(forward, 'row', forward_pairs)  8.84 us
    dot_general x1, matrix products, body(): jnp.dot(chosen, q_weight, preferred_element_type=jnp.float32)  8.41 us
    dot_general x1, matrix products, body(): products = jnp.dot(arranged, o_weight, preferred_element_type=jnp.float32)  8.31 us
    ppermute x6, waiting for transfers between devices, ring_reduce_scatter(): got_backward = lax.ppermute(backward, 'row', backward_pairs)  6.01 us
    ppermute x6, starting transfers between devices, ring_all_gather(): backward = lax.ppermute(backward, 'row', backward_pairs)  2.92 us
  transfers between devices with their start and end apart: 30, of which 20 were waited for; matrix products, arithmetic and copies ran while one was open for 7% of the time, Pallas kernels for 0%

profile of v9, /device:TPU:0, one launch (start us, length us, event | category | flops | bytes accessed | tf_op | source)
XLA Modules:
  0.0 95.1 jit_solution(10553263733180335332)
XLA Ops:
  2.3 2.9 %fusion.31 = f32[256,2048]{1,0:T(8,128)} fusion(bf16[128,2048]{1,0:T(8,128)(2,1)} %param.11, s32[256]{0:T(256)S(1)} %broadcast_select_fusion.1), kind=kOutput, calls=%fused_computation.59 | convolution fusion | flops 134250496 | bytes 2622464 | tf_op jit(solution)/shard_map/dot_general | solution.py:178
  5.8 2.1 %fusion.6 = bf16[256,2048]{1,0:T(8,128)(2,1)S(1)} fusion(f32[256,2048]{1,0:T(8,128)} %fusion.31, bf16[128,2048]{1,0:T(8,128)(2,1)S(1)} %collective-permute-done, s32[256]{0:T(256)S(1)} %get-tuple-element.11), kind=kOutput, calls=%fused_computation.11 | convolution fusion | flops 135299072 | bytes 3671040 | tf_op jit(solution)/shard_map/dot_general | solution.py:179
  8.9 8.4 %convolution_convert_fusion.1 = bf16[256,4096]{1,0:T(8,128)(2,1)S(1)} fusion(bf16[256,2048]{1,0:T(8,128)(2,1)S(1)} %fusion.6, bf16[2048,4096]{1,0:T(8,128)(2,1)} %param.12), kind=kOutput, calls=%fused_computation.5 | convolution fusion | flops 4296015872 | bytes 19922944 | tf_op jit(solution)/shard_map/dot_general | solution.py:186
  17.6 2.7 %collective-permute-start.1 = (bf16[32,2304]{1,0:T(8,128)(2,1)S(1)}, bf16[32,2304]{1,0:T(8,128)(2,1)S(1)}, u32[]{:S(2)}, u32[]{:S(2)}) collective-permute-start(bf16[32,2304]{1,0:T(8,128)(2,1)S(1)} %get-tuple-element.20), channel_id=1, source_target_pairs={{0,4},{4,8},{8,12},{12,14},{14,10},{10,6},{6,2},{2,0},{1,5},{5,9},... | collective-permute-start | bytes 442376 | tf_op jit(solution)/shard_map/ppermute | solution.py:122
  20.5 2.1 %collective-permute-start.8 = (bf16[32,2304]{1,0:T(8,128)(2,1)S(1)}, bf16[32,2304]{1,0:T(8,128)(2,1)S(1)}, u32[]{:S(2)}, u32[]{:S(2)}) collective-permute-start(bf16[32,2304]{1,0:T(8,128)(2,1)S(1)} %get-tuple-element.26), channel_id=1, source_target_pairs={{0,4},{4,8},{8,12},{12,14},{14,10},{10,6},{6,2},{2,0},{1,5},{5,9},... | collective-permute-start | bytes 442376 | tf_op jit(solution)/shard_map/ppermute | solution.py:122
  22.6 2.4 %collective-permute-done.1 = bf16[32,2304]{1,0:T(8,128)(2,1)S(1)} collective-permute-done((bf16[32,2304]{1,0:T(8,128)(2,1)S(1)}, bf16[32,2304]{1,0:T(8,128)(2,1)S(1)}, u32[]{:S(2)}, u32[]{:S(2)}) %collective-permute-start.1) | collective-permute-done | bytes 147488 | tf_op jit(solution)/shard_map/ppermute | solution.py:122
  25.1 2.1 %collective-permute-start.2 = (bf16[32,2304]{1,0:T(8,128)(2,1)S(1)}, bf16[32,2304]{1,0:T(8,128)(2,1)S(1)}, u32[]{:S(2)}, u32[]{:S(2)}) collective-permute-start(bf16[32,2304]{1,0:T(8,128)(2,1)S(1)} %add_convert_fusion.10), channel_id=1, source_target_pairs={{0,4},{4,8},{8,12},{12,14},{14,10},{10,6},{6,2},{2,0},{1,5},{5,9},... | collective-permute-start | bytes 442376 | tf_op jit(solution)/shard_map/ppermute | solution.py:122
  28.2 2.1 %collective-permute-start.9 = (bf16[32,2304]{1,0:T(8,128)(2,1)S(1)}, bf16[32,2304]{1,0:T(8,128)(2,1)S(1)}, u32[]{:S(2)}, u32[]{:S(2)}) collective-permute-start(bf16[32,2304]{1,0:T(8,128)(2,1)S(1)} %add_convert_fusion.5), channel_id=1, source_target_pairs={{0,4},{4,8},{8,12},{12,14},{14,10},{10,6},{6,2},{2,0},{1,5},{5,9},... | collective-permute-start | bytes 442376 | tf_op jit(solution)/shard_map/ppermute | solution.py:122
  30.4 1.3 %collective-permute-done.2 = bf16[32,2304]{1,0:T(8,128)(2,1)S(1)} collective-permute-done((bf16[32,2304]{1,0:T(8,128)(2,1)S(1)}, bf16[32,2304]{1,0:T(8,128)(2,1)S(1)}, u32[]{:S(2)}, u32[]{:S(2)}) %collective-permute-start.2) | collective-permute-done | bytes 147488 | tf_op jit(solution)/shard_map/ppermute | solution.py:122
  31.8 2.1 %collective-permute-start.3 = (bf16[32,2304]{1,0:T(8,128)(2,1)S(1)}, bf16[32,2304]{1,0:T(8,128)(2,1)S(1)}, u32[]{:S(2)}, u32[]{:S(2)}) collective-permute-start(bf16[32,2304]{1,0:T(8,128)(2,1)S(1)} %get-tuple-element.18), channel_id=1, source_target_pairs={{0,4},{4,8},{8,12},{12,14},{14,10},{10,6},{6,2},{2,0},{1,5},{5,9},... | collective-permute-start | bytes 442376 | tf_op jit(solution)/shard_map/ppermute | solution.py:122
  35.1 2.1 %collective-permute-start.10 = (bf16[32,2304]{1,0:T(8,128)(2,1)S(1)}, bf16[32,2304]{1,0:T(8,128)(2,1)S(1)}, u32[]{:S(2)}, u32[]{:S(2)}) collective-permute-start(bf16[32,2304]{1,0:T(8,128)(2,1)S(1)} %get-tuple-element.24), channel_id=1, source_target_pairs={{0,4},{4,8},{8,12},{12,14},{14,10},{10,6},{6,2},{2,0},{1,5},{5,9},... | collective-permute-start | bytes 442376 | tf_op jit(solution)/shard_map/ppermute | solution.py:122
  37.2 1.3 %collective-permute-done.3 = bf16[32,2304]{1,0:T(8,128)(2,1)S(1)} collective-permute-done((bf16[32,2304]{1,0:T(8,128)(2,1)S(1)}, bf16[32,2304]{1,0:T(8,128)(2,1)S(1)}, u32[]{:S(2)}, u32[]{:S(2)}) %collective-permute-start.3) | collective-permute-done | bytes 147488 | tf_op jit(solution)/shard_map/ppermute | solution.py:122
  38.5 2.1 %collective-permute-done.6 = bf16[32,2304]{1,0:T(8,128)(2,1)S(1)} collective-permute-done((bf16[32,2304]{1,0:T(8,128)(2,1)S(1)}, bf16[32,2304]{1,0:T(8,128)(2,1)S(1)}, u32[]{:S(2)}, u32[]{:S(2)}) %collective-permute-start.6) | collective-permute-done | bytes 147488 | tf_op jit(solution)/shard_map/ppermute | solution.py:124
  40.7 1.6 %collective-permute-start.4 = (bf16[32,2304]{1,0:T(8,128)(2,1)S(1)}, bf16[32,2304]{1,0:T(8,128)(2,1)S(1)}, u32[]{:S(2)}, u32[]{:S(2)}) collective-permute-start(bf16[32,2304]{1,0:T(8,128)(2,1)S(1)} %get-tuple-element.16), channel_id=1, source_target_pairs={{0,4},{4,8},{8,12},{12,14},{14,10},{10,6},{6,2},{2,0},{1,5},{5,9},... | collective-permute-start | bytes 442376 | tf_op jit(solution)/shard_map/ppermute | solution.py:122
  43.8 1.6 %collective-permute-start.11 = (bf16[32,2304]{1,0:T(8,128)(2,1)S(1)}, bf16[32,2304]{1,0:T(8,128)(2,1)S(1)}, u32[]{:S(2)}, u32[]{:S(2)}) collective-permute-start(bf16[32,2304]{1,0:T(8,128)(2,1)S(1)} %get-tuple-element.22), channel_id=1, source_target_pairs={{0,4},{4,8},{8,12},{12,14},{14,10},{10,6},{6,2},{2,0},{1,5},{5,9},... | collective-permute-start | bytes 442376 | tf_op jit(solution)/shard_map/ppermute | solution.py:122
  46.6 1.3 %collective-permute-done.7 = bf16[32,2304]{1,0:T(8,128)(2,1)S(1)} collective-permute-done((bf16[32,2304]{1,0:T(8,128)(2,1)S(1)}, bf16[32,2304]{1,0:T(8,128)(2,1)S(1)}, u32[]{:S(2)}, u32[]{:S(2)}) %collective-permute-start.7) | collective-permute-done | bytes 147488 | tf_op jit(solution)/shard_map/ppermute | solution.py:124
  49.0 1.6 %collective-permute-done.14 = bf16[32,2304]{1,0:T(8,128)(2,1)S(1)} collective-permute-done((bf16[32,2304]{1,0:T(8,128)(2,1)S(1)}, bf16[32,2304]{1,0:T(8,128)(2,1)S(1)}, u32[]{:S(2)}, u32[]{:S(2)}) %collective-permute-start.14) | collective-permute-done | bytes 147488 | tf_op jit(solution)/shard_map/ppermute | solution.py:124
  53.6 1.4 %fusion.1 = f32[2,2,16,16]{2,3,1,0:T(8,128)S(1)} fusion(f32[2,2,16,16,1536]{4,3,2,1,0:T(8,128)S(1)} %get-tuple-element.45, f32[2,2,16,16]{2,3,1,0:T(8,128)S(1)} %max.7, pred[2,1536]{1,0:T(4,128)(4,1)S(1)} %iota_compare_fusion.7), kind=kLoop, calls=%fused_computation.6 | loop fusion | flops 6290432 | bytes 6302720 | tf_op jit(solution)/shard_map/vmap()/reduce_sum | solution.py:44
  55.0 1.9 %fusion.13 = f32[2,16,2,16,128]{4,3,1,2,0:T(8,128)S(1)} fusion(bf16[2,1536,2,128,1]{3,2,1,0,4:T(2,128)(2,1)S(1)} %bitcast.64, f32[2,2,16,16,1536]{4,3,2,1,0:T(8,128)S(1)} %get-tuple-element.45, f32[2,2,16,16]{2,3,1,0:T(8,128)S(1)} %max.7, pred[2,1536]{1,0:T(4,128)(4,1)S(1)} %iota_compare_fusion.7), kind=kOutput, calls=%fused_computation.18 | convolution fusion | flops 408944640 | bytes 8395776 | tf_op jit(solution)/shard_map/vmap(kgnc,ckd->nkgd)/dot_general | solution.py:45
  57.5 1.6 %collective-permute-start.15 = (bf16[32,2048]{1,0:T(8,128)(2,1)S(1)}, bf16[32,2048]{1,0:T(8,128)(2,1)S(1)}, u32[]{:S(2)}, u32[]{:S(2)}) collective-permute-start(bf16[32,2048]{1,0:T(8,128)(2,1)S(1)} %get-tuple-element.30), channel_id=1, source_target_pairs={{0,4},{4,8},{8,12},{12,14},{14,10},{10,6},{6,2},{2,0},{1,5},{5,9},... | collective-permute-start | bytes 393224 | tf_op jit(solution)/shard_map/ppermute | solution.py:138
  59.6 1.6 %collective-permute-start.22 = (bf16[32,2048]{1,0:T(8,128)(2,1)S(1)}, bf16[32,2048]{1,0:T(8,128)(2,1)S(1)}, u32[]{:S(2)}, u32[]{:S(2)}) collective-permute-start(bf16[32,2048]{1,0:T(8,128)(2,1)S(1)} %get-tuple-element.33), channel_id=1, source_target_pairs={{0,4},{4,8},{8,12},{12,14},{14,10},{10,6},{6,2},{2,0},{1,5},{5,9},... | collective-permute-start | bytes 393224 | tf_op jit(solution)/shard_map/ppermute | solution.py:138
  61.9 2.0 %collective-permute-done.15 = bf16[32,2048]{1,0:T(8,128)(2,1)S(1)} collective-permute-done((bf16[32,2048]{1,0:T(8,128)(2,1)S(1)}, bf16[32,2048]{1,0:T(8,128)(2,1)S(1)}, u32[]{:S(2)}, u32[]{:S(2)}) %collective-permute-start.15) | collective-permute-done | bytes 131104 | tf_op jit(solution)/shard_map/ppermute | solution.py:138
  63.9 1.6 %collective-permute-start.17 = (bf16[32,2048]{1,0:T(8,128)(2,1)S(1)}, bf16[32,2048]{1,0:T(8,128)(2,1)S(1)}, u32[]{:S(2)}, u32[]{:S(2)}) collective-permute-start(bf16[32,2048]{1,0:T(8,128)(2,1)S(1)} %collective-permute-done.15), channel_id=1, source_target_pairs={{0,4},{4,8},{8,12},{12,14},{14,10},{10,6},{6,2},{2,0},{1,5},{5,9},... | collective-permute-start | bytes 393224 | tf_op jit(solution)/shard_map/ppermute | solution.py:138
  66.7 1.6 %collective-permute-start.24 = (bf16[32,2048]{1,0:T(8,128)(2,1)S(1)}, bf16[32,2048]{1,0:T(8,128)(2,1)S(1)}, u32[]{:S(2)}, u32[]{:S(2)}) collective-permute-start(bf16[32,2048]{1,0:T(8,128)(2,1)S(1)} %collective-permute-done.22), channel_id=1, source_target_pairs={{0,4},{4,8},{8,12},{12,14},{14,10},{10,6},{6,2},{2,0},{1,5},{5,9},... | collective-permute-start | bytes 393224 | tf_op jit(solution)/shard_map/ppermute | solution.py:138
  68.9 1.4 %collective-permute-done.17 = bf16[32,2048]{1,0:T(8,128)(2,1)S(1)} collective-permute-done((bf16[32,2048]{1,0:T(8,128)(2,1)S(1)}, bf16[32,2048]{1,0:T(8,128)(2,1)S(1)}, u32[]{:S(2)}, u32[]{:S(2)}) %collective-permute-start.17) | collective-permute-done | bytes 131104 | tf_op jit(solution)/shard_map/ppermute | solution.py:138
  70.2 1.6 %collective-permute-start.19 = (bf16[32,2048]{1,0:T(8,128)(2,1)S(1)}, bf16[32,2048]{1,0:T(8,128)(2,1)S(1)}, u32[]{:S(2)}, u32[]{:S(2)}) collective-permute-start(bf16[32,2048]{1,0:T(8,128)(2,1)S(1)} %collective-permute-done.17), channel_id=1, source_target_pairs={{0,4},{4,8},{8,12},{12,14},{14,10},{10,6},{6,2},{2,0},{1,5},{5,9},... | collective-permute-start | bytes 393224 | tf_op jit(solution)/shard_map/ppermute | solution.py:138
  73.1 1.6 %collective-permute-start.26 = (bf16[32,2048]{1,0:T(8,128)(2,1)S(1)}, bf16[32,2048]{1,0:T(8,128)(2,1)S(1)}, u32[]{:S(2)}, u32[]{:S(2)}) collective-permute-start(bf16[32,2048]{1,0:T(8,128)(2,1)S(1)} %collective-permute-done.24), channel_id=1, source_target_pairs={{0,4},{4,8},{8,12},{12,14},{14,10},{10,6},{6,2},{2,0},{1,5},{5,9},... | collective-permute-start | bytes 393224 | tf_op jit(solution)/shard_map/ppermute | solution.py:138
  75.9 1.6 %collective-permute-start.21 = (bf16[32,2048]{1,0:T(8,128)(2,1)S(1)}, bf16[32,2048]{1,0:T(8,128)(2,1)S(1)}, u32[]{:S(2)}, u32[]{:S(2)}) collective-permute-start(bf16[32,2048]{1,0:T(8,128)(2,1)S(1)} %collective-permute-done.19), channel_id=1, source_target_pairs={{0,4},{4,8},{8,12},{12,14},{14,10},{10,6},{6,2},{2,0},{1,5},{5,9},... | collective-permute-start | bytes 393224 | tf_op jit(solution)/shard_map/ppermute | solution.py:138
  78.1 1.6 %collective-permute-start.28 = (bf16[32,2048]{1,0:T(8,128)(2,1)S(1)}, bf16[32,2048]{1,0:T(8,128)(2,1)S(1)}, u32[]{:S(2)}, u32[]{:S(2)}) collective-permute-start(bf16[32,2048]{1,0:T(8,128)(2,1)S(1)} %collective-permute-done.26), channel_id=1, source_target_pairs={{0,4},{4,8},{8,12},{12,14},{14,10},{10,6},{6,2},{2,0},{1,5},{5,9},... | collective-permute-start | bytes 393224 | tf_op jit(solution)/shard_map/ppermute | solution.py:138
  80.9 2.1 %collective-permute-done.28 = bf16[32,2048]{1,0:T(8,128)(2,1)S(1)} collective-permute-done((bf16[32,2048]{1,0:T(8,128)(2,1)S(1)}, bf16[32,2048]{1,0:T(8,128)(2,1)S(1)}, u32[]{:S(2)}, u32[]{:S(2)}) %collective-permute-start.28) | collective-permute-done | bytes 131104 | tf_op jit(solution)/shard_map/ppermute | solution.py:138
  83.8 8.3 %fusion.54 = f32[256,2048]{1,0:T(8,128)S(1)} fusion(bf16[256,4096]{1,0:T(8,128)(2,1)S(1)} %convolution_convert_fusion, bf16[4096,2048]{1,0:T(8,128)(2,1)} %param.15), kind=kOutput, calls=%fused_computation.142 | convolution fusion | flops 4294967296 | bytes 20971520 | tf_op jit(solution)/shard_map/dot_general | solution.py:238
  92.3 1.9 %collective-permute-done.29 = bf16[128,2048]{1,0:T(8,128)(2,1)S(1)} collective-permute-done((bf16[128,2048]{1,0:T(8,128)(2,1)S(1)}, bf16[128,2048]{1,0:T(8,128)(2,1)S(1)}, u32[]{:S(2)}, u32[]{:S(2)}) %collective-permute-start.29) | collective-permute-done | bytes 524320 | tf_op jit(solution)/shard_map/ppermute | solution.py:239
  (128 shorter events, 22.8 us)
Async XLA Ops:
  0.0 51.3 %copy-start = (bf16[2,1536,2,128]{3,2,1,0:T(2,128)(2,1)S(1)}, bf16[2,1536,2,128]{3,2,1,0:T(2,128)(2,1)}, u32[]{:S(2)}) copy-start(bf16[2,1536,2,128]{3,2,1,0:T(2,128)(2,1)} %param.16) | copy-start | bytes 4718596
  0.0 5.8 %collective-permute-start = (bf16[128,2048]{1,0:T(8,128)(2,1)}, bf16[128,2048]{1,0:T(8,128)(2,1)S(1)}, u32[]{:S(2)}, u32[]{:S(2)}) collective-permute-start(bf16[128,2048]{1,0:T(8,128)(2,1)} %param.11), channel_id=1, source_target_pairs={{0,1},{1,0},{2,3},{3,2},{4,5},{5,4},{6,7},{7,6},{8,9},{9,8},{10,11... | collective-permute-start | bytes 1572872 | tf_op jit(solution)/shard_map/ppermute | solution.py:166
  17.6 7.4 %collective-permute-start.1 = (bf16[32,2304]{1,0:T(8,128)(2,1)S(1)}, bf16[32,2304]{1,0:T(8,128)(2,1)S(1)}, u32[]{:S(2)}, u32[]{:S(2)}) collective-permute-start(bf16[32,2304]{1,0:T(8,128)(2,1)S(1)} %get-tuple-element.20), channel_id=1, source_target_pairs={{0,4},{4,8},{8,12},{12,14},{14,10},{10,6},{6,2},{2,0},{1,5},{5,9},... | collective-permute-start | bytes 442376 | tf_op jit(solution)/shard_map/ppermute | solution.py:122
  20.4 10.0 %collective-permute-start.5 = (bf16[32,2304]{1,0:T(8,128)(2,1)S(1)}, bf16[32,2304]{1,0:T(8,128)(2,1)S(1)}, u32[]{:S(2)}, u32[]{:S(2)}) collective-permute-start(bf16[32,2304]{1,0:T(8,128)(2,1)S(1)} %get-tuple-element.21), channel_id=1, source_target_pairs={{0,2},{4,0},{8,4},{12,8},{14,12},{10,14},{6,10},{2,6},{1,3},{5,1},... | collective-permute-start | bytes 442376 | tf_op jit(solution)/shard_map/ppermute | solution.py:124
  20.5 7.7 %collective-permute-start.8 = (bf16[32,2304]{1,0:T(8,128)(2,1)S(1)}, bf16[32,2304]{1,0:T(8,128)(2,1)S(1)}, u32[]{:S(2)}, u32[]{:S(2)}) collective-permute-start(bf16[32,2304]{1,0:T(8,128)(2,1)S(1)} %get-tuple-element.26), channel_id=1, source_target_pairs={{0,4},{4,8},{8,12},{12,14},{14,10},{10,6},{6,2},{2,0},{1,5},{5,9},... | collective-permute-start | bytes 442376 | tf_op jit(solution)/shard_map/ppermute | solution.py:122
  22.6 11.3 %collective-permute-start.12 = (bf16[32,2304]{1,0:T(8,128)(2,1)S(1)}, bf16[32,2304]{1,0:T(8,128)(2,1)S(1)}, u32[]{:S(2)}, u32[]{:S(2)}) collective-permute-start(bf16[32,2304]{1,0:T(8,128)(2,1)S(1)} %get-tuple-element.27), channel_id=1, source_target_pairs={{0,2},{4,0},{8,4},{12,8},{14,12},{10,14},{6,10},{2,6},{1,3},{5,1},... | collective-permute-start | bytes 442376 | tf_op jit(solution)/shard_map/ppermute | solution.py:124
  25.1 6.6 %collective-permute-start.2 = (bf16[32,2304]{1,0:T(8,128)(2,1)S(1)}, bf16[32,2304]{1,0:T(8,128)(2,1)S(1)}, u32[]{:S(2)}, u32[]{:S(2)}) collective-permute-start(bf16[32,2304]{1,0:T(8,128)(2,1)S(1)} %add_convert_fusion.10), channel_id=1, source_target_pairs={{0,4},{4,8},{8,12},{12,14},{14,10},{10,6},{6,2},{2,0},{1,5},{5,9},... | collective-permute-start | bytes 442376 | tf_op jit(solution)/shard_map/ppermute | solution.py:122
  28.2 6.8 %collective-permute-start.9 = (bf16[32,2304]{1,0:T(8,128)(2,1)S(1)}, bf16[32,2304]{1,0:T(8,128)(2,1)S(1)}, u32[]{:S(2)}, u32[]{:S(2)}) collective-permute-start(bf16[32,2304]{1,0:T(8,128)(2,1)S(1)} %add_convert_fusion.5), channel_id=1, source_target_pairs={{0,4},{4,8},{8,12},{12,14},{14,10},{10,6},{6,2},{2,0},{1,5},{5,9},... | collective-permute-start | bytes 442376 | tf_op jit(solution)/shard_map/ppermute | solution.py:122
  31.8 6.7 %collective-permute-start.3 = (bf16[32,2304]{1,0:T(8,128)(2,1)S(1)}, bf16[32,2304]{1,0:T(8,128)(2,1)S(1)}, u32[]{:S(2)}, u32[]{:S(2)}) collective-permute-start(bf16[32,2304]{1,0:T(8,128)(2,1)S(1)} %get-tuple-element.18), channel_id=1, source_target_pairs={{0,4},{4,8},{8,12},{12,14},{14,10},{10,6},{6,2},{2,0},{1,5},{5,9},... | collective-permute-start | bytes 442376 | tf_op jit(solution)/shard_map/ppermute | solution.py:122
  33.9 6.7 %collective-permute-start.6 = (bf16[32,2304]{1,0:T(8,128)(2,1)S(1)}, bf16[32,2304]{1,0:T(8,128)(2,1)S(1)}, u32[]{:S(2)}, u32[]{:S(2)}) collective-permute-start(bf16[32,2304]{1,0:T(8,128)(2,1)S(1)} %get-tuple-element.19), channel_id=1, source_target_pairs={{0,2},{4,0},{8,4},{12,8},{14,12},{10,14},{6,10},{2,6},{1,3},{5,1},... | collective-permute-start | bytes 442376 | tf_op jit(solution)/shard_map/ppermute | solution.py:124
  35.1 7.7 %collective-permute-start.10 = (bf16[32,2304]{1,0:T(8,128)(2,1)S(1)}, bf16[32,2304]{1,0:T(8,128)(2,1)S(1)}, u32[]{:S(2)}, u32[]{:S(2)}) collective-permute-start(bf16[32,2304]{1,0:T(8,128)(2,1)S(1)} %get-tuple-element.24), channel_id=1, source_target_pairs={{0,4},{4,8},{8,12},{12,14},{14,10},{10,6},{6,2},{2,0},{1,5},{5,9},... | collective-permute-start | bytes 442376 | tf_op jit(solution)/shard_map/ppermute | solution.py:122
  37.2 6.6 %collective-permute-start.13 = (bf16[32,2304]{1,0:T(8,128)(2,1)S(1)}, bf16[32,2304]{1,0:T(8,128)(2,1)S(1)}, u32[]{:S(2)}, u32[]{:S(2)}) collective-permute-start(bf16[32,2304]{1,0:T(8,128)(2,1)S(1)} %get-tuple-element.25), channel_id=1, source_target_pairs={{0,2},{4,0},{8,4},{12,8},{14,12},{10,14},{6,10},{2,6},{1,3},{5,1},... | collective-permute-start | bytes 442376 | tf_op jit(solution)/shard_map/ppermute | solution.py:124
  40.7 5.9 %collective-permute-start.4 = (bf16[32,2304]{1,0:T(8,128)(2,1)S(1)}, bf16[32,2304]{1,0:T(8,128)(2,1)S(1)}, u32[]{:S(2)}, u32[]{:S(2)}) collective-permute-start(bf16[32,2304]{1,0:T(8,128)(2,1)S(1)} %get-tuple-element.16), channel_id=1, source_target_pairs={{0,4},{4,8},{8,12},{12,14},{14,10},{10,6},{6,2},{2,0},{1,5},{5,9},... | collective-permute-start | bytes 442376 | tf_op jit(solution)/shard_map/ppermute | solution.py:122
  42.3 5.5 %collective-permute-start.7 = (bf16[32,2304]{1,0:T(8,128)(2,1)S(1)}, bf16[32,2304]{1,0:T(8,128)(2,1)S(1)}, u32[]{:S(2)}, u32[]{:S(2)}) collective-permute-start(bf16[32,2304]{1,0:T(8,128)(2,1)S(1)} %get-tuple-element.17), channel_id=1, source_target_pairs={{0,2},{4,0},{8,4},{12,8},{14,12},{10,14},{6,10},{2,6},{1,3},{5,1},... | collective-permute-start | bytes 442376 | tf_op jit(solution)/shard_map/ppermute | solution.py:124
  43.8 5.2 %collective-permute-start.11 = (bf16[32,2304]{1,0:T(8,128)(2,1)S(1)}, bf16[32,2304]{1,0:T(8,128)(2,1)S(1)}, u32[]{:S(2)}, u32[]{:S(2)}) collective-permute-start(bf16[32,2304]{1,0:T(8,128)(2,1)S(1)} %get-tuple-element.22), channel_id=1, source_target_pairs={{0,4},{4,8},{8,12},{12,14},{14,10},{10,6},{6,2},{2,0},{1,5},{5,9},... | collective-permute-start | bytes 442376 | tf_op jit(solution)/shard_map/ppermute | solution.py:122
  45.5 5.1 %collective-permute-start.14 = (bf16[32,2304]{1,0:T(8,128)(2,1)S(1)}, bf16[32,2304]{1,0:T(8,128)(2,1)S(1)}, u32[]{:S(2)}, u32[]{:S(2)}) collective-permute-start(bf16[32,2304]{1,0:T(8,128)(2,1)S(1)} %get-tuple-element.23), channel_id=1, source_target_pairs={{0,2},{4,0},{8,4},{12,8},{14,12},{10,14},{6,10},{2,6},{1,3},{5,1},... | collective-permute-start | bytes 442376 | tf_op jit(solution)/shard_map/ppermute | solution.py:124
  57.5 6.4 %collective-permute-start.15 = (bf16[32,2048]{1,0:T(8,128)(2,1)S(1)}, bf16[32,2048]{1,0:T(8,128)(2,1)S(1)}, u32[]{:S(2)}, u32[]{:S(2)}) collective-permute-start(bf16[32,2048]{1,0:T(8,128)(2,1)S(1)} %get-tuple-element.30), channel_id=1, source_target_pairs={{0,4},{4,8},{8,12},{12,14},{14,10},{10,6},{6,2},{2,0},{1,5},{5,9},... | collective-permute-start | bytes 393224 | tf_op jit(solution)/shard_map/ppermute | solution.py:138
  59.1 6.4 %collective-permute-start.16 = (bf16[32,2048]{1,0:T(8,128)(2,1)S(1)}, bf16[32,2048]{1,0:T(8,128)(2,1)S(1)}, u32[]{:S(2)}, u32[]{:S(2)}) collective-permute-start(bf16[32,2048]{1,0:T(8,128)(2,1)S(1)} %get-tuple-element.30), channel_id=1, source_target_pairs={{0,2},{4,0},{8,4},{12,8},{14,12},{10,14},{6,10},{2,6},{1,3},{5,1},... | collective-permute-start | bytes 393224 | tf_op jit(solution)/shard_map/ppermute | solution.py:141
  59.6 7.2 %collective-permute-start.22 = (bf16[32,2048]{1,0:T(8,128)(2,1)S(1)}, bf16[32,2048]{1,0:T(8,128)(2,1)S(1)}, u32[]{:S(2)}, u32[]{:S(2)}) collective-permute-start(bf16[32,2048]{1,0:T(8,128)(2,1)S(1)} %get-tuple-element.33), channel_id=1, source_target_pairs={{0,4},{4,8},{8,12},{12,14},{14,10},{10,6},{6,2},{2,0},{1,5},{5,9},... | collective-permute-start | bytes 393224 | tf_op jit(solution)/shard_map/ppermute | solution.py:138
  61.2 7.2 %collective-permute-start.23 = (bf16[32,2048]{1,0:T(8,128)(2,1)S(1)}, bf16[32,2048]{1,0:T(8,128)(2,1)S(1)}, u32[]{:S(2)}, u32[]{:S(2)}) collective-permute-start(bf16[32,2048]{1,0:T(8,128)(2,1)S(1)} %get-tuple-element.33), channel_id=1, source_target_pairs={{0,2},{4,0},{8,4},{12,8},{14,12},{10,14},{6,10},{2,6},{1,3},{5,1},... | collective-permute-start | bytes 393224 | tf_op jit(solution)/shard_map/ppermute | solution.py:141
  63.9 6.3 %collective-permute-start.17 = (bf16[32,2048]{1,0:T(8,128)(2,1)S(1)}, bf16[32,2048]{1,0:T(8,128)(2,1)S(1)}, u32[]{:S(2)}, u32[]{:S(2)}) collective-permute-start(bf16[32,2048]{1,0:T(8,128)(2,1)S(1)} %collective-permute-done.15), channel_id=1, source_target_pairs={{0,4},{4,8},{8,12},{12,14},{14,10},{10,6},{6,2},{2,0},{1,5},{5,9},... | collective-permute-start | bytes 393224 | tf_op jit(solution)/shard_map/ppermute | solution.py:138
  65.5 6.3 %collective-permute-start.18 = (bf16[32,2048]{1,0:T(8,128)(2,1)S(1)}, bf16[32,2048]{1,0:T(8,128)(2,1)S(1)}, u32[]{:S(2)}, u32[]{:S(2)}) collective-permute-start(bf16[32,2048]{1,0:T(8,128)(2,1)S(1)} %collective-permute-done.16), channel_id=1, source_target_pairs={{0,2},{4,0},{8,4},{12,8},{14,12},{10,14},{6,10},{2,6},{1,3},{5,1},... | collective-permute-start | bytes 393224 | tf_op jit(solution)/shard_map/ppermute | solution.py:141
  66.7 6.4 %collective-permute-start.24 = (bf16[32,2048]{1,0:T(8,128)(2,1)S(1)}, bf16[32,2048]{1,0:T(8,128)(2,1)S(1)}, u32[]{:S(2)}, u32[]{:S(2)}) collective-permute-start(bf16[32,2048]{1,0:T(8,128)(2,1)S(1)} %collective-permute-done.22), channel_id=1, source_target_pairs={{0,4},{4,8},{8,12},{12,14},{14,10},{10,6},{6,2},{2,0},{1,5},{5,9},... | collective-permute-start | bytes 393224 | tf_op jit(solution)/shard_map/ppermute | solution.py:138
  68.3 6.4 %collective-permute-start.25 = (bf16[32,2048]{1,0:T(8,128)(2,1)S(1)}, bf16[32,2048]{1,0:T(8,128)(2,1)S(1)}, u32[]{:S(2)}, u32[]{:S(2)}) collective-permute-start(bf16[32,2048]{1,0:T(8,128)(2,1)S(1)} %collective-permute-done.23), channel_id=1, source_target_pairs={{0,2},{4,0},{8,4},{12,8},{14,12},{10,14},{6,10},{2,6},{1,3},{5,1},... | collective-permute-start | bytes 393224 | tf_op jit(solution)/shard_map/ppermute | solution.py:141
  70.2 5.7 %collective-permute-start.19 = (bf16[32,2048]{1,0:T(8,128)(2,1)S(1)}, bf16[32,2048]{1,0:T(8,128)(2,1)S(1)}, u32[]{:S(2)}, u32[]{:S(2)}) collective-permute-start(bf16[32,2048]{1,0:T(8,128)(2,1)S(1)} %collective-permute-done.17), channel_id=1, source_target_pairs={{0,4},{4,8},{8,12},{12,14},{14,10},{10,6},{6,2},{2,0},{1,5},{5,9},... | collective-permute-start | bytes 393224 | tf_op jit(solution)/shard_map/ppermute | solution.py:138
  71.8 7.8 %collective-permute-start.20 = (bf16[32,2048]{1,0:T(8,128)(2,1)S(1)}, bf16[32,2048]{1,0:T(8,128)(2,1)S(1)}, u32[]{:S(2)}, u32[]{:S(2)}) collective-permute-start(bf16[32,2048]{1,0:T(8,128)(2,1)S(1)} %collective-permute-done.18), channel_id=1, source_target_pairs={{0,2},{4,0},{8,4},{12,8},{14,12},{10,14},{6,10},{2,6},{1,3},{5,1},... | collective-permute-start | bytes 393224 | tf_op jit(solution)/shard_map/ppermute | solution.py:141
  73.1 5.0 %collective-permute-start.26 = (bf16[32,2048]{1,0:T(8,128)(2,1)S(1)}, bf16[32,2048]{1,0:T(8,128)(2,1)S(1)}, u32[]{:S(2)}, u32[]{:S(2)}) collective-permute-start(bf16[32,2048]{1,0:T(8,128)(2,1)S(1)} %collective-permute-done.24), channel_id=1, source_target_pairs={{0,4},{4,8},{8,12},{12,14},{14,10},{10,6},{6,2},{2,0},{1,5},{5,9},... | collective-permute-start | bytes 393224 | tf_op jit(solution)/shard_map/ppermute | solution.py:138
  74.7 5.0 %collective-permute-start.27 = (bf16[32,2048]{1,0:T(8,128)(2,1)S(1)}, bf16[32,2048]{1,0:T(8,128)(2,1)S(1)}, u32[]{:S(2)}, u32[]{:S(2)}) collective-permute-start(bf16[32,2048]{1,0:T(8,128)(2,1)S(1)} %collective-permute-done.25), channel_id=1, source_target_pairs={{0,2},{4,0},{8,4},{12,8},{14,12},{10,14},{6,10},{2,6},{1,3},{5,1},... | collective-permute-start | bytes 393224 | tf_op jit(solution)/shard_map/ppermute | solution.py:141
  75.9 5.0 %collective-permute-start.21 = (bf16[32,2048]{1,0:T(8,128)(2,1)S(1)}, bf16[32,2048]{1,0:T(8,128)(2,1)S(1)}, u32[]{:S(2)}, u32[]{:S(2)}) collective-permute-start(bf16[32,2048]{1,0:T(8,128)(2,1)S(1)} %collective-permute-done.19), channel_id=1, source_target_pairs={{0,4},{4,8},{8,12},{12,14},{14,10},{10,6},{6,2},{2,0},{1,5},{5,9},... | collective-permute-start | bytes 393224 | tf_op jit(solution)/shard_map/ppermute | solution.py:138
  78.1 5.0 %collective-permute-start.28 = (bf16[32,2048]{1,0:T(8,128)(2,1)S(1)}, bf16[32,2048]{1,0:T(8,128)(2,1)S(1)}, u32[]{:S(2)}, u32[]{:S(2)}) collective-permute-start(bf16[32,2048]{1,0:T(8,128)(2,1)S(1)} %collective-permute-done.26), channel_id=1, source_target_pairs={{0,4},{4,8},{8,12},{12,14},{14,10},{10,6},{6,2},{2,0},{1,5},{5,9},... | collective-permute-start | bytes 393224 | tf_op jit(solution)/shard_map/ppermute | solution.py:138
  83.8 11.3 %copy-start.1 = (bf16[2,1536,2,128]{3,2,1,0:T(2,128)(2,1)S(1)}, bf16[2,1536,2,128]{3,2,1,0:T(2,128)(2,1)}, u32[]{:S(2)}) copy-start(bf16[2,1536,2,128]{3,2,1,0:T(2,128)(2,1)} %param.16) | copy-start | bytes 4718596
  92.2 2.0 %collective-permute-start.29 = (bf16[128,2048]{1,0:T(8,128)(2,1)S(1)}, bf16[128,2048]{1,0:T(8,128)(2,1)S(1)}, u32[]{:S(2)}, u32[]{:S(2)}) collective-permute-start(bf16[128,2048]{1,0:T(8,128)(2,1)S(1)} %slice.211), channel_id=1, source_target_pairs={{0,1},{1,0},{2,3},{3,2},{4,5},{5,4},{6,7},{7,6},{8,9},{9,8},{10,11... | collective-permute-start | bytes 1572872 | tf_op jit(solution)/shard_map/ppermute | solution.py:239
  (6 other events, 21.4 us)

commit v10 on v9

--- a/solution.py
+++ b/solution.py
@@ -106,7 +106,7 @@
                     slots[r, k * seq_dev + j] = ring[(p + k) % n_row] * seq_dev + j
             for slot in range(n_row * seq_dev):
                 offset = (position_of[slot // seq_dev] - p) % n_row
-                stacked_row[r, slot] = (stacked_of_offset[offset] * seq_dev + slot % seq_dev) * new_len
+                stacked_row[r, slot] = ((slot % seq_dev) * n_row + stacked_of_offset[offset]) * new_len
         return slots, stacked_row
 
     def add_bf16(a, b):
@@ -178,50 +178,34 @@
             jnp.dot(pick_own, tokens, preferred_element_type=jnp.float32)
             + jnp.dot(pick_other, other_tokens, preferred_element_type=jnp.float32)
         ).astype(jnp.bfloat16)
-        n_kv = k_cache.shape[2]
-        q_cols = q_weight.shape[1] // n_kv
-        k_cols = key_matrix.shape[1] // n_kv
+        q_part = jnp.dot(chosen, q_weight, preferred_element_type=jnp.float32).astype(jnp.bfloat16)
         k_part = jnp.dot(chosen, key_matrix, preferred_element_type=jnp.float32).astype(jnp.bfloat16)
         v_part = jnp.dot(chosen, value_matrix, preferred_element_type=jnp.float32).astype(jnp.bfloat16)
-        q_all = jnp.dot(chosen, q_weight, preferred_element_type=jnp.float32).astype(jnp.bfloat16)
-        q_sums, k_sums, v_sums = [], [], []
-        for h in range(n_kv):
-            q_part = q_all[:, h * q_cols : (h + 1) * q_cols]
-            joined = jnp.concatenate(
-                [q_part, k_part[:, h * k_cols : (h + 1) * k_cols], v_part[:, h * k_cols : (h + 1) * k_cols]],
-                axis=1,
+        q_cols = q_part.shape[1]
+        k_cols = k_part.shape[1]
+        joined = jnp.concatenate([q_part, k_part, v_part], axis=1)
+        starts = lookup(cache_len, sequences[:seq_dev])
+        gathered = []
+        late = None
+        for j in range(seq_dev):
+            blocks = [
+                joined[k * block_rows + j * new_len : k * block_rows + (j + 1) * new_len] for k in range(n_row)
+            ]
+            summed = ring_reduce_scatter(blocks)
+            if late is None:
+                summed, late_slot_seq, late_row = lax.optimization_barrier((summed, slot_seq, row_index))
+                late = True
+            token_places = (starts[j] + jnp.arange(new_len)).astype(jnp.float32)
+            queries = apply_turning(summed[:, :q_cols].reshape(new_len, -1, head_dim), token_places).astype(
+                jnp.bfloat16
             )
-            blocks = [joined[k * block_rows : (k + 1) * block_rows] for k in range(n_row)]
-            summed = ring_reduce_scatter(blocks)
-            q_sums.append(summed[:, :q_cols])
-            k_sums.append(summed[:, q_cols : q_cols + k_cols])
-            v_sums.append(summed[:, q_cols + k_cols :])
-        q_sum = jnp.concatenate(q_sums, axis=1)
-        key_total_sum = jnp.concatenate(k_sums, axis=1)
-        value_total_sum = jnp.concatenate(v_sums, axis=1)
-        q_sum, late_slot_seq, late_row = lax.optimization_barrier((q_sum, slot_seq, row_index))
-        starts = lookup(cache_len, sequences[:seq_dev])
-        token_places = (starts[:, None] + jnp.arange(new_len)[None, :]).reshape(-1).astype(jnp.float32)
-        row_total = q_sum.shape[0]
-        queries = apply_turning(q_sum.reshape(row_total, -1, head_dim), token_places).astype(
-            jnp.bfloat16
-        )
-        rotated_keys = apply_turning(
-            key_total_sum.reshape(row_total, -1, head_dim), token_places
-        ).astype(jnp.bfloat16)
-        values = value_total_sum.reshape(row_total, -1, head_dim).astype(jnp.bfloat16)
-        results = jax.vmap(attend)(
-            queries.reshape(seq_dev, new_len, -1, head_dim),
-            rotated_keys.reshape(seq_dev, new_len, -1, head_dim),
-            values.reshape(seq_dev, new_len, -1, head_dim),
-            k_cache,
-            value_cache,
-            starts,
-        )
-        attended = results.reshape(seq_dev * new_len, -1)
-        stacked = jnp.concatenate(
-            [ring_all_gather(attended[:, h * q_cols : (h + 1) * q_cols]) for h in range(n_kv)], axis=1
-        )
+            rotated_keys = apply_turning(
+                summed[:, q_cols : q_cols + k_cols].reshape(new_len, -1, head_dim), token_places
+            ).astype(jnp.bfloat16)
+            values = summed[:, q_cols + k_cols :].reshape(new_len, -1, head_dim).astype(jnp.bfloat16)
+            attended = attend(queries, rotated_keys, values, k_cache[j], value_cache[j], starts[j])
+            gathered.append(ring_all_gather(attended))
+        stacked = jnp.concatenate(gathered, axis=0)
         late_mine = jnp.arange(n_row, dtype=jnp.int32)[:, None] == late_row
         row_of_slot = jnp.sum(jnp.where(late_mine, jnp.asarray(stacked_table), 0), axis=0)
         seq_ids = jnp.arange(slot_total, dtype=jnp.int32)

time: 95.3 us -> 107 us (1.12)
  local copies, waits for them, and re-layouts: 1.15 us -> 13 us
  other arithmetic: 5.92 us -> 15.7 us
  waiting for transfers between devices: 26.2 us -> 19.9 us
  matrix products: 27.7 us -> 23.7 us
    slice x11 -> x8, local copies, waits for them, and re-layouts: 0.32 us -> 6.3 us  [the longest x1 3.12 us: body(): k_cache[j]]
    unnamed x29 -> x63, local copies, waits for them, and re-layouts: 0.25 us -> 2.99 us
    ppermute x8, waiting for transfers between devices: 9.39 us -> 7 us  [ring_all_gather(): forward = lax.ppermute(forward, 'row', forward_pairs)]
    dot_general x1, matrix products: 2.85 us -> 0.47 us  [body(): jnp.dot(pick_own, tokens, preferred_element_type=jnp.float32)]
    ppermute x6, waiting for transfers between devices: 6.01 us -> 3.63 us  [ring_reduce_scatter(): got_backward = lax.ppermute(backward, 'row', backward_pairs)]
    lt x1 -> x2, other arithmetic: 0.08 us -> 2.38 us  [attend(): valid_cache = jnp.arange(cached_keys.shape[0]) < length]
    ppermute x8, starting transfers between devices: 16.6 us -> 14.5 us  [ring_reduce_scatter(): got_forward = lax.ppermute(forward, 'row', forward_pairs)]
    add x2, other arithmetic: 0.11 us -> 1.86 us  [ring_reduce_scatter(): total = total + got_backward.astype(jnp.float32)]
  transfers between devices with their start and end apart: 30 -> 30, of which waited for: 20 -> 19; matrix products, arithmetic and copies ran while one was open for 7% -> 22% of each run, Pallas kernels for 0% -> 0%
where the time goes in v10:
time: 107 us
  starting transfers between devices  33.5 us (31%)
  matrix products  23.7 us (22%)
  waiting for transfers between devices  19.9 us (19%)
  other arithmetic  15.7 us (15%)
  local copies, waits for them, and re-layouts  13 us (12%)
    ppermute x8, starting transfers between devices, ring_reduce_scatter(): got_forward = lax.ppermute(forward, 'row', forward_pairs)  14.5 us
    ppermute x8, starting transfers between devices, ring_all_gather(): forward = lax.ppermute(forward, 'row', forward_pairs)  12.2 us
    dot_general x1, matrix products, body(): jnp.dot(chosen, q_weight, preferred_element_type=jnp.float32)  8.41 us
    dot_general x1, matrix products, body(): products = jnp.dot(arranged, o_weight, preferred_element_type=jnp.float32)  8.28 us
    ppermute x8, waiting for transfers between devices, ring_reduce_scatter(): got_forward = lax.ppermute(forward, 'row', forward_pairs)  7.31 us
    ppermute x8, waiting for transfers between devices, ring_all_gather(): forward = lax.ppermute(forward, 'row', forward_pairs)  7 us
    ppermute x6, starting transfers between devices, ring_all_gather(): backward = lax.ppermute(backward, 'row', backward_pairs)  3.95 us
    ppermute x6, waiting for transfers between devices, ring_reduce_scatter(): got_backward = lax.ppermute(backward, 'row', backward_pairs)  3.63 us
  transfers between devices with their start and end apart: 30, of which 19 were waited for; matrix products, arithmetic and copies ran while one was open for 22% of the time, Pallas kernels for 0%

profile of v10, /device:TPU:0, one launch (start us, length us, event | category | flops | bytes accessed | tf_op | source)
XLA Modules:
  0.0 106.5 jit_solution(17299654709785194039)
XLA Ops:
  3.9 3.1 %fusion.65 = (bf16[1,1536,2,128]{3,2,1,0:T(2,128)(2,1)}, bf16[1,1536,2,128]{3,2,1,0:T(2,128)(2,1)}) fusion(bf16[2,1536,2,128]{3,2,1,0:T(2,128)(2,1)} %param.16), kind=kLoop, calls=%fused_computation.170 | loop fusion | bytes 3145728 | tf_op jit(solution)/shard_map/slice | solution.py:206
  7.0 1.9 %fusion.64 = (bf16[1,1536,2,128]{3,2,1,0:T(2,128)(2,1)S(1)}, bf16[1,1536,2,128]{3,2,1,0:T(2,128)(2,1)}) fusion(bf16[2,1536,2,128]{3,2,1,0:T(2,128)(2,1)S(1)} %copy-done.5), kind=kLoop, calls=%fused_computation.169 | loop fusion | bytes 3145728 | tf_op jit(solution)/shard_map/slice | solution.py:206
  9.9 8.4 %convolution_convert_fusion.1 = bf16[256,4096]{1,0:T(8,128)(2,1)S(1)} fusion(bf16[256,2048]{1,0:T(8,128)(2,1)S(1)} %fusion.8, bf16[2048,4096]{1,0:T(8,128)(2,1)} %param.12), kind=kOutput, calls=%fused_computation.1 | convolution fusion | flops 4296015872 | bytes 19922944 | tf_op jit(solution)/shard_map/dot_general | solution.py:181
  20.2 2.7 %collective-permute-start.15 = (bf16[16,4608]{1,0:T(8,128)(2,1)S(1)}, bf16[16,4608]{1,0:T(8,128)(2,1)S(1)}, u32[]{:S(2)}, u32[]{:S(2)}) collective-permute-start(bf16[16,4608]{1,0:T(8,128)(2,1)S(1)} %get-tuple-element.24), channel_id=1, source_target_pairs={{0,4},{4,8},{8,12},{12,14},{14,10},{10,6},{6,2},{2,0},{1,5},{5,9},... | collective-permute-start | bytes 442376 | tf_op jit(solution)/shard_map/ppermute | solution.py:122
  24.2 1.6 %collective-permute-start.1 = (bf16[16,4608]{1,0:T(8,128)(2,1)S(1)}, bf16[16,4608]{1,0:T(8,128)(2,1)S(1)}, u32[]{:S(2)}, u32[]{:S(2)}) collective-permute-start(bf16[16,4608]{1,0:T(8,128)(2,1)S(1)} %get-tuple-element.27), channel_id=1, source_target_pairs={{0,4},{4,8},{8,12},{12,14},{14,10},{10,6},{6,2},{2,0},{1,5},{5,9},... | collective-permute-start | bytes 442376 | tf_op jit(solution)/shard_map/ppermute | solution.py:122
  26.3 1.3 %collective-permute-done.15 = bf16[16,4608]{1,0:T(8,128)(2,1)S(1)} collective-permute-done((bf16[16,4608]{1,0:T(8,128)(2,1)S(1)}, bf16[16,4608]{1,0:T(8,128)(2,1)S(1)}, u32[]{:S(2)}, u32[]{:S(2)}) %collective-permute-start.15) | collective-permute-done | bytes 147488 | tf_op jit(solution)/shard_map/ppermute | solution.py:122
  27.6 2.1 %collective-permute-start.16 = (bf16[16,4608]{1,0:T(8,128)(2,1)S(1)}, bf16[16,4608]{1,0:T(8,128)(2,1)S(1)}, u32[]{:S(2)}, u32[]{:S(2)}) collective-permute-start(bf16[16,4608]{1,0:T(8,128)(2,1)S(1)} %add_convert_fusion.4), channel_id=1, source_target_pairs={{0,4},{4,8},{8,12},{12,14},{14,10},{10,6},{6,2},{2,0},{1,5},{5,9},... | collective-permute-start | bytes 442376 | tf_op jit(solution)/shard_map/ppermute | solution.py:122
  31.5 2.2 %collective-permute-done.16 = bf16[16,4608]{1,0:T(8,128)(2,1)S(1)} collective-permute-done((bf16[16,4608]{1,0:T(8,128)(2,1)S(1)}, bf16[16,4608]{1,0:T(8,128)(2,1)S(1)}, u32[]{:S(2)}, u32[]{:S(2)}) %collective-permute-start.16) | collective-permute-done | bytes 147488 | tf_op jit(solution)/shard_map/ppermute | solution.py:122
  34.5 1.8 %collective-permute-start.17 = (bf16[16,4608]{1,0:T(8,128)(2,1)}, bf16[16,4608]{1,0:T(8,128)(2,1)}, u32[]{:S(2)}, u32[]{:S(2)}) collective-permute-start(bf16[16,4608]{1,0:T(8,128)(2,1)} %get-tuple-element.21), channel_id=1, source_target_pairs={{0,4},{4,8},{8,12},{12,14},{14,10},{10,6},{6,2},{2,0},{1,5},{5,9},... | collective-permute-start | bytes 442376 | tf_op jit(solution)/shard_map/ppermute | solution.py:122
  36.3 1.6 %collective-permute-start.2 = (bf16[16,4608]{1,0:T(8,128)(2,1)}, bf16[16,4608]{1,0:T(8,128)(2,1)}, u32[]{:S(2)}, u32[]{:S(2)}) collective-permute-start(bf16[16,4608]{1,0:T(8,128)(2,1)} %get-tuple-element.23), channel_id=1, source_target_pairs={{0,4},{4,8},{8,12},{12,14},{14,10},{10,6},{6,2},{2,0},{1,5},{5,9},... | collective-permute-start | bytes 442376 | tf_op jit(solution)/shard_map/ppermute | solution.py:122
  38.9 1.3 %iota_compare_fusion.7 = pred[1536]{0:T(1024)(128)(4,1)} fusion(s32[]{:T(128)} %bitcast.17), kind=kLoop, calls=%fused_computation.125 | loop fusion | flops 1536 | bytes 1540 | tf_op jit(solution)/shard_map/lt | solution.py:33
  40.1 1.3 %collective-permute-done.17 = bf16[16,4608]{1,0:T(8,128)(2,1)} collective-permute-done((bf16[16,4608]{1,0:T(8,128)(2,1)}, bf16[16,4608]{1,0:T(8,128)(2,1)}, u32[]{:S(2)}, u32[]{:S(2)}) %collective-permute-start.17) | collective-permute-done | bytes 147488 | tf_op jit(solution)/shard_map/ppermute | solution.py:122
  41.4 1.6 %collective-permute-done.2 = bf16[16,4608]{1,0:T(8,128)(2,1)} collective-permute-done((bf16[16,4608]{1,0:T(8,128)(2,1)}, bf16[16,4608]{1,0:T(8,128)(2,1)}, u32[]{:S(2)}, u32[]{:S(2)}) %collective-permute-start.2) | collective-permute-done | bytes 147488 | tf_op jit(solution)/shard_map/ppermute | solution.py:122
  43.3 1.2 %add_convert_fusion.2 = (bf16[16,4608]{1,0:T(8,128)(2,1)S(1)}, bf16[16,4608]{1,0:T(8,128)(2,1)S(1)}, bf16[16,4608]{1,0:T(8,128)(2,1)S(1)}, bf16[16,4608]{1,0:T(8,128)(2,1)S(1)}) fusion(bf16[16,4608]{1,0:T(8,128)(2,1)} %collective-permute-done.17, bf16[256,4608]{1,0:T(8,128)(2,1)S(1)} %pad_maximum_fusion, bf16[16,4608]{1,0:T(8,128)(2,1)} %collective-permute-done.20, ...), kind=kLoop, calls=%fused_computation.49 | loop fusion | flops 1179648 | bytes 1769472 | tf_op jit(solution)/shard_map/convert_element_type | solution.py:113
  44.5 1.6 %collective-permute-start.18 = (bf16[16,4608]{1,0:T(8,128)(2,1)S(1)}, bf16[16,4608]{1,0:T(8,128)(2,1)S(1)}, u32[]{:S(2)}, u32[]{:S(2)}) collective-permute-start(bf16[16,4608]{1,0:T(8,128)(2,1)S(1)} %get-tuple-element.17), channel_id=1, source_target_pairs={{0,4},{4,8},{8,12},{12,14},{14,10},{10,6},{6,2},{2,0},{1,5},{5,9},... | collective-permute-start | bytes 442376 | tf_op jit(solution)/shard_map/ppermute | solution.py:122
  46.6 1.6 %collective-permute-start.3 = (bf16[16,4608]{1,0:T(8,128)(2,1)S(1)}, bf16[16,4608]{1,0:T(8,128)(2,1)S(1)}, u32[]{:S(2)}, u32[]{:S(2)}) collective-permute-start(bf16[16,4608]{1,0:T(8,128)(2,1)S(1)} %get-tuple-element.20), channel_id=1, source_target_pairs={{0,4},{4,8},{8,12},{12,14},{14,10},{10,6},{6,2},{2,0},{1,5},{5,9},... | collective-permute-start | bytes 442376 | tf_op jit(solution)/shard_map/ppermute | solution.py:122
  51.7 1.6 %collective-permute-done.6 = bf16[16,4608]{1,0:T(8,128)(2,1)S(1)} collective-permute-done((bf16[16,4608]{1,0:T(8,128)(2,1)S(1)}, bf16[16,4608]{1,0:T(8,128)(2,1)S(1)}, u32[]{:S(2)}, u32[]{:S(2)}) %collective-permute-start.6) | collective-permute-done | bytes 147488 | tf_op jit(solution)/shard_map/ppermute | solution.py:124
  55.4 1.5 %collective-permute-start.4 = (bf16[16,4608]{1,0:T(8,128)(2,1)}, bf16[16,4608]{1,0:T(8,128)(2,1)}, u32[]{:S(2)}, u32[]{:S(2)}) collective-permute-start(bf16[16,4608]{1,0:T(8,128)(2,1)} %get-tuple-element.16), channel_id=1, source_target_pairs={{0,4},{4,8},{8,12},{12,14},{14,10},{10,6},{6,2},{2,0},{1,5},{5,9},... | collective-permute-start | bytes 442376 | tf_op jit(solution)/shard_map/ppermute | solution.py:122
  59.0 1.3 %convert_element_type.233 = bf16[16,2,128]{2,1,0:T(2,128)(2,1)} reshape(bf16[16,256]{1,0:T(8,128)(2,1)} %slice.220) | data formatting | bytes 16384 | tf_op jit(solution)/shard_map/convert_element_type | solution.py:205
  60.3 1.5 %fusion.66 = (f32[16,2,64]{2,1,0:T(2,128)}, f32[16,2,64]{2,1,0:T(2,128)}) fusion(f32[16,2,128]{2,1,0:T(2,128)} %reshape.267), kind=kLoop, calls=%fused_computation.171 | loop fusion | bytes 32768 | tf_op jit(solution)/shard_map/slice | solution.py:18
  67.7 1.4 %collective-permute-start.8 = (bf16[16,4096]{1,0:T(8,128)(2,1)S(1)}, bf16[16,4096]{1,0:T(8,128)(2,1)S(1)}, u32[]{:S(2)}, u32[]{:S(2)}) collective-permute-start(bf16[16,4096]{1,0:T(8,128)(2,1)S(1)} %bitcast.132), channel_id=1, source_target_pairs={{0,4},{4,8},{8,12},{12,14},{14,10},{10,6},{6,2},{2,0},{1,5},{5,9},... | collective-permute-start | bytes 393224 | tf_op jit(solution)/shard_map/ppermute | solution.py:138
  72.8 1.4 %collective-permute-start.22 = (bf16[16,4096]{1,0:T(8,128)(2,1)S(1)}, bf16[16,4096]{1,0:T(8,128)(2,1)S(1)}, u32[]{:S(2)}, u32[]{:S(2)}) collective-permute-start(bf16[16,4096]{1,0:T(8,128)(2,1)S(1)} %bitcast.134), channel_id=1, source_target_pairs={{0,4},{4,8},{8,12},{12,14},{14,10},{10,6},{6,2},{2,0},{1,5},{5,9},... | collective-permute-start | bytes 393224 | tf_op jit(solution)/shard_map/ppermute | solution.py:138
  75.2 1.4 %collective-permute-start.10 = (bf16[16,4096]{1,0:T(8,128)(2,1)S(1)}, bf16[16,4096]{1,0:T(8,128)(2,1)S(1)}, u32[]{:S(2)}, u32[]{:S(2)}) collective-permute-start(bf16[16,4096]{1,0:T(8,128)(2,1)S(1)} %collective-permute-done.8), channel_id=1, source_target_pairs={{0,4},{4,8},{8,12},{12,14},{14,10},{10,6},{6,2},{2,0},{1,5},{5,9},... | collective-permute-start | bytes 393224 | tf_op jit(solution)/shard_map/ppermute | solution.py:138
  78.4 1.8 %collective-permute-start.24 = (bf16[16,4096]{1,0:T(8,128)(2,1)S(1)}, bf16[16,4096]{1,0:T(8,128)(2,1)S(1)}, u32[]{:S(2)}, u32[]{:S(2)}) collective-permute-start(bf16[16,4096]{1,0:T(8,128)(2,1)S(1)} %collective-permute-done.22), channel_id=1, source_target_pairs={{0,4},{4,8},{8,12},{12,14},{14,10},{10,6},{6,2},{2,0},{1,5},{5,9},... | collective-permute-start | bytes 393224 | tf_op jit(solution)/shard_map/ppermute | solution.py:138
  81.7 1.4 %collective-permute-start.12 = (bf16[16,4096]{1,0:T(8,128)(2,1)S(1)}, bf16[16,4096]{1,0:T(8,128)(2,1)S(1)}, u32[]{:S(2)}, u32[]{:S(2)}) collective-permute-start(bf16[16,4096]{1,0:T(8,128)(2,1)S(1)} %collective-permute-done.10), channel_id=1, source_target_pairs={{0,4},{4,8},{8,12},{12,14},{14,10},{10,6},{6,2},{2,0},{1,5},{5,9},... | collective-permute-start | bytes 393224 | tf_op jit(solution)/shard_map/ppermute | solution.py:138
  84.6 1.4 %collective-permute-start.26 = (bf16[16,4096]{1,0:T(8,128)(2,1)S(1)}, bf16[16,4096]{1,0:T(8,128)(2,1)S(1)}, u32[]{:S(2)}, u32[]{:S(2)}) collective-permute-start(bf16[16,4096]{1,0:T(8,128)(2,1)S(1)} %collective-permute-done.24), channel_id=1, source_target_pairs={{0,4},{4,8},{8,12},{12,14},{14,10},{10,6},{6,2},{2,0},{1,5},{5,9},... | collective-permute-start | bytes 393224 | tf_op jit(solution)/shard_map/ppermute | solution.py:138
  87.7 1.7 %collective-permute-start.14 = (bf16[16,4096]{1,0:T(8,128)(2,1)S(1)}, bf16[16,4096]{1,0:T(8,128)(2,1)S(1)}, u32[]{:S(2)}, u32[]{:S(2)}) collective-permute-start(bf16[16,4096]{1,0:T(8,128)(2,1)S(1)} %collective-permute-done.12), channel_id=1, source_target_pairs={{0,4},{4,8},{8,12},{12,14},{14,10},{10,6},{6,2},{2,0},{1,5},{5,9},... | collective-permute-start | bytes 393224 | tf_op jit(solution)/shard_map/ppermute | solution.py:138
  89.5 1.8 %collective-permute-start.28 = (bf16[16,4096]{1,0:T(8,128)(2,1)S(1)}, bf16[16,4096]{1,0:T(8,128)(2,1)S(1)}, u32[]{:S(2)}, u32[]{:S(2)}) collective-permute-start(bf16[16,4096]{1,0:T(8,128)(2,1)S(1)} %collective-permute-done.26), channel_id=1, source_target_pairs={{0,4},{4,8},{8,12},{12,14},{14,10},{10,6},{6,2},{2,0},{1,5},{5,9},... | collective-permute-start | bytes 393224 | tf_op jit(solution)/shard_map/ppermute | solution.py:138
  91.4 1.3 %collective-permute-done.14 = bf16[16,4096]{1,0:T(8,128)(2,1)S(1)} collective-permute-done((bf16[16,4096]{1,0:T(8,128)(2,1)S(1)}, bf16[16,4096]{1,0:T(8,128)(2,1)S(1)}, u32[]{:S(2)}, u32[]{:S(2)}) %collective-permute-start.14) | collective-permute-done | bytes 131104 | tf_op jit(solution)/shard_map/ppermute | solution.py:138
  92.8 1.7 %collective-permute-done.28 = bf16[16,4096]{1,0:T(8,128)(2,1)S(1)} collective-permute-done((bf16[16,4096]{1,0:T(8,128)(2,1)S(1)}, bf16[16,4096]{1,0:T(8,128)(2,1)S(1)}, u32[]{:S(2)}, u32[]{:S(2)}) %collective-permute-start.28) | collective-permute-done | bytes 131104 | tf_op jit(solution)/shard_map/ppermute | solution.py:138
  95.3 8.3 %fusion.73 = f32[256,2048]{1,0:T(8,128)S(1)} fusion(bf16[256,4096]{1,0:T(8,128)(2,1)S(1)} %convolution_convert_fusion, bf16[4096,2048]{1,0:T(8,128)(2,1)} %param.15), kind=kOutput, calls=%fused_computation.178 | convolution fusion | flops 4294967296 | bytes 20971520 | tf_op jit(solution)/shard_map/dot_general | solution.py:222
  103.7 1.9 %collective-permute-done.29 = bf16[128,2048]{1,0:T(8,128)(2,1)S(1)} collective-permute-done((bf16[128,2048]{1,0:T(8,128)(2,1)S(1)}, bf16[128,2048]{1,0:T(8,128)(2,1)S(1)}, u32[]{:S(2)}, u32[]{:S(2)}) %collective-permute-start.29) | collective-permute-done | bytes 524320 | tf_op jit(solution)/shard_map/ppermute | solution.py:223
  (163 shorter events, 39.4 us)
Async XLA Ops:
  0.0 18.3 %copy-start = (bf16[2048,256]{1,0:T(8,128)(2,1)S(1)}, bf16[2048,256]{1,0:T(8,128)(2,1)}, u32[]{:S(2)}) copy-start(bf16[2048,256]{1,0:T(8,128)(2,1)} %param.14) | copy-start | bytes 3145732
  0.0 9.4 %collective-permute-start = (bf16[128,2048]{1,0:T(8,128)(2,1)}, bf16[128,2048]{1,0:T(8,128)(2,1)S(1)}, u32[]{:S(2)}, u32[]{:S(2)}) collective-permute-start(bf16[128,2048]{1,0:T(8,128)(2,1)} %param.11), channel_id=1, source_target_pairs={{0,1},{1,0},{2,3},{3,2},{4,5},{5,4},{6,7},{7,6},{8,9},{9,8},{10,11... | collective-permute-start | bytes 1572872 | tf_op jit(solution)/shard_map/ppermute | solution.py:166
  20.2 7.4 %collective-permute-start.15 = (bf16[16,4608]{1,0:T(8,128)(2,1)S(1)}, bf16[16,4608]{1,0:T(8,128)(2,1)S(1)}, u32[]{:S(2)}, u32[]{:S(2)}) collective-permute-start(bf16[16,4608]{1,0:T(8,128)(2,1)S(1)} %get-tuple-element.24), channel_id=1, source_target_pairs={{0,4},{4,8},{8,12},{12,14},{14,10},{10,6},{6,2},{2,0},{1,5},{5,9},... | collective-permute-start | bytes 442376 | tf_op jit(solution)/shard_map/ppermute | solution.py:122
  24.2 6.8 %collective-permute-start.1 = (bf16[16,4608]{1,0:T(8,128)(2,1)S(1)}, bf16[16,4608]{1,0:T(8,128)(2,1)S(1)}, u32[]{:S(2)}, u32[]{:S(2)}) collective-permute-start(bf16[16,4608]{1,0:T(8,128)(2,1)S(1)} %get-tuple-element.27), channel_id=1, source_target_pairs={{0,4},{4,8},{8,12},{12,14},{14,10},{10,6},{6,2},{2,0},{1,5},{5,9},... | collective-permute-start | bytes 442376 | tf_op jit(solution)/shard_map/ppermute | solution.py:122
  25.9 5.6 %collective-permute-start.19 = (bf16[16,4608]{1,0:T(8,128)(2,1)S(1)}, bf16[16,4608]{1,0:T(8,128)(2,1)S(1)}, u32[]{:S(2)}, u32[]{:S(2)}) collective-permute-start(bf16[16,4608]{1,0:T(8,128)(2,1)S(1)} %get-tuple-element.25), channel_id=1, source_target_pairs={{0,2},{4,0},{8,4},{12,8},{14,12},{10,14},{6,10},{2,6},{1,3},{5,1},... | collective-permute-start | bytes 442376 | tf_op jit(solution)/shard_map/ppermute | solution.py:124
  27.6 6.0 %collective-permute-start.16 = (bf16[16,4608]{1,0:T(8,128)(2,1)S(1)}, bf16[16,4608]{1,0:T(8,128)(2,1)S(1)}, u32[]{:S(2)}, u32[]{:S(2)}) collective-permute-start(bf16[16,4608]{1,0:T(8,128)(2,1)S(1)} %add_convert_fusion.4), channel_id=1, source_target_pairs={{0,4},{4,8},{8,12},{12,14},{14,10},{10,6},{6,2},{2,0},{1,5},{5,9},... | collective-permute-start | bytes 442376 | tf_op jit(solution)/shard_map/ppermute | solution.py:122
  30.5 9.6 %collective-permute-start.5 = (bf16[16,4608]{1,0:T(8,128)(2,1)S(1)}, bf16[16,4608]{1,0:T(8,128)(2,1)S(1)}, u32[]{:S(2)}, u32[]{:S(2)}) collective-permute-start(bf16[16,4608]{1,0:T(8,128)(2,1)S(1)} %get-tuple-element.26), channel_id=1, source_target_pairs={{0,2},{4,0},{8,4},{12,8},{14,12},{10,14},{6,10},{2,6},{1,3},{5,1},... | collective-permute-start | bytes 442376 | tf_op jit(solution)/shard_map/ppermute | solution.py:124
  34.5 7.0 %collective-permute-start.17 = (bf16[16,4608]{1,0:T(8,128)(2,1)}, bf16[16,4608]{1,0:T(8,128)(2,1)}, u32[]{:S(2)}, u32[]{:S(2)}) collective-permute-start(bf16[16,4608]{1,0:T(8,128)(2,1)} %get-tuple-element.21), channel_id=1, source_target_pairs={{0,4},{4,8},{8,12},{12,14},{14,10},{10,6},{6,2},{2,0},{1,5},{5,9},... | collective-permute-start | bytes 442376 | tf_op jit(solution)/shard_map/ppermute | solution.py:122
  36.3 6.8 %collective-permute-start.2 = (bf16[16,4608]{1,0:T(8,128)(2,1)}, bf16[16,4608]{1,0:T(8,128)(2,1)}, u32[]{:S(2)}, u32[]{:S(2)}) collective-permute-start(bf16[16,4608]{1,0:T(8,128)(2,1)} %get-tuple-element.23), channel_id=1, source_target_pairs={{0,4},{4,8},{8,12},{12,14},{14,10},{10,6},{6,2},{2,0},{1,5},{5,9},... | collective-permute-start | bytes 442376 | tf_op jit(solution)/shard_map/ppermute | solution.py:122
  37.8 5.5 %collective-permute-start.20 = (bf16[16,4608]{1,0:T(8,128)(2,1)}, bf16[16,4608]{1,0:T(8,128)(2,1)}, u32[]{:S(2)}, u32[]{:S(2)}) collective-permute-start(bf16[16,4608]{1,0:T(8,128)(2,1)} %get-tuple-element.22), channel_id=1, source_target_pairs={{0,2},{4,0},{8,4},{12,8},{14,12},{10,14},{6,10},{2,6},{1,3},{5,1},... | collective-permute-start | bytes 442376 | tf_op jit(solution)/shard_map/ppermute | solution.py:124
  44.5 5.8 %collective-permute-start.18 = (bf16[16,4608]{1,0:T(8,128)(2,1)S(1)}, bf16[16,4608]{1,0:T(8,128)(2,1)S(1)}, u32[]{:S(2)}, u32[]{:S(2)}) collective-permute-start(bf16[16,4608]{1,0:T(8,128)(2,1)S(1)} %get-tuple-element.17), channel_id=1, source_target_pairs={{0,4},{4,8},{8,12},{12,14},{14,10},{10,6},{6,2},{2,0},{1,5},{5,9},... | collective-permute-start | bytes 442376 | tf_op jit(solution)/shard_map/ppermute | solution.py:122
  46.1 5.1 %collective-permute-start.21 = (bf16[16,4608]{1,0:T(8,128)(2,1)S(1)}, bf16[16,4608]{1,0:T(8,128)(2,1)S(1)}, u32[]{:S(2)}, u32[]{:S(2)}) collective-permute-start(bf16[16,4608]{1,0:T(8,128)(2,1)S(1)} %get-tuple-element.18), channel_id=1, source_target_pairs={{0,2},{4,0},{8,4},{12,8},{14,12},{10,14},{6,10},{2,6},{1,3},{5,1},... | collective-permute-start | bytes 442376 | tf_op jit(solution)/shard_map/ppermute | solution.py:124
  46.6 5.1 %collective-permute-start.3 = (bf16[16,4608]{1,0:T(8,128)(2,1)S(1)}, bf16[16,4608]{1,0:T(8,128)(2,1)S(1)}, u32[]{:S(2)}, u32[]{:S(2)}) collective-permute-start(bf16[16,4608]{1,0:T(8,128)(2,1)S(1)} %get-tuple-element.20), channel_id=1, source_target_pairs={{0,4},{4,8},{8,12},{12,14},{14,10},{10,6},{6,2},{2,0},{1,5},{5,9},... | collective-permute-start | bytes 442376 | tf_op jit(solution)/shard_map/ppermute | solution.py:122
  48.1 5.1 %collective-permute-start.6 = (bf16[16,4608]{1,0:T(8,128)(2,1)S(1)}, bf16[16,4608]{1,0:T(8,128)(2,1)S(1)}, u32[]{:S(2)}, u32[]{:S(2)}) collective-permute-start(bf16[16,4608]{1,0:T(8,128)(2,1)S(1)} %get-tuple-element.19), channel_id=1, source_target_pairs={{0,2},{4,0},{8,4},{12,8},{14,12},{10,14},{6,10},{2,6},{1,3},{5,1},... | collective-permute-start | bytes 442376 | tf_op jit(solution)/shard_map/ppermute | solution.py:124
  55.4 6.4 %collective-permute-start.4 = (bf16[16,4608]{1,0:T(8,128)(2,1)}, bf16[16,4608]{1,0:T(8,128)(2,1)}, u32[]{:S(2)}, u32[]{:S(2)}) collective-permute-start(bf16[16,4608]{1,0:T(8,128)(2,1)} %get-tuple-element.16), channel_id=1, source_target_pairs={{0,4},{4,8},{8,12},{12,14},{14,10},{10,6},{6,2},{2,0},{1,5},{5,9},... | collective-permute-start | bytes 442376 | tf_op jit(solution)/shard_map/ppermute | solution.py:122
  56.9 5.2 %collective-permute-start.7 = (bf16[16,4608]{1,0:T(8,128)(2,1)S(1)}, bf16[16,4608]{1,0:T(8,128)(2,1)}, u32[]{:S(2)}, u32[]{:S(2)}) collective-permute-start(bf16[16,4608]{1,0:T(8,128)(2,1)S(1)} %get-tuple-element.15), channel_id=1, source_target_pairs={{0,2},{4,0},{8,4},{12,8},{14,12},{10,14},{6,10},{2,6},{1,3},{5,1},... | collective-permute-start | bytes 442376 | tf_op jit(solution)/shard_map/ppermute | solution.py:124
  67.7 7.5 %collective-permute-start.8 = (bf16[16,4096]{1,0:T(8,128)(2,1)S(1)}, bf16[16,4096]{1,0:T(8,128)(2,1)S(1)}, u32[]{:S(2)}, u32[]{:S(2)}) collective-permute-start(bf16[16,4096]{1,0:T(8,128)(2,1)S(1)} %bitcast.132), channel_id=1, source_target_pairs={{0,4},{4,8},{8,12},{12,14},{14,10},{10,6},{6,2},{2,0},{1,5},{5,9},... | collective-permute-start | bytes 393224 | tf_op jit(solution)/shard_map/ppermute | solution.py:138
  69.1 7.5 %collective-permute-start.9 = (bf16[16,4096]{1,0:T(8,128)(2,1)S(1)}, bf16[16,4096]{1,0:T(8,128)(2,1)S(1)}, u32[]{:S(2)}, u32[]{:S(2)}) collective-permute-start(bf16[16,4096]{1,0:T(8,128)(2,1)S(1)} %bitcast.133), channel_id=1, source_target_pairs={{0,2},{4,0},{8,4},{12,8},{14,12},{10,14},{6,10},{2,6},{1,3},{5,1},... | collective-permute-start | bytes 393224 | tf_op jit(solution)/shard_map/ppermute | solution.py:141
  72.8 5.6 %collective-permute-start.22 = (bf16[16,4096]{1,0:T(8,128)(2,1)S(1)}, bf16[16,4096]{1,0:T(8,128)(2,1)S(1)}, u32[]{:S(2)}, u32[]{:S(2)}) collective-permute-start(bf16[16,4096]{1,0:T(8,128)(2,1)S(1)} %bitcast.134), channel_id=1, source_target_pairs={{0,4},{4,8},{8,12},{12,14},{14,10},{10,6},{6,2},{2,0},{1,5},{5,9},... | collective-permute-start | bytes 393224 | tf_op jit(solution)/shard_map/ppermute | solution.py:138
  74.2 6.0 %collective-permute-start.23 = (bf16[16,4096]{1,0:T(8,128)(2,1)S(1)}, bf16[16,4096]{1,0:T(8,128)(2,1)S(1)}, u32[]{:S(2)}, u32[]{:S(2)}) collective-permute-start(bf16[16,4096]{1,0:T(8,128)(2,1)S(1)} %bitcast.135), channel_id=1, source_target_pairs={{0,2},{4,0},{8,4},{12,8},{14,12},{10,14},{6,10},{2,6},{1,3},{5,1},... | collective-permute-start | bytes 393224 | tf_op jit(solution)/shard_map/ppermute | solution.py:141
  75.2 6.4 %collective-permute-start.10 = (bf16[16,4096]{1,0:T(8,128)(2,1)S(1)}, bf16[16,4096]{1,0:T(8,128)(2,1)S(1)}, u32[]{:S(2)}, u32[]{:S(2)}) collective-permute-start(bf16[16,4096]{1,0:T(8,128)(2,1)S(1)} %collective-permute-done.8), channel_id=1, source_target_pairs={{0,4},{4,8},{8,12},{12,14},{14,10},{10,6},{6,2},{2,0},{1,5},{5,9},... | collective-permute-start | bytes 393224 | tf_op jit(solution)/shard_map/ppermute | solution.py:138
  76.6 6.4 %collective-permute-start.11 = (bf16[16,4096]{1,0:T(8,128)(2,1)S(1)}, bf16[16,4096]{1,0:T(8,128)(2,1)S(1)}, u32[]{:S(2)}, u32[]{:S(2)}) collective-permute-start(bf16[16,4096]{1,0:T(8,128)(2,1)S(1)} %collective-permute-done.9), channel_id=1, source_target_pairs={{0,2},{4,0},{8,4},{12,8},{14,12},{10,14},{6,10},{2,6},{1,3},{5,1},... | collective-permute-start | bytes 393224 | tf_op jit(solution)/shard_map/ppermute | solution.py:141
  78.4 6.1 %collective-permute-start.24 = (bf16[16,4096]{1,0:T(8,128)(2,1)S(1)}, bf16[16,4096]{1,0:T(8,128)(2,1)S(1)}, u32[]{:S(2)}, u32[]{:S(2)}) collective-permute-start(bf16[16,4096]{1,0:T(8,128)(2,1)S(1)} %collective-permute-done.22), channel_id=1, source_target_pairs={{0,4},{4,8},{8,12},{12,14},{14,10},{10,6},{6,2},{2,0},{1,5},{5,9},... | collective-permute-start | bytes 393224 | tf_op jit(solution)/shard_map/ppermute | solution.py:138
  80.2 5.8 %collective-permute-start.25 = (bf16[16,4096]{1,0:T(8,128)(2,1)S(1)}, bf16[16,4096]{1,0:T(8,128)(2,1)S(1)}, u32[]{:S(2)}, u32[]{:S(2)}) collective-permute-start(bf16[16,4096]{1,0:T(8,128)(2,1)S(1)} %collective-permute-done.23), channel_id=1, source_target_pairs={{0,2},{4,0},{8,4},{12,8},{14,12},{10,14},{6,10},{2,6},{1,3},{5,1},... | collective-permute-start | bytes 393224 | tf_op jit(solution)/shard_map/ppermute | solution.py:141
  81.7 6.0 %collective-permute-start.12 = (bf16[16,4096]{1,0:T(8,128)(2,1)S(1)}, bf16[16,4096]{1,0:T(8,128)(2,1)S(1)}, u32[]{:S(2)}, u32[]{:S(2)}) collective-permute-start(bf16[16,4096]{1,0:T(8,128)(2,1)S(1)} %collective-permute-done.10), channel_id=1, source_target_pairs={{0,4},{4,8},{8,12},{12,14},{14,10},{10,6},{6,2},{2,0},{1,5},{5,9},... | collective-permute-start | bytes 393224 | tf_op jit(solution)/shard_map/ppermute | solution.py:138
  83.1 8.3 %collective-permute-start.13 = (bf16[16,4096]{1,0:T(8,128)(2,1)S(1)}, bf16[16,4096]{1,0:T(8,128)(2,1)S(1)}, u32[]{:S(2)}, u32[]{:S(2)}) collective-permute-start(bf16[16,4096]{1,0:T(8,128)(2,1)S(1)} %collective-permute-done.11), channel_id=1, source_target_pairs={{0,2},{4,0},{8,4},{12,8},{14,12},{10,14},{6,10},{2,6},{1,3},{5,1},... | collective-permute-start | bytes 393224 | tf_op jit(solution)/shard_map/ppermute | solution.py:141
  84.6 5.0 %collective-permute-start.26 = (bf16[16,4096]{1,0:T(8,128)(2,1)S(1)}, bf16[16,4096]{1,0:T(8,128)(2,1)S(1)}, u32[]{:S(2)}, u32[]{:S(2)}) collective-permute-start(bf16[16,4096]{1,0:T(8,128)(2,1)S(1)} %collective-permute-done.24), channel_id=1, source_target_pairs={{0,4},{4,8},{8,12},{12,14},{14,10},{10,6},{6,2},{2,0},{1,5},{5,9},... | collective-permute-start | bytes 393224 | tf_op jit(solution)/shard_map/ppermute | solution.py:138
  86.0 6.8 %collective-permute-start.27 = (bf16[16,4096]{1,0:T(8,128)(2,1)S(1)}, bf16[16,4096]{1,0:T(8,128)(2,1)S(1)}, u32[]{:S(2)}, u32[]{:S(2)}) collective-permute-start(bf16[16,4096]{1,0:T(8,128)(2,1)S(1)} %collective-permute-done.25), channel_id=1, source_target_pairs={{0,2},{4,0},{8,4},{12,8},{14,12},{10,14},{6,10},{2,6},{1,3},{5,1},... | collective-permute-start | bytes 393224 | tf_op jit(solution)/shard_map/ppermute | solution.py:141
  87.7 5.0 %collective-permute-start.14 = (bf16[16,4096]{1,0:T(8,128)(2,1)S(1)}, bf16[16,4096]{1,0:T(8,128)(2,1)S(1)}, u32[]{:S(2)}, u32[]{:S(2)}) collective-permute-start(bf16[16,4096]{1,0:T(8,128)(2,1)S(1)} %collective-permute-done.12), channel_id=1, source_target_pairs={{0,4},{4,8},{8,12},{12,14},{14,10},{10,6},{6,2},{2,0},{1,5},{5,9},... | collective-permute-start | bytes 393224 | tf_op jit(solution)/shard_map/ppermute | solution.py:138
  89.5 5.0 %collective-permute-start.28 = (bf16[16,4096]{1,0:T(8,128)(2,1)S(1)}, bf16[16,4096]{1,0:T(8,128)(2,1)S(1)}, u32[]{:S(2)}, u32[]{:S(2)}) collective-permute-start(bf16[16,4096]{1,0:T(8,128)(2,1)S(1)} %collective-permute-done.26), channel_id=1, source_target_pairs={{0,4},{4,8},{8,12},{12,14},{14,10},{10,6},{6,2},{2,0},{1,5},{5,9},... | collective-permute-start | bytes 393224 | tf_op jit(solution)/shard_map/ppermute | solution.py:138
  95.3 11.2 %copy-start.1 = (bf16[2048,256]{1,0:T(8,128)(2,1)S(1)}, bf16[2048,256]{1,0:T(8,128)(2,1)}, u32[]{:S(2)}) copy-start(bf16[2048,256]{1,0:T(8,128)(2,1)} %param.14) | copy-start | bytes 3145732
  103.7 2.0 %collective-permute-start.29 = (bf16[128,2048]{1,0:T(8,128)(2,1)S(1)}, bf16[128,2048]{1,0:T(8,128)(2,1)S(1)}, u32[]{:S(2)}, u32[]{:S(2)}) collective-permute-start(bf16[128,2048]{1,0:T(8,128)(2,1)S(1)} %slice.219), channel_id=1, source_target_pairs={{0,1},{1,0},{2,3},{3,2},{4,5},{5,4},{6,7},{7,6},{8,9},{9,8},{10,11... | collective-permute-start | bytes 1572872 | tf_op jit(solution)/shard_map/ppermute | solution.py:223
  (19 other events, 44.6 us)
